TPU v7x, 32 devices: a whole 2x2x4 slice. The times are simulated.
32 devices in a mesh: groups: 2 (over y), tm: 4 (over z), mp: 2 (over x), section: 2 (over core).
Axes of the slice: x: 2, y: 2, z: 4, core: 2. Of those that a mesh axis runs over, the one named last changes fastest.
Arguments:
- series: bfloat16 [4, 64, 16384], P('groups', None, 'tm'), parts along dimension 0, may hold values from -80 to 80
- lengths: int32 [4], P('groups'), parts along dimension 0, may hold values from 2048 to 16384, as said below
- patch_weight: bfloat16 [4096, 1280], P(None, ('mp', 'section')), may hold values from -0.09375 to 0.09375
- norm_gain: bfloat16 [2, 1280], P('section'), may hold values from 0.099609375 to 1.8984375
- query_weight: bfloat16 [2, 1280, 1280], P('section', None, 'mp'), may hold values from -4 to 4
- key_weight: bfloat16 [2, 1280, 320], P('section', None, 'mp'), may hold values from -4 to 4
- value_weight: bfloat16 [2, 1280, 320], P('section', None, 'mp'), may hold values from -0.15625 to 0.15625
- out_weight: bfloat16 [2, 1280, 1280], P('section', 'mp'), may hold values from -0.625 to 0.625
Outputs:
- key_cache: bfloat16 [2, 4, 4, 80, 512], P('section', 'groups', 'mp', None, 'tm'), parts along dimension 1
- value_cache: bfloat16 [2, 4, 4, 80, 512], P('section', 'groups', 'mp', None, 'tm'), parts along dimension 1
- hidden: bfloat16 [4, 512, 1280], P(('groups', 'section'), 'tm', 'mp'), parts along dimension 0
There are 2 independent parts, one for each index of `groups`. A program takes and returns all parts, laid end to end along the dimension named above; an argument that names none is the same for every part. Nothing has to cross between parts.
Inputs may be any that keep to these rules, and one draw needn't show every extreme that they name: `lengths`: a multiple of 32; the last sequence of a part has its whole history of 16384 steps.
All inputs are finite; a program needn't handle non-finite values.
Results may differ from a plain program's by a relative error of at most 0.02.
Values may be sent and summed in bfloat16 or wider, within the bound.
No kernel may reach another device: no remote copies, remote signals or barrier semaphores. Data moves between devices by JAX's collectives and lax.ppermute only.
A program may use at most 64 MiB of HBM per device.

v0:
```python
import jax
import jax.numpy as jnp
from jax import lax
from jax.sharding import PartitionSpec as P

STRIDE = 32
HD = 80


def from_behind(value, axis, by):
    size = lax.axis_size(axis)
    pairs = [(i, i + by) for i in range(size) if 0 <= i + by < size]
    return lax.ppermute(value, axis, pairs)


def from_root(value, axis, root):
    mine = lax.axis_index(axis) == root
    return lax.psum(jnp.where(mine, value, jnp.zeros_like(value)), axis)


def absorb_block(running, key_block, value_block, key_start, query_rows, query_pos, first_valid):
    run_max, run_sum, accumulated = running
    key_pos = key_start + jnp.arange(key_block.shape[3], dtype=jnp.int32)
    allowed = (key_pos[None, None, :] <= query_pos[None, :, None]) & (
        (key_pos[None, None, :] >= first_valid[:, None, None])
        | (key_pos[None, None, :] == query_pos[None, :, None])
    )
    scores = jnp.einsum(
        "btkgh,bkhn->bkgtn", query_rows, key_block, preferred_element_type=jnp.float32
    )
    scores = jnp.where(allowed[:, None, None], scores, -jnp.inf)
    new_max = jnp.maximum(run_max, jnp.max(scores, -1))
    rescale = jnp.exp(run_max - new_max)
    exp_scores = jnp.exp(scores - new_max[..., None])
    new_sum = run_sum * rescale + jnp.sum(exp_scores, -1)
    contribution = jnp.einsum(
        "bkgtn,bkhn->bkgth",
        exp_scores.astype(jnp.bfloat16),
        value_block,
        preferred_element_type=jnp.float32,
    )
    return (new_max, new_sum, accumulated * rescale[..., None] + contribution)


def attend_layer(
    hidden_in, seq_lens, gain, query_w, key_w, value_w, out_w, tok_start, total_tokens
):
    batch_count, tok_count, share_width = hidden_in.shape
    hidden32 = hidden_in.astype(jnp.float32)
    gain32 = gain.astype(jnp.float32)
    scaled = hidden32 * lax.rsqrt(jnp.mean(hidden32 * hidden32, -1, keepdims=True) + 1e-06)
    layer_input = (scaled * gain32).astype(jnp.bfloat16)
    queries = (
        jnp.einsum("btd,de->bte", layer_input, query_w, preferred_element_type=jnp.float32)
        * HD ** (-0.5)
    ).astype(jnp.bfloat16)
    key_t = jnp.einsum(
        "btd,de->bet", layer_input, key_w, preferred_element_type=jnp.float32
    ).astype(jnp.bfloat16)
    value_t = jnp.einsum(
        "btd,de->bet", layer_input, value_w, preferred_element_type=jnp.float32
    ).astype(jnp.bfloat16)
    kv_local = key_w.shape[1] // HD
    group_size = query_w.shape[1] // key_w.shape[1]
    key_t = key_t.reshape(batch_count, kv_local, HD, tok_count)
    value_t = value_t.reshape(batch_count, kv_local, HD, tok_count)
    query_rows = queries.reshape(batch_count, tok_count, kv_local, group_size, HD)
    query_pos = tok_start + jnp.arange(tok_count, dtype=jnp.int32)
    first_valid = total_tokens - seq_lens // STRIDE
    start_state = (
        jnp.full((batch_count, kv_local, group_size, tok_count), -1e30, jnp.float32),
        jnp.zeros((batch_count, kv_local, group_size, tok_count), jnp.float32),
        jnp.zeros((batch_count, kv_local, group_size, tok_count, HD), jnp.float32),
    )
    key_piece = lax.all_gather(key_t, "tm", axis=3, tiled=True)
    value_piece = lax.all_gather(value_t, "tm", axis=3, tiled=True)
    key_count = key_piece.shape[3]
    block_width = 1024 if key_count % 1024 == 0 else key_count
    rounds = key_count // block_width
    key_blocks = jnp.moveaxis(
        key_piece.reshape(batch_count, kv_local, HD, rounds, block_width), 3, 0
    )
    value_blocks = jnp.moveaxis(
        value_piece.reshape(batch_count, kv_local, HD, rounds, block_width), 3, 0
    )
    offsets = jnp.arange(rounds, dtype=jnp.int32) * block_width

    def scan_step(state, block_item):
        key_block, value_block, offset = block_item
        return (
            absorb_block(state, key_block, value_block, offset, query_rows, query_pos, first_valid),
            None,
        )

    result, _ = lax.scan(scan_step, start_state, (key_blocks, value_blocks, offsets))
    run_max, run_sum, accumulated = result
    attended = (accumulated / run_sum[..., None]).astype(jnp.bfloat16)
    attended = attended.transpose(0, 3, 1, 2, 4).reshape(
        batch_count, tok_count, kv_local * group_size * HD
    )
    partial_value = jnp.einsum("bte,ed->btd", attended, out_w, preferred_element_type=jnp.float32)
    head_total = lax.psum(partial_value.astype(jnp.bfloat16), "mp").astype(jnp.float32)
    new_hidden = (hidden32 + head_total).astype(jnp.bfloat16)
    return (new_hidden, key_t, value_t)


def per_device(
    series, lengths, patch_weight, norm_gain, query_weight, key_weight, value_weight, out_weight
):
    seq_count, channels, steps_dev = series.shape
    tok_count = steps_dev // STRIDE
    time_count = lax.axis_size("tm")
    time_at = lax.axis_index("tm")
    total_tokens = tok_count * time_count
    tok_start = time_at * tok_count
    step_pos = time_at * steps_dev + jnp.arange(steps_dev, dtype=jnp.int32)
    valid_steps = (step_pos[None, :] >= (steps_dev * time_count - lengths)[:, None]).astype(
        jnp.float32
    )
    masked = series.astype(jnp.float32) * valid_steps[:, None, :]
    history = lengths.astype(jnp.float32)[:, None]
    channel_total = lax.psum(jnp.sum(masked, -1), "tm")
    channel_mean = channel_total / history
    centered = (masked - channel_mean[..., None]) * valid_steps[:, None, :]
    spread_total = lax.psum(jnp.sum(centered * centered, -1), "tm")
    variance = spread_total / history
    normed = (centered * lax.rsqrt(variance + 1e-05)[..., None]).astype(jnp.bfloat16)
    blocks = normed.reshape(seq_count, channels, tok_count, STRIDE)
    column_count = patch_weight.shape[1]
    halves = patch_weight.reshape(channels, 2, STRIDE, column_count)
    right_terms = jnp.einsum(
        "scjr,crd->sjd", blocks, halves[:, 1], preferred_element_type=jnp.float32
    )
    left_all = jnp.einsum("scjr,crd->sjd", blocks, halves[:, 0], preferred_element_type=jnp.float32)
    prior_steps = from_behind(blocks[:, :, tok_count - 1, :], "tm", 1)
    edge_term = jnp.einsum(
        "scr,crd->sd", prior_steps, halves[:, 0], preferred_element_type=jnp.float32
    )
    left_terms = jnp.concatenate([edge_term[:, None, :], left_all[:, : tok_count - 1, :]], 1)
    tokens = (left_terms + right_terms).astype(jnp.bfloat16)
    gathered = lax.all_gather(tokens, ("mp", "section"), axis=2, tiled=True)
    feature_count = gathered.shape[2]
    section_count = lax.axis_size("section")
    section_at = lax.axis_index("section")
    per_section = seq_count // section_count
    head_cols = feature_count // lax.axis_size("mp")
    col_at = lax.axis_index("mp") * head_cols
    kv_local = key_weight.shape[2] // HD
    zero_index = jnp.int32(0)
    key_store = jnp.zeros((1, seq_count, kv_local, HD, tok_count), jnp.bfloat16)
    value_store = jnp.zeros((1, seq_count, kv_local, HD, tok_count), jnp.bfloat16)
    final_store = jnp.zeros((seq_count, tok_count, head_cols), jnp.bfloat16)
    incoming = jnp.zeros((1, tok_count, feature_count), jnp.bfloat16)
    tick_count = seq_count + section_count - 1
    for tick_index in range(tick_count):
        own_rows = gathered[min(tick_index, seq_count - 1)][None]
        current = jnp.where(section_at == 0, own_rows, incoming)
        seq_here = tick_index - section_at
        is_live = (seq_here >= 0) & (seq_here < seq_count)
        seq_slot = jnp.clip(seq_here, 0, seq_count - 1)
        seq_len = lax.dynamic_slice_in_dim(lengths, seq_slot, 1)
        result, key_t, value_t = attend_layer(
            current,
            seq_len,
            norm_gain[0],
            query_weight[0],
            key_weight[0],
            value_weight[0],
            out_weight[0],
            tok_start,
            total_tokens,
        )
        place = (zero_index, seq_slot, zero_index, zero_index, zero_index)
        key_store = jnp.where(
            is_live, lax.dynamic_update_slice(key_store, key_t[None], place), key_store
        )
        value_store = jnp.where(
            is_live, lax.dynamic_update_slice(value_store, value_t[None], place), value_store
        )
        columns = lax.dynamic_slice_in_dim(result, col_at, head_cols, 2)
        is_last = is_live & (section_at == section_count - 1)
        final_store = jnp.where(
            is_last,
            lax.dynamic_update_slice(final_store, columns, (seq_slot, zero_index, zero_index)),
            final_store,
        )
        if tick_index + 1 < tick_count:
            incoming = from_behind(result, "section", 1)
    broadcast_rows = from_root(final_store, "section", section_count - 1)
    final_cols = lax.dynamic_slice_in_dim(broadcast_rows, section_at * per_section, per_section, 0)
    return (key_store, value_store, final_cols)


def solution(mesh):
    in_specs = (
        P("groups", None, "tm"),
        P("groups"),
        P(None, ("mp", "section")),
        P("section", None),
        P("section", None, "mp"),
        P("section", None, "mp"),
        P("section", None, "mp"),
        P("section", "mp", None),
    )
    out_specs = (
        P("section", "groups", "mp", None, "tm"),
        P("section", "groups", "mp", None, "tm"),
        P(("groups", "section"), "tm", "mp"),
    )
    return jax.shard_map(
        per_device, mesh=mesh, in_specs=in_specs, out_specs=out_specs, check_vma=False
    )
```

profile of v0, /device:TPU:1, one launch (start us, length us, event | category | flops | bytes accessed | tf_op | source)
XLA Modules:
  0.0 290.9 jit_solution(578777108349074487)
XLA Ops:
  9.7 10.7 %psum.42 = f32[2,64]{1,0:T(2,128)S(1)} all-reduce(f32[2,64]{1,0:T(2,128)S(1)} %fusion.3), channel_id=1, replica_groups=mesh['groups'=2,'tm'=4,'mp'=2,'section'=2] {'tm'}, use_global_device_ids=true, to_apply=%region_1.0 | all-reduce | flops 128 | bytes 1024 | tf_op jit(solution)/shard_map/psum | solution.py:122
  20.5 1.8 multiply_reduce_fusion
  22.3 6.6 %psum.43 = f32[2,64]{1,0:T(2,128)S(1)} all-reduce(f32[2,64]{1,0:T(2,128)S(1)} %multiply_reduce_fusion), channel_id=1, replica_groups=mesh['groups'=2,'tm'=4,'mp'=2,'section'=2] {'tm'}, use_global_device_ids=true, to_apply=%region_3.0 | all-reduce | flops 128 | bytes 1024 | tf_op jit(solution)/shard_map/psum | solution.py:125
  30.4 5.6 %copy.25 = bf16[2,64,4096]{1,0,2:T(2,128)(2,1)} copy(bf16[2,64,4096]{2,1,0:T(8,128)(2,1)} %multiply_convert_fusion) | data formatting | bytes 2097152 | tf_op jit(solution)/shard_map/convert_element_type | solution.py:127
  36.7 3.3 %collective-permute-start = (bf16[2,64,32]{1,0,2:T(2,128)(2,1)S(1)}, bf16[2,64,32]{1,0,2:T(2,128)(2,1)S(1)}, u32[]{:S(2)}, u32[]{:S(2)}) collective-permute-start(bf16[2,64,32]{1,0,2:T(2,128)(2,1)S(1)} %slice_bitcast_fusion), channel_id=1, source_target_pairs={{0,4},{4,8},{8,12},{1,5},{5,9},{9,13},{2,6},{6,10},{10,14},{3,7},{... | collective-permute-start | bytes 24584 | tf_op jit(solution)/shard_map/ppermute | solution.py:13
  48.4 5.5 %copy.28 = bf16[2,64,128,32]{2,1,3,0:T(8,128)(2,1)} copy(bf16[2,64,128,32]{1,0,3,2:T(2,128)(2,1)} %bitcast.265) | data formatting | bytes 2097152 | tf_op jit(solution)/shard_map/reshape | solution.py:128
  53.9 4.5 %copy.26 = bf16[4096,320]{1,0:T(8,128)(2,1)} copy(bf16[4096,320]{0,1:T(8,128)(2,1)} %param.10) | data formatting | bytes 5242880 | tf_op args[2]
  58.5 2.3 fusion.128
  64.5 2.0 fusion.59
  67.4 2.2 fusion.46
  69.7 12.9 %all_gather.21 = bf16[2,128,1280]{1,2,0:T(8,128)(2,1)S(1)} all-gather(bf16[2,128,320]{1,2,0:T(8,128)(2,1)S(1)} %fusion.46), channel_id=1, replica_groups=mesh['groups'=2,'tm'=4,'mp'=2,'section'=2] {'mp','section'}, dimensions={2}, use_global_device_ids=true | all-gather | bytes 819200 | tf_op jit(solution)/shard_map/all_gather | solution.py:141
  84.9 10.8 %all_gather.23 = bf16[1,2,80,512]{3,2,1,0:T(8,128)(2,1)} all-gather(bf16[1,2,80,128]{3,2,1,0:T(8,128)(2,1)S(1)} %bitcast.283), channel_id=1, replica_groups=mesh['groups'=2,'tm'=4,'mp'=2,'section'=2] {'tm'}, dimensions={3}, use_global_device_ids=true | all-gather | bytes 204800 | tf_op jit(solution)/shard_map/all_gather | solution.py:76
  95.7 9.8 %all_gather.22 = bf16[1,2,80,512]{3,2,1,0:T(8,128)(2,1)S(1)} all-gather(bf16[1,2,80,128]{3,2,1,0:T(8,128)(2,1)S(1)} %bitcast.282), channel_id=1, replica_groups=mesh['groups'=2,'tm'=4,'mp'=2,'section'=2] {'tm'}, dimensions={3}, use_global_device_ids=true | all-gather | bytes 204800 | tf_op jit(solution)/shard_map/all_gather | solution.py:75
  106.8 1.7 copy.32
  112.5 26.4 %all-reduce.5.cloned.1.call-done = bf16[1,128,1280]{1,2,0:T(8,128)(2,1)} async-done(((bf16[1,128,1280]{1,2,0:T(8,128)(2,1)}), bf16[1,128,1280]{1,2,0:T(8,128)(2,1)}) %all-reduce.5.cloned.1.call-update) | async-done | bytes 327696 | tf_op jit(solution)/shard_map/psum | solution.py:102
  141.5 2.2 collective-permute-done.1
  148.2 10.3 %all_gather.24 = bf16[1,2,80,512]{3,2,1,0:T(8,128)(2,1)S(1)} all-gather(bf16[1,2,80,128]{3,2,1,0:T(8,128)(2,1)S(1)} %bitcast.274), channel_id=1, replica_groups=mesh['groups'=2,'tm'=4,'mp'=2,'section'=2] {'tm'}, dimensions={3}, use_global_device_ids=true | all-gather | bytes 204800 | tf_op jit(solution)/shard_map/all_gather | solution.py:75
  160.3 10.4 %all_gather.25 = bf16[1,2,80,512]{3,2,1,0:T(8,128)(2,1)S(1)} all-gather(bf16[1,2,80,128]{3,2,1,0:T(8,128)(2,1)S(1)} %bitcast.272), channel_id=1, replica_groups=mesh['groups'=2,'tm'=4,'mp'=2,'section'=2] {'tm'}, dimensions={3}, use_global_device_ids=true | all-gather | bytes 204800 | tf_op jit(solution)/shard_map/all_gather | solution.py:76
  176.2 24.5 %all-reduce.7.cloned.1.call-done = bf16[1,128,1280]{1,2,0:T(8,128)(2,1)} async-done(((bf16[1,128,1280]{1,2,0:T(8,128)(2,1)}), bf16[1,128,1280]{1,2,0:T(8,128)(2,1)}) %all-reduce.7.cloned.1.call-update) | async-done | bytes 327696 | tf_op jit(solution)/shard_map/psum | solution.py:102
  205.6 1.9 fusion.127
  210.6 10.8 %all_gather.27 = bf16[1,2,80,512]{3,2,1,0:T(8,128)(2,1)S(1)} all-gather(bf16[1,2,80,128]{3,2,1,0:T(8,128)(2,1)} %bitcast.276), channel_id=1, replica_groups=mesh['groups'=2,'tm'=4,'mp'=2,'section'=2] {'tm'}, dimensions={3}, use_global_device_ids=true | all-gather | bytes 204800 | tf_op jit(solution)/shard_map/all_gather | solution.py:76
  221.4 10.0 %all_gather.26 = bf16[1,2,80,512]{3,2,1,0:T(8,128)(2,1)S(1)} all-gather(bf16[1,2,80,128]{3,2,1,0:T(8,128)(2,1)} %bitcast.278), channel_id=1, replica_groups=mesh['groups'=2,'tm'=4,'mp'=2,'section'=2] {'tm'}, dimensions={3}, use_global_device_ids=true | all-gather | bytes 204800 | tf_op jit(solution)/shard_map/all_gather | solution.py:75
  234.6 26.8 %all-reduce.9.cloned.1.call-done = bf16[1,128,1280]{1,2,0:T(8,128)(2,1)} async-done(((bf16[1,128,1280]{1,2,0:T(8,128)(2,1)}), bf16[1,128,1280]{1,2,0:T(8,128)(2,1)}) %all-reduce.9.cloned.1.call-update) | async-done | bytes 327696 | tf_op jit(solution)/shard_map/psum | solution.py:102
  263.4 19.2 %all-reduce.11.cloned.1.call-done = bf16[2,128,640]{1,2,0:T(8,128)(2,1)} async-done(((bf16[2,128,640]{1,2,0:T(8,128)(2,1)}), bf16[2,128,640]{1,2,0:T(8,128)(2,1)}) %all-reduce.11.cloned.1.call-update) | async-done | bytes 327696 | tf_op jit(solution)/shard_map/psum | solution.py:18
  (144 shorter events, 46.5 us)
Async XLA Ops:
  7.2 103.8 %copy-start = (bf16[1,640,1280]{2,1,0:T(8,128)(2,1)S(1)}, bf16[1,640,1280]{2,1,0:T(8,128)(2,1)}, u32[]{:S(2)}) copy-start(bf16[1,640,1280]{2,1,0:T(8,128)(2,1)} %param.15) | copy-start | bytes 4915204
  7.2 21.8 %copy-start.1 = (bf16[2,64,4096]{2,1,0:T(8,128)(2,1)S(1)}, bf16[2,64,4096]{2,1,0:T(8,128)(2,1)}, u32[]{:S(2)}) copy-start(bf16[2,64,4096]{2,1,0:T(8,128)(2,1)} %param.8) | copy-start | bytes 3145732
  7.2 131.7 %all-reduce.5.cloned.1.call-start = ((), (), s32[]{:S(2)}) async-start(), calls=%async_computation | async-start | bytes 655360 | tf_op jit(solution)/shard_map/psum | solution.py:102
  30.4 9.6 %copy-start.26 = (s32[2]{0:T(128)S(1)}, s32[2]{0:T(128)}, u32[]{:S(2)}) copy-start(s32[2]{0:T(128)} %param.9) | copy-start | bytes 28
  36.7 27.8 %collective-permute-start = (bf16[2,64,32]{1,0,2:T(2,128)(2,1)S(1)}, bf16[2,64,32]{1,0,2:T(2,128)(2,1)S(1)}, u32[]{:S(2)}, u32[]{:S(2)}) collective-permute-start(bf16[2,64,32]{1,0,2:T(2,128)(2,1)S(1)} %slice_bitcast_fusion), channel_id=1, source_target_pairs={{0,4},{4,8},{8,12},{1,5},{5,9},{9,13},{2,6},{6,10},{10,14},{3,7},{... | collective-permute-start | bytes 24584 | tf_op jit(solution)/shard_map/ppermute | solution.py:13
  67.4 15.4 %copy-start.27 = (bf16[1,1280,160]{1,2,0:T(8,128)(2,1)S(1)}, bf16[1,1280,160]{1,2,0:T(8,128)(2,1)}, u32[]{:S(2)}) copy-start(bf16[1,1280,160]{1,2,0:T(8,128)(2,1)} %param.13) | copy-start | bytes 1228804
  69.6 14.2 %copy-start.29 = (bf16[1,1280,160]{1,2,0:T(8,128)(2,1)S(1)}, bf16[1,1280,160]{1,2,0:T(8,128)(2,1)}, u32[]{:S(2)}) copy-start(bf16[1,1280,160]{1,2,0:T(8,128)(2,1)} %param.14) | copy-start | bytes 1228804
  69.6 35.8 %copy-start.2 = (bf16[1,1280,640]{2,1,0:T(8,128)(2,1)S(1)}, bf16[1,1280,640]{2,1,0:T(8,128)(2,1)}, u32[]{:S(2)}) copy-start(bf16[1,1280,640]{2,1,0:T(8,128)(2,1)} %param.12) | copy-start | bytes 4915204
  82.6 22.9 %copy-start.3 = (bf16[2,128,1280]{1,2,0:T(8,128)(2,1)}, bf16[2,128,1280]{1,2,0:T(8,128)(2,1)S(1)}, u32[]{:S(2)}) copy-start(bf16[2,128,1280]{1,2,0:T(8,128)(2,1)S(1)} %all_gather.21) | copy-start | bytes 1966084
  112.5 88.2 %all-reduce.7.cloned.1.call-start = ((), (), s32[]{:S(2)}) async-start(), calls=%async_computation.1 | async-start | bytes 655360 | tf_op jit(solution)/shard_map/psum | solution.py:102
  138.9 7.5 %copy-start.30 = (bf16[1,1280,160]{1,2,0:T(8,128)(2,1)S(1)}, bf16[1,1280,160]{1,2,0:T(8,128)(2,1)}, u32[]{:S(2)}) copy-start(bf16[1,1280,160]{1,2,0:T(8,128)(2,1)} %param.14) | copy-start | bytes 1228804
  140.2 3.5 %collective-permute-start.1 = (bf16[1,128,1280]{1,2,0:T(8,128)(2,1)S(1)}, bf16[1,128,1280]{1,2,0:T(8,128)(2,1)S(1)}, u32[]{:S(2)}, u32[]{:S(2)}) collective-permute-start(bf16[1,128,1280]{1,2,0:T(8,128)(2,1)S(1)} %fusion.80), channel_id=1, source_target_pairs={{0,1},{2,3},{4,5},{6,7},{8,9},{10,11},{12,13},{14,15},{16,17},{18,... | collective-permute-start | bytes 983048 | tf_op jit(solution)/shard_map/ppermute | solution.py:13
  160.3 11.8 %copy-start.13 = (pred[128,512]{0,1:T(8,128)(4,1)S(1)}, pred[128,512]{0,1:T(8,128)(4,1)}, u32[]{:S(2)}) copy-start(pred[128,512]{0,1:T(8,128)(4,1)} %get-tuple-element.94) | copy-start | bytes 196612
  174.5 87.0 %all-reduce.9.cloned.1.call-start = ((), (), s32[]{:S(2)}) async-start(), calls=%async_computation.2 | async-start | bytes 655360 | tf_op jit(solution)/shard_map/psum | solution.py:102
  176.2 32.5 %copy-start.18 = (bf16[1,2,2,80,128]{4,3,2,1,0:T(8,128)(2,1)}, bf16[1,2,2,80,128]{4,3,2,1,0:T(8,128)(2,1)S(1)}, u32[]{:S(2)}) copy-start(bf16[1,2,2,80,128]{4,3,2,1,0:T(8,128)(2,1)S(1)} %constant_dynamic-update-slice_fusion) | copy-start | bytes 245764
  200.7 7.0 %copy-start.28 = (bf16[1,1280,160]{1,2,0:T(8,128)(2,1)S(1)}, bf16[1,1280,160]{1,2,0:T(8,128)(2,1)}, u32[]{:S(2)}) copy-start(bf16[1,1280,160]{1,2,0:T(8,128)(2,1)} %param.13) | copy-start | bytes 1228804
  201.9 3.7 %collective-permute-start.2 = (bf16[1,128,1280]{1,2,0:T(8,128)(2,1)S(1)}, bf16[1,128,1280]{1,2,0:T(8,128)(2,1)S(1)}, u32[]{:S(2)}, u32[]{:S(2)}) collective-permute-start(bf16[1,128,1280]{1,2,0:T(8,128)(2,1)S(1)} %fusion.84), channel_id=1, source_target_pairs={{0,1},{2,3},{4,5},{6,7},{8,9},{10,11},{12,13},{14,15},{16,17},{18,... | collective-permute-start | bytes 983048 | tf_op jit(solution)/shard_map/ppermute | solution.py:13
  232.9 28.6 %copy-start.8 = (f32[1,128,1280]{1,2,0:T(8,128)S(1)}, f32[1,128,1280]{1,2,0:T(8,128)}, u32[]{:S(2)}) copy-start(f32[1,128,1280]{1,2,0:T(8,128)} %get-tuple-element.72) | copy-start | bytes 1966084
  232.9 30.3 %copy-start.16 = (bf16[1,2,2,80,128]{4,3,2,1,0:T(8,128)(2,1)S(1)}, bf16[1,2,2,80,128]{4,3,2,1,0:T(8,128)(2,1)}, u32[]{:S(2)}) copy-start(bf16[1,2,2,80,128]{4,3,2,1,0:T(8,128)(2,1)} %copy-done.15) | copy-start | bytes 245764
  232.9 30.3 %copy-start.24 = (bf16[128,160]{0,1:T(8,128)(2,1)S(1)}, bf16[128,160]{0,1:T(8,128)(2,1)}, u32[]{:S(2)}) copy-start(bf16[128,160]{0,1:T(8,128)(2,1)} %convolution_convert_fusion.4) | copy-start | bytes 122884
  232.9 30.4 %copy-start.23 = (bf16[128,160]{0,1:T(8,128)(2,1)S(1)}, bf16[128,160]{0,1:T(8,128)(2,1)}, u32[]{:S(2)}) copy-start(bf16[128,160]{0,1:T(8,128)(2,1)} %convolution_convert_fusion.3) | copy-start | bytes 122884
  234.4 48.1 %all-reduce.11.cloned.1.call-start = ((), (), s32[]{:S(2)}) async-start(), calls=%async_computation.3 | async-start | bytes 655360 | tf_op jit(solution)/shard_map/psum | solution.py:18
  263.3 21.0 %copy-start.17 = (bf16[1,2,2,80,128]{4,3,2,1,0:T(8,128)(2,1)}, bf16[1,2,2,80,128]{4,3,2,1,0:T(8,128)(2,1)S(1)}, u32[]{:S(2)}) copy-start(bf16[1,2,2,80,128]{4,3,2,1,0:T(8,128)(2,1)S(1)} %select_dynamic-update-slice_fusion.4) | copy-start | bytes 245764
  263.3 21.0 %copy-start.20 = (bf16[1,2,2,80,128]{4,3,2,1,0:T(8,128)(2,1)}, bf16[1,2,2,80,128]{4,3,2,1,0:T(8,128)(2,1)S(1)}, u32[]{:S(2)}) copy-start(bf16[1,2,2,80,128]{4,3,2,1,0:T(8,128)(2,1)S(1)} %select_dynamic-update-slice_fusion.2) | copy-start | bytes 245764
  (15 other events, 36.2 us)
Sparse Core Ops, SparseCore 0:
  112.6 26.2 all-reduce.4
  174.6 26.0 all-reduce.6
  234.5 26.8 all-reduce.8
  263.8 18.7 all-reduce.10
where the time goes:
time: 293 us; the launch traced here: 291 us
  waiting for transfers between devices  99.5 us (34%)
  blocking collectives  92.3 us (32%)
  local copies, waits for them, and re-layouts  28.5 us (10%)
  matrix products  24.7 us (8%)
  between operations  22.1 us (8%)
  other arithmetic  17.5 us (6%)
  starting transfers between devices  6.19 us (2%)
    psum x3, waiting for transfers between devices, attend_layer(): lax.psum(partial_value.astype(jnp.bfloat16), 'mp').astype(jnp.float32)  77.7 us
    all_gather x3, blocking collectives, attend_layer(): value_piece = lax.all_gather(value_t, 'tm', axis=3, tiled=True)  32 us
    all_gather x3, blocking collectives, attend_layer(): key_piece = lax.all_gather(key_t, 'tm', axis=3, tiled=True)  30.1 us
    psum x1, waiting for transfers between devices, from_root(): return lax.psum(jnp.where(mine, value, jnp.zeros_like(value)), axis)  19.2 us
    all_gather x1, blocking collectives, per_device(): gathered = lax.all_gather(tokens, ('mp', 'section'), axis=2, tiled=True)  12.9 us
    psum x1, blocking collectives, per_device(): channel_total = lax.psum(jnp.sum(masked, -1), 'tm')  10.7 us
    unnamed x66, local copies, waits for them, and re-layouts  6.62 us
    psum x1, blocking collectives, per_device(): spread_total = lax.psum(jnp.sum(centered * centered, -1), 'tm')  6.6 us
  transfers between devices with their start and end apart: 7, of which 6 were waited for; matrix products, arithmetic and copies ran while one was open for 7% of the time, Pallas kernels for 0%

commit v1 on v0

v1 whole, which is shorter than its diff:
```python
import jax
import jax.numpy as jnp
from jax import lax
from jax.sharding import PartitionSpec as P

STRIDE = 32
HD = 80
SMALL_GROUP = 4


def shift_from(value, axis, size, by, cyclic):
    pairs = [(i, (i + by) % size) for i in range(size) if cyclic or i + by < size]
    return lax.ppermute(value, axis, pairs)


def gather_ordered(value, axis, size, me):
    if size > SMALL_GROUP:
        return lax.all_gather(value, axis, axis=0)
    received = [value] + [shift_from(value, axis, size, by, True) for by in range(1, size)]
    stack = jnp.stack(received, 0)
    order = (me - jnp.arange(size, dtype=jnp.int32)) % size
    return jnp.take(stack, order, axis=0)


def gather_causal(value, axis, size, me, width):
    if size > SMALL_GROUP:
        gathered = lax.all_gather(value, axis, axis=value.ndim - 1, tiled=True)
        return gathered, jnp.arange(size * width, dtype=jnp.int32)
    pieces = []
    positions = []
    local = jnp.arange(width, dtype=jnp.int32)
    for by in range(size - 1, 0, -1):
        pieces.append(shift_from(value, axis, size, by, False))
        positions.append((me - by) * width + local)
    pieces.append(value)
    positions.append(me * width + local)
    return jnp.concatenate(pieces, -1), jnp.concatenate(positions, 0)


def absorb_block(running, key_block, value_block, key_pos, query_rows, query_pos, first_valid):
    run_max, run_sum, accumulated = running
    allowed = (key_pos[None, None, :] <= query_pos[None, :, None]) & (
        (key_pos[None, None, :] >= first_valid[:, None, None])
        | (key_pos[None, None, :] == query_pos[None, :, None])
    )
    scores = jnp.einsum(
        "btkgh,bkhn->bkgtn", query_rows, key_block, preferred_element_type=jnp.float32
    )
    scores = jnp.where(allowed[:, None, None], scores, -jnp.inf)
    new_max = jnp.maximum(run_max, jnp.max(scores, -1))
    rescale = jnp.exp(run_max - new_max)
    exp_scores = jnp.exp(scores - new_max[..., None])
    new_sum = run_sum * rescale + jnp.sum(exp_scores, -1)
    contribution = jnp.einsum(
        "bkgtn,bkhn->bkgth",
        exp_scores.astype(jnp.bfloat16),
        value_block,
        preferred_element_type=jnp.float32,
    )
    return (new_max, new_sum, accumulated * rescale[..., None] + contribution)


def attend_layer(hidden_in, seq_lens, gain, query_w, key_w, value_w, out_w, sizes):
    tm_n, tm_at, total_tokens = sizes
    batch_count, tok_count, feature_count = hidden_in.shape
    hidden32 = hidden_in.astype(jnp.float32)
    gain32 = gain.astype(jnp.float32)
    scaled = hidden32 * lax.rsqrt(jnp.mean(hidden32 * hidden32, -1, keepdims=True) + 1e-06)
    layer_input = (scaled * gain32).astype(jnp.bfloat16)
    queries = (
        jnp.einsum("btd,de->bte", layer_input, query_w, preferred_element_type=jnp.float32)
        * HD ** (-0.5)
    ).astype(jnp.bfloat16)
    key_t = jnp.einsum(
        "btd,de->bet", layer_input, key_w, preferred_element_type=jnp.float32
    ).astype(jnp.bfloat16)
    value_t = jnp.einsum(
        "btd,de->bet", layer_input, value_w, preferred_element_type=jnp.float32
    ).astype(jnp.bfloat16)
    kv_local = key_w.shape[1] // HD
    group_size = query_w.shape[1] // key_w.shape[1]
    key_t = key_t.reshape(batch_count, kv_local, HD, tok_count)
    value_t = value_t.reshape(batch_count, kv_local, HD, tok_count)
    query_rows = queries.reshape(batch_count, tok_count, kv_local, group_size, HD)
    query_pos = tm_at * tok_count + jnp.arange(tok_count, dtype=jnp.int32)
    first_valid = total_tokens - seq_lens // STRIDE
    both, key_pos = gather_causal(jnp.stack([key_t, value_t], 0), "tm", tm_n, tm_at, tok_count)
    key_count = both.shape[-1]
    block_width = 1024 if key_count % 1024 == 0 else key_count
    rounds = key_count // block_width
    blocks = jnp.moveaxis(
        both.reshape(2, batch_count, kv_local, HD, rounds, block_width), 4, 0
    )
    pos_blocks = key_pos.reshape(rounds, block_width)
    start_state = (
        jnp.full((batch_count, kv_local, group_size, tok_count), -1e30, jnp.float32),
        jnp.zeros((batch_count, kv_local, group_size, tok_count), jnp.float32),
        jnp.zeros((batch_count, kv_local, group_size, tok_count, HD), jnp.float32),
    )
    if rounds == 1:
        result = absorb_block(
            start_state, blocks[0, 0], blocks[0, 1], pos_blocks[0], query_rows, query_pos,
            first_valid,
        )
    else:

        def scan_step(state, block_item):
            kv_block, pos_block = block_item
            return (
                absorb_block(
                    state, kv_block[0], kv_block[1], pos_block, query_rows, query_pos,
                    first_valid,
                ),
                None,
            )

        result, _ = lax.scan(scan_step, start_state, (blocks, pos_blocks))
    run_max, run_sum, accumulated = result
    attended = (accumulated / run_sum[..., None]).astype(jnp.bfloat16)
    attended = attended.transpose(0, 3, 1, 2, 4).reshape(
        batch_count, tok_count, kv_local * group_size * HD
    )
    partial_value = jnp.einsum("bte,ed->btd", attended, out_w, preferred_element_type=jnp.float32)
    return partial_value.astype(jnp.bfloat16), key_t, value_t


def per_device(
    series, lengths, patch_weight, norm_gain, query_weight, key_weight, value_weight, out_weight,
    *, tm_n, mp_n, sec_n
):
    seq_count, channels, steps_dev = series.shape
    tok_count = steps_dev // STRIDE
    tm_at = lax.axis_index("tm")
    mp_at = lax.axis_index("mp")
    sec_at = lax.axis_index("section")
    feat_axes = ("mp", "section")
    feat_n = mp_n * sec_n
    feat_at = mp_at * sec_n + sec_at
    total_steps = steps_dev * tm_n
    total_tokens = tok_count * tm_n

    prior_raw = shift_from(series[:, :, steps_dev - STRIDE :], "tm", tm_n, 1, False)

    first_step = total_steps - lengths
    step_pos = tm_at * steps_dev + jnp.arange(steps_dev, dtype=jnp.int32)
    valid = (step_pos[None, :] >= first_step[:, None]).astype(jnp.float32)
    values = series.astype(jnp.float32)
    masked = values * valid[:, None, :]
    local_sum = jnp.sum(masked, -1)
    shard_lo = jnp.arange(tm_n, dtype=jnp.int32) * steps_dev
    counts = jnp.clip(
        shard_lo[None, :] + steps_dev - jnp.maximum(shard_lo[None, :], first_step[:, None]),
        0,
        steps_dev,
    ).astype(jnp.float32)
    my_count = jnp.sum(valid, -1)
    local_mean = local_sum / jnp.maximum(my_count, 1.0)[:, None]
    local_dev = (values - local_mean[..., None]) * valid[:, None, :]
    local_m2 = jnp.sum(local_dev * local_dev, -1)
    stats = gather_ordered(jnp.stack([local_sum, local_m2], 0), "tm", tm_n, tm_at)
    history = lengths.astype(jnp.float32)[:, None]
    shard_sums = stats[:, 0]
    shard_m2 = stats[:, 1]
    channel_mean = jnp.sum(shard_sums, 0) / history
    shard_counts = jnp.moveaxis(counts, 1, 0)[:, :, None]
    shard_means = shard_sums / jnp.maximum(shard_counts, 1.0)
    gap = shard_means - channel_mean[None]
    spread_total = jnp.sum(shard_m2 + shard_counts * gap * gap, 0)
    variance = spread_total / history
    inv_std = lax.rsqrt(variance + 1e-05)[..., None]

    centered = (masked - channel_mean[..., None]) * valid[:, None, :]
    normed = (centered * inv_std).astype(jnp.bfloat16)
    prior_pos = tm_at * steps_dev - STRIDE + jnp.arange(STRIDE, dtype=jnp.int32)
    prior_valid = ((prior_pos[None, :] >= first_step[:, None]) & (prior_pos[None, :] >= 0)).astype(
        jnp.float32
    )[:, None, :]
    prior_normed = (
        (prior_raw.astype(jnp.float32) * prior_valid - channel_mean[..., None])
        * prior_valid
        * inv_std
    ).astype(jnp.bfloat16)

    blocks = normed.reshape(seq_count, channels, tok_count, STRIDE)
    column_count = patch_weight.shape[1]
    halves = patch_weight.reshape(channels, 2, STRIDE, column_count)
    right_terms = jnp.einsum(
        "scjr,crd->sjd", blocks, halves[:, 1], preferred_element_type=jnp.float32
    )
    left_all = jnp.einsum("scjr,crd->sjd", blocks, halves[:, 0], preferred_element_type=jnp.float32)
    edge_term = jnp.einsum(
        "scr,crd->sd", prior_normed, halves[:, 0], preferred_element_type=jnp.float32
    )
    left_terms = jnp.concatenate([edge_term[:, None, :], left_all[:, : tok_count - 1, :]], 1)
    tokens = (left_terms + right_terms).astype(jnp.bfloat16)

    pieces = gather_ordered(tokens, feat_axes, feat_n, feat_at)
    hidden0 = jnp.moveaxis(pieces, 0, 2).reshape(seq_count, tok_count, feat_n * column_count)
    feature_count = hidden0.shape[2]
    head_cols = feature_count // mp_n
    sizes = (tm_n, tm_at, total_tokens)

    partial0, key0, value0 = attend_layer(
        hidden0, lengths, norm_gain[0], query_weight[0], key_weight[0], value_weight[0],
        out_weight[0], sizes,
    )
    arrivals = []
    for by in range(mp_n):
        pairs = [(m * sec_n, ((m + by) % mp_n) * sec_n + 1) for m in range(mp_n)]
        arrivals.append(lax.ppermute(partial0, feat_axes, pairs))
    if mp_n > 1:
        order = (mp_at - jnp.arange(mp_n, dtype=jnp.int32)) % mp_n
        arrivals = jnp.take(jnp.stack(arrivals, 0), order, axis=0)
        head_sum = jnp.sum(arrivals.astype(jnp.float32), 0)
    else:
        head_sum = arrivals[0].astype(jnp.float32)
    hidden1 = (hidden0.astype(jnp.float32) + head_sum).astype(jnp.bfloat16)

    partial1, key1, value1 = attend_layer(
        hidden1, lengths, norm_gain[0], query_weight[0], key_weight[0], value_weight[0],
        out_weight[0], sizes,
    )
    is_first = sec_at == 0
    key_store = jnp.where(is_first, key0, key1)[None]
    value_store = jnp.where(is_first, value0, value1)[None]

    per_section = seq_count // sec_n
    low_rows = partial1[:per_section]
    high_rows = partial1[per_section:]
    low_hidden = hidden1[:per_section]
    to_low = []
    to_high = []
    for by in range(mp_n):
        target_mp = (mp_at + by) % mp_n
        cols = lax.dynamic_slice_in_dim(low_rows, target_mp * head_cols, head_cols, 2)
        if by == 0:
            cols = jnp.stack(
                [lax.dynamic_slice_in_dim(low_hidden, target_mp * head_cols, head_cols, 2), cols], 0
            )
        pairs = [(m * sec_n + 1, ((m + by) % mp_n) * sec_n) for m in range(mp_n)]
        to_low.append(lax.ppermute(cols, feat_axes, pairs))
        if by > 0:
            cols_high = lax.dynamic_slice_in_dim(high_rows, target_mp * head_cols, head_cols, 2)
            pairs = [(m * sec_n + 1, ((m + by) % mp_n) * sec_n + 1) for m in range(mp_n)]
            to_high.append(lax.ppermute(cols_high, feat_axes, pairs))
    low_total = to_low[0][0].astype(jnp.float32) + (
        to_low[0][1].astype(jnp.float32)
        + sum(piece.astype(jnp.float32) for piece in to_low[1:])
    )
    own_high = lax.dynamic_slice_in_dim(high_rows, mp_at * head_cols, head_cols, 2)
    own_hidden = lax.dynamic_slice_in_dim(hidden1[per_section:], mp_at * head_cols, head_cols, 2)
    high_total = own_hidden.astype(jnp.float32) + (
        own_high.astype(jnp.float32) + sum(piece.astype(jnp.float32) for piece in to_high)
    )
    final_cols = jnp.where(is_first, low_total, high_total).astype(jnp.bfloat16)
    return (key_store, value_store, final_cols)


def solution(mesh):
    sizes = dict(tm_n=mesh.shape["tm"], mp_n=mesh.shape["mp"], sec_n=mesh.shape["section"])
    in_specs = (
        P("groups", None, "tm"),
        P("groups"),
        P(None, ("mp", "section")),
        P("section", None),
        P("section", None, "mp"),
        P("section", None, "mp"),
        P("section", None, "mp"),
        P("section", "mp", None),
    )
    out_specs = (
        P("section", "groups", "mp", None, "tm"),
        P("section", "groups", "mp", None, "tm"),
        P(("groups", "section"), "tm", "mp"),
    )

    def body(*args):
        return per_device(*args, **sizes)

    return jax.shard_map(body, mesh=mesh, in_specs=in_specs, out_specs=out_specs, check_vma=False)
```

time: 293 us -> 136 us (0.46)
  the two profiles are of different devices: /device:TPU:1 before, /device:TPU:17 now
where the time goes in v1:
time: 136 us; the launch traced here: 135 us
  waiting for transfers between devices  40.1 us (29%)
  local copies, waits for them, and re-layouts  29.4 us (22%)
  starting transfers between devices  25.7 us (19%)
  other arithmetic  22.3 us (16%)
  matrix products  16.2 us (12%)
  between operations  1.36 us (1%)
    ppermute x13, waiting for transfers between devices, shift_from(): return lax.ppermute(value, axis, pairs)  30.9 us
    ppermute x13, starting transfers between devices, shift_from(): return lax.ppermute(value, axis, pairs)  16 us
    ppermute x2, waiting for transfers between devices, per_device(): arrivals.append(lax.ppermute(partial0, feat_axes, pairs))  6.72 us
    unnamed x31, local copies, waits for them, and re-layouts  5.63 us
    ppermute x2, starting transfers between devices, per_device(): to_low.append(lax.ppermute(cols, feat_axes, pairs))  3.97 us
    convert_element_type x2, local copies, waits for them, and re-layouts, attend_layer(): hidden32 = hidden_in.astype(jnp.float32)  3.95 us
    slice x1, local copies, waits for them, and re-layouts, per_device(): halves[:, 0]  3.91 us
    reshape x1, local copies, waits for them, and re-layouts, per_device(): blocks = normed.reshape(seq_count, channels, tok_count, STRIDE)  3.29 us
  transfers between devices with their start and end apart: 18, of which 9 were waited for; matrix products, arithmetic and copies ran while one was open for 23% of the time, Pallas kernels for 0%

profile of v1, /device:TPU:17, one launch (start us, length us, event | category | flops | bytes accessed | tf_op | source)
XLA Modules:
  0.0 135.0 jit_solution(18108917678711232653)
XLA Ops:
  6.6 2.2 %collective-permute-start = (bf16[2,64,32]{2,1,0:T(8,128)(2,1)S(1)}, bf16[2,64,32]{2,1,0:T(8,128)(2,1)S(1)}, u32[]{:S(2)}, u32[]{:S(2)}) collective-permute-start(bf16[2,64,32]{2,1,0:T(8,128)(2,1)S(1)} %slice.49), channel_id=1, source_target_pairs={{0,4},{4,8},{8,12},{1,5},{5,9},{9,13},{2,6},{6,10},{10,14},{3,7},{... | collective-permute-start | bytes 24584 | tf_op jit(solution)/shard_map/ppermute | solution.py:13
  9.0 4.5 %copy.23 = bf16[4096,320]{1,0:T(8,128)(2,1)} copy(bf16[4096,320]{0,1:T(8,128)(2,1)} %param.10) | data formatting | bytes 5242880 | tf_op args[2]
  13.5 3.9 %fusion.112 = (bf16[64,1,32,320]{3,2,1,0:T(8,128)(2,1)}, bf16[64,1,32,320]{3,2,1,0:T(8,128)(2,1)}) fusion(bf16[64,2,32,320]{3,2,1,0:T(8,128)(2,1)} %bitcast.265), kind=kLoop, calls=%fused_computation.201 | loop fusion | bytes 5242880 | tf_op jit(solution)/shard_map/slice | solution.py:192
  20.4 2.8 %copy.26 = bf16[2,64,4096]{1,2,0:T(8,128)(2,1)} copy(bf16[2,64,4096]{2,1,0:T(8,128)(2,1)} %fusion.10) | data formatting | bytes 2097152 | tf_op jit(solution)/shard_map/convert_element_type | solution.py:173
  23.2 3.3 %copy.27 = bf16[2,64,128,32]{2,1,3,0:T(8,128)(2,1)S(1)} copy(bf16[2,64,128,32]{1,3,2,0:T(8,128)(2,1)} %bitcast.274) | data formatting | bytes 2097152 | tf_op jit(solution)/shard_map/reshape | solution.py:184
  26.5 2.9 %fusion.65 = f32[2,128,320]{1,2,0:T(8,128)} fusion(bf16[2,64,128,32]{2,1,3,0:T(8,128)(2,1)S(1)} %copy.27, bf16[64,1,32,320]{3,2,1,0:T(8,128)(2,1)} %get-tuple-element.3), kind=kOutput, calls=%fused_computation.68 | convolution fusion | flops 335544320 | bytes 2686976 | tf_op jit(solution)/shard_map/scjr,crd->sjd/dot_general | solution.py:190
  29.6 2.0 %fusion.71 = f32[2,1,320]{2,0,1:T(2,128)S(1)} fusion(bf16[2,64,32]{1,0,2:T(2,128)(2,1)S(1)} %copy.25, bf16[64,1,32,320]{3,2,1,0:T(8,128)(2,1)} %get-tuple-element.3), kind=kOutput, calls=%fused_computation.76 | convolution fusion | flops 2621440 | bytes 1321472 | tf_op jit(solution)/shard_map/scr,crd->sd/dot_general | solution.py:191
  31.8 2.2 %fusion.70 = bf16[2,128,320]{1,2,0:T(8,128)(2,1)S(1)} fusion(bf16[2,64,128,32]{2,1,3,0:T(8,128)(2,1)S(1)} %copy.27, bf16[64,1,32,320]{3,2,1,0:T(8,128)(2,1)} %get-tuple-element.4, f32[2,127,320]{1,2,0:T(8,128)} %bitcast.301, f32[2,1,320]{1,2,0:T(8,128)S(1)} %copy.28), kind=kOutput, calls=%fused_computation.71 | convolution fusion | flops 335790080 | bytes 2850816 | tf_op jit(solution)/shard_map/scjr,crd->sjd/dot_general | solution.py:187
  34.1 2.9 %collective-permute-start.4 = (bf16[2,128,320]{1,2,0:T(8,128)(2,1)S(1)}, bf16[2,128,320]{1,2,0:T(8,128)(2,1)S(1)}, u32[]{:S(2)}, u32[]{:S(2)}) collective-permute-start(bf16[2,128,320]{1,2,0:T(8,128)(2,1)S(1)} %fusion.70), channel_id=1, source_target_pairs={{0,1},{1,2},{2,3},{3,0},{4,5},{5,6},{6,7},{7,4},{8,9},{9,10},{10,1... | collective-permute-start | bytes 491528 | tf_op jit(solution)/shard_map/ppermute | solution.py:13
  37.6 2.8 %collective-permute-done.4 = bf16[2,128,320]{1,2,0:T(8,128)(2,1)S(1)} collective-permute-done((bf16[2,128,320]{1,2,0:T(8,128)(2,1)S(1)}, bf16[2,128,320]{1,2,0:T(8,128)(2,1)S(1)}, u32[]{:S(2)}, u32[]{:S(2)}) %collective-permute-start.4) | collective-permute-done | bytes 163872 | tf_op jit(solution)/shard_map/ppermute | solution.py:13
  40.4 4.2 %collective-permute-done.5 = bf16[2,128,320]{1,2,0:T(8,128)(2,1)S(1)} collective-permute-done((bf16[2,128,320]{1,2,0:T(8,128)(2,1)S(1)}, bf16[2,128,320]{1,2,0:T(8,128)(2,1)S(1)}, u32[]{:S(2)}, u32[]{:S(2)}) %collective-permute-start.5) | collective-permute-done | bytes 163872 | tf_op jit(solution)/shard_map/ppermute | solution.py:13
  55.8 5.4 %collective-permute-done.8 = bf16[2,2,2,80,128]{4,3,2,1,0:T(8,128)(2,1)} collective-permute-done((bf16[2,2,2,80,128]{4,3,2,1,0:T(8,128)(2,1)}, bf16[2,2,2,80,128]{4,3,2,1,0:T(8,128)(2,1)}, u32[]{:S(2)}, u32[]{:S(2)}) %collective-permute-start.8) | collective-permute-done | bytes 163872 | tf_op jit(solution)/shard_map/ppermute | solution.py:13
  61.2 7.1 %collective-permute-done.9 = bf16[2,2,2,80,128]{4,3,2,1,0:T(8,128)(2,1)} collective-permute-done((bf16[2,2,2,80,128]{4,3,2,1,0:T(8,128)(2,1)}, bf16[2,2,2,80,128]{4,3,2,1,0:T(8,128)(2,1)}, u32[]{:S(2)}, u32[]{:S(2)}) %collective-permute-start.9) | collective-permute-done | bytes 163872 | tf_op jit(solution)/shard_map/ppermute | solution.py:13
  77.6 2.8 %copy.44 = f32[2,128,1280]{2,1,0:T(8,128)} copy(f32[2,128,1280]{1,2,0:T(8,128)} %bitcast.275) | data formatting | bytes 2621440 | tf_op jit(solution)/shard_map/convert_element_type | solution.py:66
  80.5 6.7 %collective-permute-done.11 = bf16[2,128,1280]{2,1,0:T(8,128)(2,1)} collective-permute-done((bf16[2,128,1280]{2,1,0:T(8,128)(2,1)}, bf16[2,128,1280]{2,1,0:T(8,128)(2,1)}, u32[]{:S(2)}, u32[]{:S(2)}) %collective-permute-start.11) | collective-permute-done | bytes 655392 | tf_op jit(solution)/shard_map/ppermute | solution.py:210
  87.2 2.5 %pad_maximum_fusion = bf16[2,2,128,1280]{3,2,1,0:T(8,128)(2,1)} fusion(bf16[1,2,128,1280]{3,2,1,0:T(8,128)(2,1)} %bitcast.55, bf16[1,2,128,1280]{3,2,1,0:T(8,128)(2,1)} %bitcast.54), kind=kLoop, calls=%fused_computation.53 | loop fusion | flops 655360 | bytes 2621440 | tf_op jit(solution)/shard_map/stack | solution.py:213
  89.6 3.0 %gather_fusion.2 = bf16[2,2,128,1280]{3,2,1,0:T(8,128)(2,1)} fusion(bf16[2,2,128,1280]{3,2,1,0:T(8,128)(2,1)} %pad_maximum_fusion, s32[1024]{0:T(1024)S(1)} %pad_clamp_fusion), kind=kCustom, calls=%fused_computation.2 | custom fusion | bytes 2621448 | tf_op jit(solution)/shard_map/jit(_take)/gather | solution.py:213
  92.6 2.9 %convert_reduce_fusion = f32[2,128,1280]{2,1,0:T(8,128)} fusion(bf16[2,2,128,1280]{3,2,1,0:T(8,128)(2,1)} %gather_fusion.2, pred[2]{0:T(512)(128)(4,1)S(1)} %compare_and_fusion), kind=kLoop, calls=%fused_computation.15 | loop fusion | flops 1638400 | bytes 2621442 | tf_op jit(solution)/shard_map/reduce_sum | solution.py:214
  95.6 2.8 %copy.38 = f32[2,128,1280]{1,2,0:T(8,128)} copy(f32[2,128,1280]{2,1,0:T(8,128)} %convert_reduce_fusion) | data formatting | bytes 2621440 | tf_op jit(solution)/shard_map/reduce_sum | solution.py:214
  109.0 3.5 %collective-permute-done.13 = bf16[2,2,2,80,128]{4,3,2,1,0:T(8,128)(2,1)S(1)} collective-permute-done((bf16[2,2,2,80,128]{4,3,2,1,0:T(8,128)(2,1)}, bf16[2,2,2,80,128]{4,3,2,1,0:T(8,128)(2,1)S(1)}, u32[]{:S(2)}, u32[]{:S(2)}) %collective-permute-start.13) | collective-permute-done | bytes 163872 | tf_op jit(solution)/shard_map/ppermute | solution.py:13
  112.5 7.2 %collective-permute-done.14 = bf16[2,2,2,80,128]{4,3,2,1,0:T(8,128)(2,1)} collective-permute-done((bf16[2,2,2,80,128]{4,3,2,1,0:T(8,128)(2,1)}, bf16[2,2,2,80,128]{4,3,2,1,0:T(8,128)(2,1)}, u32[]{:S(2)}, u32[]{:S(2)}) %collective-permute-start.14) | collective-permute-done | bytes 163872 | tf_op jit(solution)/shard_map/ppermute | solution.py:13
  124.1 2.3 %collective-permute-start.15 = (bf16[2,1,128,640]{3,2,1,0:T(8,128)(2,1)S(1)}, bf16[2,1,128,640]{3,2,1,0:T(8,128)(2,1)S(1)}, u32[]{:S(2)}, u32[]{:S(2)}) collective-permute-start(bf16[2,1,128,640]{3,2,1,0:T(8,128)(2,1)S(1)} %pad_maximum_fusion.2), channel_id=1, source_target_pairs={{1,0},{3,2},{5,4},{7,6},{9,8},{11,10},{13,12},{15,14},{17,16},{19,... | collective-permute-start | bytes 983048 | tf_op jit(solution)/shard_map/ppermute | solution.py:241
  128.1 2.9 %collective-permute-start.17 = (bf16[1,128,640]{2,1,0:T(8,128)(2,1)S(1)}, bf16[1,128,640]{2,1,0:T(8,128)(2,1)S(1)}, u32[]{:S(2)}, u32[]{:S(2)}) collective-permute-start(bf16[1,128,640]{2,1,0:T(8,128)(2,1)S(1)} %constant_dynamic-slice_fusion), channel_id=1, source_target_pairs={{1,3},{3,1},{5,7},{7,5},{9,11},{11,9},{13,15},{15,13},{17,19},{19,... | collective-permute-start | bytes 491528 | tf_op jit(solution)/shard_map/ppermute | solution.py:245
  131.7 2.5 %collective-permute-done.17 = bf16[1,128,640]{2,1,0:T(8,128)(2,1)S(1)} collective-permute-done((bf16[1,128,640]{2,1,0:T(8,128)(2,1)S(1)}, bf16[1,128,640]{2,1,0:T(8,128)(2,1)S(1)}, u32[]{:S(2)}, u32[]{:S(2)}) %collective-permute-start.17) | collective-permute-done | bytes 163872 | tf_op jit(solution)/shard_map/ppermute | solution.py:245
  (143 shorter events, 48.2 us)
Async XLA Ops:
  0.6 71.3 %copy-start = (bf16[1,640,1280]{2,1,0:T(8,128)(2,1)S(1)}, bf16[1,640,1280]{2,1,0:T(8,128)(2,1)}, u32[]{:S(2)}) copy-start(bf16[1,640,1280]{2,1,0:T(8,128)(2,1)} %param.15) | copy-start | bytes 4915204
  3.9 14.1 %collective-permute-start.1 = (f32[2,2,64]{2,1,0:T(2,128)S(1)}, f32[2,2,64]{2,1,0:T(2,128)S(1)}, u32[]{:S(2)}, u32[]{:S(2)}) collective-permute-start(f32[2,2,64]{2,1,0:T(2,128)S(1)} %get-tuple-element.18), channel_id=1, source_target_pairs={{0,4},{4,8},{8,12},{12,0},{1,5},{5,9},{9,13},{13,1},{2,6},{6,10},{... | collective-permute-start | bytes 3080 | tf_op jit(solution)/shard_map/ppermute | solution.py:13
  5.3 12.8 %collective-permute-start.2 = (f32[2,2,64]{2,1,0:T(2,128)S(1)}, f32[2,2,64]{2,1,0:T(2,128)S(1)}, u32[]{:S(2)}, u32[]{:S(2)}) collective-permute-start(f32[2,2,64]{2,1,0:T(2,128)S(1)} %get-tuple-element.18), channel_id=1, source_target_pairs={{0,8},{4,12},{8,0},{12,4},{1,9},{5,13},{9,1},{13,5},{2,10},{6,14},... | collective-permute-start | bytes 3080 | tf_op jit(solution)/shard_map/ppermute | solution.py:13
  5.3 12.8 %collective-permute-start.3 = (f32[2,2,64]{2,1,0:T(2,128)S(1)}, f32[2,2,64]{2,1,0:T(2,128)S(1)}, u32[]{:S(2)}, u32[]{:S(2)}) collective-permute-start(f32[2,2,64]{2,1,0:T(2,128)S(1)} %get-tuple-element.18), channel_id=1, source_target_pairs={{0,12},{4,0},{8,4},{12,8},{1,13},{5,1},{9,5},{13,9},{2,14},{6,2},{... | collective-permute-start | bytes 3080 | tf_op jit(solution)/shard_map/ppermute | solution.py:13
  6.6 22.8 %collective-permute-start = (bf16[2,64,32]{2,1,0:T(8,128)(2,1)S(1)}, bf16[2,64,32]{2,1,0:T(8,128)(2,1)S(1)}, u32[]{:S(2)}, u32[]{:S(2)}) collective-permute-start(bf16[2,64,32]{2,1,0:T(8,128)(2,1)S(1)} %slice.49), channel_id=1, source_target_pairs={{0,4},{4,8},{8,12},{1,5},{5,9},{9,13},{2,6},{6,10},{10,14},{3,7},{... | collective-permute-start | bytes 24584 | tf_op jit(solution)/shard_map/ppermute | solution.py:13
  18.1 29.1 %copy-start.12 = (pred[4]{0:T(512)(128)(4,1)}, pred[4]{0:T(512)(128)(4,1)S(1)}, u32[]{:S(2)}) copy-start(pred[4]{0:T(512)(128)(4,1)S(1)} %get-tuple-element.27) | copy-start | bytes 16
  34.1 11.2 %copy-start.11 = (bf16[2,128,320]{1,2,0:T(8,128)(2,1)}, bf16[2,128,320]{1,2,0:T(8,128)(2,1)S(1)}, u32[]{:S(2)}) copy-start(bf16[2,128,320]{1,2,0:T(8,128)(2,1)S(1)} %fusion.70) | copy-start | bytes 491524
  34.1 6.4 %collective-permute-start.4 = (bf16[2,128,320]{1,2,0:T(8,128)(2,1)S(1)}, bf16[2,128,320]{1,2,0:T(8,128)(2,1)S(1)}, u32[]{:S(2)}, u32[]{:S(2)}) collective-permute-start(bf16[2,128,320]{1,2,0:T(8,128)(2,1)S(1)} %fusion.70), channel_id=1, source_target_pairs={{0,1},{1,2},{2,3},{3,0},{4,5},{5,6},{6,7},{7,4},{8,9},{9,10},{10,1... | collective-permute-start | bytes 491528 | tf_op jit(solution)/shard_map/ppermute | solution.py:13
  37.0 7.6 %collective-permute-start.5 = (bf16[2,128,320]{1,2,0:T(8,128)(2,1)S(1)}, bf16[2,128,320]{1,2,0:T(8,128)(2,1)S(1)}, u32[]{:S(2)}, u32[]{:S(2)}) collective-permute-start(bf16[2,128,320]{1,2,0:T(8,128)(2,1)S(1)} %fusion.70), channel_id=1, source_target_pairs={{0,2},{1,3},{2,0},{3,1},{4,6},{5,7},{6,4},{7,5},{8,10},{9,11},{10,... | collective-permute-start | bytes 491528 | tf_op jit(solution)/shard_map/ppermute | solution.py:13
  37.3 8.0 %collective-permute-start.6 = (bf16[2,128,320]{1,2,0:T(8,128)(2,1)S(1)}, bf16[2,128,320]{1,2,0:T(8,128)(2,1)S(1)}, u32[]{:S(2)}, u32[]{:S(2)}) collective-permute-start(bf16[2,128,320]{1,2,0:T(8,128)(2,1)S(1)} %fusion.70), channel_id=1, source_target_pairs={{0,3},{1,0},{2,1},{3,2},{4,7},{5,4},{6,5},{7,6},{8,11},{9,8},{10,9... | collective-permute-start | bytes 491528 | tf_op jit(solution)/shard_map/ppermute | solution.py:13
  47.6 5.5 %copy-start.4 = (bf16[1,1280,640]{2,1,0:T(8,128)(2,1)S(1)}, bf16[1,1280,640]{2,1,0:T(8,128)(2,1)}, u32[]{:S(2)}) copy-start(bf16[1,1280,640]{2,1,0:T(8,128)(2,1)} %param.12) | copy-start | bytes 4915204
  49.2 6.5 %collective-permute-start.7 = (bf16[2,2,2,80,128]{4,3,2,1,0:T(8,128)(2,1)}, bf16[2,2,2,80,128]{4,3,2,1,0:T(8,128)(2,1)S(1)}, u32[]{:S(2)}, u32[]{:S(2)}) collective-permute-start(bf16[2,2,2,80,128]{4,3,2,1,0:T(8,128)(2,1)} %pad_maximum_fusion.3), channel_id=1, source_target_pairs={{0,12},{1,13},{2,14},{3,15},{16,28},{17,29},{18,30},{19,31}} | collective-permute-start | bytes 491528 | tf_op jit(solution)/shard_map/ppermute | solution.py:13
  49.9 11.3 %collective-permute-start.8 = (bf16[2,2,2,80,128]{4,3,2,1,0:T(8,128)(2,1)}, bf16[2,2,2,80,128]{4,3,2,1,0:T(8,128)(2,1)}, u32[]{:S(2)}, u32[]{:S(2)}) collective-permute-start(bf16[2,2,2,80,128]{4,3,2,1,0:T(8,128)(2,1)} %pad_maximum_fusion.3), channel_id=1, source_target_pairs={{0,8},{4,12},{1,9},{5,13},{2,10},{6,14},{3,11},{7,15},{16,24},{20,... | collective-permute-start | bytes 491528 | tf_op jit(solution)/shard_map/ppermute | solution.py:13
  51.2 17.1 %collective-permute-start.9 = (bf16[2,2,2,80,128]{4,3,2,1,0:T(8,128)(2,1)}, bf16[2,2,2,80,128]{4,3,2,1,0:T(8,128)(2,1)}, u32[]{:S(2)}, u32[]{:S(2)}) collective-permute-start(bf16[2,2,2,80,128]{4,3,2,1,0:T(8,128)(2,1)} %pad_maximum_fusion.3), channel_id=1, source_target_pairs={{0,4},{4,8},{8,12},{1,5},{5,9},{9,13},{2,6},{6,10},{10,14},{3,7},{... | collective-permute-start | bytes 491528 | tf_op jit(solution)/shard_map/ppermute | solution.py:13
  73.5 7.0 %collective-permute-start.10 = (bf16[2,128,1280]{2,1,0:T(8,128)(2,1)}, bf16[2,128,1280]{2,1,0:T(8,128)(2,1)}, u32[]{:S(2)}, u32[]{:S(2)}) collective-permute-start(bf16[2,128,1280]{2,1,0:T(8,128)(2,1)} %convolution_convert_fusion.1), channel_id=1, source_target_pairs={{0,1},{2,3},{4,5},{6,7},{8,9},{10,11},{12,13},{14,15},{16,17},{18,... | collective-permute-start | bytes 1966088 | tf_op jit(solution)/shard_map/ppermute | solution.py:210
  74.9 12.2 %collective-permute-start.11 = (bf16[2,128,1280]{2,1,0:T(8,128)(2,1)}, bf16[2,128,1280]{2,1,0:T(8,128)(2,1)}, u32[]{:S(2)}, u32[]{:S(2)}) collective-permute-start(bf16[2,128,1280]{2,1,0:T(8,128)(2,1)} %convolution_convert_fusion.1), channel_id=1, source_target_pairs={{0,3},{2,1},{4,7},{6,5},{8,11},{10,9},{12,15},{14,13},{16,19},{18,... | collective-permute-start | bytes 1966088 | tf_op jit(solution)/shard_map/ppermute | solution.py:210
  100.5 6.0 %copy-start.5 = (bf16[1,1280,640]{2,1,0:T(8,128)(2,1)S(1)}, bf16[1,1280,640]{2,1,0:T(8,128)(2,1)}, u32[]{:S(2)}) copy-start(bf16[1,1280,640]{2,1,0:T(8,128)(2,1)} %param.12) | copy-start | bytes 4915204
  102.4 6.6 %collective-permute-start.12 = (bf16[2,2,2,80,128]{4,3,2,1,0:T(8,128)(2,1)}, bf16[2,2,2,80,128]{4,3,2,1,0:T(8,128)(2,1)S(1)}, u32[]{:S(2)}, u32[]{:S(2)}) collective-permute-start(bf16[2,2,2,80,128]{4,3,2,1,0:T(8,128)(2,1)} %pad_maximum_fusion.4), channel_id=1, source_target_pairs={{0,12},{1,13},{2,14},{3,15},{16,28},{17,29},{18,30},{19,31}} | collective-permute-start | bytes 491528 | tf_op jit(solution)/shard_map/ppermute | solution.py:13
  103.2 9.3 %collective-permute-start.13 = (bf16[2,2,2,80,128]{4,3,2,1,0:T(8,128)(2,1)}, bf16[2,2,2,80,128]{4,3,2,1,0:T(8,128)(2,1)S(1)}, u32[]{:S(2)}, u32[]{:S(2)}) collective-permute-start(bf16[2,2,2,80,128]{4,3,2,1,0:T(8,128)(2,1)} %pad_maximum_fusion.4), channel_id=1, source_target_pairs={{0,8},{4,12},{1,9},{5,13},{2,10},{6,14},{3,11},{7,15},{16,24},{20,... | collective-permute-start | bytes 491528 | tf_op jit(solution)/shard_map/ppermute | solution.py:13
  104.5 15.2 %collective-permute-start.14 = (bf16[2,2,2,80,128]{4,3,2,1,0:T(8,128)(2,1)}, bf16[2,2,2,80,128]{4,3,2,1,0:T(8,128)(2,1)}, u32[]{:S(2)}, u32[]{:S(2)}) collective-permute-start(bf16[2,2,2,80,128]{4,3,2,1,0:T(8,128)(2,1)} %pad_maximum_fusion.4), channel_id=1, source_target_pairs={{0,4},{4,8},{8,12},{1,5},{5,9},{9,13},{2,6},{6,10},{10,14},{3,7},{... | collective-permute-start | bytes 491528 | tf_op jit(solution)/shard_map/ppermute | solution.py:13
  123.9 10.2 %copy-start.10 = (bf16[1,128,1280]{2,1,0:T(8,128)(2,1)S(1)}, bf16[1,128,1280]{2,1,0:T(8,128)(2,1)}, u32[]{:S(2)}) copy-start(bf16[1,128,1280]{2,1,0:T(8,128)(2,1)} %get-tuple-element.5) | copy-start | bytes 983044
  124.1 10.1 %collective-permute-start.15 = (bf16[2,1,128,640]{3,2,1,0:T(8,128)(2,1)S(1)}, bf16[2,1,128,640]{3,2,1,0:T(8,128)(2,1)S(1)}, u32[]{:S(2)}, u32[]{:S(2)}) collective-permute-start(bf16[2,1,128,640]{3,2,1,0:T(8,128)(2,1)S(1)} %pad_maximum_fusion.2), channel_id=1, source_target_pairs={{1,0},{3,2},{5,4},{7,6},{9,8},{11,10},{13,12},{15,14},{17,16},{19,... | collective-permute-start | bytes 983048 | tf_op jit(solution)/shard_map/ppermute | solution.py:241
  126.4 5.2 %collective-permute-start.16 = (bf16[1,128,640]{2,1,0:T(8,128)(2,1)S(1)}, bf16[1,128,640]{2,1,0:T(8,128)(2,1)S(1)}, u32[]{:S(2)}, u32[]{:S(2)}) collective-permute-start(bf16[1,128,640]{2,1,0:T(8,128)(2,1)S(1)} %get-tuple-element.10), channel_id=1, source_target_pairs={{1,2},{3,0},{5,6},{7,4},{9,10},{11,8},{13,14},{15,12},{17,18},{19,... | collective-permute-start | bytes 491528 | tf_op jit(solution)/shard_map/ppermute | solution.py:241
  128.1 6.1 %collective-permute-start.17 = (bf16[1,128,640]{2,1,0:T(8,128)(2,1)S(1)}, bf16[1,128,640]{2,1,0:T(8,128)(2,1)S(1)}, u32[]{:S(2)}, u32[]{:S(2)}) collective-permute-start(bf16[1,128,640]{2,1,0:T(8,128)(2,1)S(1)} %constant_dynamic-slice_fusion), channel_id=1, source_target_pairs={{1,3},{3,1},{5,7},{7,5},{9,11},{11,9},{13,15},{15,13},{17,19},{19,... | collective-permute-start | bytes 491528 | tf_op jit(solution)/shard_map/ppermute | solution.py:245
  (9 other events, 26.8 us)

commit v2 on v1

--- a/solution.py
+++ b/solution.py
@@ -22,18 +22,19 @@
     return jnp.take(stack, order, axis=0)
 
 
-def gather_causal(value, axis, size, me, width):
-    if size > SMALL_GROUP:
-        gathered = lax.all_gather(value, axis, axis=value.ndim - 1, tiled=True)
-        return gathered, jnp.arange(size * width, dtype=jnp.int32)
+def gather_causal(value, tm_n, sec_n, tm_at, phase, width):
+    if tm_n > SMALL_GROUP:
+        gathered = lax.all_gather(value, "tm", axis=value.ndim - 1, tiled=True)
+        return gathered, jnp.arange(tm_n * width, dtype=jnp.int32)
     pieces = []
     positions = []
     local = jnp.arange(width, dtype=jnp.int32)
-    for by in range(size - 1, 0, -1):
-        pieces.append(shift_from(value, axis, size, by, False))
-        positions.append((me - by) * width + local)
+    for by in range(tm_n - 1, 0, -1):
+        pairs = [(t * sec_n + phase, (t + by) * sec_n + phase) for t in range(tm_n - by)]
+        pieces.append(lax.ppermute(value, ("tm", "section"), pairs))
+        positions.append((tm_at - by) * width + local)
     pieces.append(value)
-    positions.append(me * width + local)
+    positions.append(tm_at * width + local)
     return jnp.concatenate(pieces, -1), jnp.concatenate(positions, 0)
 
 
@@ -60,8 +61,8 @@
     return (new_max, new_sum, accumulated * rescale[..., None] + contribution)
 
 
-def attend_layer(hidden_in, seq_lens, gain, query_w, key_w, value_w, out_w, sizes):
-    tm_n, tm_at, total_tokens = sizes
+def attend_layer(hidden_in, seq_lens, gain, query_w, key_w, value_w, out_w, sizes, phase):
+    tm_n, sec_n, tm_at, total_tokens = sizes
     batch_count, tok_count, feature_count = hidden_in.shape
     hidden32 = hidden_in.astype(jnp.float32)
     gain32 = gain.astype(jnp.float32)
@@ -84,7 +85,9 @@
     query_rows = queries.reshape(batch_count, tok_count, kv_local, group_size, HD)
     query_pos = tm_at * tok_count + jnp.arange(tok_count, dtype=jnp.int32)
     first_valid = total_tokens - seq_lens // STRIDE
-    both, key_pos = gather_causal(jnp.stack([key_t, value_t], 0), "tm", tm_n, tm_at, tok_count)
+    both, key_pos = gather_causal(
+        jnp.stack([key_t, value_t], 0), tm_n, sec_n, tm_at, phase, tok_count
+    )
     key_count = both.shape[-1]
     block_width = 1024 if key_count % 1024 == 0 else key_count
     rounds = key_count // block_width
@@ -169,46 +172,38 @@
     variance = spread_total / history
     inv_std = lax.rsqrt(variance + 1e-05)[..., None]
 
-    centered = (masked - channel_mean[..., None]) * valid[:, None, :]
-    normed = (centered * inv_std).astype(jnp.bfloat16)
-    prior_pos = tm_at * steps_dev - STRIDE + jnp.arange(STRIDE, dtype=jnp.int32)
-    prior_valid = ((prior_pos[None, :] >= first_step[:, None]) & (prior_pos[None, :] >= 0)).astype(
-        jnp.float32
-    )[:, None, :]
-    prior_normed = (
-        (prior_raw.astype(jnp.float32) * prior_valid - channel_mean[..., None])
-        * prior_valid
-        * inv_std
-    ).astype(jnp.bfloat16)
-
-    blocks = normed.reshape(seq_count, channels, tok_count, STRIDE)
+    padded = jnp.concatenate([prior_raw, series], -1).astype(jnp.float32)
+    padded_pos = tm_at * steps_dev - STRIDE + jnp.arange(steps_dev + STRIDE, dtype=jnp.int32)
+    padded_valid = (
+        (padded_pos[None, :] >= first_step[:, None]) & (padded_pos[None, :] >= 0)
+    ).astype(jnp.float32)[:, None, :]
+    normed = (
+        (padded * padded_valid - channel_mean[..., None]) * padded_valid * inv_std
+    ).astype(jnp.bfloat16)
+    left = normed[:, :, :steps_dev].reshape(seq_count, channels, tok_count, STRIDE)
+    right = normed[:, :, STRIDE:].reshape(seq_count, channels, tok_count, STRIDE)
+    window = jnp.concatenate([left, right], -1).transpose(0, 2, 1, 3)
+    window = window.reshape(seq_count, tok_count, channels * 2 * STRIDE)
+    tokens = jnp.einsum(
+        "sjk,kd->sjd", window, patch_weight, preferred_element_type=jnp.float32
+    ).astype(jnp.bfloat16)
     column_count = patch_weight.shape[1]
-    halves = patch_weight.reshape(channels, 2, STRIDE, column_count)
-    right_terms = jnp.einsum(
-        "scjr,crd->sjd", blocks, halves[:, 1], preferred_element_type=jnp.float32
-    )
-    left_all = jnp.einsum("scjr,crd->sjd", blocks, halves[:, 0], preferred_element_type=jnp.float32)
-    edge_term = jnp.einsum(
-        "scr,crd->sd", prior_normed, halves[:, 0], preferred_element_type=jnp.float32
-    )
-    left_terms = jnp.concatenate([edge_term[:, None, :], left_all[:, : tok_count - 1, :]], 1)
-    tokens = (left_terms + right_terms).astype(jnp.bfloat16)
-
-    pieces = gather_ordered(tokens, feat_axes, feat_n, feat_at)
-    hidden0 = jnp.moveaxis(pieces, 0, 2).reshape(seq_count, tok_count, feat_n * column_count)
+    hidden0 = lax.all_gather(tokens, feat_axes, axis=2, tiled=True)
     feature_count = hidden0.shape[2]
     head_cols = feature_count // mp_n
-    sizes = (tm_n, tm_at, total_tokens)
+    sizes = (tm_n, sec_n, tm_at, total_tokens)
 
     partial0, key0, value0 = attend_layer(
         hidden0, lengths, norm_gain[0], query_weight[0], key_weight[0], value_weight[0],
-        out_weight[0], sizes,
+        out_weight[0], sizes, 0,
     )
     arrivals = []
     for by in range(mp_n):
         pairs = [(m * sec_n, ((m + by) % mp_n) * sec_n + 1) for m in range(mp_n)]
         arrivals.append(lax.ppermute(partial0, feat_axes, pairs))
-    if mp_n > 1:
+    if mp_n == 2:
+        head_sum = arrivals[0].astype(jnp.float32) + arrivals[1].astype(jnp.float32)
+    elif mp_n > 2:
         order = (mp_at - jnp.arange(mp_n, dtype=jnp.int32)) % mp_n
         arrivals = jnp.take(jnp.stack(arrivals, 0), order, axis=0)
         head_sum = jnp.sum(arrivals.astype(jnp.float32), 0)
@@ -218,7 +213,7 @@
 
     partial1, key1, value1 = attend_layer(
         hidden1, lengths, norm_gain[0], query_weight[0], key_weight[0], value_weight[0],
-        out_weight[0], sizes,
+        out_weight[0], sizes, 1,
     )
     is_first = sec_at == 0
     key_store = jnp.where(is_first, key0, key1)[None]

time: 136 us -> 116 us (0.85)
  the two profiles are of different devices: /device:TPU:17 before, /device:TPU:1 now
where the time goes in v2:
time: 116 us; the launch traced here: 115 us
  starting transfers between devices  28.9 us (25%)
  local copies, waits for them, and re-layouts  23.3 us (20%)
  other arithmetic  20.5 us (18%)
  waiting for transfers between devices  16.8 us (14%)
  matrix products  14.4 us (12%)
  blocking collectives  9.65 us (8%)
  between operations  1.19 us (1%)
    ppermute x2, waiting for transfers between devices, per_device(): arrivals.append(lax.ppermute(partial0, feat_axes, pairs))  14.5 us
    ppermute x6, starting transfers between devices, gather_causal(): pieces.append(lax.ppermute(value, ('tm', 'section'), pairs))  12.8 us
    all_gather x1, blocking collectives, per_device(): hidden0 = lax.all_gather(tokens, feat_axes, axis=2, tiled=True)  9.65 us
    transpose x1, local copies, waits for them, and re-layouts, per_device(): window = jnp.concatenate([left, right], -1).transpose(0, 2, 1, 3)  8.49 us
    ppermute x4, starting transfers between devices, shift_from(): return lax.ppermute(value, axis, pairs)  7.83 us
    transpose x1, other arithmetic, per_device(): window = jnp.concatenate([left, right], -1).transpose(0, 2, 1, 3)  5.57 us
    slice x2, local copies, waits for them, and re-layouts, per_device(): normed[:, :, :steps_dev].reshape(seq_count, channels, tok_count, STRIDE)  4.52 us
    dot_general x2, matrix products, attend_layer(): jnp.einsum('btd,de->bte', layer_input, query_w, preferred_element_type=jn...  3.34 us
  transfers between devices with their start and end apart: 15, of which 3 were waited for; matrix products, arithmetic and copies ran while one was open for 10% of the time, Pallas kernels for 0%

profile of v2, /device:TPU:1, one launch (start us, length us, event | category | flops | bytes accessed | tf_op | source)
XLA Modules:
  0.0 114.8 jit_solution(11749270952794227328)
XLA Ops:
  4.0 2.2 %collective-permute-start.1 = (f32[2,2,64]{2,1,0:T(2,128)S(1)}, f32[2,2,64]{2,1,0:T(2,128)S(1)}, u32[]{:S(2)}, u32[]{:S(2)}) collective-permute-start(f32[2,2,64]{2,1,0:T(2,128)S(1)} %get-tuple-element.26), channel_id=1, source_target_pairs={{0,4},{4,8},{8,12},{12,0},{1,5},{5,9},{9,13},{13,1},{2,6},{6,10},{... | collective-permute-start | bytes 3080 | tf_op jit(solution)/shard_map/ppermute | solution.py:13
  6.1 2.3 %collective-permute-start.2 = (f32[2,2,64]{2,1,0:T(2,128)S(1)}, f32[2,2,64]{2,1,0:T(2,128)S(1)}, u32[]{:S(2)}, u32[]{:S(2)}) collective-permute-start(f32[2,2,64]{2,1,0:T(2,128)S(1)} %get-tuple-element.26), channel_id=1, source_target_pairs={{0,8},{4,12},{8,0},{12,4},{1,9},{5,13},{9,1},{13,5},{2,10},{6,14},... | collective-permute-start | bytes 3080 | tf_op jit(solution)/shard_map/ppermute | solution.py:13
  9.6 2.3 %collective-permute-start = (bf16[2,64,32]{2,1,0:T(8,128)(2,1)S(1)}, bf16[2,64,32]{2,1,0:T(8,128)(2,1)S(1)}, u32[]{:S(2)}, u32[]{:S(2)}) collective-permute-start(bf16[2,64,32]{2,1,0:T(8,128)(2,1)S(1)} %slice.45), channel_id=1, source_target_pairs={{0,4},{4,8},{8,12},{1,5},{5,9},{9,13},{2,6},{6,10},{10,14},{3,7},{... | collective-permute-start | bytes 24584 | tf_op jit(solution)/shard_map/ppermute | solution.py:13
  13.7 2.0 %multiply_convert_fusion = bf16[2,64,4128]{2,1,0:T(8,128)(2,1)S(1)} fusion(bf16[2,64,4096]{2,1,0:T(8,128)(2,1)} %param.8, bf16[2,64,32]{2,1,0:T(8,128)(2,1)S(1)} %collective-permute-done, f32[2,64]{1,0:T(2,128)S(1)} %add_rsqrt_fusion.2, f32[2,64]{1,0:T(2,128)S(1)} %broadcast_divide_fusion, f32[2,4128]{1,0:T(2,128)S(1)} %and_convert_fusion), kind=kLoop, calls=%fused_computation.18 | loop fusion | flops 4755456 | bytes 2147584 | tf_op jit(solution)/shard_map/convert_element_type | solution.py:182
  15.7 1.8 %fusion.101 = (bf16[2,64,4096]{2,1,0:T(8,128)(2,1)}, bf16[2,64,4096]{2,1,0:T(8,128)(2,1)}) fusion(bf16[2,64,4128]{2,1,0:T(8,128)(2,1)S(1)} %multiply_convert_fusion), kind=kLoop, calls=%fused_computation.157 | loop fusion | bytes 4194304 | tf_op jit(solution)/shard_map/slice | solution.py:183
  17.5 2.8 %copy.31 = bf16[2,64,4096]{1,2,0:T(8,128)(2,1)} copy(bf16[2,64,4096]{2,1,0:T(8,128)(2,1)} %get-tuple-element.12) | data formatting | bytes 2097152 | tf_op jit(solution)/shard_map/slice | solution.py:184
  20.3 2.8 %copy.30 = bf16[2,64,4096]{1,2,0:T(8,128)(2,1)} copy(bf16[2,64,4096]{2,1,0:T(8,128)(2,1)} %get-tuple-element.11) | data formatting | bytes 2097152 | tf_op jit(solution)/shard_map/slice | solution.py:183
  23.0 5.6 %maximum_bitcast_fusion = bf16[2,128,64,64]{2,3,1,0:T(8,128)(2,1)} fusion(bf16[2,64,128,32]{1,3,2,0:T(8,128)(2,1)} %bitcast.205, bf16[2,64,128,32]{1,3,2,0:T(8,128)(2,1)} %bitcast.206), kind=kLoop, calls=%fused_computation.1 | loop fusion | flops 4194304 | bytes 4194304 | tf_op jit(solution)/shard_map/transpose | solution.py:185
  28.6 8.5 %copy.32 = bf16[2,128,64,64]{1,3,2,0:T(8,128)(2,1)} copy(bf16[2,128,64,64]{2,3,1,0:T(8,128)(2,1)} %maximum_bitcast_fusion) | data formatting | bytes 4194304 | tf_op jit(solution)/shard_map/transpose | solution.py:185
  37.1 2.5 %fusion.59 = bf16[2,128,320]{1,2,0:T(8,128)(2,1)S(1)} fusion(bf16[2,128,4096]{1,2,0:T(8,128)(2,1)} %bitcast.207, bf16[4096,320]{0,1:T(8,128)(2,1)S(1)} %copy-done), kind=kOutput, calls=%fused_computation.57 | convolution fusion | flops 671170560 | bytes 4882432 | tf_op jit(solution)/shard_map/sjk,kd->sjd/dot_general | solution.py:187
  39.6 9.6 %all_gather.3 = bf16[2,128,1280]{1,2,0:T(8,128)(2,1)S(1)} all-gather(bf16[2,128,320]{1,2,0:T(8,128)(2,1)S(1)} %fusion.59), channel_id=1, replica_groups=mesh['groups'=2,'tm'=4,'mp'=2,'section'=2] {'mp','section'}, dimensions={2}, use_global_device_ids=true | all-gather | bytes 819200 | tf_op jit(solution)/shard_map/all_gather | solution.py:191
  55.2 1.7 %fusion.56 = bf16[2,128,640]{2,1,0:T(8,128)(2,1)} fusion(bf16[1,1280,640]{2,1,0:T(8,128)(2,1)S(1)} %copy-done.8, bf16[2,128,1280]{1,2,0:T(8,128)(2,1)S(1)} %all_gather.3, f32[1280]{0:T(1024)S(1)} %convert_reduce_fusion, f32[2,128]{1,0:T(2,128)S(1)} %add_rsqrt_fusion.1), kind=kOutput, calls=%fused_computation.56 | convolution fusion | flops 421068800 | bytes 2627584 | tf_op jit(solution)/shard_map/btd,de->bte/dot_general | solution.py:72
  56.9 1.9 %copy.37 = bf16[2,128,640]{1,2,0:T(8,128)(2,1)} copy(bf16[2,128,640]{2,1,0:T(8,128)(2,1)} %fusion.56) | data formatting | bytes 655360 | tf_op jit(solution)/shard_map/convert_element_type | solution.py:74
  59.9 1.8 %fusion = (f32[2,2,4,128]{3,2,1,0:T(4,128)S(1)}, f32[2,2,512,128,4]{3,2,4,1,0:T(8,128)S(1)}) fusion(pred[2,128,512]{1,2,0:T(8,128)(4,1)S(1)} %or_and_fusion, bf16[2,128,2,4,80]{1,4,3,2,0:T(8,128)(2,1)} %bitcast.209, bf16[1,2,2,2,80,512]{5,4,3,2,1,0:T(8,128)(2,1)S(1)} %maximum_bitcast_fusion.1), kind=kOutput, calls=%fused_computation.6 | convolution fusion | flops 169867264 | bytes 4988928 | tf_op jit(solution)/shard_map/btkgh,bkhn->bkgtn/dot_general | solution.py:47
  63.9 1.6 %convolution_convert_fusion.1 = bf16[2,128,1280]{1,2,0:T(8,128)(2,1)} fusion(bf16[2,128,640]{1,2,0:T(8,128)(2,1)S(1)} %bitcast.223, bf16[1,640,1280]{2,1,0:T(8,128)(2,1)S(1)} %copy-done.2), kind=kOutput, calls=%fused_computation.17 | convolution fusion | flops 419758080 | bytes 2621440 | tf_op jit(solution)/shard_map/bte,ed->btd/dot_general | solution.py:126
  68.2 5.6 %collective-permute-done.7 = bf16[2,128,1280]{1,2,0:T(8,128)(2,1)} collective-permute-done((bf16[2,128,1280]{1,2,0:T(8,128)(2,1)}, bf16[2,128,1280]{1,2,0:T(8,128)(2,1)}, u32[]{:S(2)}, u32[]{:S(2)}) %collective-permute-start.7) | collective-permute-done | bytes 655392 | tf_op jit(solution)/shard_map/ppermute | solution.py:203
  73.8 8.9 %collective-permute-done.8 = bf16[2,128,1280]{1,2,0:T(8,128)(2,1)} collective-permute-done((bf16[2,128,1280]{1,2,0:T(8,128)(2,1)}, bf16[2,128,1280]{1,2,0:T(8,128)(2,1)}, u32[]{:S(2)}, u32[]{:S(2)}) %collective-permute-start.8) | collective-permute-done | bytes 655392 | tf_op jit(solution)/shard_map/ppermute | solution.py:203
  82.7 1.6 %fusion.28 = (f32[2,128]{1,0:T(2,128)S(1)}, bf16[2,128,1280]{1,2,0:T(8,128)(2,1)S(1)}) fusion(bf16[2,128,1280]{1,2,0:T(8,128)(2,1)} %collective-permute-done.8, bf16[2,128,1280]{1,2,0:T(8,128)(2,1)} %collective-permute-done.7, bf16[2,128,1280]{1,2,0:T(8,128)(2,1)S(1)} %all_gather.3), kind=kLoop, calls=%fused_computation.42 | loop fusion | flops 2948864 | bytes 2622464 | tf_op jit(solution)/shard_map/reduce_sum | solution.py:69
  85.9 4.9 %collective-permute-start.10 = (bf16[2,2,2,80,128]{4,3,2,1,0:T(8,128)(2,1)}, bf16[2,2,2,80,128]{4,3,2,1,0:T(8,128)(2,1)S(1)}, u32[]{:S(2)}, u32[]{:S(2)}) collective-permute-start(bf16[2,2,2,80,128]{4,3,2,1,0:T(8,128)(2,1)} %pad_maximum_fusion.2), channel_id=1, source_target_pairs={{1,9},{5,13},{3,11},{7,15},{17,25},{21,29},{19,27},{23,31}} | collective-permute-start | bytes 491528 | tf_op jit(solution)/shard_map/ppermute | solution.py:34
  90.8 2.0 %collective-permute-start.11 = (bf16[2,2,2,80,128]{4,3,2,1,0:T(8,128)(2,1)}, bf16[2,2,2,80,128]{4,3,2,1,0:T(8,128)(2,1)}, u32[]{:S(2)}, u32[]{:S(2)}) collective-permute-start(bf16[2,2,2,80,128]{4,3,2,1,0:T(8,128)(2,1)} %pad_maximum_fusion.2), channel_id=1, source_target_pairs={{1,5},{5,9},{9,13},{3,7},{7,11},{11,15},{17,21},{21,25},{25,29},{1... | collective-permute-start | bytes 491528 | tf_op jit(solution)/shard_map/ppermute | solution.py:34
  92.8 2.0 %collective-permute-start.9 = (bf16[2,2,2,80,128]{4,3,2,1,0:T(8,128)(2,1)}, bf16[2,2,2,80,128]{4,3,2,1,0:T(8,128)(2,1)}, u32[]{:S(2)}, u32[]{:S(2)}) collective-permute-start(bf16[2,2,2,80,128]{4,3,2,1,0:T(8,128)(2,1)} %pad_maximum_fusion.2), channel_id=1, source_target_pairs={{1,13},{3,15},{17,29},{19,31}} | collective-permute-start | bytes 491528 | tf_op jit(solution)/shard_map/ppermute | solution.py:34
  94.8 1.7 %fusion.53 = bf16[2,128,640]{2,1,0:T(8,128)(2,1)} fusion(bf16[1,1280,640]{2,1,0:T(8,128)(2,1)S(1)} %copy-done.9, bf16[2,128,1280]{1,2,0:T(8,128)(2,1)S(1)} %get-tuple-element.10, f32[2,128]{1,0:T(2,128)S(1)} %add_rsqrt_fusion, f32[1280]{0:T(1024)S(1)} %convert_reduce_fusion), kind=kOutput, calls=%fused_computation.55 | convolution fusion | flops 421068800 | bytes 2627584 | tf_op jit(solution)/shard_map/btd,de->bte/dot_general | solution.py:72
  107.8 3.1 %collective-permute-start.14 = (bf16[1,128,640]{1,2,0:T(8,128)(2,1)S(1)}, bf16[1,128,640]{1,2,0:T(8,128)(2,1)S(1)}, u32[]{:S(2)}, u32[]{:S(2)}) collective-permute-start(bf16[1,128,640]{1,2,0:T(8,128)(2,1)S(1)} %constant_dynamic-slice_fusion), channel_id=1, source_target_pairs={{1,3},{3,1},{5,7},{7,5},{9,11},{11,9},{13,15},{15,13},{17,19},{19,... | collective-permute-start | bytes 491528 | tf_op jit(solution)/shard_map/ppermute | solution.py:240
  111.6 2.3 %collective-permute-done.14 = bf16[1,128,640]{1,2,0:T(8,128)(2,1)S(1)} collective-permute-done((bf16[1,128,640]{1,2,0:T(8,128)(2,1)S(1)}, bf16[1,128,640]{1,2,0:T(8,128)(2,1)S(1)}, u32[]{:S(2)}, u32[]{:S(2)}) %collective-permute-start.14) | collective-permute-done | bytes 163872 | tf_op jit(solution)/shard_map/ppermute | solution.py:240
  (113 shorter events, 32.4 us)
Async XLA Ops:
  0.6 36.5 %copy-start = (bf16[4096,320]{0,1:T(8,128)(2,1)S(1)}, bf16[4096,320]{0,1:T(8,128)(2,1)}, u32[]{:S(2)}) copy-start(bf16[4096,320]{0,1:T(8,128)(2,1)} %param.10) | copy-start | bytes 7864324
  0.6 11.5 %copy-start.7 = (bf16[1,1280]{1,0:T(2,128)(2,1)S(1)}, bf16[1,1280]{1,0:T(2,128)(2,1)}, u32[]{:S(2)}) copy-start(bf16[1,1280]{1,0:T(2,128)(2,1)} %param.11) | copy-start | bytes 7684
  4.0 8.8 %collective-permute-start.1 = (f32[2,2,64]{2,1,0:T(2,128)S(1)}, f32[2,2,64]{2,1,0:T(2,128)S(1)}, u32[]{:S(2)}, u32[]{:S(2)}) collective-permute-start(f32[2,2,64]{2,1,0:T(2,128)S(1)} %get-tuple-element.26), channel_id=1, source_target_pairs={{0,4},{4,8},{8,12},{12,0},{1,5},{5,9},{9,13},{13,1},{2,6},{6,10},{... | collective-permute-start | bytes 3080 | tf_op jit(solution)/shard_map/ppermute | solution.py:13
  6.1 6.6 %collective-permute-start.2 = (f32[2,2,64]{2,1,0:T(2,128)S(1)}, f32[2,2,64]{2,1,0:T(2,128)S(1)}, u32[]{:S(2)}, u32[]{:S(2)}) collective-permute-start(f32[2,2,64]{2,1,0:T(2,128)S(1)} %get-tuple-element.26), channel_id=1, source_target_pairs={{0,8},{4,12},{8,0},{12,4},{1,9},{5,13},{9,1},{13,5},{2,10},{6,14},... | collective-permute-start | bytes 3080 | tf_op jit(solution)/shard_map/ppermute | solution.py:13
  8.4 4.3 %collective-permute-start.3 = (f32[2,2,64]{2,1,0:T(2,128)S(1)}, f32[2,2,64]{2,1,0:T(2,128)S(1)}, u32[]{:S(2)}, u32[]{:S(2)}) collective-permute-start(f32[2,2,64]{2,1,0:T(2,128)S(1)} %get-tuple-element.26), channel_id=1, source_target_pairs={{0,12},{4,0},{8,4},{12,8},{1,13},{5,1},{9,5},{13,9},{2,14},{6,2},{... | collective-permute-start | bytes 3080 | tf_op jit(solution)/shard_map/ppermute | solution.py:13
  9.6 4.1 %collective-permute-start = (bf16[2,64,32]{2,1,0:T(8,128)(2,1)S(1)}, bf16[2,64,32]{2,1,0:T(8,128)(2,1)S(1)}, u32[]{:S(2)}, u32[]{:S(2)}) collective-permute-start(bf16[2,64,32]{2,1,0:T(8,128)(2,1)S(1)} %slice.45), channel_id=1, source_target_pairs={{0,4},{4,8},{8,12},{1,5},{5,9},{9,13},{2,6},{6,10},{10,14},{3,7},{... | collective-permute-start | bytes 24584 | tf_op jit(solution)/shard_map/ppermute | solution.py:13
  37.1 12.4 %copy-start.10 = (bf16[1,1280,160]{1,2,0:T(8,128)(2,1)S(1)}, bf16[1,1280,160]{1,2,0:T(8,128)(2,1)}, u32[]{:S(2)}) copy-start(bf16[1,1280,160]{1,2,0:T(8,128)(2,1)} %param.14) | copy-start | bytes 1228804
  39.6 10.3 %copy-start.12 = (bf16[1,1280,160]{1,2,0:T(8,128)(2,1)S(1)}, bf16[1,1280,160]{1,2,0:T(8,128)(2,1)}, u32[]{:S(2)}) copy-start(bf16[1,1280,160]{1,2,0:T(8,128)(2,1)} %param.13) | copy-start | bytes 1228804
  51.2 7.5 %collective-permute-start.4 = (bf16[2,2,2,80,128]{4,3,2,1,0:T(8,128)(2,1)}, bf16[2,2,2,80,128]{4,3,2,1,0:T(8,128)(2,1)}, u32[]{:S(2)}, u32[]{:S(2)}) collective-permute-start(bf16[2,2,2,80,128]{4,3,2,1,0:T(8,128)(2,1)} %pad_maximum_fusion.1), channel_id=1, source_target_pairs={{0,12},{2,14},{16,28},{18,30}} | collective-permute-start | bytes 491528 | tf_op jit(solution)/shard_map/ppermute | solution.py:34
  52.5 6.2 %collective-permute-start.5 = (bf16[2,2,2,80,128]{4,3,2,1,0:T(8,128)(2,1)}, bf16[2,2,2,80,128]{4,3,2,1,0:T(8,128)(2,1)}, u32[]{:S(2)}, u32[]{:S(2)}) collective-permute-start(bf16[2,2,2,80,128]{4,3,2,1,0:T(8,128)(2,1)} %pad_maximum_fusion.1), channel_id=1, source_target_pairs={{0,8},{4,12},{2,10},{6,14},{16,24},{20,28},{18,26},{22,30}} | collective-permute-start | bytes 491528 | tf_op jit(solution)/shard_map/ppermute | solution.py:34
  53.9 4.9 %collective-permute-start.6 = (bf16[2,2,2,80,128]{4,3,2,1,0:T(8,128)(2,1)}, bf16[2,2,2,80,128]{4,3,2,1,0:T(8,128)(2,1)}, u32[]{:S(2)}, u32[]{:S(2)}) collective-permute-start(bf16[2,2,2,80,128]{4,3,2,1,0:T(8,128)(2,1)} %pad_maximum_fusion.1), channel_id=1, source_target_pairs={{0,4},{4,8},{8,12},{2,6},{6,10},{10,14},{16,20},{20,24},{24,28},{1... | collective-permute-start | bytes 491528 | tf_op jit(solution)/shard_map/ppermute | solution.py:34
  65.6 8.2 %collective-permute-start.7 = (bf16[2,128,1280]{1,2,0:T(8,128)(2,1)}, bf16[2,128,1280]{1,2,0:T(8,128)(2,1)}, u32[]{:S(2)}, u32[]{:S(2)}) collective-permute-start(bf16[2,128,1280]{1,2,0:T(8,128)(2,1)} %convolution_convert_fusion.1), channel_id=1, source_target_pairs={{0,1},{2,3},{4,5},{6,7},{8,9},{10,11},{12,13},{14,15},{16,17},{18,... | collective-permute-start | bytes 1966088 | tf_op jit(solution)/shard_map/ppermute | solution.py:203
  66.8 15.9 %collective-permute-start.8 = (bf16[2,128,1280]{1,2,0:T(8,128)(2,1)}, bf16[2,128,1280]{1,2,0:T(8,128)(2,1)}, u32[]{:S(2)}, u32[]{:S(2)}) collective-permute-start(bf16[2,128,1280]{1,2,0:T(8,128)(2,1)} %convolution_convert_fusion.1), channel_id=1, source_target_pairs={{0,3},{2,1},{4,7},{6,5},{8,11},{10,9},{12,15},{14,13},{16,19},{18,... | collective-permute-start | bytes 1966088 | tf_op jit(solution)/shard_map/ppermute | solution.py:203
  68.2 16.2 %copy-start.11 = (bf16[1,1280,160]{1,2,0:T(8,128)(2,1)S(1)}, bf16[1,1280,160]{1,2,0:T(8,128)(2,1)}, u32[]{:S(2)}) copy-start(bf16[1,1280,160]{1,2,0:T(8,128)(2,1)} %param.14) | copy-start | bytes 1228804
  68.2 16.6 %copy-start.13 = (bf16[1,1280,160]{1,2,0:T(8,128)(2,1)S(1)}, bf16[1,1280,160]{1,2,0:T(8,128)(2,1)}, u32[]{:S(2)}) copy-start(bf16[1,1280,160]{1,2,0:T(8,128)(2,1)} %param.13) | copy-start | bytes 1228804
  84.4 10.4 %copy-start.9 = (bf16[1,1280,640]{2,1,0:T(8,128)(2,1)S(1)}, bf16[1,1280,640]{2,1,0:T(8,128)(2,1)}, u32[]{:S(2)}) copy-start(bf16[1,1280,640]{2,1,0:T(8,128)(2,1)} %param.12) | copy-start | bytes 4915204
  85.9 11.4 %copy-start.5 = (bf16[2,128,160]{1,2,0:T(8,128)(2,1)S(1)}, bf16[2,128,160]{1,2,0:T(8,128)(2,1)}, u32[]{:S(2)}) copy-start(bf16[2,128,160]{1,2,0:T(8,128)(2,1)} %copy-done.4) | copy-start | bytes 245764
  85.9 14.2 %collective-permute-start.10 = (bf16[2,2,2,80,128]{4,3,2,1,0:T(8,128)(2,1)}, bf16[2,2,2,80,128]{4,3,2,1,0:T(8,128)(2,1)S(1)}, u32[]{:S(2)}, u32[]{:S(2)}) collective-permute-start(bf16[2,2,2,80,128]{4,3,2,1,0:T(8,128)(2,1)} %pad_maximum_fusion.2), channel_id=1, source_target_pairs={{1,9},{5,13},{3,11},{7,15},{17,25},{21,29},{19,27},{23,31}} | collective-permute-start | bytes 491528 | tf_op jit(solution)/shard_map/ppermute | solution.py:34
  90.8 9.3 %collective-permute-start.11 = (bf16[2,2,2,80,128]{4,3,2,1,0:T(8,128)(2,1)}, bf16[2,2,2,80,128]{4,3,2,1,0:T(8,128)(2,1)}, u32[]{:S(2)}, u32[]{:S(2)}) collective-permute-start(bf16[2,2,2,80,128]{4,3,2,1,0:T(8,128)(2,1)} %pad_maximum_fusion.2), channel_id=1, source_target_pairs={{1,5},{5,9},{9,13},{3,7},{7,11},{11,15},{17,21},{21,25},{25,29},{1... | collective-permute-start | bytes 491528 | tf_op jit(solution)/shard_map/ppermute | solution.py:34
  92.8 7.3 %collective-permute-start.9 = (bf16[2,2,2,80,128]{4,3,2,1,0:T(8,128)(2,1)}, bf16[2,2,2,80,128]{4,3,2,1,0:T(8,128)(2,1)}, u32[]{:S(2)}, u32[]{:S(2)}) collective-permute-start(bf16[2,2,2,80,128]{4,3,2,1,0:T(8,128)(2,1)} %pad_maximum_fusion.2), channel_id=1, source_target_pairs={{1,13},{3,15},{17,29},{19,31}} | collective-permute-start | bytes 491528 | tf_op jit(solution)/shard_map/ppermute | solution.py:34
  105.0 8.9 %copy-start.6 = (bf16[1,128,1280]{1,2,0:T(8,128)(2,1)S(1)}, bf16[1,128,1280]{1,2,0:T(8,128)(2,1)}, u32[]{:S(2)}) copy-start(bf16[1,128,1280]{1,2,0:T(8,128)(2,1)} %get-tuple-element.13) | copy-start | bytes 983044
  105.2 8.7 %collective-permute-start.12 = (bf16[2,1,128,640]{2,3,1,0:T(8,128)(2,1)S(1)}, bf16[2,1,128,640]{2,3,1,0:T(8,128)(2,1)S(1)}, u32[]{:S(2)}, u32[]{:S(2)}) collective-permute-start(bf16[2,1,128,640]{2,3,1,0:T(8,128)(2,1)S(1)} %pad_maximum_fusion), channel_id=1, source_target_pairs={{1,0},{3,2},{5,4},{7,6},{9,8},{11,10},{13,12},{15,14},{17,16},{19,... | collective-permute-start | bytes 983048 | tf_op jit(solution)/shard_map/ppermute | solution.py:236
  106.5 5.1 %collective-permute-start.13 = (bf16[1,128,640]{1,2,0:T(8,128)(2,1)S(1)}, bf16[1,128,640]{1,2,0:T(8,128)(2,1)S(1)}, u32[]{:S(2)}, u32[]{:S(2)}) collective-permute-start(bf16[1,128,640]{1,2,0:T(8,128)(2,1)S(1)} %get-tuple-element.18), channel_id=1, source_target_pairs={{1,2},{3,0},{5,6},{7,4},{9,10},{11,8},{13,14},{15,12},{17,18},{19,... | collective-permute-start | bytes 491528 | tf_op jit(solution)/shard_map/ppermute | solution.py:236
  107.8 6.1 %collective-permute-start.14 = (bf16[1,128,640]{1,2,0:T(8,128)(2,1)S(1)}, bf16[1,128,640]{1,2,0:T(8,128)(2,1)S(1)}, u32[]{:S(2)}, u32[]{:S(2)}) collective-permute-start(bf16[1,128,640]{1,2,0:T(8,128)(2,1)S(1)} %constant_dynamic-slice_fusion), channel_id=1, source_target_pairs={{1,3},{3,1},{5,7},{7,5},{9,11},{11,9},{13,15},{15,13},{17,19},{19,... | collective-permute-start | bytes 491528 | tf_op jit(solution)/shard_map/ppermute | solution.py:240
  (5 other events, 12.0 us)

commit v3 on v2

--- a/solution.py
+++ b/solution.py
@@ -141,8 +141,6 @@
     feat_at = mp_at * sec_n + sec_at
     total_steps = steps_dev * tm_n
     total_tokens = tok_count * tm_n
-
-    prior_raw = shift_from(series[:, :, steps_dev - STRIDE :], "tm", tm_n, 1, False)
 
     first_step = total_steps - lengths
     step_pos = tm_at * steps_dev + jnp.arange(steps_dev, dtype=jnp.int32)
@@ -160,10 +158,21 @@
     local_mean = local_sum / jnp.maximum(my_count, 1.0)[:, None]
     local_dev = (values - local_mean[..., None]) * valid[:, None, :]
     local_m2 = jnp.sum(local_dev * local_dev, -1)
-    stats = gather_ordered(jnp.stack([local_sum, local_m2], 0), "tm", tm_n, tm_at)
+    tail = series[:, :, steps_dev - STRIDE :]
+    if tm_n > SMALL_GROUP:
+        stats = lax.all_gather(jnp.stack([local_sum, local_m2], -1), "tm", axis=0)
+        prior_raw = shift_from(tail, "tm", tm_n, 1, False).astype(jnp.float32)
+    else:
+        payload = jnp.concatenate(
+            [jnp.stack([local_sum, local_m2], -1), tail.astype(jnp.float32)], -1
+        )
+        received = [payload] + [shift_from(payload, "tm", tm_n, by, True) for by in range(1, tm_n)]
+        prior_raw = received[1][..., 2:] if tm_n > 1 else jnp.zeros_like(payload[..., 2:])
+        order = (tm_at - jnp.arange(tm_n, dtype=jnp.int32)) % tm_n
+        stats = jnp.take(jnp.stack([piece[..., :2] for piece in received], 0), order, axis=0)
     history = lengths.astype(jnp.float32)[:, None]
-    shard_sums = stats[:, 0]
-    shard_m2 = stats[:, 1]
+    shard_sums = stats[..., 0]
+    shard_m2 = stats[..., 1]
     channel_mean = jnp.sum(shard_sums, 0) / history
     shard_counts = jnp.moveaxis(counts, 1, 0)[:, :, None]
     shard_means = shard_sums / jnp.maximum(shard_counts, 1.0)
@@ -172,7 +181,7 @@
     variance = spread_total / history
     inv_std = lax.rsqrt(variance + 1e-05)[..., None]
 
-    padded = jnp.concatenate([prior_raw, series], -1).astype(jnp.float32)
+    padded = jnp.concatenate([prior_raw, series.astype(jnp.float32)], -1)
     padded_pos = tm_at * steps_dev - STRIDE + jnp.arange(steps_dev + STRIDE, dtype=jnp.int32)
     padded_valid = (
         (padded_pos[None, :] >= first_step[:, None]) & (padded_pos[None, :] >= 0)
@@ -180,12 +189,11 @@
     normed = (
         (padded * padded_valid - channel_mean[..., None]) * padded_valid * inv_std
     ).astype(jnp.bfloat16)
-    left = normed[:, :, :steps_dev].reshape(seq_count, channels, tok_count, STRIDE)
-    right = normed[:, :, STRIDE:].reshape(seq_count, channels, tok_count, STRIDE)
-    window = jnp.concatenate([left, right], -1).transpose(0, 2, 1, 3)
-    window = window.reshape(seq_count, tok_count, channels * 2 * STRIDE)
+    blocks = jnp.swapaxes(normed.reshape(seq_count, channels, tok_count + 1, STRIDE), 2, 3)
+    window = jnp.concatenate([blocks[..., :tok_count], blocks[..., 1:]], 2)
+    window = window.reshape(seq_count, channels * 2 * STRIDE, tok_count)
     tokens = jnp.einsum(
-        "sjk,kd->sjd", window, patch_weight, preferred_element_type=jnp.float32
+        "kd,skj->sjd", patch_weight, window, preferred_element_type=jnp.float32
     ).astype(jnp.bfloat16)
     column_count = patch_weight.shape[1]
     hidden0 = lax.all_gather(tokens, feat_axes, axis=2, tiled=True)

time: 116 us -> 118 us (1.017)
  other arithmetic: 20.5 us -> 26.7 us
  starting transfers between devices: 28.9 us -> 25.7 us
    concatenate x0 -> x2, local copies, waits for them, and re-layouts: none -> 13.2 us  [the longest x1 8.49 us: per_device(): window = jnp.concatenate([blocks[..., :tok_count], blocks[..., 1:]], 2)]
    transpose x1 -> x0, local copies, waits for them, and re-layouts: 8.49 us -> none  [per_device(): window = jnp.concatenate([left, right], -1).transpose(0, 2, 1, 3)]
    concatenate x0 -> x3, other arithmetic: none -> 6.9 us  [the longest x1 3.57 us: per_device(): padded = jnp.concatenate([prior_raw, series.astype(jnp.float32)], -1)]
    slice x4, local copies, waits for them, and re-layouts: 7.35 us -> 1.58 us  [the longest x1 0.84 us: per_device(): tail = series[:, :, steps_dev - STRIDE:]]
    ppermute x4 -> x3, starting transfers between devices: 7.83 us -> 4.66 us  [shift_from(): return lax.ppermute(value, axis, pairs)]
    transpose x1, other arithmetic: 5.57 us -> 2.94 us  [per_device(): jnp.swapaxes(normed.reshape(seq_count, channels, tok_count + 1, STRIDE),...]
    reduce_sum x1, other arithmetic: 0.5 us -> 1.73 us  [per_device(): local_m2 = jnp.sum(local_dev * local_dev, -1)]
    convert_element_type x1 -> x2, other arithmetic: 2.04 us -> 2.79 us  [the longest x1 2.78 us: per_device(): values = series.astype(jnp.float32)]
  transfers between devices with their start and end apart: 15 -> 14, of which waited for: 3 -> 3; matrix products, arithmetic and copies ran while one was open for 10% -> 11% of each run, Pallas kernels for 0% -> 0%
where the time goes in v3:
time: 118 us; the launch traced here: 117 us
  other arithmetic  26.7 us (23%)
  starting transfers between devices  25.7 us (22%)
  local copies, waits for them, and re-layouts  22.3 us (19%)
  waiting for transfers between devices  17.1 us (14%)
  matrix products  14.4 us (12%)
  blocking collectives  9.71 us (8%)
  between operations  1.2 us (1%)
    ppermute x2, waiting for transfers between devices, per_device(): arrivals.append(lax.ppermute(partial0, feat_axes, pairs))  14.8 us
    ppermute x6, starting transfers between devices, gather_causal(): pieces.append(lax.ppermute(value, ('tm', 'section'), pairs))  12.7 us
    all_gather x1, blocking collectives, per_device(): hidden0 = lax.all_gather(tokens, feat_axes, axis=2, tiled=True)  9.71 us
    concatenate x1, local copies, waits for them, and re-layouts, per_device(): window = jnp.concatenate([blocks[..., :tok_count], blocks[..., 1:]], 2)  8.49 us
    concatenate x1, local copies, waits for them, and re-layouts, per_device(): padded = jnp.concatenate([prior_raw, series.astype(jnp.float32)], -1)  4.67 us
    ppermute x3, starting transfers between devices, shift_from(): return lax.ppermute(value, axis, pairs)  4.66 us
    concatenate x1, other arithmetic, per_device(): padded = jnp.concatenate([prior_raw, series.astype(jnp.float32)], -1)  3.57 us
    dot_general x2, matrix products, attend_layer(): jnp.einsum('btd,de->bte', layer_input, query_w, preferred_element_type=jn...  3.31 us
  transfers between devices with their start and end apart: 14, of which 3 were waited for; matrix products, arithmetic and copies ran while one was open for 11% of the time, Pallas kernels for 0%

profile of v3, /device:TPU:1, one launch (start us, length us, event | category | flops | bytes accessed | tf_op | source)
XLA Modules:
  0.0 117.1 jit_solution(7334325007315233201)
XLA Ops:
  4.3 1.7 %multiply_reduce_fusion = f32[2,64]{1,0:T(2,128)S(1)} fusion(f32[2,64]{1,0:T(2,128)S(1)} %broadcast_divide_fusion.1, f32[2,4096]{1,0:T(2,128)S(1)} %compare_convert_fusion, bf16[2,64,4096]{2,1,0:T(8,128)(2,1)} %param.8), kind=kLoop, calls=%fused_computation.25 | loop fusion | flops 2621312 | bytes 1082368 | tf_op jit(solution)/shard_map/reduce_sum | solution.py:160
  6.1 2.2 %collective-permute-start = (f32[2,64,34]{1,0,2:T(2,128)S(1)}, f32[2,64,34]{1,0,2:T(2,128)S(1)}, u32[]{:S(2)}, u32[]{:S(2)}) collective-permute-start(f32[2,64,34]{1,0,2:T(2,128)S(1)} %pad_maximum_fusion.5), channel_id=1, source_target_pairs={{0,4},{4,8},{8,12},{12,0},{1,5},{5,9},{9,13},{13,1},{2,6},{6,10},{... | collective-permute-start | bytes 52232 | tf_op jit(solution)/shard_map/ppermute | solution.py:13
  8.3 2.1 %collective-permute-start.2 = (f32[2,64,34]{1,0,2:T(2,128)S(1)}, f32[2,64,34]{1,0,2:T(2,128)S(1)}, u32[]{:S(2)}, u32[]{:S(2)}) collective-permute-start(f32[2,64,34]{1,0,2:T(2,128)S(1)} %pad_maximum_fusion.5), channel_id=1, source_target_pairs={{0,12},{4,0},{8,4},{12,8},{1,13},{5,1},{9,5},{13,9},{2,14},{6,2},{... | collective-permute-start | bytes 52232 | tf_op jit(solution)/shard_map/ppermute | solution.py:13
  11.7 2.8 %convert_element_type.168 = f32[2,64,4096]{2,1,0:T(8,128)} convert(bf16[2,64,4096]{2,1,0:T(8,128)(2,1)} %param.8) | non-fusion elementwise | flops 524288 | bytes 3145728 | tf_op jit(solution)/shard_map/convert_element_type | solution.py:148
  15.5 3.6 %pad_maximum_fusion.1 = f32[2,64,4128]{2,1,0:T(8,128)} fusion(f32[2,64,4096]{2,1,0:T(8,128)} %convert_element_type.168, f32[2,64,32]{2,1,0:T(8,128)S(1)} %copy.31), kind=kLoop, calls=%fused_computation.17 | loop fusion | flops 528384 | bytes 4227072 | tf_op jit(solution)/shard_map/concatenate | solution.py:184
  19.1 4.7 %copy.32 = f32[2,64,4128]{1,2,0:T(8,128)} copy(f32[2,64,4128]{2,1,0:T(8,128)} %pad_maximum_fusion.1) | data formatting | bytes 4227072 | tf_op jit(solution)/shard_map/concatenate | solution.py:184
  23.8 2.9 %fusion.8 = bf16[2,64,32,129]{1,2,3,0:T(8,128)(2,1)S(1)} fusion(f32[2,64,129,32]{1,3,2,0:T(8,128)} %bitcast.207, f32[2,64]{1,0:T(2,128)S(1)} %add_rsqrt_fusion.2, f32[2,64]{1,0:T(2,128)S(1)} %broadcast_divide_fusion, f32[2,129,32]{2,1,0:T(8,128)S(1)} %and_convert_fusion), kind=kLoop, calls=%fused_computation.18 | loop fusion | flops 2641920 | bytes 3204352 | tf_op jit(solution)/shard_map/transpose | solution.py:192
  27.4 3.3 %pad_maximum_fusion = bf16[2,64,64,128]{1,2,3,0:T(8,128)(2,1)} fusion(bf16[2,64,32,128]{1,2,3,0:T(8,128)(2,1)S(1)} %get-tuple-element.12, bf16[2,64,32,128]{1,2,3,0:T(8,128)(2,1)S(1)} %get-tuple-element.11), kind=kLoop, calls=%fused_computation.2 | loop fusion | flops 4194304 | bytes 4194304 | tf_op jit(solution)/shard_map/concatenate | solution.py:193
  30.7 8.5 %copy.34 = bf16[2,64,64,128]{3,2,1,0:T(8,128)(2,1)} copy(bf16[2,64,64,128]{1,2,3,0:T(8,128)(2,1)} %pad_maximum_fusion) | data formatting | bytes 4194304 | tf_op jit(solution)/shard_map/concatenate | solution.py:193
  39.2 2.5 %fusion.56 = bf16[2,128,320]{1,2,0:T(8,128)(2,1)S(1)} fusion(bf16[2,4096,128]{2,1,0:T(8,128)(2,1)} %bitcast.208, bf16[4096,320]{0,1:T(8,128)(2,1)S(1)} %copy-done), kind=kOutput, calls=%fused_computation.55 | convolution fusion | flops 671170560 | bytes 4882432 | tf_op jit(solution)/shard_map/kd,skj->sjd/dot_general | solution.py:195
  41.7 9.7 %all_gather.3 = bf16[2,128,1280]{1,2,0:T(8,128)(2,1)S(1)} all-gather(bf16[2,128,320]{1,2,0:T(8,128)(2,1)S(1)} %fusion.56), channel_id=1, replica_groups=mesh['groups'=2,'tm'=4,'mp'=2,'section'=2] {'mp','section'}, dimensions={2}, use_global_device_ids=true | all-gather | bytes 819200 | tf_op jit(solution)/shard_map/all_gather | solution.py:199
  57.3 1.7 %fusion.53 = bf16[2,128,640]{2,1,0:T(8,128)(2,1)} fusion(bf16[1,1280,640]{2,1,0:T(8,128)(2,1)S(1)} %copy-done.7, bf16[2,128,1280]{1,2,0:T(8,128)(2,1)S(1)} %all_gather.3, f32[1280]{0:T(1024)S(1)} %convert_reduce_fusion, f32[2,128]{1,0:T(2,128)S(1)} %add_rsqrt_fusion.1), kind=kOutput, calls=%fused_computation.54 | convolution fusion | flops 421068800 | bytes 2627584 | tf_op jit(solution)/shard_map/btd,de->bte/dot_general | solution.py:72
  59.0 1.9 %copy.38 = bf16[2,128,640]{1,2,0:T(8,128)(2,1)} copy(bf16[2,128,640]{2,1,0:T(8,128)(2,1)} %fusion.53) | data formatting | bytes 655360 | tf_op jit(solution)/shard_map/convert_element_type | solution.py:74
  62.0 1.8 %fusion = (f32[2,2,4,128]{3,2,1,0:T(4,128)S(1)}, f32[2,2,512,128,4]{3,2,4,1,0:T(8,128)S(1)}) fusion(pred[2,128,512]{1,2,0:T(8,128)(4,1)S(1)} %or_and_fusion, bf16[2,128,2,4,80]{1,4,3,2,0:T(8,128)(2,1)} %bitcast.210, bf16[1,2,2,2,80,512]{5,4,3,2,1,0:T(8,128)(2,1)S(1)} %maximum_bitcast_fusion), kind=kOutput, calls=%fused_computation.7 | convolution fusion | flops 169867264 | bytes 4988928 | tf_op jit(solution)/shard_map/btkgh,bkhn->bkgtn/dot_general | solution.py:47
  66.0 1.6 %convolution_convert_fusion.1 = bf16[2,128,1280]{1,2,0:T(8,128)(2,1)} fusion(bf16[2,128,640]{1,2,0:T(8,128)(2,1)S(1)} %bitcast.224, bf16[1,640,1280]{2,1,0:T(8,128)(2,1)S(1)} %copy-done.1), kind=kOutput, calls=%fused_computation.16 | convolution fusion | flops 419758080 | bytes 2621440 | tf_op jit(solution)/shard_map/bte,ed->btd/dot_general | solution.py:126
  70.3 5.8 %collective-permute-done.6 = bf16[2,128,1280]{1,2,0:T(8,128)(2,1)} collective-permute-done((bf16[2,128,1280]{1,2,0:T(8,128)(2,1)}, bf16[2,128,1280]{1,2,0:T(8,128)(2,1)}, u32[]{:S(2)}, u32[]{:S(2)}) %collective-permute-start.6) | collective-permute-done | bytes 655392 | tf_op jit(solution)/shard_map/ppermute | solution.py:211
  76.1 8.9 %collective-permute-done.7 = bf16[2,128,1280]{1,2,0:T(8,128)(2,1)} collective-permute-done((bf16[2,128,1280]{1,2,0:T(8,128)(2,1)}, bf16[2,128,1280]{1,2,0:T(8,128)(2,1)}, u32[]{:S(2)}, u32[]{:S(2)}) %collective-permute-start.7) | collective-permute-done | bytes 655392 | tf_op jit(solution)/shard_map/ppermute | solution.py:211
  85.1 1.6 %fusion.25 = (f32[2,128]{1,0:T(2,128)S(1)}, bf16[2,128,1280]{1,2,0:T(8,128)(2,1)S(1)}) fusion(bf16[2,128,1280]{1,2,0:T(8,128)(2,1)} %collective-permute-done.7, bf16[2,128,1280]{1,2,0:T(8,128)(2,1)} %collective-permute-done.6, bf16[2,128,1280]{1,2,0:T(8,128)(2,1)S(1)} %all_gather.3), kind=kLoop, calls=%fused_computation.40 | loop fusion | flops 2948864 | bytes 2622464 | tf_op jit(solution)/shard_map/reduce_sum | solution.py:69
  88.3 3.2 %collective-permute-start.10 = (bf16[2,2,2,80,128]{4,3,2,1,0:T(8,128)(2,1)}, bf16[2,2,2,80,128]{4,3,2,1,0:T(8,128)(2,1)S(1)}, u32[]{:S(2)}, u32[]{:S(2)}) collective-permute-start(bf16[2,2,2,80,128]{4,3,2,1,0:T(8,128)(2,1)} %pad_maximum_fusion.4), channel_id=1, source_target_pairs={{1,5},{5,9},{9,13},{3,7},{7,11},{11,15},{17,21},{21,25},{25,29},{1... | collective-permute-start | bytes 491528 | tf_op jit(solution)/shard_map/ppermute | solution.py:34
  91.5 2.8 %collective-permute-start.8 = (bf16[2,2,2,80,128]{4,3,2,1,0:T(8,128)(2,1)}, bf16[2,2,2,80,128]{4,3,2,1,0:T(8,128)(2,1)}, u32[]{:S(2)}, u32[]{:S(2)}) collective-permute-start(bf16[2,2,2,80,128]{4,3,2,1,0:T(8,128)(2,1)} %pad_maximum_fusion.4), channel_id=1, source_target_pairs={{1,13},{3,15},{17,29},{19,31}} | collective-permute-start | bytes 491528 | tf_op jit(solution)/shard_map/ppermute | solution.py:34
  94.3 2.8 %collective-permute-start.9 = (bf16[2,2,2,80,128]{4,3,2,1,0:T(8,128)(2,1)}, bf16[2,2,2,80,128]{4,3,2,1,0:T(8,128)(2,1)}, u32[]{:S(2)}, u32[]{:S(2)}) collective-permute-start(bf16[2,2,2,80,128]{4,3,2,1,0:T(8,128)(2,1)} %pad_maximum_fusion.4), channel_id=1, source_target_pairs={{1,9},{5,13},{3,11},{7,15},{17,25},{21,29},{19,27},{23,31}} | collective-permute-start | bytes 491528 | tf_op jit(solution)/shard_map/ppermute | solution.py:34
  97.1 1.7 %fusion.50 = bf16[2,128,640]{2,1,0:T(8,128)(2,1)} fusion(bf16[1,1280,640]{2,1,0:T(8,128)(2,1)S(1)} %copy-done.8, bf16[2,128,1280]{1,2,0:T(8,128)(2,1)S(1)} %get-tuple-element.10, f32[2,128]{1,0:T(2,128)S(1)} %add_rsqrt_fusion, f32[1280]{0:T(1024)S(1)} %convert_reduce_fusion), kind=kOutput, calls=%fused_computation.53 | convolution fusion | flops 421068800 | bytes 2627584 | tf_op jit(solution)/shard_map/btd,de->bte/dot_general | solution.py:72
  110.1 3.1 %collective-permute-start.13 = (bf16[1,128,640]{1,2,0:T(8,128)(2,1)S(1)}, bf16[1,128,640]{1,2,0:T(8,128)(2,1)S(1)}, u32[]{:S(2)}, u32[]{:S(2)}) collective-permute-start(bf16[1,128,640]{1,2,0:T(8,128)(2,1)S(1)} %constant_dynamic-slice_fusion), channel_id=1, source_target_pairs={{1,3},{3,1},{5,7},{7,5},{9,11},{11,9},{13,15},{15,13},{17,19},{19,... | collective-permute-start | bytes 491528 | tf_op jit(solution)/shard_map/ppermute | solution.py:248
  113.9 2.3 %collective-permute-done.13 = bf16[1,128,640]{1,2,0:T(8,128)(2,1)S(1)} collective-permute-done((bf16[1,128,640]{1,2,0:T(8,128)(2,1)S(1)}, bf16[1,128,640]{1,2,0:T(8,128)(2,1)S(1)}, u32[]{:S(2)}, u32[]{:S(2)}) %collective-permute-start.13) | collective-permute-done | bytes 163872 | tf_op jit(solution)/shard_map/ppermute | solution.py:248
  (118 shorter events, 32.8 us)
Async XLA Ops:
  0.6 38.5 %copy-start = (bf16[4096,320]{0,1:T(8,128)(2,1)S(1)}, bf16[4096,320]{0,1:T(8,128)(2,1)}, u32[]{:S(2)}) copy-start(bf16[4096,320]{0,1:T(8,128)(2,1)} %param.10) | copy-start | bytes 7864324
  0.6 10.4 %copy-start.6 = (bf16[1,1280]{1,0:T(2,128)(2,1)S(1)}, bf16[1,1280]{1,0:T(2,128)(2,1)}, u32[]{:S(2)}) copy-start(bf16[1,1280]{1,0:T(2,128)(2,1)} %param.11) | copy-start | bytes 7684
  6.1 8.3 %collective-permute-start = (f32[2,64,34]{1,0,2:T(2,128)S(1)}, f32[2,64,34]{1,0,2:T(2,128)S(1)}, u32[]{:S(2)}, u32[]{:S(2)}) collective-permute-start(f32[2,64,34]{1,0,2:T(2,128)S(1)} %pad_maximum_fusion.5), channel_id=1, source_target_pairs={{0,4},{4,8},{8,12},{12,0},{1,5},{5,9},{9,13},{13,1},{2,6},{6,10},{... | collective-permute-start | bytes 52232 | tf_op jit(solution)/shard_map/ppermute | solution.py:13
  8.3 6.1 %collective-permute-start.2 = (f32[2,64,34]{1,0,2:T(2,128)S(1)}, f32[2,64,34]{1,0,2:T(2,128)S(1)}, u32[]{:S(2)}, u32[]{:S(2)}) collective-permute-start(f32[2,64,34]{1,0,2:T(2,128)S(1)} %pad_maximum_fusion.5), channel_id=1, source_target_pairs={{0,12},{4,0},{8,4},{12,8},{1,13},{5,1},{9,5},{13,9},{2,14},{6,2},{... | collective-permute-start | bytes 52232 | tf_op jit(solution)/shard_map/ppermute | solution.py:13
  10.4 4.1 %collective-permute-start.1 = (f32[2,64,34]{1,0,2:T(2,128)S(1)}, f32[2,64,34]{1,0,2:T(2,128)S(1)}, u32[]{:S(2)}, u32[]{:S(2)}) collective-permute-start(f32[2,64,34]{1,0,2:T(2,128)S(1)} %pad_maximum_fusion.5), channel_id=1, source_target_pairs={{0,8},{4,12},{8,0},{12,4},{1,9},{5,13},{9,1},{13,5},{2,10},{6,14},... | collective-permute-start | bytes 52232 | tf_op jit(solution)/shard_map/ppermute | solution.py:13
  39.1 12.4 %copy-start.9 = (bf16[1,1280,160]{1,2,0:T(8,128)(2,1)S(1)}, bf16[1,1280,160]{1,2,0:T(8,128)(2,1)}, u32[]{:S(2)}) copy-start(bf16[1,1280,160]{1,2,0:T(8,128)(2,1)} %param.14) | copy-start | bytes 1228804
  41.6 10.4 %copy-start.11 = (bf16[1,1280,160]{1,2,0:T(8,128)(2,1)S(1)}, bf16[1,1280,160]{1,2,0:T(8,128)(2,1)}, u32[]{:S(2)}) copy-start(bf16[1,1280,160]{1,2,0:T(8,128)(2,1)} %param.13) | copy-start | bytes 1228804
  51.4 5.9 %copy-start.7 = (bf16[1,1280,640]{2,1,0:T(8,128)(2,1)S(1)}, bf16[1,1280,640]{2,1,0:T(8,128)(2,1)}, u32[]{:S(2)}) copy-start(bf16[1,1280,640]{2,1,0:T(8,128)(2,1)} %param.12) | copy-start | bytes 4915204
  53.3 7.5 %collective-permute-start.3 = (bf16[2,2,2,80,128]{4,3,2,1,0:T(8,128)(2,1)}, bf16[2,2,2,80,128]{4,3,2,1,0:T(8,128)(2,1)}, u32[]{:S(2)}, u32[]{:S(2)}) collective-permute-start(bf16[2,2,2,80,128]{4,3,2,1,0:T(8,128)(2,1)} %pad_maximum_fusion.3), channel_id=1, source_target_pairs={{0,12},{2,14},{16,28},{18,30}} | collective-permute-start | bytes 491528 | tf_op jit(solution)/shard_map/ppermute | solution.py:34
  54.7 6.2 %collective-permute-start.4 = (bf16[2,2,2,80,128]{4,3,2,1,0:T(8,128)(2,1)}, bf16[2,2,2,80,128]{4,3,2,1,0:T(8,128)(2,1)}, u32[]{:S(2)}, u32[]{:S(2)}) collective-permute-start(bf16[2,2,2,80,128]{4,3,2,1,0:T(8,128)(2,1)} %pad_maximum_fusion.3), channel_id=1, source_target_pairs={{0,8},{4,12},{2,10},{6,14},{16,24},{20,28},{18,26},{22,30}} | collective-permute-start | bytes 491528 | tf_op jit(solution)/shard_map/ppermute | solution.py:34
  56.0 4.9 %collective-permute-start.5 = (bf16[2,2,2,80,128]{4,3,2,1,0:T(8,128)(2,1)}, bf16[2,2,2,80,128]{4,3,2,1,0:T(8,128)(2,1)}, u32[]{:S(2)}, u32[]{:S(2)}) collective-permute-start(bf16[2,2,2,80,128]{4,3,2,1,0:T(8,128)(2,1)} %pad_maximum_fusion.3), channel_id=1, source_target_pairs={{0,4},{4,8},{8,12},{2,6},{6,10},{10,14},{16,20},{20,24},{24,28},{1... | collective-permute-start | bytes 491528 | tf_op jit(solution)/shard_map/ppermute | solution.py:34
  67.7 8.5 %collective-permute-start.6 = (bf16[2,128,1280]{1,2,0:T(8,128)(2,1)}, bf16[2,128,1280]{1,2,0:T(8,128)(2,1)}, u32[]{:S(2)}, u32[]{:S(2)}) collective-permute-start(bf16[2,128,1280]{1,2,0:T(8,128)(2,1)} %convolution_convert_fusion.1), channel_id=1, source_target_pairs={{0,1},{2,3},{4,5},{6,7},{8,9},{10,11},{12,13},{14,15},{16,17},{18,... | collective-permute-start | bytes 1966088 | tf_op jit(solution)/shard_map/ppermute | solution.py:211
  68.9 16.1 %collective-permute-start.7 = (bf16[2,128,1280]{1,2,0:T(8,128)(2,1)}, bf16[2,128,1280]{1,2,0:T(8,128)(2,1)}, u32[]{:S(2)}, u32[]{:S(2)}) collective-permute-start(bf16[2,128,1280]{1,2,0:T(8,128)(2,1)} %convolution_convert_fusion.1), channel_id=1, source_target_pairs={{0,3},{2,1},{4,7},{6,5},{8,11},{10,9},{12,15},{14,13},{16,19},{18,... | collective-permute-start | bytes 1966088 | tf_op jit(solution)/shard_map/ppermute | solution.py:211
  70.3 16.4 %copy-start.10 = (bf16[1,1280,160]{1,2,0:T(8,128)(2,1)S(1)}, bf16[1,1280,160]{1,2,0:T(8,128)(2,1)}, u32[]{:S(2)}) copy-start(bf16[1,1280,160]{1,2,0:T(8,128)(2,1)} %param.14) | copy-start | bytes 1228804
  70.3 16.9 %copy-start.12 = (bf16[1,1280,160]{1,2,0:T(8,128)(2,1)S(1)}, bf16[1,1280,160]{1,2,0:T(8,128)(2,1)}, u32[]{:S(2)}) copy-start(bf16[1,1280,160]{1,2,0:T(8,128)(2,1)} %param.13) | copy-start | bytes 1228804
  86.7 10.4 %copy-start.8 = (bf16[1,1280,640]{2,1,0:T(8,128)(2,1)S(1)}, bf16[1,1280,640]{2,1,0:T(8,128)(2,1)}, u32[]{:S(2)}) copy-start(bf16[1,1280,640]{2,1,0:T(8,128)(2,1)} %param.12) | copy-start | bytes 4915204
  88.3 11.3 %copy-start.4 = (bf16[2,128,160]{1,2,0:T(8,128)(2,1)S(1)}, bf16[2,128,160]{1,2,0:T(8,128)(2,1)}, u32[]{:S(2)}) copy-start(bf16[2,128,160]{1,2,0:T(8,128)(2,1)} %copy-done.3) | copy-start | bytes 245764
  88.3 14.1 %collective-permute-start.10 = (bf16[2,2,2,80,128]{4,3,2,1,0:T(8,128)(2,1)}, bf16[2,2,2,80,128]{4,3,2,1,0:T(8,128)(2,1)S(1)}, u32[]{:S(2)}, u32[]{:S(2)}) collective-permute-start(bf16[2,2,2,80,128]{4,3,2,1,0:T(8,128)(2,1)} %pad_maximum_fusion.4), channel_id=1, source_target_pairs={{1,5},{5,9},{9,13},{3,7},{7,11},{11,15},{17,21},{21,25},{25,29},{1... | collective-permute-start | bytes 491528 | tf_op jit(solution)/shard_map/ppermute | solution.py:34
  91.5 10.9 %collective-permute-start.8 = (bf16[2,2,2,80,128]{4,3,2,1,0:T(8,128)(2,1)}, bf16[2,2,2,80,128]{4,3,2,1,0:T(8,128)(2,1)}, u32[]{:S(2)}, u32[]{:S(2)}) collective-permute-start(bf16[2,2,2,80,128]{4,3,2,1,0:T(8,128)(2,1)} %pad_maximum_fusion.4), channel_id=1, source_target_pairs={{1,13},{3,15},{17,29},{19,31}} | collective-permute-start | bytes 491528 | tf_op jit(solution)/shard_map/ppermute | solution.py:34
  94.3 8.1 %collective-permute-start.9 = (bf16[2,2,2,80,128]{4,3,2,1,0:T(8,128)(2,1)}, bf16[2,2,2,80,128]{4,3,2,1,0:T(8,128)(2,1)}, u32[]{:S(2)}, u32[]{:S(2)}) collective-permute-start(bf16[2,2,2,80,128]{4,3,2,1,0:T(8,128)(2,1)} %pad_maximum_fusion.4), channel_id=1, source_target_pairs={{1,9},{5,13},{3,11},{7,15},{17,25},{21,29},{19,27},{23,31}} | collective-permute-start | bytes 491528 | tf_op jit(solution)/shard_map/ppermute | solution.py:34
  107.3 8.9 %copy-start.5 = (bf16[1,128,1280]{1,2,0:T(8,128)(2,1)S(1)}, bf16[1,128,1280]{1,2,0:T(8,128)(2,1)}, u32[]{:S(2)}) copy-start(bf16[1,128,1280]{1,2,0:T(8,128)(2,1)} %get-tuple-element.13) | copy-start | bytes 983044
  107.5 8.7 %collective-permute-start.11 = (bf16[2,1,128,640]{2,3,1,0:T(8,128)(2,1)S(1)}, bf16[2,1,128,640]{2,3,1,0:T(8,128)(2,1)S(1)}, u32[]{:S(2)}, u32[]{:S(2)}) collective-permute-start(bf16[2,1,128,640]{2,3,1,0:T(8,128)(2,1)S(1)} %pad_maximum_fusion.2), channel_id=1, source_target_pairs={{1,0},{3,2},{5,4},{7,6},{9,8},{11,10},{13,12},{15,14},{17,16},{19,... | collective-permute-start | bytes 983048 | tf_op jit(solution)/shard_map/ppermute | solution.py:244
  108.8 5.1 %collective-permute-start.12 = (bf16[1,128,640]{1,2,0:T(8,128)(2,1)S(1)}, bf16[1,128,640]{1,2,0:T(8,128)(2,1)S(1)}, u32[]{:S(2)}, u32[]{:S(2)}) collective-permute-start(bf16[1,128,640]{1,2,0:T(8,128)(2,1)S(1)} %get-tuple-element.18), channel_id=1, source_target_pairs={{1,2},{3,0},{5,6},{7,4},{9,10},{11,8},{13,14},{15,12},{17,18},{19,... | collective-permute-start | bytes 491528 | tf_op jit(solution)/shard_map/ppermute | solution.py:244
  110.1 6.1 %collective-permute-start.13 = (bf16[1,128,640]{1,2,0:T(8,128)(2,1)S(1)}, bf16[1,128,640]{1,2,0:T(8,128)(2,1)S(1)}, u32[]{:S(2)}, u32[]{:S(2)}) collective-permute-start(bf16[1,128,640]{1,2,0:T(8,128)(2,1)S(1)} %constant_dynamic-slice_fusion), channel_id=1, source_target_pairs={{1,3},{3,1},{5,7},{7,5},{9,11},{11,9},{13,15},{15,13},{17,19},{19,... | collective-permute-start | bytes 491528 | tf_op jit(solution)/shard_map/ppermute | solution.py:248
  (3 other events, 3.5 us)

commit v4 on v3

--- a/solution.py
+++ b/solution.py
@@ -189,11 +189,14 @@
     normed = (
         (padded * padded_valid - channel_mean[..., None]) * padded_valid * inv_std
     ).astype(jnp.bfloat16)
-    blocks = jnp.swapaxes(normed.reshape(seq_count, channels, tok_count + 1, STRIDE), 2, 3)
-    window = jnp.concatenate([blocks[..., :tok_count], blocks[..., 1:]], 2)
-    window = window.reshape(seq_count, channels * 2 * STRIDE, tok_count)
-    tokens = jnp.einsum(
-        "kd,skj->sjd", patch_weight, window, preferred_element_type=jnp.float32
+    kernel = patch_weight.reshape(channels, 2 * STRIDE, patch_weight.shape[1])
+    tokens = lax.conv_general_dilated(
+        normed,
+        kernel,
+        window_strides=(STRIDE,),
+        padding="VALID",
+        dimension_numbers=("NCW", "IWO", "NWC"),
+        preferred_element_type=jnp.float32,
     ).astype(jnp.bfloat16)
     column_count = patch_weight.shape[1]
     hidden0 = lax.all_gather(tokens, feat_axes, axis=2, tiled=True)

time: 118 us -> 112 us (0.949); the launches traced: 117 us -> 110 us
  other arithmetic: 26.7 us -> 18.6 us
  local copies, waits for them, and re-layouts: 22.3 us -> 18.6 us
  matrix products: 14.4 us -> 17.6 us
  starting transfers between devices: 25.7 us -> 26.9 us
    concatenate x2 -> x0, local copies, waits for them, and re-layouts: 13.2 us -> none  [the longest x1 8.49 us: per_device(): window = jnp.concatenate([blocks[..., :tok_count], blocks[..., 1:]], 2)]
    conv_general_dilated x0 -> x3, local copies, waits for them, and re-layouts: none -> 8.47 us  [per_device(): lax.conv_general_dilated(normed, kernel, window_strides=(STRIDE,), paddin...]
    concatenate x2 -> x0, other arithmetic: 6.88 us -> none  [the longest x1 3.57 us: per_device(): padded = jnp.concatenate([prior_raw, series.astype(jnp.float32)], -1)]
    conv_general_dilated x0 -> x1, matrix products: none -> 5.7 us  [per_device(): lax.conv_general_dilated(normed, kernel, window_strides=(STRIDE,), paddin...]
    transpose x1 -> x0, other arithmetic: 2.94 us -> none  [per_device(): jnp.swapaxes(normed.reshape(seq_count, channels, tok_count + 1, STRIDE),...]
    unnamed x28 -> x18, local copies, waits for them, and re-layouts: 2.06 us -> 4.67 us
    dot_general x1 -> x0, matrix products: 2.49 us -> none  [per_device(): jnp.einsum('kd,skj->sjd', patch_weight, window, preferred_element_type=jn...]
    convert_element_type x0 -> x1, other arithmetic: none -> 2.28 us  [per_device(): normed = ((padded * padded_valid - channel_mean[..., None]) * padded_vali...]
where the time goes in v4:
time: 112 us; the launch traced here: 110 us
  starting transfers between devices  26.9 us (24%)
  local copies, waits for them, and re-layouts  18.6 us (17%)
  other arithmetic  18.6 us (17%)
  waiting for transfers between devices  17.6 us (16%)
  matrix products  17.6 us (16%)
  blocking collectives  9.24 us (8%)
  between operations  1.25 us (1%)
    ppermute x2, waiting for transfers between devices, per_device(): arrivals.append(lax.ppermute(partial0, feat_axes, pairs))  15.5 us
    ppermute x6, starting transfers between devices, gather_causal(): pieces.append(lax.ppermute(value, ('tm', 'section'), pairs))  14 us
    all_gather x1, blocking collectives, per_device(): hidden0 = lax.all_gather(tokens, feat_axes, axis=2, tiled=True)  9.24 us
    conv_general_dilated x3, local copies, waits for them, and re-layouts, per_device(): lax.conv_general_dilated(normed, kernel, window_strides=(STRIDE,), paddin...  8.47 us
    conv_general_dilated x1, matrix products, per_device(): lax.conv_general_dilated(normed, kernel, window_strides=(STRIDE,), paddin...  5.7 us
    unnamed x18, local copies, waits for them, and re-layouts  4.67 us
    ppermute x3, starting transfers between devices, shift_from(): return lax.ppermute(value, axis, pairs)  4.66 us
    ppermute x1, starting transfers between devices, per_device(): to_high.append(lax.ppermute(cols_high, feat_axes, pairs))  3.12 us
  transfers between devices with their start and end apart: 14, of which 3 were waited for; matrix products, arithmetic and copies ran while one was open for 11% of the time, Pallas kernels for 0%

profile of v4, /device:TPU:1, one launch (start us, length us, event | category | flops | bytes accessed | tf_op | source)
XLA Modules:
  0.0 109.8 jit_solution(11126660403158282147)
XLA Ops:
  2.7 1.5 %multiply_reduce_fusion.1 = f32[2,64]{1,0:T(2,128)S(1)} fusion(f32[2,4096]{1,0:T(2,128)S(1)} %compare_convert_fusion, bf16[2,64,4096]{2,1,0:T(8,128)(2,1)} %param.8), kind=kLoop, calls=%fused_computation.34 | loop fusion | flops 1572736 | bytes 1081856 | tf_op jit(solution)/shard_map/reduce_sum | solution.py:150
  4.3 1.7 %multiply_reduce_fusion = f32[2,64]{1,0:T(2,128)S(1)} fusion(f32[2,64]{1,0:T(2,128)S(1)} %broadcast_divide_fusion.1, f32[2,4096]{1,0:T(2,128)S(1)} %compare_convert_fusion, bf16[2,64,4096]{2,1,0:T(8,128)(2,1)} %param.8), kind=kLoop, calls=%fused_computation.33 | loop fusion | flops 2621312 | bytes 1082368 | tf_op jit(solution)/shard_map/reduce_sum | solution.py:160
  6.1 4.2 %collective-permute-start.2 = (f32[2,64,34]{1,0,2:T(2,128)S(1)}, f32[2,64,34]{1,0,2:T(2,128)S(1)}, u32[]{:S(2)}, u32[]{:S(2)}) collective-permute-start(f32[2,64,34]{1,0,2:T(2,128)S(1)} %pad_maximum_fusion.3), channel_id=1, source_target_pairs={{0,12},{4,0},{8,4},{12,8},{1,13},{5,1},{9,5},{13,9},{2,14},{6,2},{... | collective-permute-start | bytes 52232 | tf_op jit(solution)/shard_map/ppermute | solution.py:13
  11.7 1.6 %convert_element_type.167 = f32[2,64,4096]{2,1,0:T(8,128)} convert(bf16[2,64,4096]{2,1,0:T(8,128)(2,1)S(1)} %copy-done.1) | non-fusion elementwise | flops 524288 | bytes 3145728 | tf_op jit(solution)/shard_map/convert_element_type | solution.py:148
  13.2 4.5 %copy.42 = bf16[4096,320]{1,0:T(8,128)(2,1)} copy(bf16[4096,320]{0,1:T(8,128)(2,1)} %param.10) | data formatting | bytes 5242880 | tf_op args[2]
  18.9 2.3 %fusion.77 = bf16[64,2,4128]{2,0,1:T(8,128)(2,1)S(1)} fusion(f32[2,64,4096]{2,1,0:T(8,128)} %convert_element_type.167, f32[2,64,32]{2,1,0:T(8,128)S(1)} %copy.38, f32[2,64]{1,0:T(2,128)S(1)} %add_rsqrt_fusion.2, f32[2,64]{1,0:T(2,128)S(1)} %broadcast_divide_fusion, f32[2,4128]{1,0:T(2,128)S(1)} %and_convert_fusion), kind=kLoop, calls=%fused_computation.70 | loop fusion | flops 3170304 | bytes 3204352 | tf_op jit(solution)/shard_map/convert_element_type | solution.py:191
  22.2 3.3 %reshape.526 = bf16[64,2,8,544]{3,2,0,1:T(8,128)(2,1)S(1)} reshape(bf16[64,2,4352]{2,0,1:T(8,128)(2,1)} %pad) | data formatting | bytes 2228224 | tf_op jit(solution)/shard_map/conv_general_dilated | solution.py:193
  25.6 4.1 %copy.41 = bf16[64,2,8,544]{0,2,1,3:T(8,128)(2,1)} copy(bf16[64,2,8,544]{3,2,0,1:T(8,128)(2,1)S(1)} %reshape.526) | data formatting | bytes 2228224 | tf_op jit(solution)/shard_map/conv_general_dilated | solution.py:193
  30.7 5.7 %fusion.72 = bf16[16,17,320]{2,0,1:T(8,128)(2,1)S(1)} fusion(bf16[64,64,320]{2,1,0:T(8,128)(2,1)} %bitcast.209, bf16[64,2,7,63]{0,2,1,3:T(8,128)(2,1)S(1)} %slice.78, bf16[64,2,8,544]{0,2,1,3:T(8,128)(2,1)} %copy.41, pred[16,17]{0,1:T(8,128)(4,1)S(1)} %copy-done.7), kind=kOutput, calls=%fused_computation.65 | convolution fusion | flops 716935168 | bytes 4022800 | tf_op jit(solution)/shard_map/conv_general_dilated | solution.py:193
  36.8 9.2 %all_gather.3 = bf16[2,128,1280]{1,0,2:T(2,128)(2,1)S(1)} all-gather(bf16[2,128,320]{1,0,2:T(2,128)(2,1)S(1)} %copy.45), channel_id=1, replica_groups=mesh['groups'=2,'tm'=4,'mp'=2,'section'=2] {'mp','section'}, dimensions={2}, use_global_device_ids=true | all-gather | bytes 819200 | tf_op jit(solution)/shard_map/all_gather | solution.py:202
  47.2 1.6 %convolution_convert_fusion.4 = bf16[2,128,160]{1,2,0:T(8,128)(2,1)S(1)} fusion(bf16[1,1280,160]{1,2,0:T(8,128)(2,1)} %param.14, bf16[2,128,1280]{2,1,0:T(8,128)(2,1)S(1)} %copy.46, f32[1280]{0:T(1024)S(1)} %convert_reduce_fusion, f32[2,128]{1,0:T(2,128)S(1)} %add_rsqrt_fusion.1), kind=kOutput, calls=%fused_computation.68 | convolution fusion | flops 106209280 | bytes 1153024 | tf_op jit(solution)/shard_map/btd,de->bet/dot_general | solution.py:78
  48.8 1.5 %convolution_convert_fusion.5 = bf16[2,128,160]{1,2,0:T(8,128)(2,1)S(1)} fusion(bf16[1,1280,160]{1,2,0:T(8,128)(2,1)} %param.13, bf16[2,128,1280]{2,1,0:T(8,128)(2,1)S(1)} %copy.46, f32[1280]{0:T(1024)S(1)} %convert_reduce_fusion, f32[2,128]{1,0:T(2,128)S(1)} %add_rsqrt_fusion.1), kind=kOutput, calls=%fused_computation.69 | convolution fusion | flops 106209280 | bytes 1153024 | tf_op jit(solution)/shard_map/btd,de->bet/dot_general | solution.py:75
  51.6 1.3 %collective-permute-start.4 = (bf16[2,2,2,80,128]{4,3,2,1,0:T(8,128)(2,1)}, bf16[2,2,2,80,128]{4,3,2,1,0:T(8,128)(2,1)}, u32[]{:S(2)}, u32[]{:S(2)}) collective-permute-start(bf16[2,2,2,80,128]{4,3,2,1,0:T(8,128)(2,1)} %pad_maximum_fusion.1), channel_id=1, source_target_pairs={{0,8},{4,12},{2,10},{6,14},{16,24},{20,28},{18,26},{22,30}} | collective-permute-start | bytes 491528 | tf_op jit(solution)/shard_map/ppermute | solution.py:34
  52.9 1.3 %collective-permute-start.3 = (bf16[2,2,2,80,128]{4,3,2,1,0:T(8,128)(2,1)}, bf16[2,2,2,80,128]{4,3,2,1,0:T(8,128)(2,1)}, u32[]{:S(2)}, u32[]{:S(2)}) collective-permute-start(bf16[2,2,2,80,128]{4,3,2,1,0:T(8,128)(2,1)} %pad_maximum_fusion.1), channel_id=1, source_target_pairs={{0,12},{2,14},{16,28},{18,30}} | collective-permute-start | bytes 491528 | tf_op jit(solution)/shard_map/ppermute | solution.py:34
  58.9 1.5 %convolution_convert_fusion.1 = bf16[2,128,1280]{2,1,0:T(8,128)(2,1)} fusion(bf16[2,128,640]{1,2,0:T(8,128)(2,1)S(1)} %bitcast.225, bf16[1,640,1280]{2,1,0:T(8,128)(2,1)S(1)} %copy-done), kind=kOutput, calls=%fused_computation.16 | convolution fusion | flops 419758080 | bytes 2621440 | tf_op jit(solution)/shard_map/bte,ed->btd/dot_general | solution.py:126
  61.7 1.3 %collective-permute-start.6 = (bf16[2,128,1280]{2,1,0:T(8,128)(2,1)}, bf16[2,128,1280]{2,1,0:T(8,128)(2,1)}, u32[]{:S(2)}, u32[]{:S(2)}) collective-permute-start(bf16[2,128,1280]{2,1,0:T(8,128)(2,1)} %convolution_convert_fusion.1), channel_id=1, source_target_pairs={{0,1},{2,3},{4,5},{6,7},{8,9},{10,11},{12,13},{14,15},{16,17},{18,... | collective-permute-start | bytes 1966088 | tf_op jit(solution)/shard_map/ppermute | solution.py:214
  63.1 15.5 %collective-permute-done.7 = bf16[2,128,1280]{2,1,0:T(8,128)(2,1)} collective-permute-done((bf16[2,128,1280]{2,1,0:T(8,128)(2,1)}, bf16[2,128,1280]{2,1,0:T(8,128)(2,1)}, u32[]{:S(2)}, u32[]{:S(2)}) %collective-permute-start.7) | collective-permute-done | bytes 655392 | tf_op jit(solution)/shard_map/ppermute | solution.py:214
  78.6 1.7 %fusion.35 = (f32[2,128]{1,0:T(2,128)S(1)}, bf16[2,128,1280]{2,1,0:T(8,128)(2,1)S(1)}) fusion(bf16[2,128,1280]{2,1,0:T(8,128)(2,1)} %collective-permute-done.7, bf16[2,128,1280]{2,1,0:T(8,128)(2,1)} %collective-permute-done.6, bf16[2,128,1280]{2,1,0:T(8,128)(2,1)S(1)} %copy.46), kind=kLoop, calls=%fused_computation.48 | loop fusion | flops 2948864 | bytes 2622464 | tf_op jit(solution)/shard_map/reduce_sum | solution.py:69
  83.2 7.5 %collective-permute-start.9 = (bf16[2,2,2,80,128]{4,3,2,1,0:T(8,128)(2,1)}, bf16[2,2,2,80,128]{4,3,2,1,0:T(8,128)(2,1)}, u32[]{:S(2)}, u32[]{:S(2)}) collective-permute-start(bf16[2,2,2,80,128]{4,3,2,1,0:T(8,128)(2,1)} %pad_maximum_fusion.2), channel_id=1, source_target_pairs={{1,9},{5,13},{3,11},{7,15},{17,25},{21,29},{19,27},{23,31}} | collective-permute-start | bytes 491528 | tf_op jit(solution)/shard_map/ppermute | solution.py:34
  90.7 1.9 %collective-permute-start.8 = (bf16[2,2,2,80,128]{4,3,2,1,0:T(8,128)(2,1)}, bf16[2,2,2,80,128]{4,3,2,1,0:T(8,128)(2,1)}, u32[]{:S(2)}, u32[]{:S(2)}) collective-permute-start(bf16[2,2,2,80,128]{4,3,2,1,0:T(8,128)(2,1)} %pad_maximum_fusion.2), channel_id=1, source_target_pairs={{1,13},{3,15},{17,29},{19,31}} | collective-permute-start | bytes 491528 | tf_op jit(solution)/shard_map/ppermute | solution.py:34
  92.6 1.4 %fusion.61 = bf16[2,128,640]{2,1,0:T(8,128)(2,1)} fusion(bf16[1,1280,640]{2,1,0:T(8,128)(2,1)S(1)} %copy-done.4, bf16[2,128,1280]{2,1,0:T(8,128)(2,1)S(1)} %get-tuple-element.4, f32[2,128]{1,0:T(2,128)S(1)} %add_rsqrt_fusion, f32[1280]{0:T(1024)S(1)} %convert_reduce_fusion), kind=kOutput, calls=%fused_computation.62 | convolution fusion | flops 421068800 | bytes 2627584 | tf_op jit(solution)/shard_map/btd,de->bte/dot_general | solution.py:72
  100.5 1.3 %collective-permute-start.11 = (bf16[2,1,128,640]{3,2,1,0:T(8,128)(2,1)S(1)}, bf16[2,1,128,640]{3,2,1,0:T(8,128)(2,1)S(1)}, u32[]{:S(2)}, u32[]{:S(2)}) collective-permute-start(bf16[2,1,128,640]{3,2,1,0:T(8,128)(2,1)S(1)} %pad_maximum_fusion), channel_id=1, source_target_pairs={{1,0},{3,2},{5,4},{7,6},{9,8},{11,10},{13,12},{15,14},{17,16},{19,... | collective-permute-start | bytes 983048 | tf_op jit(solution)/shard_map/ppermute | solution.py:247
  101.8 3.1 %collective-permute-start.13 = (bf16[1,128,640]{2,1,0:T(8,128)(2,1)S(1)}, bf16[1,128,640]{2,1,0:T(8,128)(2,1)S(1)}, u32[]{:S(2)}, u32[]{:S(2)}) collective-permute-start(bf16[1,128,640]{2,1,0:T(8,128)(2,1)S(1)} %constant_dynamic-slice_fusion), channel_id=1, source_target_pairs={{1,3},{3,1},{5,7},{7,5},{9,11},{11,9},{13,15},{15,13},{17,19},{19,... | collective-permute-start | bytes 491528 | tf_op jit(solution)/shard_map/ppermute | solution.py:251
  105.0 1.3 %collective-permute-start.12 = (bf16[1,128,640]{2,1,0:T(8,128)(2,1)S(1)}, bf16[1,128,640]{2,1,0:T(8,128)(2,1)S(1)}, u32[]{:S(2)}, u32[]{:S(2)}) collective-permute-start(bf16[1,128,640]{2,1,0:T(8,128)(2,1)S(1)} %get-tuple-element.10), channel_id=1, source_target_pairs={{1,2},{3,0},{5,6},{7,4},{9,10},{11,8},{13,14},{15,12},{17,18},{19,... | collective-permute-start | bytes 491528 | tf_op jit(solution)/shard_map/ppermute | solution.py:247
  (112 shorter events, 28.0 us)
Async XLA Ops:
  0.6 58.2 %copy-start = (bf16[1,640,1280]{2,1,0:T(8,128)(2,1)S(1)}, bf16[1,640,1280]{2,1,0:T(8,128)(2,1)}, u32[]{:S(2)}) copy-start(bf16[1,640,1280]{2,1,0:T(8,128)(2,1)} %param.15) | copy-start | bytes 4915204
  0.6 11.0 %copy-start.1 = (bf16[2,64,4096]{2,1,0:T(8,128)(2,1)S(1)}, bf16[2,64,4096]{2,1,0:T(8,128)(2,1)}, u32[]{:S(2)}) copy-start(bf16[2,64,4096]{2,1,0:T(8,128)(2,1)} %param.8) | copy-start | bytes 3145732
  0.7 10.6 %copy-start.2 = (bf16[1,1280]{1,0:T(2,128)(2,1)S(1)}, bf16[1,1280]{1,0:T(2,128)(2,1)}, u32[]{:S(2)}) copy-start(bf16[1,1280]{1,0:T(2,128)(2,1)} %param.11) | copy-start | bytes 7684
  6.1 11.6 %collective-permute-start.2 = (f32[2,64,34]{1,0,2:T(2,128)S(1)}, f32[2,64,34]{1,0,2:T(2,128)S(1)}, u32[]{:S(2)}, u32[]{:S(2)}) collective-permute-start(f32[2,64,34]{1,0,2:T(2,128)S(1)} %pad_maximum_fusion.3), channel_id=1, source_target_pairs={{0,12},{4,0},{8,4},{12,8},{1,13},{5,1},{9,5},{13,9},{2,14},{6,2},{... | collective-permute-start | bytes 52232 | tf_op jit(solution)/shard_map/ppermute | solution.py:13
  10.3 7.4 %collective-permute-start.1 = (f32[2,64,34]{1,0,2:T(2,128)S(1)}, f32[2,64,34]{1,0,2:T(2,128)S(1)}, u32[]{:S(2)}, u32[]{:S(2)}) collective-permute-start(f32[2,64,34]{1,0,2:T(2,128)S(1)} %pad_maximum_fusion.3), channel_id=1, source_target_pairs={{0,8},{4,12},{8,0},{12,4},{1,9},{5,13},{9,1},{13,5},{2,10},{6,14},... | collective-permute-start | bytes 52232 | tf_op jit(solution)/shard_map/ppermute | solution.py:13
  10.3 7.5 %collective-permute-start = (f32[2,64,34]{1,0,2:T(2,128)S(1)}, f32[2,64,34]{1,0,2:T(2,128)S(1)}, u32[]{:S(2)}, u32[]{:S(2)}) collective-permute-start(f32[2,64,34]{1,0,2:T(2,128)S(1)} %pad_maximum_fusion.3), channel_id=1, source_target_pairs={{0,4},{4,8},{8,12},{12,0},{1,5},{5,9},{9,13},{13,1},{2,6},{6,10},{... | collective-permute-start | bytes 52232 | tf_op jit(solution)/shard_map/ppermute | solution.py:13
  25.6 5.2 %copy-start.7 = (pred[16,17]{0,1:T(8,128)(4,1)S(1)}, pred[16,17]{0,1:T(8,128)(4,1)}, u32[]{:S(2)}) copy-start(pred[16,17]{0,1:T(8,128)(4,1)} %constant.128) | copy-start | bytes 820
  47.0 7.3 %copy-start.3 = (bf16[1,1280,640]{2,1,0:T(8,128)(2,1)S(1)}, bf16[1,1280,640]{2,1,0:T(8,128)(2,1)}, u32[]{:S(2)}) copy-start(bf16[1,1280,640]{2,1,0:T(8,128)(2,1)} %param.12) | copy-start | bytes 4915204
  51.0 4.3 %collective-permute-start.5 = (bf16[2,2,2,80,128]{4,3,2,1,0:T(8,128)(2,1)}, bf16[2,2,2,80,128]{4,3,2,1,0:T(8,128)(2,1)S(1)}, u32[]{:S(2)}, u32[]{:S(2)}) collective-permute-start(bf16[2,2,2,80,128]{4,3,2,1,0:T(8,128)(2,1)} %pad_maximum_fusion.1), channel_id=1, source_target_pairs={{0,4},{4,8},{8,12},{2,6},{6,10},{10,14},{16,20},{20,24},{24,28},{1... | collective-permute-start | bytes 491528 | tf_op jit(solution)/shard_map/ppermute | solution.py:34
  51.6 3.6 %collective-permute-start.4 = (bf16[2,2,2,80,128]{4,3,2,1,0:T(8,128)(2,1)}, bf16[2,2,2,80,128]{4,3,2,1,0:T(8,128)(2,1)}, u32[]{:S(2)}, u32[]{:S(2)}) collective-permute-start(bf16[2,2,2,80,128]{4,3,2,1,0:T(8,128)(2,1)} %pad_maximum_fusion.1), channel_id=1, source_target_pairs={{0,8},{4,12},{2,10},{6,14},{16,24},{20,28},{18,26},{22,30}} | collective-permute-start | bytes 491528 | tf_op jit(solution)/shard_map/ppermute | solution.py:34
  52.9 2.3 %collective-permute-start.3 = (bf16[2,2,2,80,128]{4,3,2,1,0:T(8,128)(2,1)}, bf16[2,2,2,80,128]{4,3,2,1,0:T(8,128)(2,1)}, u32[]{:S(2)}, u32[]{:S(2)}) collective-permute-start(bf16[2,2,2,80,128]{4,3,2,1,0:T(8,128)(2,1)} %pad_maximum_fusion.1), channel_id=1, source_target_pairs={{0,12},{2,14},{16,28},{18,30}} | collective-permute-start | bytes 491528 | tf_op jit(solution)/shard_map/ppermute | solution.py:34
  58.9 21.4 %copy-start.5 = (bf16[1,1280,160]{1,2,0:T(8,128)(2,1)S(1)}, bf16[1,1280,160]{1,2,0:T(8,128)(2,1)}, u32[]{:S(2)}) copy-start(bf16[1,1280,160]{1,2,0:T(8,128)(2,1)} %param.14) | copy-start | bytes 1228804
  60.4 18.1 %collective-permute-start.7 = (bf16[2,128,1280]{2,1,0:T(8,128)(2,1)}, bf16[2,128,1280]{2,1,0:T(8,128)(2,1)}, u32[]{:S(2)}, u32[]{:S(2)}) collective-permute-start(bf16[2,128,1280]{2,1,0:T(8,128)(2,1)} %convolution_convert_fusion.1), channel_id=1, source_target_pairs={{0,3},{2,1},{4,7},{6,5},{8,11},{10,9},{12,15},{14,13},{16,19},{18,... | collective-permute-start | bytes 1966088 | tf_op jit(solution)/shard_map/ppermute | solution.py:214
  61.7 16.9 %collective-permute-start.6 = (bf16[2,128,1280]{2,1,0:T(8,128)(2,1)}, bf16[2,128,1280]{2,1,0:T(8,128)(2,1)}, u32[]{:S(2)}, u32[]{:S(2)}) collective-permute-start(bf16[2,128,1280]{2,1,0:T(8,128)(2,1)} %convolution_convert_fusion.1), channel_id=1, source_target_pairs={{0,1},{2,3},{4,5},{6,7},{8,9},{10,11},{12,13},{14,15},{16,17},{18,... | collective-permute-start | bytes 1966088 | tf_op jit(solution)/shard_map/ppermute | solution.py:214
  63.0 17.7 %copy-start.6 = (bf16[1,1280,160]{1,2,0:T(8,128)(2,1)S(1)}, bf16[1,1280,160]{1,2,0:T(8,128)(2,1)}, u32[]{:S(2)}) copy-start(bf16[1,1280,160]{1,2,0:T(8,128)(2,1)} %param.13) | copy-start | bytes 1228804
  80.3 12.4 %copy-start.4 = (bf16[1,1280,640]{2,1,0:T(8,128)(2,1)S(1)}, bf16[1,1280,640]{2,1,0:T(8,128)(2,1)}, u32[]{:S(2)}) copy-start(bf16[1,1280,640]{2,1,0:T(8,128)(2,1)} %param.12) | copy-start | bytes 4915204
  81.9 14.1 %collective-permute-start.10 = (bf16[2,2,2,80,128]{4,3,2,1,0:T(8,128)(2,1)}, bf16[2,2,2,80,128]{4,3,2,1,0:T(8,128)(2,1)S(1)}, u32[]{:S(2)}, u32[]{:S(2)}) collective-permute-start(bf16[2,2,2,80,128]{4,3,2,1,0:T(8,128)(2,1)} %pad_maximum_fusion.2), channel_id=1, source_target_pairs={{1,5},{5,9},{9,13},{3,7},{7,11},{11,15},{17,21},{21,25},{25,29},{1... | collective-permute-start | bytes 491528 | tf_op jit(solution)/shard_map/ppermute | solution.py:34
  83.2 12.8 %collective-permute-start.9 = (bf16[2,2,2,80,128]{4,3,2,1,0:T(8,128)(2,1)}, bf16[2,2,2,80,128]{4,3,2,1,0:T(8,128)(2,1)}, u32[]{:S(2)}, u32[]{:S(2)}) collective-permute-start(bf16[2,2,2,80,128]{4,3,2,1,0:T(8,128)(2,1)} %pad_maximum_fusion.2), channel_id=1, source_target_pairs={{1,9},{5,13},{3,11},{7,15},{17,25},{21,29},{19,27},{23,31}} | collective-permute-start | bytes 491528 | tf_op jit(solution)/shard_map/ppermute | solution.py:34
  90.7 5.3 %collective-permute-start.8 = (bf16[2,2,2,80,128]{4,3,2,1,0:T(8,128)(2,1)}, bf16[2,2,2,80,128]{4,3,2,1,0:T(8,128)(2,1)}, u32[]{:S(2)}, u32[]{:S(2)}) collective-permute-start(bf16[2,2,2,80,128]{4,3,2,1,0:T(8,128)(2,1)} %pad_maximum_fusion.2), channel_id=1, source_target_pairs={{1,13},{3,15},{17,29},{19,31}} | collective-permute-start | bytes 491528 | tf_op jit(solution)/shard_map/ppermute | solution.py:34
  100.5 8.5 %collective-permute-start.11 = (bf16[2,1,128,640]{3,2,1,0:T(8,128)(2,1)S(1)}, bf16[2,1,128,640]{3,2,1,0:T(8,128)(2,1)S(1)}, u32[]{:S(2)}, u32[]{:S(2)}) collective-permute-start(bf16[2,1,128,640]{3,2,1,0:T(8,128)(2,1)S(1)} %pad_maximum_fusion), channel_id=1, source_target_pairs={{1,0},{3,2},{5,4},{7,6},{9,8},{11,10},{13,12},{15,14},{17,16},{19,... | collective-permute-start | bytes 983048 | tf_op jit(solution)/shard_map/ppermute | solution.py:247
  101.8 6.1 %collective-permute-start.13 = (bf16[1,128,640]{2,1,0:T(8,128)(2,1)S(1)}, bf16[1,128,640]{2,1,0:T(8,128)(2,1)S(1)}, u32[]{:S(2)}, u32[]{:S(2)}) collective-permute-start(bf16[1,128,640]{2,1,0:T(8,128)(2,1)S(1)} %constant_dynamic-slice_fusion), channel_id=1, source_target_pairs={{1,3},{3,1},{5,7},{7,5},{9,11},{11,9},{13,15},{15,13},{17,19},{19,... | collective-permute-start | bytes 491528 | tf_op jit(solution)/shard_map/ppermute | solution.py:251
  105.0 4.0 %collective-permute-start.12 = (bf16[1,128,640]{2,1,0:T(8,128)(2,1)S(1)}, bf16[1,128,640]{2,1,0:T(8,128)(2,1)S(1)}, u32[]{:S(2)}, u32[]{:S(2)}) collective-permute-start(bf16[1,128,640]{2,1,0:T(8,128)(2,1)S(1)} %get-tuple-element.10), channel_id=1, source_target_pairs={{1,2},{3,0},{5,6},{7,4},{9,10},{11,8},{13,14},{15,12},{17,18},{19,... | collective-permute-start | bytes 491528 | tf_op jit(solution)/shard_map/ppermute | solution.py:247

commit v5 on v4

--- a/solution.py
+++ b/solution.py
@@ -123,6 +123,8 @@
     attended = attended.transpose(0, 3, 1, 2, 4).reshape(
         batch_count, tok_count, kv_local * group_size * HD
     )
+    if out_w is None:
+        return attended, key_t, value_t
     partial_value = jnp.einsum("bte,ed->btd", attended, out_w, preferred_element_type=jnp.float32)
     return partial_value.astype(jnp.bfloat16), key_t, value_t
 
@@ -138,7 +140,10 @@
     sec_at = lax.axis_index("section")
     feat_axes = ("mp", "section")
     feat_n = mp_n * sec_n
-    feat_at = mp_at * sec_n + sec_at
+    to_second = [
+        [(m * sec_n, ((m + by) % mp_n) * sec_n + 1) for m in range(mp_n)] for by in range(mp_n)
+    ]
+    moved_rows = [lax.ppermute(out_weight[0], feat_axes, pairs) for pairs in to_second]
     total_steps = steps_dev * tm_n
     total_tokens = tok_count * tm_n
 
@@ -204,22 +209,15 @@
     head_cols = feature_count // mp_n
     sizes = (tm_n, sec_n, tm_at, total_tokens)
 
-    partial0, key0, value0 = attend_layer(
+    attended0, key0, value0 = attend_layer(
         hidden0, lengths, norm_gain[0], query_weight[0], key_weight[0], value_weight[0],
-        out_weight[0], sizes, 0,
-    )
-    arrivals = []
-    for by in range(mp_n):
-        pairs = [(m * sec_n, ((m + by) % mp_n) * sec_n + 1) for m in range(mp_n)]
-        arrivals.append(lax.ppermute(partial0, feat_axes, pairs))
-    if mp_n == 2:
-        head_sum = arrivals[0].astype(jnp.float32) + arrivals[1].astype(jnp.float32)
-    elif mp_n > 2:
-        order = (mp_at - jnp.arange(mp_n, dtype=jnp.int32)) % mp_n
-        arrivals = jnp.take(jnp.stack(arrivals, 0), order, axis=0)
-        head_sum = jnp.sum(arrivals.astype(jnp.float32), 0)
-    else:
-        head_sum = arrivals[0].astype(jnp.float32)
+        None, sizes, 0,
+    )
+    head_sum = None
+    for pairs, rows in zip(to_second, moved_rows):
+        arrived = lax.ppermute(attended0, feat_axes, pairs)
+        term = jnp.einsum("bte,ed->btd", arrived, rows, preferred_element_type=jnp.float32)
+        head_sum = term if head_sum is None else head_sum + term
     hidden1 = (hidden0.astype(jnp.float32) + head_sum).astype(jnp.bfloat16)
 
     partial1, key1, value1 = attend_layer(

time: 112 us -> 111 us (level); the launches traced: 110 us -> 110 us
  waiting for transfers between devices: 17.6 us -> 14.2 us
  other arithmetic: 18.6 us -> 15.7 us
  blocking collectives: 9.24 us -> 11.7 us
  local copies, waits for them, and re-layouts: 18.6 us -> 20.5 us
  matrix products: 17.6 us -> 19.3 us
    dot_general x0 -> x2, matrix products: none -> 4.42 us  [per_device(): jnp.einsum('bte,ed->btd', arrived, rows, preferred_element_type=jnp.float32)]
    ppermute x2 -> x4, waiting for transfers between devices: 15.5 us -> 11.1 us  [the longest x2 11.1 us: per_device(): arrived = lax.ppermute(attended0, feat_axes, pairs)]
    ppermute x2 -> x4, starting transfers between devices: 2.57 us -> 5.14 us  [the longest x2 2.57 us: per_device(): lax.ppermute(out_weight[0], feat_axes, pairs)]
    all_gather x1, blocking collectives: 9.24 us -> 11.7 us  [per_device(): hidden0 = lax.all_gather(tokens, feat_axes, axis=2, tiled=True)]
    ppermute x1, waiting for transfers between devices: 0.98 us -> 2.98 us  [per_device(): to_high.append(lax.ppermute(cols_high, feat_axes, pairs))]
    reduce_sum x2 -> x1, other arithmetic: 1.89 us -> 0.21 us  [attend_layer(): jnp.mean(hidden32 * hidden32, -1, keepdims=True) + 1e-06]
    dot_general x2 -> x1, matrix products: 2.26 us -> 0.71 us  [attend_layer(): jnp.einsum('bte,ed->btd', attended, out_w, preferred_element_type=jnp.flo...]
    reduce_sum x1, other arithmetic: 1.73 us -> 0.5 us  [per_device(): local_m2 = jnp.sum(local_dev * local_dev, -1)]
  transfers between devices with their start and end apart: 14 -> 16, of which waited for: 3 -> 2; matrix products, arithmetic and copies ran while one was open for 11% -> 37% of each run, Pallas kernels for 0% -> 0%
where the time goes in v5:
time: 111 us; the launch traced here: 110 us
  starting transfers between devices  27.9 us (25%)
  local copies, waits for them, and re-layouts  20.5 us (18%)
  matrix products  19.3 us (17%)
  other arithmetic  15.7 us (14%)
  waiting for transfers between devices  14.2 us (13%)
  blocking collectives  11.7 us (11%)
  between operations  1.28 us (1%)
    ppermute x6, starting transfers between devices, gather_causal(): pieces.append(lax.ppermute(value, ('tm', 'section'), pairs))  13.1 us
    all_gather x1, blocking collectives, per_device(): hidden0 = lax.all_gather(tokens, feat_axes, axis=2, tiled=True)  11.7 us
    ppermute x2, waiting for transfers between devices, per_device(): arrived = lax.ppermute(attended0, feat_axes, pairs)  11.1 us
    conv_general_dilated x3, local copies, waits for them, and re-layouts, per_device(): lax.conv_general_dilated(normed, kernel, window_strides=(STRIDE,), paddin...  8.47 us
    conv_general_dilated x1, matrix products, per_device(): lax.conv_general_dilated(normed, kernel, window_strides=(STRIDE,), paddin...  5.7 us
    unnamed x18, local copies, waits for them, and re-layouts  5.64 us
    ppermute x3, starting transfers between devices, shift_from(): return lax.ppermute(value, axis, pairs)  4.66 us
    dot_general x2, matrix products, per_device(): jnp.einsum('bte,ed->btd', arrived, rows, preferred_element_type=jnp.float32)  4.42 us
  transfers between devices with their start and end apart: 16, of which 2 were waited for; matrix products, arithmetic and copies ran while one was open for 37% of the time, Pallas kernels for 0%

profile of v5, /device:TPU:1, one launch (start us, length us, event | category | flops | bytes accessed | tf_op | source)
XLA Modules:
  0.0 110.5 jit_solution(5946059973483623563)
XLA Ops:
  2.7 1.5 %multiply_reduce_fusion.1 = f32[2,64]{1,0:T(2,128)S(1)} fusion(f32[2,4096]{1,0:T(2,128)S(1)} %compare_convert_fusion, bf16[2,64,4096]{2,1,0:T(8,128)(2,1)} %param.8), kind=kLoop, calls=%fused_computation.36 | loop fusion | flops 1572736 | bytes 1081856 | tf_op jit(solution)/shard_map/reduce_sum | solution.py:155
  4.9 2.2 %collective-permute-start = (f32[2,64,34]{1,0,2:T(2,128)S(1)}, f32[2,64,34]{1,0,2:T(2,128)S(1)}, u32[]{:S(2)}, u32[]{:S(2)}) collective-permute-start(f32[2,64,34]{1,0,2:T(2,128)S(1)} %pad_maximum_fusion.3), channel_id=1, source_target_pairs={{0,4},{4,8},{8,12},{12,0},{1,5},{5,9},{9,13},{13,1},{2,6},{6,10},{... | collective-permute-start | bytes 52232 | tf_op jit(solution)/shard_map/ppermute | solution.py:13
  7.1 2.1 %collective-permute-start.2 = (f32[2,64,34]{1,0,2:T(2,128)S(1)}, f32[2,64,34]{1,0,2:T(2,128)S(1)}, u32[]{:S(2)}, u32[]{:S(2)}) collective-permute-start(f32[2,64,34]{1,0,2:T(2,128)S(1)} %pad_maximum_fusion.3), channel_id=1, source_target_pairs={{0,12},{4,0},{8,4},{12,8},{1,13},{5,1},{9,5},{13,9},{2,14},{6,2},{... | collective-permute-start | bytes 52232 | tf_op jit(solution)/shard_map/ppermute | solution.py:13
  13.0 1.6 %convert_element_type.158 = f32[2,64,4096]{2,1,0:T(8,128)} convert(bf16[2,64,4096]{2,1,0:T(8,128)(2,1)S(1)} %copy-done.1) | non-fusion elementwise | flops 524288 | bytes 3145728 | tf_op jit(solution)/shard_map/convert_element_type | solution.py:153
  14.6 4.5 %copy.44 = bf16[4096,320]{1,0:T(8,128)(2,1)} copy(bf16[4096,320]{0,1:T(8,128)(2,1)} %param.10) | data formatting | bytes 5242880 | tf_op args[2]
  20.2 2.3 %fusion.80 = bf16[64,2,4128]{2,0,1:T(8,128)(2,1)S(1)} fusion(f32[2,64,4096]{2,1,0:T(8,128)} %convert_element_type.158, f32[2,64,32]{2,1,0:T(8,128)S(1)} %copy.40, f32[2,64]{1,0:T(2,128)S(1)} %add_rsqrt_fusion.2, f32[2,64]{1,0:T(2,128)S(1)} %broadcast_divide_fusion, f32[2,4128]{1,0:T(2,128)S(1)} %and_convert_fusion), kind=kLoop, calls=%fused_computation.72 | loop fusion | flops 3170304 | bytes 3204352 | tf_op jit(solution)/shard_map/convert_element_type | solution.py:196
  23.6 3.3 %reshape.526 = bf16[64,2,8,544]{3,2,0,1:T(8,128)(2,1)S(1)} reshape(bf16[64,2,4352]{2,0,1:T(8,128)(2,1)} %pad) | data formatting | bytes 2228224 | tf_op jit(solution)/shard_map/conv_general_dilated | solution.py:198
  26.9 4.1 %copy.43 = bf16[64,2,8,544]{0,2,1,3:T(8,128)(2,1)} copy(bf16[64,2,8,544]{3,2,0,1:T(8,128)(2,1)S(1)} %reshape.526) | data formatting | bytes 2228224 | tf_op jit(solution)/shard_map/conv_general_dilated | solution.py:198
  32.1 5.7 %fusion.75 = bf16[16,17,320]{2,0,1:T(8,128)(2,1)S(1)} fusion(bf16[64,64,320]{2,1,0:T(8,128)(2,1)} %bitcast.216, bf16[64,2,7,63]{0,2,1,3:T(8,128)(2,1)S(1)} %slice.78, bf16[64,2,8,544]{0,2,1,3:T(8,128)(2,1)} %copy.43, pred[16,17]{0,1:T(8,128)(4,1)S(1)} %copy-done.7), kind=kOutput, calls=%fused_computation.67 | convolution fusion | flops 716935168 | bytes 4022800 | tf_op jit(solution)/shard_map/conv_general_dilated | solution.py:198
  38.2 11.7 %all_gather.3 = bf16[2,128,1280]{1,0,2:T(2,128)(2,1)S(1)} all-gather(bf16[2,128,320]{1,0,2:T(2,128)(2,1)S(1)} %copy.47), channel_id=1, replica_groups=mesh['groups'=2,'tm'=4,'mp'=2,'section'=2] {'mp','section'}, dimensions={2}, use_global_device_ids=true | all-gather | bytes 819200 | tf_op jit(solution)/shard_map/all_gather | solution.py:207
  51.0 1.5 %convolution_convert_fusion.3 = bf16[2,128,160]{1,2,0:T(8,128)(2,1)S(1)} fusion(bf16[1,1280,160]{1,2,0:T(8,128)(2,1)} %param.14, bf16[2,128,1280]{2,1,0:T(8,128)(2,1)S(1)} %copy.48, f32[1280]{0:T(1024)S(1)} %convert_reduce_fusion, f32[2,128]{1,0:T(2,128)S(1)} %add_rsqrt_fusion.1), kind=kOutput, calls=%fused_computation.70 | convolution fusion | flops 106209280 | bytes 1153024 | tf_op jit(solution)/shard_map/btd,de->bet/dot_general | solution.py:78
  54.3 1.3 %collective-permute-start.4 = (bf16[2,2,2,80,128]{4,3,2,1,0:T(8,128)(2,1)}, bf16[2,2,2,80,128]{4,3,2,1,0:T(8,128)(2,1)}, u32[]{:S(2)}, u32[]{:S(2)}) collective-permute-start(bf16[2,2,2,80,128]{4,3,2,1,0:T(8,128)(2,1)} %pad_maximum_fusion.1), channel_id=1, source_target_pairs={{0,8},{4,12},{2,10},{6,14},{16,24},{20,28},{18,26},{22,30}} | collective-permute-start | bytes 491528 | tf_op jit(solution)/shard_map/ppermute | solution.py:34
  55.6 1.3 %collective-permute-start.5 = (bf16[2,2,2,80,128]{4,3,2,1,0:T(8,128)(2,1)}, bf16[2,2,2,80,128]{4,3,2,1,0:T(8,128)(2,1)}, u32[]{:S(2)}, u32[]{:S(2)}) collective-permute-start(bf16[2,2,2,80,128]{4,3,2,1,0:T(8,128)(2,1)} %pad_maximum_fusion.1), channel_id=1, source_target_pairs={{0,4},{4,8},{8,12},{2,6},{6,10},{10,14},{16,20},{20,24},{24,28},{1... | collective-permute-start | bytes 491528 | tf_op jit(solution)/shard_map/ppermute | solution.py:34
  65.0 11.1 %collective-permute-done.8 = bf16[2,128,640]{2,1,0:T(8,128)(2,1)S(1)} collective-permute-done((bf16[2,128,640]{2,1,0:T(8,128)(2,1)}, bf16[2,128,640]{2,1,0:T(8,128)(2,1)S(1)}, u32[]{:S(2)}, u32[]{:S(2)}) %collective-permute-start.8) | collective-permute-done | bytes 327712 | tf_op jit(solution)/shard_map/ppermute | solution.py:218
  76.2 2.1 %fusion.32 = f32[2,128,1280]{2,1,0:T(8,128)S(1)} fusion(bf16[2,128,640]{2,1,0:T(8,128)(2,1)S(1)} %collective-permute-done.8, bf16[640,1280]{1,0:T(8,128)(2,1)} %collective-permute-done.9), kind=kOutput, calls=%fused_computation.42 | convolution fusion | flops 419430400 | bytes 3276800 | tf_op jit(solution)/shard_map/bte,ed->btd/dot_general | solution.py:219
  78.3 2.3 %fusion.39 = (f32[2,128]{1,0:T(2,128)S(1)}, bf16[2,128,1280]{2,1,0:T(8,128)(2,1)S(1)}) fusion(f32[2,128,1280]{2,1,0:T(8,128)S(1)} %fusion.32, bf16[2,128,640]{2,1,0:T(8,128)(2,1)S(1)} %collective-permute-done.6, bf16[640,1280]{1,0:T(8,128)(2,1)} %collective-permute-done.7, bf16[2,128,1280]{2,1,0:T(8,128)(2,1)S(1)} %copy.48), kind=kOutput, calls=%fused_computation.51 | convolution fusion | flops 421723904 | bytes 4588544 | tf_op jit(solution)/shard_map/bte,ed->btd/dot_general | solution.py:219
  82.8 5.0 %collective-permute-start.10 = (bf16[2,2,2,80,128]{4,3,2,1,0:T(8,128)(2,1)}, bf16[2,2,2,80,128]{4,3,2,1,0:T(8,128)(2,1)S(1)}, u32[]{:S(2)}, u32[]{:S(2)}) collective-permute-start(bf16[2,2,2,80,128]{4,3,2,1,0:T(8,128)(2,1)} %pad_maximum_fusion.2), channel_id=1, source_target_pairs={{1,13},{3,15},{17,29},{19,31}} | collective-permute-start | bytes 491528 | tf_op jit(solution)/shard_map/ppermute | solution.py:34
  87.8 2.2 %collective-permute-start.11 = (bf16[2,2,2,80,128]{4,3,2,1,0:T(8,128)(2,1)}, bf16[2,2,2,80,128]{4,3,2,1,0:T(8,128)(2,1)}, u32[]{:S(2)}, u32[]{:S(2)}) collective-permute-start(bf16[2,2,2,80,128]{4,3,2,1,0:T(8,128)(2,1)} %pad_maximum_fusion.2), channel_id=1, source_target_pairs={{1,9},{5,13},{3,11},{7,15},{17,25},{21,29},{19,27},{23,31}} | collective-permute-start | bytes 491528 | tf_op jit(solution)/shard_map/ppermute | solution.py:34
  90.0 2.6 %collective-permute-start.12 = (bf16[2,2,2,80,128]{4,3,2,1,0:T(8,128)(2,1)}, bf16[2,2,2,80,128]{4,3,2,1,0:T(8,128)(2,1)}, u32[]{:S(2)}, u32[]{:S(2)}) collective-permute-start(bf16[2,2,2,80,128]{4,3,2,1,0:T(8,128)(2,1)} %pad_maximum_fusion.2), channel_id=1, source_target_pairs={{1,5},{5,9},{9,13},{3,7},{7,11},{11,15},{17,21},{21,25},{25,29},{1... | collective-permute-start | bytes 491528 | tf_op jit(solution)/shard_map/ppermute | solution.py:34
  92.6 1.5 %fusion.64 = bf16[2,128,640]{2,1,0:T(8,128)(2,1)} fusion(bf16[1,1280,640]{2,1,0:T(8,128)(2,1)S(1)} %copy-done, bf16[2,128,1280]{2,1,0:T(8,128)(2,1)S(1)} %get-tuple-element.21, f32[2,128]{1,0:T(2,128)S(1)} %add_rsqrt_fusion, f32[1280]{0:T(1024)S(1)} %convert_reduce_fusion), kind=kOutput, calls=%fused_computation.64 | convolution fusion | flops 421068800 | bytes 2627584 | tf_op jit(solution)/shard_map/btd,de->bte/dot_general | solution.py:72
  100.9 1.3 %collective-permute-start.13 = (bf16[2,1,128,640]{3,2,1,0:T(8,128)(2,1)S(1)}, bf16[2,1,128,640]{3,2,1,0:T(8,128)(2,1)S(1)}, u32[]{:S(2)}, u32[]{:S(2)}) collective-permute-start(bf16[2,1,128,640]{3,2,1,0:T(8,128)(2,1)S(1)} %pad_maximum_fusion), channel_id=1, source_target_pairs={{1,0},{3,2},{5,4},{7,6},{9,8},{11,10},{13,12},{15,14},{17,16},{19,... | collective-permute-start | bytes 983048 | tf_op jit(solution)/shard_map/ppermute | solution.py:245
  102.3 1.3 %collective-permute-start.14 = (bf16[1,128,640]{2,1,0:T(8,128)(2,1)S(1)}, bf16[1,128,640]{2,1,0:T(8,128)(2,1)S(1)}, u32[]{:S(2)}, u32[]{:S(2)}) collective-permute-start(bf16[1,128,640]{2,1,0:T(8,128)(2,1)S(1)} %get-tuple-element.8), channel_id=1, source_target_pairs={{1,2},{3,0},{5,6},{7,4},{9,10},{11,8},{13,14},{15,12},{17,18},{19,... | collective-permute-start | bytes 491528 | tf_op jit(solution)/shard_map/ppermute | solution.py:245
  103.6 2.4 %collective-permute-start.15 = (bf16[1,128,640]{2,1,0:T(8,128)(2,1)S(1)}, bf16[1,128,640]{2,1,0:T(8,128)(2,1)S(1)}, u32[]{:S(2)}, u32[]{:S(2)}) collective-permute-start(bf16[1,128,640]{2,1,0:T(8,128)(2,1)S(1)} %constant_dynamic-slice_fusion), channel_id=1, source_target_pairs={{1,3},{3,1},{5,7},{7,5},{9,11},{11,9},{13,15},{15,13},{17,19},{19,... | collective-permute-start | bytes 491528 | tf_op jit(solution)/shard_map/ppermute | solution.py:249
  106.7 3.0 %collective-permute-done.15 = bf16[1,128,640]{2,1,0:T(8,128)(2,1)S(1)} collective-permute-done((bf16[1,128,640]{2,1,0:T(8,128)(2,1)S(1)}, bf16[1,128,640]{2,1,0:T(8,128)(2,1)S(1)}, u32[]{:S(2)}, u32[]{:S(2)}) %collective-permute-start.15) | collective-permute-done | bytes 163872 | tf_op jit(solution)/shard_map/ppermute | solution.py:249
  (117 shorter events, 31.3 us)
Async XLA Ops:
  0.6 56.3 %copy-start = (bf16[1,1280,640]{2,1,0:T(8,128)(2,1)S(1)}, bf16[1,1280,640]{2,1,0:T(8,128)(2,1)}, u32[]{:S(2)}) copy-start(bf16[1,1280,640]{2,1,0:T(8,128)(2,1)} %param.12) | copy-start | bytes 4915204
  0.6 3.6 %copy-start.1 = (bf16[2,64,4096]{2,1,0:T(8,128)(2,1)S(1)}, bf16[2,64,4096]{2,1,0:T(8,128)(2,1)}, u32[]{:S(2)}) copy-start(bf16[2,64,4096]{2,1,0:T(8,128)(2,1)} %param.8) | copy-start | bytes 3145732
  0.7 11.7 %copy-start.3 = (bf16[1,1280]{1,0:T(2,128)(2,1)S(1)}, bf16[1,1280]{1,0:T(2,128)(2,1)}, u32[]{:S(2)}) copy-start(bf16[1,1280]{1,0:T(2,128)(2,1)} %param.11) | copy-start | bytes 7684
  4.9 14.2 %collective-permute-start = (f32[2,64,34]{1,0,2:T(2,128)S(1)}, f32[2,64,34]{1,0,2:T(2,128)S(1)}, u32[]{:S(2)}, u32[]{:S(2)}) collective-permute-start(f32[2,64,34]{1,0,2:T(2,128)S(1)} %pad_maximum_fusion.3), channel_id=1, source_target_pairs={{0,4},{4,8},{8,12},{12,0},{1,5},{5,9},{9,13},{13,1},{2,6},{6,10},{... | collective-permute-start | bytes 52232 | tf_op jit(solution)/shard_map/ppermute | solution.py:13
  7.1 12.0 %collective-permute-start.2 = (f32[2,64,34]{1,0,2:T(2,128)S(1)}, f32[2,64,34]{1,0,2:T(2,128)S(1)}, u32[]{:S(2)}, u32[]{:S(2)}) collective-permute-start(f32[2,64,34]{1,0,2:T(2,128)S(1)} %pad_maximum_fusion.3), channel_id=1, source_target_pairs={{0,12},{4,0},{8,4},{12,8},{1,13},{5,1},{9,5},{13,9},{2,14},{6,2},{... | collective-permute-start | bytes 52232 | tf_op jit(solution)/shard_map/ppermute | solution.py:13
  9.2 10.0 %collective-permute-start.1 = (f32[2,64,34]{1,0,2:T(2,128)S(1)}, f32[2,64,34]{1,0,2:T(2,128)S(1)}, u32[]{:S(2)}, u32[]{:S(2)}) collective-permute-start(f32[2,64,34]{1,0,2:T(2,128)S(1)} %pad_maximum_fusion.3), channel_id=1, source_target_pairs={{0,8},{4,12},{8,0},{12,4},{1,9},{5,13},{9,1},{13,5},{2,10},{6,14},... | collective-permute-start | bytes 52232 | tf_op jit(solution)/shard_map/ppermute | solution.py:13
  9.6 66.6 %collective-permute-start.9 = (bf16[640,1280]{1,0:T(8,128)(2,1)}, bf16[640,1280]{1,0:T(8,128)(2,1)}, u32[]{:S(2)}, u32[]{:S(2)}) collective-permute-start(bf16[640,1280]{1,0:T(8,128)(2,1)} %bitcast.217), channel_id=1, source_target_pairs={{0,3},{2,1},{4,7},{6,5},{8,11},{10,9},{12,15},{14,13},{16,19},{18,... | collective-permute-start | bytes 4915208 | tf_op jit(solution)/shard_map/ppermute | solution.py:146
  10.9 67.5 %collective-permute-start.7 = (bf16[640,1280]{1,0:T(8,128)(2,1)}, bf16[640,1280]{1,0:T(8,128)(2,1)}, u32[]{:S(2)}, u32[]{:S(2)}) collective-permute-start(bf16[640,1280]{1,0:T(8,128)(2,1)} %bitcast.218), channel_id=1, source_target_pairs={{0,1},{2,3},{4,5},{6,7},{8,9},{10,11},{12,13},{14,15},{16,17},{18,... | collective-permute-start | bytes 4915208 | tf_op jit(solution)/shard_map/ppermute | solution.py:146
  26.9 5.2 %copy-start.7 = (pred[16,17]{0,1:T(8,128)(4,1)S(1)}, pred[16,17]{0,1:T(8,128)(4,1)}, u32[]{:S(2)}) copy-start(pred[16,17]{0,1:T(8,128)(4,1)} %constant.128) | copy-start | bytes 820
  50.8 1.7 %copy-start.5 = (bf16[1,1280,160]{1,2,0:T(8,128)(2,1)S(1)}, bf16[1,1280,160]{1,2,0:T(8,128)(2,1)}, u32[]{:S(2)}) copy-start(bf16[1,1280,160]{1,2,0:T(8,128)(2,1)} %param.13) | copy-start | bytes 1228804
  53.6 4.3 %collective-permute-start.3 = (bf16[2,2,2,80,128]{4,3,2,1,0:T(8,128)(2,1)}, bf16[2,2,2,80,128]{4,3,2,1,0:T(8,128)(2,1)S(1)}, u32[]{:S(2)}, u32[]{:S(2)}) collective-permute-start(bf16[2,2,2,80,128]{4,3,2,1,0:T(8,128)(2,1)} %pad_maximum_fusion.1), channel_id=1, source_target_pairs={{0,12},{2,14},{16,28},{18,30}} | collective-permute-start | bytes 491528 | tf_op jit(solution)/shard_map/ppermute | solution.py:34
  54.3 3.6 %collective-permute-start.4 = (bf16[2,2,2,80,128]{4,3,2,1,0:T(8,128)(2,1)}, bf16[2,2,2,80,128]{4,3,2,1,0:T(8,128)(2,1)}, u32[]{:S(2)}, u32[]{:S(2)}) collective-permute-start(bf16[2,2,2,80,128]{4,3,2,1,0:T(8,128)(2,1)} %pad_maximum_fusion.1), channel_id=1, source_target_pairs={{0,8},{4,12},{2,10},{6,14},{16,24},{20,28},{18,26},{22,30}} | collective-permute-start | bytes 491528 | tf_op jit(solution)/shard_map/ppermute | solution.py:34
  55.6 2.3 %collective-permute-start.5 = (bf16[2,2,2,80,128]{4,3,2,1,0:T(8,128)(2,1)}, bf16[2,2,2,80,128]{4,3,2,1,0:T(8,128)(2,1)}, u32[]{:S(2)}, u32[]{:S(2)}) collective-permute-start(bf16[2,2,2,80,128]{4,3,2,1,0:T(8,128)(2,1)} %pad_maximum_fusion.1), channel_id=1, source_target_pairs={{0,4},{4,8},{8,12},{2,6},{6,10},{10,14},{16,20},{20,24},{24,28},{1... | collective-permute-start | bytes 491528 | tf_op jit(solution)/shard_map/ppermute | solution.py:34
  62.4 13.8 %collective-permute-start.8 = (bf16[2,128,640]{2,1,0:T(8,128)(2,1)}, bf16[2,128,640]{2,1,0:T(8,128)(2,1)S(1)}, u32[]{:S(2)}, u32[]{:S(2)}) collective-permute-start(bf16[2,128,640]{2,1,0:T(8,128)(2,1)} %copy.51), channel_id=1, source_target_pairs={{0,3},{2,1},{4,7},{6,5},{8,11},{10,9},{12,15},{14,13},{16,19},{18,... | collective-permute-start | bytes 983048 | tf_op jit(solution)/shard_map/ppermute | solution.py:218
  63.7 14.6 %collective-permute-start.6 = (bf16[2,128,640]{2,1,0:T(8,128)(2,1)}, bf16[2,128,640]{2,1,0:T(8,128)(2,1)S(1)}, u32[]{:S(2)}, u32[]{:S(2)}) collective-permute-start(bf16[2,128,640]{2,1,0:T(8,128)(2,1)} %copy.51), channel_id=1, source_target_pairs={{0,1},{2,3},{4,5},{6,7},{8,9},{10,11},{12,13},{14,15},{16,17},{18,... | collective-permute-start | bytes 983048 | tf_op jit(solution)/shard_map/ppermute | solution.py:218
  78.3 2.4 %copy-start.4 = (bf16[1,1280,160]{1,2,0:T(8,128)(2,1)S(1)}, bf16[1,1280,160]{1,2,0:T(8,128)(2,1)}, u32[]{:S(2)}) copy-start(bf16[1,1280,160]{1,2,0:T(8,128)(2,1)} %param.14) | copy-start | bytes 1228804
  80.6 1.0 copy-start.6
  82.8 13.2 %collective-permute-start.10 = (bf16[2,2,2,80,128]{4,3,2,1,0:T(8,128)(2,1)}, bf16[2,2,2,80,128]{4,3,2,1,0:T(8,128)(2,1)S(1)}, u32[]{:S(2)}, u32[]{:S(2)}) collective-permute-start(bf16[2,2,2,80,128]{4,3,2,1,0:T(8,128)(2,1)} %pad_maximum_fusion.2), channel_id=1, source_target_pairs={{1,13},{3,15},{17,29},{19,31}} | collective-permute-start | bytes 491528 | tf_op jit(solution)/shard_map/ppermute | solution.py:34
  87.8 8.2 %collective-permute-start.11 = (bf16[2,2,2,80,128]{4,3,2,1,0:T(8,128)(2,1)}, bf16[2,2,2,80,128]{4,3,2,1,0:T(8,128)(2,1)}, u32[]{:S(2)}, u32[]{:S(2)}) collective-permute-start(bf16[2,2,2,80,128]{4,3,2,1,0:T(8,128)(2,1)} %pad_maximum_fusion.2), channel_id=1, source_target_pairs={{1,9},{5,13},{3,11},{7,15},{17,25},{21,29},{19,27},{23,31}} | collective-permute-start | bytes 491528 | tf_op jit(solution)/shard_map/ppermute | solution.py:34
  90.0 6.0 %collective-permute-start.12 = (bf16[2,2,2,80,128]{4,3,2,1,0:T(8,128)(2,1)}, bf16[2,2,2,80,128]{4,3,2,1,0:T(8,128)(2,1)}, u32[]{:S(2)}, u32[]{:S(2)}) collective-permute-start(bf16[2,2,2,80,128]{4,3,2,1,0:T(8,128)(2,1)} %pad_maximum_fusion.2), channel_id=1, source_target_pairs={{1,5},{5,9},{9,13},{3,7},{7,11},{11,15},{17,21},{21,25},{25,29},{1... | collective-permute-start | bytes 491528 | tf_op jit(solution)/shard_map/ppermute | solution.py:34
  98.6 1.4 %copy-start.2 = (bf16[1,640,1280]{2,1,0:T(8,128)(2,1)S(1)}, bf16[1,640,1280]{2,1,0:T(8,128)(2,1)}, u32[]{:S(2)}) copy-start(bf16[1,640,1280]{2,1,0:T(8,128)(2,1)} %param.15) | copy-start | bytes 4915204
  100.9 8.7 %collective-permute-start.13 = (bf16[2,1,128,640]{3,2,1,0:T(8,128)(2,1)S(1)}, bf16[2,1,128,640]{3,2,1,0:T(8,128)(2,1)S(1)}, u32[]{:S(2)}, u32[]{:S(2)}) collective-permute-start(bf16[2,1,128,640]{3,2,1,0:T(8,128)(2,1)S(1)} %pad_maximum_fusion), channel_id=1, source_target_pairs={{1,0},{3,2},{5,4},{7,6},{9,8},{11,10},{13,12},{15,14},{17,16},{19,... | collective-permute-start | bytes 983048 | tf_op jit(solution)/shard_map/ppermute | solution.py:245
  102.3 4.4 %collective-permute-start.14 = (bf16[1,128,640]{2,1,0:T(8,128)(2,1)S(1)}, bf16[1,128,640]{2,1,0:T(8,128)(2,1)S(1)}, u32[]{:S(2)}, u32[]{:S(2)}) collective-permute-start(bf16[1,128,640]{2,1,0:T(8,128)(2,1)S(1)} %get-tuple-element.8), channel_id=1, source_target_pairs={{1,2},{3,0},{5,6},{7,4},{9,10},{11,8},{13,14},{15,12},{17,18},{19,... | collective-permute-start | bytes 491528 | tf_op jit(solution)/shard_map/ppermute | solution.py:245
  103.6 6.1 %collective-permute-start.15 = (bf16[1,128,640]{2,1,0:T(8,128)(2,1)S(1)}, bf16[1,128,640]{2,1,0:T(8,128)(2,1)S(1)}, u32[]{:S(2)}, u32[]{:S(2)}) collective-permute-start(bf16[1,128,640]{2,1,0:T(8,128)(2,1)S(1)} %constant_dynamic-slice_fusion), channel_id=1, source_target_pairs={{1,3},{3,1},{5,7},{7,5},{9,11},{11,9},{13,15},{15,13},{17,19},{19,... | collective-permute-start | bytes 491528 | tf_op jit(solution)/shard_map/ppermute | solution.py:249

commit v6 on v5

--- a/solution.py
+++ b/solution.py
@@ -186,24 +186,38 @@
     variance = spread_total / history
     inv_std = lax.rsqrt(variance + 1e-05)[..., None]
 
-    padded = jnp.concatenate([prior_raw, series.astype(jnp.float32)], -1)
-    padded_pos = tm_at * steps_dev - STRIDE + jnp.arange(steps_dev + STRIDE, dtype=jnp.int32)
-    padded_valid = (
-        (padded_pos[None, :] >= first_step[:, None]) & (padded_pos[None, :] >= 0)
-    ).astype(jnp.float32)[:, None, :]
+    raw_blocks = jnp.swapaxes(series.reshape(seq_count, channels, tok_count, STRIDE), 2, 3)
+    block_pos = (
+        tm_at * steps_dev
+        + jnp.arange(tok_count, dtype=jnp.int32)[None, :] * STRIDE
+        + jnp.arange(STRIDE, dtype=jnp.int32)[:, None]
+    )
+    block_valid = (block_pos[None] >= first_step[:, None, None]).astype(jnp.float32)[:, None]
     normed = (
-        (padded * padded_valid - channel_mean[..., None]) * padded_valid * inv_std
-    ).astype(jnp.bfloat16)
-    kernel = patch_weight.reshape(channels, 2 * STRIDE, patch_weight.shape[1])
-    tokens = lax.conv_general_dilated(
-        normed,
-        kernel,
-        window_strides=(STRIDE,),
-        padding="VALID",
-        dimension_numbers=("NCW", "IWO", "NWC"),
+        (raw_blocks.astype(jnp.float32) * block_valid - channel_mean[..., None, None])
+        * block_valid
+        * inv_std[..., None]
+    ).astype(jnp.bfloat16)
+    prior_pos = tm_at * steps_dev - STRIDE + jnp.arange(STRIDE, dtype=jnp.int32)
+    prior_valid = ((prior_pos[None, :] >= first_step[:, None]) & (prior_pos[None, :] >= 0)).astype(
+        jnp.float32
+    )[:, None, :]
+    prior_normed = (
+        (prior_raw * prior_valid - channel_mean[..., None]) * prior_valid * inv_std
+    ).astype(jnp.bfloat16)
+    column_count = patch_weight.shape[1]
+    halves = patch_weight.T.reshape(column_count, channels, 2, STRIDE)
+    flat = normed.reshape(seq_count, channels * STRIDE, tok_count)
+    left_w = halves[:, :, 0].reshape(column_count, channels * STRIDE)
+    right_w = halves[:, :, 1].reshape(column_count, channels * STRIDE)
+    right_terms = jnp.einsum("dk,skj->sdj", right_w, flat, preferred_element_type=jnp.float32)
+    left_all = jnp.einsum("dk,skj->sdj", left_w, flat, preferred_element_type=jnp.float32)
+    edge_term = jnp.einsum(
+        "dk,sk->sd", left_w, prior_normed.reshape(seq_count, channels * STRIDE),
         preferred_element_type=jnp.float32,
-    ).astype(jnp.bfloat16)
-    column_count = patch_weight.shape[1]
+    )
+    left_terms = jnp.concatenate([edge_term[:, :, None], left_all[:, :, : tok_count - 1]], 2)
+    tokens = jnp.swapaxes((left_terms + right_terms).astype(jnp.bfloat16), 1, 2)
     hidden0 = lax.all_gather(tokens, feat_axes, axis=2, tiled=True)
     feature_count = hidden0.shape[2]
     head_cols = feature_count // mp_n

time: 111 us -> 121 us (1.090)
  local copies, waits for them, and re-layouts: 20.5 us -> 29.2 us
  other arithmetic: 15.7 us -> 19.3 us
  waiting for transfers between devices: 14.2 us -> 12.5 us
  matrix products: 19.3 us -> 18 us
    conv_general_dilated x3 -> x0, local copies, waits for them, and re-layouts: 8.47 us -> none  [per_device(): lax.conv_general_dilated(normed, kernel, window_strides=(STRIDE,), paddin...]
    convert_element_type x5 -> x4, local copies, waits for them, and re-layouts: 1.45 us -> 8.69 us  [the longest x1 5.17 us: per_device(): normed = ((raw_blocks.astype(jnp.float32) * block_valid - channel_mean[.....]
    conv_general_dilated x1 -> x0, matrix products: 5.7 us -> none  [per_device(): lax.conv_general_dilated(normed, kernel, window_strides=(STRIDE,), paddin...]
    slice x2 -> x1, local copies, waits for them, and re-layouts: 0.1 us -> 3.4 us  [per_device(): left_w = halves[:, :, 0].reshape(column_count, channels * STRIDE)]
    dot_general x0 -> x3, matrix products: none -> 3.11 us  [the longest x1 2.07 us: per_device(): jnp.einsum('dk,skj->sdj', left_w, flat, preferred_element_type=jnp.float32)]
    unnamed x18 -> x33, local copies, waits for them, and re-layouts: 5.64 us -> 7.33 us
    ppermute x2, waiting for transfers between devices: 11.1 us -> 9.46 us  [per_device(): arrived = lax.ppermute(attended0, feat_axes, pairs)]
    another operation x3, local copies, waits for them, and re-layouts: 0.01 us -> 1.37 us  [per_device(): jnp.stack([piece[..., :2] for piece in received], 0)]
  transfers between devices with their start and end apart: 16 -> 16, of which waited for: 2 -> 2; matrix products, arithmetic and copies ran while one was open for 37% -> 41% of each run, Pallas kernels for 0% -> 0%
where the time goes in v6:
time: 121 us; the launch traced here: 120 us
  local copies, waits for them, and re-layouts  29.2 us (24%)
  starting transfers between devices  28.4 us (23%)
  other arithmetic  19.3 us (16%)
  matrix products  18 us (15%)
  waiting for transfers between devices  12.5 us (10%)
  blocking collectives  11.8 us (10%)
  between operations  1.22 us (1%)
    ppermute x6, starting transfers between devices, gather_causal(): pieces.append(lax.ppermute(value, ('tm', 'section'), pairs))  13.4 us
    all_gather x1, blocking collectives, per_device(): hidden0 = lax.all_gather(tokens, feat_axes, axis=2, tiled=True)  11.8 us
    ppermute x2, waiting for transfers between devices, per_device(): arrived = lax.ppermute(attended0, feat_axes, pairs)  9.46 us
    unnamed x33, local copies, waits for them, and re-layouts  7.33 us
    convert_element_type x1, local copies, waits for them, and re-layouts, per_device(): normed = ((raw_blocks.astype(jnp.float32) * block_valid - channel_mean[.....  5.17 us
    dot_general x2, matrix products, per_device(): jnp.einsum('bte,ed->btd', arrived, rows, preferred_element_type=jnp.float32)  4.68 us
    ppermute x3, starting transfers between devices, shift_from(): return lax.ppermute(value, axis, pairs)  4.6 us
    convert_element_type x1, other arithmetic, per_device(): normed = ((raw_blocks.astype(jnp.float32) * block_valid - channel_mean[.....  3.84 us
  transfers between devices with their start and end apart: 16, of which 2 were waited for; matrix products, arithmetic and copies ran while one was open for 41% of the time, Pallas kernels for 0%

profile of v6, /device:TPU:1, one launch (start us, length us, event | category | flops | bytes accessed | tf_op | source)
XLA Modules:
  0.0 120.4 jit_solution(9902928845256736899)
XLA Ops:
  0.7 1.3 %fusion.90 = (s32[2]{0:T(128)S(1)}, s32[2]{0:T(128)S(1)}, f32[2]{0:T(128)}) fusion(s32[2]{0:T(128)} %param.9), kind=kLoop, calls=%fused_computation.151 | loop fusion | flops 36 | bytes 32 | tf_op jit(solution)/shard_map/sub | solution.py:87
  3.2 1.5 %multiply_reduce_fusion.1 = f32[2,64]{1,0:T(2,128)S(1)} fusion(f32[2,4096]{1,0:T(2,128)S(1)} %compare_convert_fusion.1, bf16[2,64,4096]{2,1,0:T(8,128)(2,1)} %param.8), kind=kLoop, calls=%fused_computation.23 | loop fusion | flops 1572736 | bytes 1081856 | tf_op jit(solution)/shard_map/reduce_sum | solution.py:155
  6.0 2.1 %collective-permute-start = (f32[2,64,34]{1,0,2:T(2,128)}, f32[2,64,34]{1,0,2:T(2,128)S(1)}, u32[]{:S(2)}, u32[]{:S(2)}) collective-permute-start(f32[2,64,34]{1,0,2:T(2,128)} %pad_maximum_fusion.3), channel_id=1, source_target_pairs={{0,4},{4,8},{8,12},{12,0},{1,5},{5,9},{9,13},{13,1},{2,6},{6,10},{... | collective-permute-start | bytes 52232 | tf_op jit(solution)/shard_map/ppermute | solution.py:13
  8.2 2.0 %collective-permute-start.2 = (f32[2,64,34]{1,0,2:T(2,128)}, f32[2,64,34]{1,0,2:T(2,128)}, u32[]{:S(2)}, u32[]{:S(2)}) collective-permute-start(f32[2,64,34]{1,0,2:T(2,128)} %pad_maximum_fusion.3), channel_id=1, source_target_pairs={{0,12},{4,0},{8,4},{12,8},{1,13},{5,1},{9,5},{13,9},{2,14},{6,2},{... | collective-permute-start | bytes 52232 | tf_op jit(solution)/shard_map/ppermute | solution.py:13
  14.2 4.5 %copy.89 = bf16[4096,320]{1,0:T(8,128)(2,1)} copy(bf16[4096,320]{0,1:T(8,128)(2,1)} %param.10) | data formatting | bytes 5242880 | tf_op args[2]
  18.7 3.4 %fusion.100 = (bf16[320,64,1,32]{0,3,2,1:T(8,128)(2,1)S(1)}, bf16[320,64,1,32]{0,3,2,1:T(8,128)(2,1)}) fusion(bf16[320,64,2,32]{0,3,2,1:T(8,128)(2,1)} %bitcast.241), kind=kLoop, calls=%fused_computation.168 | loop fusion | bytes 5242880 | tf_op jit(solution)/shard_map/slice | solution.py:211
  23.9 3.3 %copy.90 = f32[2,64,4096]{1,2,0:T(8,128)} copy(bf16[2,64,4096]{2,1,0:T(8,128)(2,1)} %param.8) | data formatting | bytes 3145728 | tf_op jit(solution)/shard_map/convert_element_type | solution.py:153
  31.6 3.8 %multiply_convert_fusion = bf16[2,64,32,128]{1,2,3,0:T(8,128)(2,1)} fusion(f32[2,64,32,128]{1,2,3,0:T(8,128)} %bitcast.238, f32[2,64]{1,0:T(2,128)S(1)} %add_rsqrt_fusion.2, f32[2,64]{1,0:T(2,128)S(1)} %broadcast_divide_fusion, f32[2,32,128]{1,2,0:T(8,128)S(1)} %compare_convert_fusion), kind=kLoop, calls=%fused_computation.5 | loop fusion | flops 2621440 | bytes 3179520 | tf_op jit(solution)/shard_map/convert_element_type | solution.py:200
  35.5 5.2 %copy.91 = bf16[2,64,32,128]{3,2,1,0:T(8,128)(2,1)} copy(bf16[2,64,32,128]{1,2,3,0:T(8,128)(2,1)} %multiply_convert_fusion) | data formatting | bytes 2097152 | tf_op jit(solution)/shard_map/convert_element_type | solution.py:200
  42.2 2.1 %convolution_bitcast_fusion.1 = f32[2,320,128]{2,1,0:T(8,128)S(1)} fusion(bf16[2,2048,128]{2,1,0:T(8,128)(2,1)} %bitcast.242, bf16[320,2048,1]{0,1,2:T(8,128)(2,1)S(1)} %bitcast.240), kind=kOutput, calls=%fused_computation.54 | convolution fusion | flops 335544320 | bytes 2686976 | tf_op jit(solution)/shard_map/dk,skj->sdj/dot_general | solution.py:214
  45.1 11.8 %all_gather.3 = bf16[2,128,1280]{1,2,0:T(8,128)(2,1)S(1)} all-gather(bf16[2,128,320]{1,2,0:T(8,128)(2,1)S(1)} %fusion.58), channel_id=1, replica_groups=mesh['groups'=2,'tm'=4,'mp'=2,'section'=2] {'mp','section'}, dimensions={2}, use_global_device_ids=true | all-gather | bytes 819200 | tf_op jit(solution)/shard_map/all_gather | solution.py:221
  64.3 1.7 %fusion = (f32[2,2,4,128]{3,2,1,0:T(4,128)S(1)}, f32[2,2,512,128,4]{3,2,4,1,0:T(8,128)S(1)}) fusion(pred[2,128,512]{1,2,0:T(8,128)(4,1)S(1)} %or_and_fusion, bf16[2,128,2,4,80]{1,4,3,2,0:T(8,128)(2,1)} %bitcast.248, bf16[1,2,2,2,80,512]{5,4,3,2,1,0:T(8,128)(2,1)S(1)} %maximum_bitcast_fusion), kind=kOutput, calls=%fused_computation.6 | convolution fusion | flops 169867264 | bytes 4988928 | tf_op jit(solution)/shard_map/btkgh,bkhn->bkgtn/dot_general | solution.py:47
  66.8 1.7 %fusion.68 = bf16[2,128,2,4,80]{1,4,3,2,0:T(8,128)(2,1)} fusion(f32[2,2,512,128,4]{3,2,4,1,0:T(8,128)S(1)} %get-tuple-element.33, f32[2,2,4,128]{3,2,1,0:T(4,128)S(1)} %get-tuple-element.26, pred[2,128,512]{1,2,0:T(8,128)(4,1)S(1)} %or_and_fusion, bf16[1,2,2,2,80,512]{5,4,3,2,1,0:T(8,128)(2,1)S(1)} %maximum_bitcast_fusion, ...), kind=kOutput, calls=%fused_computation.65 | convolution fusion | flops 171409408 | bytes 5005312 | tf_op jit(solution)/shard_map/bkgtn,bkhn->bkgth/dot_general | solution.py:55
  68.5 1.9 %copy.100 = bf16[2,128,640]{2,1,0:T(8,128)(2,1)} copy(bf16[2,128,640]{1,2,0:T(8,128)(2,1)} %bitcast.263) | data formatting | bytes 655360 | tf_op jit(solution)/shard_map/reshape | solution.py:123
  71.6 1.5 %collective-permute-start.6 = (bf16[2,128,640]{2,1,0:T(8,128)(2,1)}, bf16[2,128,640]{2,1,0:T(8,128)(2,1)S(1)}, u32[]{:S(2)}, u32[]{:S(2)}) collective-permute-start(bf16[2,128,640]{2,1,0:T(8,128)(2,1)} %copy.100), channel_id=1, source_target_pairs={{0,1},{2,3},{4,5},{6,7},{8,9},{10,11},{12,13},{14,15},{16,17},{18,... | collective-permute-start | bytes 983048 | tf_op jit(solution)/shard_map/ppermute | solution.py:232
  73.1 9.5 %collective-permute-done.8 = bf16[2,128,640]{2,1,0:T(8,128)(2,1)S(1)} collective-permute-done((bf16[2,128,640]{2,1,0:T(8,128)(2,1)}, bf16[2,128,640]{2,1,0:T(8,128)(2,1)S(1)}, u32[]{:S(2)}, u32[]{:S(2)}) %collective-permute-start.8) | collective-permute-done | bytes 327712 | tf_op jit(solution)/shard_map/ppermute | solution.py:232
  82.6 2.2 %fusion.19 = f32[2,128,1280]{1,2,0:T(8,128)S(1)} fusion(bf16[2,128,640]{2,1,0:T(8,128)(2,1)S(1)} %collective-permute-done.8, bf16[640,1280]{1,0:T(8,128)(2,1)} %collective-permute-done.9), kind=kOutput, calls=%fused_computation.29 | convolution fusion | flops 419430400 | bytes 3276800 | tf_op jit(solution)/shard_map/bte,ed->btd/dot_general | solution.py:233
  85.6 2.5 %fusion.26 = (f32[2,128]{1,0:T(2,128)S(1)}, bf16[2,128,1280]{1,2,0:T(8,128)(2,1)S(1)}) fusion(f32[2,128,1280]{1,2,0:T(8,128)S(1)} %fusion.19, bf16[2,128,640]{2,1,0:T(8,128)(2,1)} %copy-done.7, bf16[640,1280]{1,0:T(8,128)(2,1)} %collective-permute-done.7, bf16[2,128,1280]{1,2,0:T(8,128)(2,1)S(1)} %all_gather.3), kind=kOutput, calls=%fused_computation.38 | convolution fusion | flops 421723904 | bytes 4588544 | tf_op jit(solution)/shard_map/bte,ed->btd/dot_general | solution.py:233
  89.6 6.0 %collective-permute-start.10 = (bf16[2,2,2,80,128]{4,3,2,1,0:T(8,128)(2,1)}, bf16[2,2,2,80,128]{4,3,2,1,0:T(8,128)(2,1)S(1)}, u32[]{:S(2)}, u32[]{:S(2)}) collective-permute-start(bf16[2,2,2,80,128]{4,3,2,1,0:T(8,128)(2,1)} %pad_maximum_fusion.2), channel_id=1, source_target_pairs={{1,13},{3,15},{17,29},{19,31}} | collective-permute-start | bytes 491528 | tf_op jit(solution)/shard_map/ppermute | solution.py:34
  95.6 2.0 %collective-permute-start.11 = (bf16[2,2,2,80,128]{4,3,2,1,0:T(8,128)(2,1)}, bf16[2,2,2,80,128]{4,3,2,1,0:T(8,128)(2,1)}, u32[]{:S(2)}, u32[]{:S(2)}) collective-permute-start(bf16[2,2,2,80,128]{4,3,2,1,0:T(8,128)(2,1)} %pad_maximum_fusion.2), channel_id=1, source_target_pairs={{1,9},{5,13},{3,11},{7,15},{17,25},{21,29},{19,27},{23,31}} | collective-permute-start | bytes 491528 | tf_op jit(solution)/shard_map/ppermute | solution.py:34
  97.6 2.8 %collective-permute-start.12 = (bf16[2,2,2,80,128]{4,3,2,1,0:T(8,128)(2,1)}, bf16[2,2,2,80,128]{4,3,2,1,0:T(8,128)(2,1)}, u32[]{:S(2)}, u32[]{:S(2)}) collective-permute-start(bf16[2,2,2,80,128]{4,3,2,1,0:T(8,128)(2,1)} %pad_maximum_fusion.2), channel_id=1, source_target_pairs={{1,5},{5,9},{9,13},{3,7},{7,11},{11,15},{17,21},{21,25},{25,29},{1... | collective-permute-start | bytes 491528 | tf_op jit(solution)/shard_map/ppermute | solution.py:34
  100.4 1.6 %fusion.50 = bf16[2,128,640]{2,1,0:T(8,128)(2,1)} fusion(bf16[1,1280,640]{2,1,0:T(8,128)(2,1)S(1)} %copy-done, bf16[2,128,1280]{1,2,0:T(8,128)(2,1)S(1)} %get-tuple-element.35, f32[2,128]{1,0:T(2,128)S(1)} %add_rsqrt_fusion, f32[1280]{0:T(1024)S(1)} %copy-done.9), kind=kOutput, calls=%fused_computation.50 | convolution fusion | flops 421068800 | bytes 2627584 | tf_op jit(solution)/shard_map/btd,de->bte/dot_general | solution.py:72
  113.4 2.4 %collective-permute-start.15 = (bf16[1,128,640]{1,2,0:T(8,128)(2,1)S(1)}, bf16[1,128,640]{1,2,0:T(8,128)(2,1)S(1)}, u32[]{:S(2)}, u32[]{:S(2)}) collective-permute-start(bf16[1,128,640]{1,2,0:T(8,128)(2,1)S(1)} %constant_dynamic-slice_fusion), channel_id=1, source_target_pairs={{1,3},{3,1},{5,7},{7,5},{9,11},{11,9},{13,15},{15,13},{17,19},{19,... | collective-permute-start | bytes 491528 | tf_op jit(solution)/shard_map/ppermute | solution.py:263
  116.5 3.0 %collective-permute-done.15 = bf16[1,128,640]{1,2,0:T(8,128)(2,1)S(1)} collective-permute-done((bf16[1,128,640]{1,2,0:T(8,128)(2,1)S(1)}, bf16[1,128,640]{1,2,0:T(8,128)(2,1)S(1)}, u32[]{:S(2)}, u32[]{:S(2)}) %collective-permute-start.15) | collective-permute-done | bytes 163872 | tf_op jit(solution)/shard_map/ppermute | solution.py:263
  (133 shorter events, 39.4 us)
Async XLA Ops:
  0.6 60.1 %copy-start = (bf16[1,1280,640]{2,1,0:T(8,128)(2,1)S(1)}, bf16[1,1280,640]{2,1,0:T(8,128)(2,1)}, u32[]{:S(2)}) copy-start(bf16[1,1280,640]{2,1,0:T(8,128)(2,1)} %param.12) | copy-start | bytes 4915204
  0.6 4.1 %copy-start.1 = (bf16[2,64,4096]{2,1,0:T(8,128)(2,1)S(1)}, bf16[2,64,4096]{2,1,0:T(8,128)(2,1)}, u32[]{:S(2)}) copy-start(bf16[2,64,4096]{2,1,0:T(8,128)(2,1)} %param.8) | copy-start | bytes 3145732
  6.0 21.3 %collective-permute-start = (f32[2,64,34]{1,0,2:T(2,128)}, f32[2,64,34]{1,0,2:T(2,128)S(1)}, u32[]{:S(2)}, u32[]{:S(2)}) collective-permute-start(f32[2,64,34]{1,0,2:T(2,128)} %pad_maximum_fusion.3), channel_id=1, source_target_pairs={{0,4},{4,8},{8,12},{12,0},{1,5},{5,9},{9,13},{13,1},{2,6},{6,10},{... | collective-permute-start | bytes 52232 | tf_op jit(solution)/shard_map/ppermute | solution.py:13
  8.2 19.2 %collective-permute-start.2 = (f32[2,64,34]{1,0,2:T(2,128)}, f32[2,64,34]{1,0,2:T(2,128)}, u32[]{:S(2)}, u32[]{:S(2)}) collective-permute-start(f32[2,64,34]{1,0,2:T(2,128)} %pad_maximum_fusion.3), channel_id=1, source_target_pairs={{0,12},{4,0},{8,4},{12,8},{1,13},{5,1},{9,5},{13,9},{2,14},{6,2},{... | collective-permute-start | bytes 52232 | tf_op jit(solution)/shard_map/ppermute | solution.py:13
  10.2 17.8 %collective-permute-start.1 = (f32[2,64,34]{1,0,2:T(2,128)}, f32[2,64,34]{1,0,2:T(2,128)}, u32[]{:S(2)}, u32[]{:S(2)}) collective-permute-start(f32[2,64,34]{1,0,2:T(2,128)} %pad_maximum_fusion.3), channel_id=1, source_target_pairs={{0,8},{4,12},{8,0},{12,4},{1,9},{5,13},{9,1},{13,5},{2,10},{6,14},... | collective-permute-start | bytes 52232 | tf_op jit(solution)/shard_map/ppermute | solution.py:13
  10.6 72.0 %collective-permute-start.9 = (bf16[640,1280]{1,0:T(8,128)(2,1)}, bf16[640,1280]{1,0:T(8,128)(2,1)}, u32[]{:S(2)}, u32[]{:S(2)}) collective-permute-start(bf16[640,1280]{1,0:T(8,128)(2,1)} %bitcast.245), channel_id=1, source_target_pairs={{0,3},{2,1},{4,7},{6,5},{8,11},{10,9},{12,15},{14,13},{16,19},{18,... | collective-permute-start | bytes 4915208 | tf_op jit(solution)/shard_map/ppermute | solution.py:146
  11.9 73.7 %collective-permute-start.7 = (bf16[640,1280]{1,0:T(8,128)(2,1)}, bf16[640,1280]{1,0:T(8,128)(2,1)}, u32[]{:S(2)}, u32[]{:S(2)}) collective-permute-start(bf16[640,1280]{1,0:T(8,128)(2,1)} %bitcast.246), channel_id=1, source_target_pairs={{0,1},{2,3},{4,5},{6,7},{8,9},{10,11},{12,13},{14,15},{16,17},{18,... | collective-permute-start | bytes 4915208 | tf_op jit(solution)/shard_map/ppermute | solution.py:146
  18.7 3.4 %copy-start.10 = (bf16[1,1280]{1,0:T(2,128)(2,1)S(1)}, bf16[1,1280]{1,0:T(2,128)(2,1)}, u32[]{:S(2)}) copy-start(bf16[1,1280]{1,0:T(2,128)(2,1)} %param.11) | copy-start | bytes 7684
  44.3 12.8 %copy-start.9 = (f32[1280]{0:T(1024)S(1)}, f32[1280]{0:T(1024)}, u32[]{:S(2)}) copy-start(f32[1280]{0:T(1024)} %convert_reduce_fusion) | copy-start | bytes 15364
  44.3 12.7 %copy-start.11 = (bf16[1,1280,160]{1,2,0:T(8,128)(2,1)S(1)}, bf16[1,1280,160]{1,2,0:T(8,128)(2,1)}, u32[]{:S(2)}) copy-start(bf16[1,1280,160]{1,2,0:T(8,128)(2,1)} %param.14) | copy-start | bytes 1228804
  45.1 12.4 %copy-start.13 = (bf16[1,1280,160]{1,2,0:T(8,128)(2,1)S(1)}, bf16[1,1280,160]{1,2,0:T(8,128)(2,1)}, u32[]{:S(2)}) copy-start(bf16[1,1280,160]{1,2,0:T(8,128)(2,1)} %param.13) | copy-start | bytes 1228804
  58.0 4.5 %collective-permute-start.3 = (bf16[2,2,2,80,128]{4,3,2,1,0:T(8,128)(2,1)S(1)}, bf16[2,2,2,80,128]{4,3,2,1,0:T(8,128)(2,1)S(1)}, u32[]{:S(2)}, u32[]{:S(2)}) collective-permute-start(bf16[2,2,2,80,128]{4,3,2,1,0:T(8,128)(2,1)S(1)} %pad_maximum_fusion.1), channel_id=1, source_target_pairs={{0,12},{2,14},{16,28},{18,30}} | collective-permute-start | bytes 491528 | tf_op jit(solution)/shard_map/ppermute | solution.py:34
  58.7 3.8 %collective-permute-start.4 = (bf16[2,2,2,80,128]{4,3,2,1,0:T(8,128)(2,1)S(1)}, bf16[2,2,2,80,128]{4,3,2,1,0:T(8,128)(2,1)S(1)}, u32[]{:S(2)}, u32[]{:S(2)}) collective-permute-start(bf16[2,2,2,80,128]{4,3,2,1,0:T(8,128)(2,1)S(1)} %pad_maximum_fusion.1), channel_id=1, source_target_pairs={{0,8},{4,12},{2,10},{6,14},{16,24},{20,28},{18,26},{22,30}} | collective-permute-start | bytes 491528 | tf_op jit(solution)/shard_map/ppermute | solution.py:34
  59.4 3.8 %collective-permute-start.5 = (bf16[2,2,2,80,128]{4,3,2,1,0:T(8,128)(2,1)S(1)}, bf16[2,2,2,80,128]{4,3,2,1,0:T(8,128)(2,1)}, u32[]{:S(2)}, u32[]{:S(2)}) collective-permute-start(bf16[2,2,2,80,128]{4,3,2,1,0:T(8,128)(2,1)S(1)} %pad_maximum_fusion.1), channel_id=1, source_target_pairs={{0,4},{4,8},{8,12},{2,6},{6,10},{10,14},{16,20},{20,24},{24,28},{1... | collective-permute-start | bytes 491528 | tf_op jit(solution)/shard_map/ppermute | solution.py:34
  70.3 12.3 %collective-permute-start.8 = (bf16[2,128,640]{2,1,0:T(8,128)(2,1)}, bf16[2,128,640]{2,1,0:T(8,128)(2,1)S(1)}, u32[]{:S(2)}, u32[]{:S(2)}) collective-permute-start(bf16[2,128,640]{2,1,0:T(8,128)(2,1)} %copy.100), channel_id=1, source_target_pairs={{0,3},{2,1},{4,7},{6,5},{8,11},{10,9},{12,15},{14,13},{16,19},{18,... | collective-permute-start | bytes 983048 | tf_op jit(solution)/shard_map/ppermute | solution.py:232
  71.6 13.2 %collective-permute-start.6 = (bf16[2,128,640]{2,1,0:T(8,128)(2,1)}, bf16[2,128,640]{2,1,0:T(8,128)(2,1)S(1)}, u32[]{:S(2)}, u32[]{:S(2)}) collective-permute-start(bf16[2,128,640]{2,1,0:T(8,128)(2,1)} %copy.100), channel_id=1, source_target_pairs={{0,1},{2,3},{4,5},{6,7},{8,9},{10,11},{12,13},{14,15},{16,17},{18,... | collective-permute-start | bytes 983048 | tf_op jit(solution)/shard_map/ppermute | solution.py:232
  84.9 3.7 %copy-start.14 = (bf16[1,1280,160]{1,2,0:T(8,128)(2,1)S(1)}, bf16[1,1280,160]{1,2,0:T(8,128)(2,1)}, u32[]{:S(2)}) copy-start(bf16[1,1280,160]{1,2,0:T(8,128)(2,1)} %param.13) | copy-start | bytes 1228804
  89.6 16.0 %collective-permute-start.10 = (bf16[2,2,2,80,128]{4,3,2,1,0:T(8,128)(2,1)}, bf16[2,2,2,80,128]{4,3,2,1,0:T(8,128)(2,1)S(1)}, u32[]{:S(2)}, u32[]{:S(2)}) collective-permute-start(bf16[2,2,2,80,128]{4,3,2,1,0:T(8,128)(2,1)} %pad_maximum_fusion.2), channel_id=1, source_target_pairs={{1,13},{3,15},{17,29},{19,31}} | collective-permute-start | bytes 491528 | tf_op jit(solution)/shard_map/ppermute | solution.py:34
  95.6 10.1 %collective-permute-start.11 = (bf16[2,2,2,80,128]{4,3,2,1,0:T(8,128)(2,1)}, bf16[2,2,2,80,128]{4,3,2,1,0:T(8,128)(2,1)}, u32[]{:S(2)}, u32[]{:S(2)}) collective-permute-start(bf16[2,2,2,80,128]{4,3,2,1,0:T(8,128)(2,1)} %pad_maximum_fusion.2), channel_id=1, source_target_pairs={{1,9},{5,13},{3,11},{7,15},{17,25},{21,29},{19,27},{23,31}} | collective-permute-start | bytes 491528 | tf_op jit(solution)/shard_map/ppermute | solution.py:34
  97.6 8.1 %collective-permute-start.12 = (bf16[2,2,2,80,128]{4,3,2,1,0:T(8,128)(2,1)}, bf16[2,2,2,80,128]{4,3,2,1,0:T(8,128)(2,1)}, u32[]{:S(2)}, u32[]{:S(2)}) collective-permute-start(bf16[2,2,2,80,128]{4,3,2,1,0:T(8,128)(2,1)} %pad_maximum_fusion.2), channel_id=1, source_target_pairs={{1,5},{5,9},{9,13},{3,7},{7,11},{11,15},{17,21},{21,25},{25,29},{1... | collective-permute-start | bytes 491528 | tf_op jit(solution)/shard_map/ppermute | solution.py:34
  110.6 8.9 %copy-start.6 = (bf16[1,128,1280]{1,2,0:T(8,128)(2,1)S(1)}, bf16[1,128,1280]{1,2,0:T(8,128)(2,1)}, u32[]{:S(2)}) copy-start(bf16[1,128,1280]{1,2,0:T(8,128)(2,1)} %get-tuple-element.17) | copy-start | bytes 983044
  110.8 8.7 %collective-permute-start.13 = (bf16[2,1,128,640]{2,3,1,0:T(8,128)(2,1)S(1)}, bf16[2,1,128,640]{2,3,1,0:T(8,128)(2,1)S(1)}, u32[]{:S(2)}, u32[]{:S(2)}) collective-permute-start(bf16[2,1,128,640]{2,3,1,0:T(8,128)(2,1)S(1)} %pad_maximum_fusion), channel_id=1, source_target_pairs={{1,0},{3,2},{5,4},{7,6},{9,8},{11,10},{13,12},{15,14},{17,16},{19,... | collective-permute-start | bytes 983048 | tf_op jit(solution)/shard_map/ppermute | solution.py:259
  112.1 4.4 %collective-permute-start.14 = (bf16[1,128,640]{1,2,0:T(8,128)(2,1)S(1)}, bf16[1,128,640]{1,2,0:T(8,128)(2,1)S(1)}, u32[]{:S(2)}, u32[]{:S(2)}) collective-permute-start(bf16[1,128,640]{1,2,0:T(8,128)(2,1)S(1)} %get-tuple-element.22), channel_id=1, source_target_pairs={{1,2},{3,0},{5,6},{7,4},{9,10},{11,8},{13,14},{15,12},{17,18},{19,... | collective-permute-start | bytes 491528 | tf_op jit(solution)/shard_map/ppermute | solution.py:259
  113.4 6.1 %collective-permute-start.15 = (bf16[1,128,640]{1,2,0:T(8,128)(2,1)S(1)}, bf16[1,128,640]{1,2,0:T(8,128)(2,1)S(1)}, u32[]{:S(2)}, u32[]{:S(2)}) collective-permute-start(bf16[1,128,640]{1,2,0:T(8,128)(2,1)S(1)} %constant_dynamic-slice_fusion), channel_id=1, source_target_pairs={{1,3},{3,1},{5,7},{7,5},{9,11},{11,9},{13,15},{15,13},{17,19},{19,... | collective-permute-start | bytes 491528 | tf_op jit(solution)/shard_map/ppermute | solution.py:263
  (7 other events, 12.3 us)

commit v7 on v5

--- a/solution.py
+++ b/solution.py
@@ -164,17 +164,10 @@
     local_dev = (values - local_mean[..., None]) * valid[:, None, :]
     local_m2 = jnp.sum(local_dev * local_dev, -1)
     tail = series[:, :, steps_dev - STRIDE :]
-    if tm_n > SMALL_GROUP:
-        stats = lax.all_gather(jnp.stack([local_sum, local_m2], -1), "tm", axis=0)
-        prior_raw = shift_from(tail, "tm", tm_n, 1, False).astype(jnp.float32)
-    else:
-        payload = jnp.concatenate(
-            [jnp.stack([local_sum, local_m2], -1), tail.astype(jnp.float32)], -1
-        )
-        received = [payload] + [shift_from(payload, "tm", tm_n, by, True) for by in range(1, tm_n)]
-        prior_raw = received[1][..., 2:] if tm_n > 1 else jnp.zeros_like(payload[..., 2:])
-        order = (tm_at - jnp.arange(tm_n, dtype=jnp.int32)) % tm_n
-        stats = jnp.take(jnp.stack([piece[..., :2] for piece in received], 0), order, axis=0)
+    payload = jnp.concatenate([jnp.stack([local_sum, local_m2], -1), tail.astype(jnp.float32)], -1)
+    gathered = lax.all_gather(payload, "tm", axis=0)
+    stats = gathered[..., :2]
+    prior_raw = jnp.take(gathered, (tm_at + tm_n - 1) % tm_n, axis=0)[..., 2:]
     history = lengths.astype(jnp.float32)[:, None]
     shard_sums = stats[..., 0]
     shard_m2 = stats[..., 1]

time: 111 us -> 121 us (1.090)
  blocking collectives: 11.7 us -> 22.9 us
  starting transfers between devices: 27.9 us -> 18.9 us
  waiting for transfers between devices: 14.2 us -> 22.5 us
    all_gather x0 -> x1, blocking collectives: none -> 12.5 us  [per_device(): gathered = lax.all_gather(payload, 'tm', axis=0)]
    ppermute x2, waiting for transfers between devices: 11.1 us -> 20.2 us  [per_device(): arrived = lax.ppermute(attended0, feat_axes, pairs)]
    ppermute x6, starting transfers between devices: 13.1 us -> 7.87 us  [gather_causal(): pieces.append(lax.ppermute(value, ('tm', 'section'), pairs))]
    ppermute x3 -> x0, starting transfers between devices: 4.66 us -> none  [shift_from(): return lax.ppermute(value, axis, pairs)]
    dot_general x1, matrix products: 0.71 us -> 2.14 us  [attend_layer(): jnp.einsum('bte,ed->btd', attended, out_w, preferred_element_type=jnp.flo...]
    reduce_sum x1, other arithmetic: 1.53 us -> 0.3 us  [per_device(): local_sum = jnp.sum(masked, -1)]
    convert_element_type x1, other arithmetic: 1.57 us -> 2.79 us  [per_device(): values = series.astype(jnp.float32)]
    all_gather x1, blocking collectives: 11.7 us -> 10.4 us  [per_device(): hidden0 = lax.all_gather(tokens, feat_axes, axis=2, tiled=True)]
  transfers between devices with their start and end apart: 16 -> 13, of which waited for: 2 -> 2; matrix products, arithmetic and copies ran while one was open for 37% -> 10% of each run, Pallas kernels for 0% -> 0%
where the time goes in v7:
time: 121 us
  blocking collectives  22.9 us (19%)
  waiting for transfers between devices  22.5 us (19%)
  local copies, waits for them, and re-layouts  19.7 us (16%)
  matrix products  19.7 us (16%)
  starting transfers between devices  18.9 us (16%)
  other arithmetic  15.4 us (13%)
  between operations  1.27 us (1%)
    ppermute x2, waiting for transfers between devices, per_device(): arrived = lax.ppermute(attended0, feat_axes, pairs)  20.2 us
    all_gather x1, blocking collectives, per_device(): gathered = lax.all_gather(payload, 'tm', axis=0)  12.5 us
    all_gather x1, blocking collectives, per_device(): hidden0 = lax.all_gather(tokens, feat_axes, axis=2, tiled=True)  10.4 us
    conv_general_dilated x3, local copies, waits for them, and re-layouts, per_device(): lax.conv_general_dilated(normed, kernel, window_strides=(STRIDE,), paddin...  8.47 us
    ppermute x6, starting transfers between devices, gather_causal(): pieces.append(lax.ppermute(value, ('tm', 'section'), pairs))  7.87 us
    conv_general_dilated x1, matrix products, per_device(): lax.conv_general_dilated(normed, kernel, window_strides=(STRIDE,), paddin...  5.69 us
    unnamed x18, local copies, waits for them, and re-layouts  5.46 us
    dot_general x2, matrix products, per_device(): jnp.einsum('bte,ed->btd', arrived, rows, preferred_element_type=jnp.float32)  4.41 us
  transfers between devices with their start and end apart: 13, of which 2 were waited for; matrix products, arithmetic and copies ran while one was open for 10% of the time, Pallas kernels for 0%

profile of v7, /device:TPU:1, one launch (start us, length us, event | category | flops | bytes accessed | tf_op | source)
XLA Modules:
  0.0 120.5 jit_solution(7408829382813735317)
XLA Ops:
  2.8 2.8 %convert_element_type.158 = f32[2,64,4096]{2,1,0:T(8,128)} convert(bf16[2,64,4096]{2,1,0:T(8,128)(2,1)} %param.8) | non-fusion elementwise | flops 524288 | bytes 3145728 | tf_op jit(solution)/shard_map/convert_element_type | solution.py:153
  6.6 12.5 %all-gather = f32[8,64,34]{1,2,0:T(8,128)S(1)} all-gather(f32[2,64,34]{1,2,0:T(8,128)S(1)} %pad_maximum_fusion.3), channel_id=2, replica_groups=mesh['groups'=2,'tm'=4,'mp'=2,'section'=2] {'tm'}, dimensions={0}, use_global_device_ids=true | all-gather | bytes 87040 | tf_op jit(solution)/shard_map/all_gather | solution.py:168
  19.7 2.3 %fusion.80 = bf16[64,2,4128]{2,0,1:T(8,128)(2,1)S(1)} fusion(f32[2,64,4096]{2,1,0:T(8,128)} %convert_element_type.158, f32[2,64,32]{2,1,0:T(8,128)S(1)} %copy.44, f32[2,64]{1,0:T(2,128)S(1)} %add_rsqrt_fusion.2, f32[2,64]{1,0:T(2,128)S(1)} %broadcast_divide_fusion, f32[2,4128]{1,0:T(2,128)S(1)} %and_convert_fusion), kind=kLoop, calls=%fused_computation.71 | loop fusion | flops 3170304 | bytes 3204352 | tf_op jit(solution)/shard_map/convert_element_type | solution.py:189
  23.0 3.3 %reshape.497 = bf16[64,2,8,544]{3,2,0,1:T(8,128)(2,1)S(1)} reshape(bf16[64,2,4352]{2,0,1:T(8,128)(2,1)} %pad.2) | data formatting | bytes 2228224 | tf_op jit(solution)/shard_map/conv_general_dilated | solution.py:191
  26.3 4.1 %copy.46 = bf16[64,2,8,544]{0,2,1,3:T(8,128)(2,1)} copy(bf16[64,2,8,544]{3,2,0,1:T(8,128)(2,1)S(1)} %reshape.497) | data formatting | bytes 2228224 | tf_op jit(solution)/shard_map/conv_general_dilated | solution.py:191
  31.5 4.5 %copy.47 = bf16[4096,320]{1,0:T(8,128)(2,1)} copy(bf16[4096,320]{0,1:T(8,128)(2,1)} %param.10) | data formatting | bytes 5242880 | tf_op args[2]
  36.0 5.7 %fusion.75 = bf16[16,17,320]{2,0,1:T(8,128)(2,1)S(1)} fusion(bf16[64,64,320]{2,1,0:T(8,128)(2,1)} %bitcast.210, bf16[64,2,7,63]{0,2,1,3:T(8,128)(2,1)S(1)} %slice.75, bf16[64,2,8,544]{0,2,1,3:T(8,128)(2,1)} %copy.46, pred[16,17]{0,1:T(8,128)(4,1)S(1)} %copy-done.7), kind=kOutput, calls=%fused_computation.66 | convolution fusion | flops 716935168 | bytes 4022800 | tf_op jit(solution)/shard_map/conv_general_dilated | solution.py:191
  42.2 10.4 %all_gather.11 = bf16[2,128,1280]{1,0,2:T(2,128)(2,1)S(1)} all-gather(bf16[2,128,320]{1,0,2:T(2,128)(2,1)S(1)} %copy.50), channel_id=1, replica_groups=mesh['groups'=2,'tm'=4,'mp'=2,'section'=2] {'mp','section'}, dimensions={2}, use_global_device_ids=true | all-gather | bytes 819200 | tf_op jit(solution)/shard_map/all_gather | solution.py:200
  56.4 1.4 %collective-permute-start.1 = (bf16[2,2,2,80,128]{4,3,2,1,0:T(8,128)(2,1)}, bf16[2,2,2,80,128]{4,3,2,1,0:T(8,128)(2,1)}, u32[]{:S(2)}, u32[]{:S(2)}) collective-permute-start(bf16[2,2,2,80,128]{4,3,2,1,0:T(8,128)(2,1)} %pad_maximum_fusion.1), channel_id=1, source_target_pairs={{0,8},{4,12},{2,10},{6,14},{16,24},{20,28},{18,26},{22,30}} | collective-permute-start | bytes 491528 | tf_op jit(solution)/shard_map/ppermute | solution.py:34
  57.7 1.3 %collective-permute-start.2 = (bf16[2,2,2,80,128]{4,3,2,1,0:T(8,128)(2,1)}, bf16[2,2,2,80,128]{4,3,2,1,0:T(8,128)(2,1)}, u32[]{:S(2)}, u32[]{:S(2)}) collective-permute-start(bf16[2,2,2,80,128]{4,3,2,1,0:T(8,128)(2,1)} %pad_maximum_fusion.1), channel_id=1, source_target_pairs={{0,4},{4,8},{8,12},{2,6},{6,10},{10,14},{16,20},{20,24},{24,28},{1... | collective-permute-start | bytes 491528 | tf_op jit(solution)/shard_map/ppermute | solution.py:34
  60.3 1.5 %collective-permute-start.4 = (bf16[640,1280]{1,0:T(8,128)(2,1)}, bf16[640,1280]{1,0:T(8,128)(2,1)}, u32[]{:S(2)}, u32[]{:S(2)}) collective-permute-start(bf16[640,1280]{1,0:T(8,128)(2,1)} %bitcast.35), channel_id=1, source_target_pairs={{0,1},{2,3},{4,5},{6,7},{8,9},{10,11},{12,13},{14,15},{16,17},{18,... | collective-permute-start | bytes 4915208 | tf_op jit(solution)/shard_map/ppermute | solution.py:146
  69.1 1.3 %collective-permute-start.3 = (bf16[2,128,640]{2,1,0:T(8,128)(2,1)}, bf16[2,128,640]{2,1,0:T(8,128)(2,1)S(1)}, u32[]{:S(2)}, u32[]{:S(2)}) collective-permute-start(bf16[2,128,640]{2,1,0:T(8,128)(2,1)} %copy.54), channel_id=1, source_target_pairs={{0,1},{2,3},{4,5},{6,7},{8,9},{10,11},{12,13},{14,15},{16,17},{18,... | collective-permute-start | bytes 983048 | tf_op jit(solution)/shard_map/ppermute | solution.py:211
  70.4 20.2 %collective-permute-done.5 = bf16[2,128,640]{2,1,0:T(8,128)(2,1)S(1)} collective-permute-done((bf16[2,128,640]{2,1,0:T(8,128)(2,1)}, bf16[2,128,640]{2,1,0:T(8,128)(2,1)S(1)}, u32[]{:S(2)}, u32[]{:S(2)}) %collective-permute-start.5) | collective-permute-done | bytes 327712 | tf_op jit(solution)/shard_map/ppermute | solution.py:211
  90.6 2.1 %fusion.32 = f32[2,128,1280]{2,1,0:T(8,128)S(1)} fusion(bf16[2,128,640]{2,1,0:T(8,128)(2,1)S(1)} %collective-permute-done.5, bf16[640,1280]{1,0:T(8,128)(2,1)} %collective-permute-done.6), kind=kOutput, calls=%fused_computation.41 | convolution fusion | flops 419430400 | bytes 3276800 | tf_op jit(solution)/shard_map/bte,ed->btd/dot_general | solution.py:212
  92.8 2.3 %fusion.39 = (f32[2,128]{1,0:T(2,128)S(1)}, bf16[2,128,1280]{2,1,0:T(8,128)(2,1)S(1)}) fusion(f32[2,128,1280]{2,1,0:T(8,128)S(1)} %fusion.32, bf16[2,128,640]{2,1,0:T(8,128)(2,1)S(1)} %collective-permute-done.3, bf16[640,1280]{1,0:T(8,128)(2,1)} %collective-permute-done.4, bf16[2,128,1280]{2,1,0:T(8,128)(2,1)S(1)} %copy.51), kind=kOutput, calls=%fused_computation.50 | convolution fusion | flops 421723904 | bytes 4588544 | tf_op jit(solution)/shard_map/bte,ed->btd/dot_general | solution.py:212
  97.2 1.3 %collective-permute-start.7 = (bf16[2,2,2,80,128]{4,3,2,1,0:T(8,128)(2,1)}, bf16[2,2,2,80,128]{4,3,2,1,0:T(8,128)(2,1)S(1)}, u32[]{:S(2)}, u32[]{:S(2)}) collective-permute-start(bf16[2,2,2,80,128]{4,3,2,1,0:T(8,128)(2,1)} %pad_maximum_fusion.2), channel_id=1, source_target_pairs={{1,13},{3,15},{17,29},{19,31}} | collective-permute-start | bytes 491528 | tf_op jit(solution)/shard_map/ppermute | solution.py:34
  98.5 1.3 %collective-permute-start.8 = (bf16[2,2,2,80,128]{4,3,2,1,0:T(8,128)(2,1)}, bf16[2,2,2,80,128]{4,3,2,1,0:T(8,128)(2,1)S(1)}, u32[]{:S(2)}, u32[]{:S(2)}) collective-permute-start(bf16[2,2,2,80,128]{4,3,2,1,0:T(8,128)(2,1)} %pad_maximum_fusion.2), channel_id=1, source_target_pairs={{1,9},{5,13},{3,11},{7,15},{17,25},{21,29},{19,27},{23,31}} | collective-permute-start | bytes 491528 | tf_op jit(solution)/shard_map/ppermute | solution.py:34
  99.8 2.0 %collective-permute-start.9 = (bf16[2,2,2,80,128]{4,3,2,1,0:T(8,128)(2,1)}, bf16[2,2,2,80,128]{4,3,2,1,0:T(8,128)(2,1)}, u32[]{:S(2)}, u32[]{:S(2)}) collective-permute-start(bf16[2,2,2,80,128]{4,3,2,1,0:T(8,128)(2,1)} %pad_maximum_fusion.2), channel_id=1, source_target_pairs={{1,5},{5,9},{9,13},{3,7},{7,11},{11,15},{17,21},{21,25},{25,29},{1... | collective-permute-start | bytes 491528 | tf_op jit(solution)/shard_map/ppermute | solution.py:34
  101.8 1.4 %fusion.64 = bf16[2,128,640]{2,1,0:T(8,128)(2,1)} fusion(bf16[1,1280,640]{2,1,0:T(8,128)(2,1)S(1)} %copy-done, bf16[2,128,1280]{2,1,0:T(8,128)(2,1)S(1)} %get-tuple-element.32, f32[2,128]{1,0:T(2,128)S(1)} %add_rsqrt_fusion, f32[1280]{0:T(1024)S(1)} %convert_reduce_fusion), kind=kOutput, calls=%fused_computation.63 | convolution fusion | flops 421068800 | bytes 2627584 | tf_op jit(solution)/shard_map/btd,de->bte/dot_general | solution.py:72
  108.7 2.1 %convolution_convert_fusion = bf16[2,128,1280]{2,1,0:T(8,128)(2,1)S(1)} fusion(bf16[2,128,640]{1,2,0:T(8,128)(2,1)S(1)} %bitcast.225, bf16[1,640,1280]{2,1,0:T(8,128)(2,1)} %param.15), kind=kOutput, calls=%fused_computation.16 | convolution fusion | flops 419758080 | bytes 2621440 | tf_op jit(solution)/shard_map/bte,ed->btd/dot_general | solution.py:128
  111.0 1.3 %collective-permute-start.10 = (bf16[2,1,128,640]{3,2,1,0:T(8,128)(2,1)S(1)}, bf16[2,1,128,640]{3,2,1,0:T(8,128)(2,1)S(1)}, u32[]{:S(2)}, u32[]{:S(2)}) collective-permute-start(bf16[2,1,128,640]{3,2,1,0:T(8,128)(2,1)S(1)} %pad_maximum_fusion), channel_id=1, source_target_pairs={{1,0},{3,2},{5,4},{7,6},{9,8},{11,10},{13,12},{15,14},{17,16},{19,... | collective-permute-start | bytes 983048 | tf_op jit(solution)/shard_map/ppermute | solution.py:238
  112.3 1.3 %collective-permute-start.11 = (bf16[1,128,640]{2,1,0:T(8,128)(2,1)S(1)}, bf16[1,128,640]{2,1,0:T(8,128)(2,1)S(1)}, u32[]{:S(2)}, u32[]{:S(2)}) collective-permute-start(bf16[1,128,640]{2,1,0:T(8,128)(2,1)S(1)} %get-tuple-element.19), channel_id=1, source_target_pairs={{1,2},{3,0},{5,6},{7,4},{9,10},{11,8},{13,14},{15,12},{17,18},{19,... | collective-permute-start | bytes 491528 | tf_op jit(solution)/shard_map/ppermute | solution.py:238
  113.6 3.1 %collective-permute-start.12 = (bf16[1,128,640]{2,1,0:T(8,128)(2,1)S(1)}, bf16[1,128,640]{2,1,0:T(8,128)(2,1)S(1)}, u32[]{:S(2)}, u32[]{:S(2)}) collective-permute-start(bf16[1,128,640]{2,1,0:T(8,128)(2,1)S(1)} %constant_dynamic-slice_fusion), channel_id=1, source_target_pairs={{1,3},{3,1},{5,7},{7,5},{9,11},{11,9},{13,15},{15,13},{17,19},{19,... | collective-permute-start | bytes 491528 | tf_op jit(solution)/shard_map/ppermute | solution.py:242
  117.4 2.3 %collective-permute-done.12 = bf16[1,128,640]{2,1,0:T(8,128)(2,1)S(1)} collective-permute-done((bf16[1,128,640]{2,1,0:T(8,128)(2,1)S(1)}, bf16[1,128,640]{2,1,0:T(8,128)(2,1)S(1)}, u32[]{:S(2)}, u32[]{:S(2)}) %collective-permute-start.12) | collective-permute-done | bytes 163872 | tf_op jit(solution)/shard_map/ppermute | solution.py:242
  (104 shorter events, 27.4 us)
Async XLA Ops:
  0.6 61.2 %copy-start = (bf16[1,1280,640]{2,1,0:T(8,128)(2,1)S(1)}, bf16[1,1280,640]{2,1,0:T(8,128)(2,1)}, u32[]{:S(2)}) copy-start(bf16[1,1280,640]{2,1,0:T(8,128)(2,1)} %param.12) | copy-start | bytes 4915204
  1.6 4.1 %copy-start.1 = (bf16[2,64,4096]{2,1,0:T(8,128)(2,1)S(1)}, bf16[2,64,4096]{2,1,0:T(8,128)(2,1)}, u32[]{:S(2)}) copy-start(bf16[2,64,4096]{2,1,0:T(8,128)(2,1)} %param.8) | copy-start | bytes 3145732
  31.5 4.6 %copy-start.7 = (pred[16,17]{0,1:T(8,128)(4,1)S(1)}, pred[16,17]{0,1:T(8,128)(4,1)}, u32[]{:S(2)}) copy-start(pred[16,17]{0,1:T(8,128)(4,1)} %constant.145) | copy-start | bytes 820
  42.0 11.8 %copy-start.2 = (bf16[1,1280]{1,0:T(2,128)(2,1)S(1)}, bf16[1,1280]{1,0:T(2,128)(2,1)}, u32[]{:S(2)}) copy-start(bf16[1,1280]{1,0:T(2,128)(2,1)} %param.11) | copy-start | bytes 7684
  42.0 11.8 %copy-start.3 = (bf16[1,1280,160]{1,2,0:T(8,128)(2,1)S(1)}, bf16[1,1280,160]{1,2,0:T(8,128)(2,1)}, u32[]{:S(2)}) copy-start(bf16[1,1280,160]{1,2,0:T(8,128)(2,1)} %param.14) | copy-start | bytes 1228804
  53.5 1.0 copy-start.5
  55.7 7.6 %collective-permute-start = (bf16[2,2,2,80,128]{4,3,2,1,0:T(8,128)(2,1)}, bf16[2,2,2,80,128]{4,3,2,1,0:T(8,128)(2,1)S(1)}, u32[]{:S(2)}, u32[]{:S(2)}) collective-permute-start(bf16[2,2,2,80,128]{4,3,2,1,0:T(8,128)(2,1)} %pad_maximum_fusion.1), channel_id=1, source_target_pairs={{0,12},{2,14},{16,28},{18,30}} | collective-permute-start | bytes 491528 | tf_op jit(solution)/shard_map/ppermute | solution.py:34
  56.4 6.9 %collective-permute-start.1 = (bf16[2,2,2,80,128]{4,3,2,1,0:T(8,128)(2,1)}, bf16[2,2,2,80,128]{4,3,2,1,0:T(8,128)(2,1)}, u32[]{:S(2)}, u32[]{:S(2)}) collective-permute-start(bf16[2,2,2,80,128]{4,3,2,1,0:T(8,128)(2,1)} %pad_maximum_fusion.1), channel_id=1, source_target_pairs={{0,8},{4,12},{2,10},{6,14},{16,24},{20,28},{18,26},{22,30}} | collective-permute-start | bytes 491528 | tf_op jit(solution)/shard_map/ppermute | solution.py:34
  57.7 5.6 %collective-permute-start.2 = (bf16[2,2,2,80,128]{4,3,2,1,0:T(8,128)(2,1)}, bf16[2,2,2,80,128]{4,3,2,1,0:T(8,128)(2,1)}, u32[]{:S(2)}, u32[]{:S(2)}) collective-permute-start(bf16[2,2,2,80,128]{4,3,2,1,0:T(8,128)(2,1)} %pad_maximum_fusion.1), channel_id=1, source_target_pairs={{0,4},{4,8},{8,12},{2,6},{6,10},{10,14},{16,20},{20,24},{24,28},{1... | collective-permute-start | bytes 491528 | tf_op jit(solution)/shard_map/ppermute | solution.py:34
  59.0 31.6 %collective-permute-start.6 = (bf16[640,1280]{1,0:T(8,128)(2,1)}, bf16[640,1280]{1,0:T(8,128)(2,1)}, u32[]{:S(2)}, u32[]{:S(2)}) collective-permute-start(bf16[640,1280]{1,0:T(8,128)(2,1)} %bitcast.35), channel_id=1, source_target_pairs={{0,3},{2,1},{4,7},{6,5},{8,11},{10,9},{12,15},{14,13},{16,19},{18,... | collective-permute-start | bytes 4915208 | tf_op jit(solution)/shard_map/ppermute | solution.py:146
  60.3 32.4 %collective-permute-start.4 = (bf16[640,1280]{1,0:T(8,128)(2,1)}, bf16[640,1280]{1,0:T(8,128)(2,1)}, u32[]{:S(2)}, u32[]{:S(2)}) collective-permute-start(bf16[640,1280]{1,0:T(8,128)(2,1)} %bitcast.35), channel_id=1, source_target_pairs={{0,1},{2,3},{4,5},{6,7},{8,9},{10,11},{12,13},{14,15},{16,17},{18,... | collective-permute-start | bytes 4915208 | tf_op jit(solution)/shard_map/ppermute | solution.py:146
  67.8 22.8 %collective-permute-start.5 = (bf16[2,128,640]{2,1,0:T(8,128)(2,1)}, bf16[2,128,640]{2,1,0:T(8,128)(2,1)S(1)}, u32[]{:S(2)}, u32[]{:S(2)}) collective-permute-start(bf16[2,128,640]{2,1,0:T(8,128)(2,1)} %copy.54), channel_id=1, source_target_pairs={{0,3},{2,1},{4,7},{6,5},{8,11},{10,9},{12,15},{14,13},{16,19},{18,... | collective-permute-start | bytes 983048 | tf_op jit(solution)/shard_map/ppermute | solution.py:211
  69.1 23.6 %collective-permute-start.3 = (bf16[2,128,640]{2,1,0:T(8,128)(2,1)}, bf16[2,128,640]{2,1,0:T(8,128)(2,1)S(1)}, u32[]{:S(2)}, u32[]{:S(2)}) collective-permute-start(bf16[2,128,640]{2,1,0:T(8,128)(2,1)} %copy.54), channel_id=1, source_target_pairs={{0,1},{2,3},{4,5},{6,7},{8,9},{10,11},{12,13},{14,15},{16,17},{18,... | collective-permute-start | bytes 983048 | tf_op jit(solution)/shard_map/ppermute | solution.py:211
  92.7 2.4 %copy-start.4 = (bf16[1,1280,160]{1,2,0:T(8,128)(2,1)S(1)}, bf16[1,1280,160]{1,2,0:T(8,128)(2,1)}, u32[]{:S(2)}) copy-start(bf16[1,1280,160]{1,2,0:T(8,128)(2,1)} %param.14) | copy-start | bytes 1228804
  95.1 1.0 copy-start.6
  97.2 7.9 %collective-permute-start.7 = (bf16[2,2,2,80,128]{4,3,2,1,0:T(8,128)(2,1)}, bf16[2,2,2,80,128]{4,3,2,1,0:T(8,128)(2,1)S(1)}, u32[]{:S(2)}, u32[]{:S(2)}) collective-permute-start(bf16[2,2,2,80,128]{4,3,2,1,0:T(8,128)(2,1)} %pad_maximum_fusion.2), channel_id=1, source_target_pairs={{1,13},{3,15},{17,29},{19,31}} | collective-permute-start | bytes 491528 | tf_op jit(solution)/shard_map/ppermute | solution.py:34
  98.5 6.6 %collective-permute-start.8 = (bf16[2,2,2,80,128]{4,3,2,1,0:T(8,128)(2,1)}, bf16[2,2,2,80,128]{4,3,2,1,0:T(8,128)(2,1)S(1)}, u32[]{:S(2)}, u32[]{:S(2)}) collective-permute-start(bf16[2,2,2,80,128]{4,3,2,1,0:T(8,128)(2,1)} %pad_maximum_fusion.2), channel_id=1, source_target_pairs={{1,9},{5,13},{3,11},{7,15},{17,25},{21,29},{19,27},{23,31}} | collective-permute-start | bytes 491528 | tf_op jit(solution)/shard_map/ppermute | solution.py:34
  99.8 5.3 %collective-permute-start.9 = (bf16[2,2,2,80,128]{4,3,2,1,0:T(8,128)(2,1)}, bf16[2,2,2,80,128]{4,3,2,1,0:T(8,128)(2,1)}, u32[]{:S(2)}, u32[]{:S(2)}) collective-permute-start(bf16[2,2,2,80,128]{4,3,2,1,0:T(8,128)(2,1)} %pad_maximum_fusion.2), channel_id=1, source_target_pairs={{1,5},{5,9},{9,13},{3,7},{7,11},{11,15},{17,21},{21,25},{25,29},{1... | collective-permute-start | bytes 491528 | tf_op jit(solution)/shard_map/ppermute | solution.py:34
  111.0 8.7 %collective-permute-start.10 = (bf16[2,1,128,640]{3,2,1,0:T(8,128)(2,1)S(1)}, bf16[2,1,128,640]{3,2,1,0:T(8,128)(2,1)S(1)}, u32[]{:S(2)}, u32[]{:S(2)}) collective-permute-start(bf16[2,1,128,640]{3,2,1,0:T(8,128)(2,1)S(1)} %pad_maximum_fusion), channel_id=1, source_target_pairs={{1,0},{3,2},{5,4},{7,6},{9,8},{11,10},{13,12},{15,14},{17,16},{19,... | collective-permute-start | bytes 983048 | tf_op jit(solution)/shard_map/ppermute | solution.py:238
  112.3 5.1 %collective-permute-start.11 = (bf16[1,128,640]{2,1,0:T(8,128)(2,1)S(1)}, bf16[1,128,640]{2,1,0:T(8,128)(2,1)S(1)}, u32[]{:S(2)}, u32[]{:S(2)}) collective-permute-start(bf16[1,128,640]{2,1,0:T(8,128)(2,1)S(1)} %get-tuple-element.19), channel_id=1, source_target_pairs={{1,2},{3,0},{5,6},{7,4},{9,10},{11,8},{13,14},{15,12},{17,18},{19,... | collective-permute-start | bytes 491528 | tf_op jit(solution)/shard_map/ppermute | solution.py:238
  113.6 6.1 %collective-permute-start.12 = (bf16[1,128,640]{2,1,0:T(8,128)(2,1)S(1)}, bf16[1,128,640]{2,1,0:T(8,128)(2,1)S(1)}, u32[]{:S(2)}, u32[]{:S(2)}) collective-permute-start(bf16[1,128,640]{2,1,0:T(8,128)(2,1)S(1)} %constant_dynamic-slice_fusion), channel_id=1, source_target_pairs={{1,3},{3,1},{5,7},{7,5},{9,11},{11,9},{13,15},{15,13},{17,19},{19,... | collective-permute-start | bytes 491528 | tf_op jit(solution)/shard_map/ppermute | solution.py:242

commit v8 on v5

--- a/solution.py
+++ b/solution.py
@@ -195,14 +195,24 @@
         (padded * padded_valid - channel_mean[..., None]) * padded_valid * inv_std
     ).astype(jnp.bfloat16)
     kernel = patch_weight.reshape(channels, 2 * STRIDE, patch_weight.shape[1])
+    chunk_tok = 16 if tok_count % 16 == 0 else tok_count
+    chunk_count = tok_count // chunk_tok
+    chunks = jnp.stack(
+        [
+            normed[:, :, q * chunk_tok * STRIDE : (q + 1) * chunk_tok * STRIDE + STRIDE]
+            for q in range(chunk_count)
+        ],
+        1,
+    ).reshape(seq_count * chunk_count, channels, chunk_tok * STRIDE + STRIDE)
     tokens = lax.conv_general_dilated(
-        normed,
+        chunks,
         kernel,
         window_strides=(STRIDE,),
         padding="VALID",
         dimension_numbers=("NCW", "IWO", "NWC"),
         preferred_element_type=jnp.float32,
     ).astype(jnp.bfloat16)
+    tokens = tokens.reshape(seq_count, tok_count, tokens.shape[2])
     column_count = patch_weight.shape[1]
     hidden0 = lax.all_gather(tokens, feat_axes, axis=2, tiled=True)
     feature_count = hidden0.shape[2]

time: 111 us -> 106 us (0.955)
  local copies, waits for them, and re-layouts: 20.5 us -> 14.5 us
    conv_general_dilated x3 -> x0, local copies, waits for them, and re-layouts: 8.47 us -> none  [per_device(): lax.conv_general_dilated(normed, kernel, window_strides=(STRIDE,), paddin...]
    another operation x0 -> x2, local copies, waits for them, and re-layouts: none -> 3.56 us  [per_device(): jnp.stack([normed[:, :, q * chunk_tok * STRIDE:(q + 1) * chunk_tok * STRI...]
    convert_element_type x5 -> x1, local copies, waits for them, and re-layouts: 1.45 us -> 0.04 us  [per_device(): tokens = lax.conv_general_dilated(chunks, kernel, window_strides=(STRIDE,...]
    unnamed x18 -> x23, local copies, waits for them, and re-layouts: 5.64 us -> 5.8 us
  transfers between devices with their start and end apart: 16 -> 16, of which waited for: 2 -> 2; matrix products, arithmetic and copies ran while one was open for 37% -> 34% of each run, Pallas kernels for 0% -> 0%
where the time goes in v8:
time: 106 us; the launch traced here: 105 us
  starting transfers between devices  27.9 us (26%)
  matrix products  19.8 us (19%)
  other arithmetic  15.7 us (15%)
  local copies, waits for them, and re-layouts  14.5 us (14%)
  waiting for transfers between devices  14.1 us (13%)
  blocking collectives  11.7 us (11%)
  between operations  1.29 us (1%)
    ppermute x6, starting transfers between devices, gather_causal(): pieces.append(lax.ppermute(value, ('tm', 'section'), pairs))  13.1 us
    all_gather x1, blocking collectives, per_device(): hidden0 = lax.all_gather(tokens, feat_axes, axis=2, tiled=True)  11.7 us
    ppermute x2, waiting for transfers between devices, per_device(): arrived = lax.ppermute(attended0, feat_axes, pairs)  11.1 us
    conv_general_dilated x1, matrix products, per_device(): lax.conv_general_dilated(chunks, kernel, window_strides=(STRIDE,), paddin...  6.23 us
    unnamed x23, local copies, waits for them, and re-layouts  5.8 us
    ppermute x3, starting transfers between devices, shift_from(): return lax.ppermute(value, axis, pairs)  4.66 us
    dot_general x2, matrix products, per_device(): jnp.einsum('bte,ed->btd', arrived, rows, preferred_element_type=jnp.float32)  4.42 us
    another operation x2, local copies, waits for them, and re-layouts, per_device(): jnp.stack([normed[:, :, q * chunk_tok * STRIDE:(q + 1) * chunk_tok * STRI...  3.56 us
  transfers between devices with their start and end apart: 16, of which 2 were waited for; matrix products, arithmetic and copies ran while one was open for 34% of the time, Pallas kernels for 0%

profile of v8, /device:TPU:1, one launch (start us, length us, event | category | flops | bytes accessed | tf_op | source)
XLA Modules:
  0.0 105.0 jit_solution(9428289226070645890)
XLA Ops:
  2.7 1.5 %multiply_reduce_fusion.1 = f32[2,64]{1,0:T(2,128)S(1)} fusion(f32[2,4096]{1,0:T(2,128)S(1)} %compare_convert_fusion, bf16[2,64,4096]{2,1,0:T(8,128)(2,1)} %param.8), kind=kLoop, calls=%fused_computation.30 | loop fusion | flops 1572736 | bytes 1081856 | tf_op jit(solution)/shard_map/reduce_sum | solution.py:155
  4.9 2.2 %collective-permute-start = (f32[2,64,34]{1,0,2:T(2,128)S(1)}, f32[2,64,34]{1,0,2:T(2,128)S(1)}, u32[]{:S(2)}, u32[]{:S(2)}) collective-permute-start(f32[2,64,34]{1,0,2:T(2,128)S(1)} %pad_maximum_fusion.3), channel_id=1, source_target_pairs={{0,4},{4,8},{8,12},{12,0},{1,5},{5,9},{9,13},{13,1},{2,6},{6,10},{... | collective-permute-start | bytes 52232 | tf_op jit(solution)/shard_map/ppermute | solution.py:13
  7.1 2.1 %collective-permute-start.2 = (f32[2,64,34]{1,0,2:T(2,128)S(1)}, f32[2,64,34]{1,0,2:T(2,128)S(1)}, u32[]{:S(2)}, u32[]{:S(2)}) collective-permute-start(f32[2,64,34]{1,0,2:T(2,128)S(1)} %pad_maximum_fusion.3), channel_id=1, source_target_pairs={{0,12},{4,0},{8,4},{12,8},{1,13},{5,1},{9,5},{13,9},{2,14},{6,2},{... | collective-permute-start | bytes 52232 | tf_op jit(solution)/shard_map/ppermute | solution.py:13
  10.9 1.3 %collective-permute-start.7 = (bf16[640,1280]{1,0:T(8,128)(2,1)}, bf16[640,1280]{1,0:T(8,128)(2,1)}, u32[]{:S(2)}, u32[]{:S(2)}) collective-permute-start(bf16[640,1280]{1,0:T(8,128)(2,1)} %bitcast.245), channel_id=1, source_target_pairs={{0,1},{2,3},{4,5},{6,7},{8,9},{10,11},{12,13},{14,15},{16,17},{18,... | collective-permute-start | bytes 4915208 | tf_op jit(solution)/shard_map/ppermute | solution.py:146
  13.0 1.6 %convert_element_type.158 = f32[2,64,4096]{2,1,0:T(8,128)} convert(bf16[2,64,4096]{2,1,0:T(8,128)(2,1)S(1)} %copy-done.1) | non-fusion elementwise | flops 524288 | bytes 3145728 | tf_op jit(solution)/shard_map/convert_element_type | solution.py:153
  14.6 4.5 %copy.41 = bf16[4096,320]{1,0:T(8,128)(2,1)} copy(bf16[4096,320]{0,1:T(8,128)(2,1)} %param.10) | data formatting | bytes 5242880 | tf_op args[2]
  20.2 2.3 %fusion.14 = bf16[2,64,4128]{2,1,0:T(8,128)(2,1)S(1)} fusion(f32[2,64,4096]{2,1,0:T(8,128)} %convert_element_type.158, f32[2,64,32]{2,1,0:T(8,128)S(1)} %copy.38, f32[2,64]{1,0:T(2,128)S(1)} %add_rsqrt_fusion.2, f32[2,64]{1,0:T(2,128)S(1)} %broadcast_divide_fusion, f32[2,4128]{1,0:T(2,128)S(1)} %and_convert_fusion), kind=kLoop, calls=%fused_computation.22 | loop fusion | flops 3170304 | bytes 3204352 | tf_op jit(solution)/shard_map/convert_element_type | solution.py:196
  22.7 3.5 %copy.40 = bf16[2,8,64,544]{2,1,0,3:T(8,128)(2,1)} copy(bf16[2,8,64,544]{3,2,0,1:T(8,128)(2,1)S(1)} %fusion.95) | data formatting | bytes 2228224 | tf_op jit(solution)/shard_map/stack | solution.py:200
  26.3 6.2 %fusion.63 = bf16[16,16,320]{2,0,1:T(8,128)(2,1)S(1)} fusion(bf16[64,64,320]{2,1,0:T(8,128)(2,1)} %bitcast.243, bf16[2,8,64,544]{2,1,0,3:T(8,128)(2,1)} %copy.40), kind=kOutput, calls=%fused_computation.59 | convolution fusion | flops 671170560 | bytes 3899392 | tf_op jit(solution)/shard_map/conv_general_dilated | solution.py:207
  32.7 11.7 %all_gather.3 = bf16[2,128,1280]{1,0,2:T(2,128)(2,1)S(1)} all-gather(bf16[2,128,320]{1,0,2:T(2,128)(2,1)S(1)} %copy.44), channel_id=1, replica_groups=mesh['groups'=2,'tm'=4,'mp'=2,'section'=2] {'mp','section'}, dimensions={2}, use_global_device_ids=true | all-gather | bytes 819200 | tf_op jit(solution)/shard_map/all_gather | solution.py:217
  45.6 1.5 %convolution_convert_fusion.3 = bf16[2,128,160]{1,2,0:T(8,128)(2,1)S(1)} fusion(bf16[1,1280,160]{1,2,0:T(8,128)(2,1)} %param.14, bf16[2,128,1280]{2,1,0:T(8,128)(2,1)S(1)} %copy.45, f32[1280]{0:T(1024)S(1)} %convert_reduce_fusion, f32[2,128]{1,0:T(2,128)S(1)} %add_rsqrt_fusion.1), kind=kOutput, calls=%fused_computation.62 | convolution fusion | flops 106209280 | bytes 1153024 | tf_op jit(solution)/shard_map/btd,de->bet/dot_general | solution.py:78
  48.9 1.3 %collective-permute-start.4 = (bf16[2,2,2,80,128]{4,3,2,1,0:T(8,128)(2,1)}, bf16[2,2,2,80,128]{4,3,2,1,0:T(8,128)(2,1)}, u32[]{:S(2)}, u32[]{:S(2)}) collective-permute-start(bf16[2,2,2,80,128]{4,3,2,1,0:T(8,128)(2,1)} %pad_maximum_fusion.1), channel_id=1, source_target_pairs={{0,8},{4,12},{2,10},{6,14},{16,24},{20,28},{18,26},{22,30}} | collective-permute-start | bytes 491528 | tf_op jit(solution)/shard_map/ppermute | solution.py:34
  50.2 1.3 %collective-permute-start.5 = (bf16[2,2,2,80,128]{4,3,2,1,0:T(8,128)(2,1)}, bf16[2,2,2,80,128]{4,3,2,1,0:T(8,128)(2,1)}, u32[]{:S(2)}, u32[]{:S(2)}) collective-permute-start(bf16[2,2,2,80,128]{4,3,2,1,0:T(8,128)(2,1)} %pad_maximum_fusion.1), channel_id=1, source_target_pairs={{0,4},{4,8},{8,12},{2,6},{6,10},{10,14},{16,20},{20,24},{24,28},{1... | collective-permute-start | bytes 491528 | tf_op jit(solution)/shard_map/ppermute | solution.py:34
  59.6 11.1 %collective-permute-done.8 = bf16[2,128,640]{2,1,0:T(8,128)(2,1)S(1)} collective-permute-done((bf16[2,128,640]{2,1,0:T(8,128)(2,1)}, bf16[2,128,640]{2,1,0:T(8,128)(2,1)S(1)}, u32[]{:S(2)}, u32[]{:S(2)}) %collective-permute-start.8) | collective-permute-done | bytes 327712 | tf_op jit(solution)/shard_map/ppermute | solution.py:228
  70.7 2.1 %fusion.26 = f32[2,128,1280]{2,1,0:T(8,128)S(1)} fusion(bf16[2,128,640]{2,1,0:T(8,128)(2,1)S(1)} %collective-permute-done.8, bf16[640,1280]{1,0:T(8,128)(2,1)} %collective-permute-done.9), kind=kOutput, calls=%fused_computation.36 | convolution fusion | flops 419430400 | bytes 3276800 | tf_op jit(solution)/shard_map/bte,ed->btd/dot_general | solution.py:229
  72.9 2.3 %fusion.33 = (f32[2,128]{1,0:T(2,128)S(1)}, bf16[2,128,1280]{2,1,0:T(8,128)(2,1)S(1)}) fusion(f32[2,128,1280]{2,1,0:T(8,128)S(1)} %fusion.26, bf16[2,128,640]{2,1,0:T(8,128)(2,1)S(1)} %collective-permute-done.6, bf16[640,1280]{1,0:T(8,128)(2,1)} %collective-permute-done.7, bf16[2,128,1280]{2,1,0:T(8,128)(2,1)S(1)} %copy.45), kind=kOutput, calls=%fused_computation.45 | convolution fusion | flops 421723904 | bytes 4588544 | tf_op jit(solution)/shard_map/bte,ed->btd/dot_general | solution.py:229
  77.4 5.0 %collective-permute-start.10 = (bf16[2,2,2,80,128]{4,3,2,1,0:T(8,128)(2,1)}, bf16[2,2,2,80,128]{4,3,2,1,0:T(8,128)(2,1)S(1)}, u32[]{:S(2)}, u32[]{:S(2)}) collective-permute-start(bf16[2,2,2,80,128]{4,3,2,1,0:T(8,128)(2,1)} %pad_maximum_fusion.2), channel_id=1, source_target_pairs={{1,13},{3,15},{17,29},{19,31}} | collective-permute-start | bytes 491528 | tf_op jit(solution)/shard_map/ppermute | solution.py:34
  82.4 2.2 %collective-permute-start.11 = (bf16[2,2,2,80,128]{4,3,2,1,0:T(8,128)(2,1)}, bf16[2,2,2,80,128]{4,3,2,1,0:T(8,128)(2,1)}, u32[]{:S(2)}, u32[]{:S(2)}) collective-permute-start(bf16[2,2,2,80,128]{4,3,2,1,0:T(8,128)(2,1)} %pad_maximum_fusion.2), channel_id=1, source_target_pairs={{1,9},{5,13},{3,11},{7,15},{17,25},{21,29},{19,27},{23,31}} | collective-permute-start | bytes 491528 | tf_op jit(solution)/shard_map/ppermute | solution.py:34
  84.5 2.6 %collective-permute-start.12 = (bf16[2,2,2,80,128]{4,3,2,1,0:T(8,128)(2,1)}, bf16[2,2,2,80,128]{4,3,2,1,0:T(8,128)(2,1)}, u32[]{:S(2)}, u32[]{:S(2)}) collective-permute-start(bf16[2,2,2,80,128]{4,3,2,1,0:T(8,128)(2,1)} %pad_maximum_fusion.2), channel_id=1, source_target_pairs={{1,5},{5,9},{9,13},{3,7},{7,11},{11,15},{17,21},{21,25},{25,29},{1... | collective-permute-start | bytes 491528 | tf_op jit(solution)/shard_map/ppermute | solution.py:34
  87.2 1.4 %fusion.57 = bf16[2,128,640]{2,1,0:T(8,128)(2,1)} fusion(bf16[1,1280,640]{2,1,0:T(8,128)(2,1)S(1)} %copy-done, bf16[2,128,1280]{2,1,0:T(8,128)(2,1)S(1)} %get-tuple-element.21, f32[2,128]{1,0:T(2,128)S(1)} %add_rsqrt_fusion, f32[1280]{0:T(1024)S(1)} %convert_reduce_fusion), kind=kOutput, calls=%fused_computation.57 | convolution fusion | flops 421068800 | bytes 2627584 | tf_op jit(solution)/shard_map/btd,de->bte/dot_general | solution.py:72
  95.5 1.3 %collective-permute-start.13 = (bf16[2,1,128,640]{3,2,1,0:T(8,128)(2,1)S(1)}, bf16[2,1,128,640]{3,2,1,0:T(8,128)(2,1)S(1)}, u32[]{:S(2)}, u32[]{:S(2)}) collective-permute-start(bf16[2,1,128,640]{3,2,1,0:T(8,128)(2,1)S(1)} %pad_maximum_fusion), channel_id=1, source_target_pairs={{1,0},{3,2},{5,4},{7,6},{9,8},{11,10},{13,12},{15,14},{17,16},{19,... | collective-permute-start | bytes 983048 | tf_op jit(solution)/shard_map/ppermute | solution.py:255
  96.8 1.3 %collective-permute-start.14 = (bf16[1,128,640]{2,1,0:T(8,128)(2,1)S(1)}, bf16[1,128,640]{2,1,0:T(8,128)(2,1)S(1)}, u32[]{:S(2)}, u32[]{:S(2)}) collective-permute-start(bf16[1,128,640]{2,1,0:T(8,128)(2,1)S(1)} %get-tuple-element.8), channel_id=1, source_target_pairs={{1,2},{3,0},{5,6},{7,4},{9,10},{11,8},{13,14},{15,12},{17,18},{19,... | collective-permute-start | bytes 491528 | tf_op jit(solution)/shard_map/ppermute | solution.py:255
  98.1 2.4 %collective-permute-start.15 = (bf16[1,128,640]{2,1,0:T(8,128)(2,1)S(1)}, bf16[1,128,640]{2,1,0:T(8,128)(2,1)S(1)}, u32[]{:S(2)}, u32[]{:S(2)}) collective-permute-start(bf16[1,128,640]{2,1,0:T(8,128)(2,1)S(1)} %constant_dynamic-slice_fusion), channel_id=1, source_target_pairs={{1,3},{3,1},{5,7},{7,5},{9,11},{11,9},{13,15},{15,13},{17,19},{19,... | collective-permute-start | bytes 491528 | tf_op jit(solution)/shard_map/ppermute | solution.py:259
  101.2 3.0 %collective-permute-done.15 = bf16[1,128,640]{2,1,0:T(8,128)(2,1)S(1)} collective-permute-done((bf16[1,128,640]{2,1,0:T(8,128)(2,1)S(1)}, bf16[1,128,640]{2,1,0:T(8,128)(2,1)S(1)}, u32[]{:S(2)}, u32[]{:S(2)}) %collective-permute-start.15) | collective-permute-done | bytes 163872 | tf_op jit(solution)/shard_map/ppermute | solution.py:259
  (118 shorter events, 27.9 us)
Async XLA Ops:
  0.6 50.9 %copy-start = (bf16[1,1280,640]{2,1,0:T(8,128)(2,1)S(1)}, bf16[1,1280,640]{2,1,0:T(8,128)(2,1)}, u32[]{:S(2)}) copy-start(bf16[1,1280,640]{2,1,0:T(8,128)(2,1)} %param.12) | copy-start | bytes 4915204
  0.6 3.6 %copy-start.1 = (bf16[2,64,4096]{2,1,0:T(8,128)(2,1)S(1)}, bf16[2,64,4096]{2,1,0:T(8,128)(2,1)}, u32[]{:S(2)}) copy-start(bf16[2,64,4096]{2,1,0:T(8,128)(2,1)} %param.8) | copy-start | bytes 3145732
  0.7 11.7 %copy-start.3 = (bf16[1,1280]{1,0:T(2,128)(2,1)S(1)}, bf16[1,1280]{1,0:T(2,128)(2,1)}, u32[]{:S(2)}) copy-start(bf16[1,1280]{1,0:T(2,128)(2,1)} %param.11) | copy-start | bytes 7684
  4.9 14.2 %collective-permute-start = (f32[2,64,34]{1,0,2:T(2,128)S(1)}, f32[2,64,34]{1,0,2:T(2,128)S(1)}, u32[]{:S(2)}, u32[]{:S(2)}) collective-permute-start(f32[2,64,34]{1,0,2:T(2,128)S(1)} %pad_maximum_fusion.3), channel_id=1, source_target_pairs={{0,4},{4,8},{8,12},{12,0},{1,5},{5,9},{9,13},{13,1},{2,6},{6,10},{... | collective-permute-start | bytes 52232 | tf_op jit(solution)/shard_map/ppermute | solution.py:13
  7.1 12.1 %collective-permute-start.2 = (f32[2,64,34]{1,0,2:T(2,128)S(1)}, f32[2,64,34]{1,0,2:T(2,128)S(1)}, u32[]{:S(2)}, u32[]{:S(2)}) collective-permute-start(f32[2,64,34]{1,0,2:T(2,128)S(1)} %pad_maximum_fusion.3), channel_id=1, source_target_pairs={{0,12},{4,0},{8,4},{12,8},{1,13},{5,1},{9,5},{13,9},{2,14},{6,2},{... | collective-permute-start | bytes 52232 | tf_op jit(solution)/shard_map/ppermute | solution.py:13
  9.2 10.0 %collective-permute-start.1 = (f32[2,64,34]{1,0,2:T(2,128)S(1)}, f32[2,64,34]{1,0,2:T(2,128)S(1)}, u32[]{:S(2)}, u32[]{:S(2)}) collective-permute-start(f32[2,64,34]{1,0,2:T(2,128)S(1)} %pad_maximum_fusion.3), channel_id=1, source_target_pairs={{0,8},{4,12},{8,0},{12,4},{1,9},{5,13},{9,1},{13,5},{2,10},{6,14},... | collective-permute-start | bytes 52232 | tf_op jit(solution)/shard_map/ppermute | solution.py:13
  9.6 61.2 %collective-permute-start.9 = (bf16[640,1280]{1,0:T(8,128)(2,1)}, bf16[640,1280]{1,0:T(8,128)(2,1)}, u32[]{:S(2)}, u32[]{:S(2)}) collective-permute-start(bf16[640,1280]{1,0:T(8,128)(2,1)} %bitcast.244), channel_id=1, source_target_pairs={{0,3},{2,1},{4,7},{6,5},{8,11},{10,9},{12,15},{14,13},{16,19},{18,... | collective-permute-start | bytes 4915208 | tf_op jit(solution)/shard_map/ppermute | solution.py:146
  10.9 62.0 %collective-permute-start.7 = (bf16[640,1280]{1,0:T(8,128)(2,1)}, bf16[640,1280]{1,0:T(8,128)(2,1)}, u32[]{:S(2)}, u32[]{:S(2)}) collective-permute-start(bf16[640,1280]{1,0:T(8,128)(2,1)} %bitcast.245), channel_id=1, source_target_pairs={{0,1},{2,3},{4,5},{6,7},{8,9},{10,11},{12,13},{14,15},{16,17},{18,... | collective-permute-start | bytes 4915208 | tf_op jit(solution)/shard_map/ppermute | solution.py:146
  45.3 1.7 %copy-start.5 = (bf16[1,1280,160]{1,2,0:T(8,128)(2,1)S(1)}, bf16[1,1280,160]{1,2,0:T(8,128)(2,1)}, u32[]{:S(2)}) copy-start(bf16[1,1280,160]{1,2,0:T(8,128)(2,1)} %param.13) | copy-start | bytes 1228804
  48.2 4.3 %collective-permute-start.3 = (bf16[2,2,2,80,128]{4,3,2,1,0:T(8,128)(2,1)}, bf16[2,2,2,80,128]{4,3,2,1,0:T(8,128)(2,1)S(1)}, u32[]{:S(2)}, u32[]{:S(2)}) collective-permute-start(bf16[2,2,2,80,128]{4,3,2,1,0:T(8,128)(2,1)} %pad_maximum_fusion.1), channel_id=1, source_target_pairs={{0,12},{2,14},{16,28},{18,30}} | collective-permute-start | bytes 491528 | tf_op jit(solution)/shard_map/ppermute | solution.py:34
  48.9 3.6 %collective-permute-start.4 = (bf16[2,2,2,80,128]{4,3,2,1,0:T(8,128)(2,1)}, bf16[2,2,2,80,128]{4,3,2,1,0:T(8,128)(2,1)}, u32[]{:S(2)}, u32[]{:S(2)}) collective-permute-start(bf16[2,2,2,80,128]{4,3,2,1,0:T(8,128)(2,1)} %pad_maximum_fusion.1), channel_id=1, source_target_pairs={{0,8},{4,12},{2,10},{6,14},{16,24},{20,28},{18,26},{22,30}} | collective-permute-start | bytes 491528 | tf_op jit(solution)/shard_map/ppermute | solution.py:34
  50.2 2.3 %collective-permute-start.5 = (bf16[2,2,2,80,128]{4,3,2,1,0:T(8,128)(2,1)}, bf16[2,2,2,80,128]{4,3,2,1,0:T(8,128)(2,1)}, u32[]{:S(2)}, u32[]{:S(2)}) collective-permute-start(bf16[2,2,2,80,128]{4,3,2,1,0:T(8,128)(2,1)} %pad_maximum_fusion.1), channel_id=1, source_target_pairs={{0,4},{4,8},{8,12},{2,6},{6,10},{10,14},{16,20},{20,24},{24,28},{1... | collective-permute-start | bytes 491528 | tf_op jit(solution)/shard_map/ppermute | solution.py:34
  57.0 13.7 %collective-permute-start.8 = (bf16[2,128,640]{2,1,0:T(8,128)(2,1)}, bf16[2,128,640]{2,1,0:T(8,128)(2,1)S(1)}, u32[]{:S(2)}, u32[]{:S(2)}) collective-permute-start(bf16[2,128,640]{2,1,0:T(8,128)(2,1)} %copy.48), channel_id=1, source_target_pairs={{0,3},{2,1},{4,7},{6,5},{8,11},{10,9},{12,15},{14,13},{16,19},{18,... | collective-permute-start | bytes 983048 | tf_op jit(solution)/shard_map/ppermute | solution.py:228
  58.3 14.6 %collective-permute-start.6 = (bf16[2,128,640]{2,1,0:T(8,128)(2,1)}, bf16[2,128,640]{2,1,0:T(8,128)(2,1)S(1)}, u32[]{:S(2)}, u32[]{:S(2)}) collective-permute-start(bf16[2,128,640]{2,1,0:T(8,128)(2,1)} %copy.48), channel_id=1, source_target_pairs={{0,1},{2,3},{4,5},{6,7},{8,9},{10,11},{12,13},{14,15},{16,17},{18,... | collective-permute-start | bytes 983048 | tf_op jit(solution)/shard_map/ppermute | solution.py:228
  72.9 2.4 %copy-start.4 = (bf16[1,1280,160]{1,2,0:T(8,128)(2,1)S(1)}, bf16[1,1280,160]{1,2,0:T(8,128)(2,1)}, u32[]{:S(2)}) copy-start(bf16[1,1280,160]{1,2,0:T(8,128)(2,1)} %param.14) | copy-start | bytes 1228804
  75.2 1.0 copy-start.6
  77.4 13.2 %collective-permute-start.10 = (bf16[2,2,2,80,128]{4,3,2,1,0:T(8,128)(2,1)}, bf16[2,2,2,80,128]{4,3,2,1,0:T(8,128)(2,1)S(1)}, u32[]{:S(2)}, u32[]{:S(2)}) collective-permute-start(bf16[2,2,2,80,128]{4,3,2,1,0:T(8,128)(2,1)} %pad_maximum_fusion.2), channel_id=1, source_target_pairs={{1,13},{3,15},{17,29},{19,31}} | collective-permute-start | bytes 491528 | tf_op jit(solution)/shard_map/ppermute | solution.py:34
  82.4 8.2 %collective-permute-start.11 = (bf16[2,2,2,80,128]{4,3,2,1,0:T(8,128)(2,1)}, bf16[2,2,2,80,128]{4,3,2,1,0:T(8,128)(2,1)}, u32[]{:S(2)}, u32[]{:S(2)}) collective-permute-start(bf16[2,2,2,80,128]{4,3,2,1,0:T(8,128)(2,1)} %pad_maximum_fusion.2), channel_id=1, source_target_pairs={{1,9},{5,13},{3,11},{7,15},{17,25},{21,29},{19,27},{23,31}} | collective-permute-start | bytes 491528 | tf_op jit(solution)/shard_map/ppermute | solution.py:34
  84.5 6.0 %collective-permute-start.12 = (bf16[2,2,2,80,128]{4,3,2,1,0:T(8,128)(2,1)}, bf16[2,2,2,80,128]{4,3,2,1,0:T(8,128)(2,1)}, u32[]{:S(2)}, u32[]{:S(2)}) collective-permute-start(bf16[2,2,2,80,128]{4,3,2,1,0:T(8,128)(2,1)} %pad_maximum_fusion.2), channel_id=1, source_target_pairs={{1,5},{5,9},{9,13},{3,7},{7,11},{11,15},{17,21},{21,25},{25,29},{1... | collective-permute-start | bytes 491528 | tf_op jit(solution)/shard_map/ppermute | solution.py:34
  93.2 1.4 %copy-start.2 = (bf16[1,640,1280]{2,1,0:T(8,128)(2,1)S(1)}, bf16[1,640,1280]{2,1,0:T(8,128)(2,1)}, u32[]{:S(2)}) copy-start(bf16[1,640,1280]{2,1,0:T(8,128)(2,1)} %param.15) | copy-start | bytes 4915204
  95.5 8.7 %collective-permute-start.13 = (bf16[2,1,128,640]{3,2,1,0:T(8,128)(2,1)S(1)}, bf16[2,1,128,640]{3,2,1,0:T(8,128)(2,1)S(1)}, u32[]{:S(2)}, u32[]{:S(2)}) collective-permute-start(bf16[2,1,128,640]{3,2,1,0:T(8,128)(2,1)S(1)} %pad_maximum_fusion), channel_id=1, source_target_pairs={{1,0},{3,2},{5,4},{7,6},{9,8},{11,10},{13,12},{15,14},{17,16},{19,... | collective-permute-start | bytes 983048 | tf_op jit(solution)/shard_map/ppermute | solution.py:255
  96.8 4.4 %collective-permute-start.14 = (bf16[1,128,640]{2,1,0:T(8,128)(2,1)S(1)}, bf16[1,128,640]{2,1,0:T(8,128)(2,1)S(1)}, u32[]{:S(2)}, u32[]{:S(2)}) collective-permute-start(bf16[1,128,640]{2,1,0:T(8,128)(2,1)S(1)} %get-tuple-element.8), channel_id=1, source_target_pairs={{1,2},{3,0},{5,6},{7,4},{9,10},{11,8},{13,14},{15,12},{17,18},{19,... | collective-permute-start | bytes 491528 | tf_op jit(solution)/shard_map/ppermute | solution.py:255
  98.1 6.1 %collective-permute-start.15 = (bf16[1,128,640]{2,1,0:T(8,128)(2,1)S(1)}, bf16[1,128,640]{2,1,0:T(8,128)(2,1)S(1)}, u32[]{:S(2)}, u32[]{:S(2)}) collective-permute-start(bf16[1,128,640]{2,1,0:T(8,128)(2,1)S(1)} %constant_dynamic-slice_fusion), channel_id=1, source_target_pairs={{1,3},{3,1},{5,7},{7,5},{9,11},{11,9},{13,15},{15,13},{17,19},{19,... | collective-permute-start | bytes 491528 | tf_op jit(solution)/shard_map/ppermute | solution.py:259

commit v9 on v8

--- a/solution.py
+++ b/solution.py
@@ -140,10 +140,6 @@
     sec_at = lax.axis_index("section")
     feat_axes = ("mp", "section")
     feat_n = mp_n * sec_n
-    to_second = [
-        [(m * sec_n, ((m + by) % mp_n) * sec_n + 1) for m in range(mp_n)] for by in range(mp_n)
-    ]
-    moved_rows = [lax.ppermute(out_weight[0], feat_axes, pairs) for pairs in to_second]
     total_steps = steps_dev * tm_n
     total_tokens = tok_count * tm_n
 
@@ -219,14 +215,14 @@
     head_cols = feature_count // mp_n
     sizes = (tm_n, sec_n, tm_at, total_tokens)
 
-    attended0, key0, value0 = attend_layer(
+    partial0, key0, value0 = attend_layer(
         hidden0, lengths, norm_gain[0], query_weight[0], key_weight[0], value_weight[0],
-        None, sizes, 0,
+        out_weight[0], sizes, 0,
     )
     head_sum = None
-    for pairs, rows in zip(to_second, moved_rows):
-        arrived = lax.ppermute(attended0, feat_axes, pairs)
-        term = jnp.einsum("bte,ed->btd", arrived, rows, preferred_element_type=jnp.float32)
+    for by in range(mp_n):
+        pairs = [(m * sec_n, ((m + by) % mp_n) * sec_n + 1) for m in range(mp_n)]
+        term = lax.ppermute(partial0, feat_axes, pairs).astype(jnp.float32)
         head_sum = term if head_sum is None else head_sum + term
     hidden1 = (hidden0.astype(jnp.float32) + head_sum).astype(jnp.bfloat16)
 

time: 106 us -> 104 us (0.981)
  waiting for transfers between devices: 14.1 us -> 17.6 us
  matrix products: 19.8 us -> 17 us
  blocking collectives: 11.7 us -> 9.24 us
  other arithmetic: 15.7 us -> 17.4 us
  local copies, waits for them, and re-layouts: 14.5 us -> 13.1 us
    dot_general x2 -> x0, matrix products: 4.42 us -> none  [per_device(): jnp.einsum('bte,ed->btd', arrived, rows, preferred_element_type=jnp.float32)]
    ppermute x4 -> x2, waiting for transfers between devices: 11.1 us -> 15.5 us  [per_device(): term = lax.ppermute(partial0, feat_axes, pairs).astype(jnp.float32)]
    ppermute x4 -> x2, starting transfers between devices: 5.14 us -> 2.57 us  [per_device(): term = lax.ppermute(partial0, feat_axes, pairs).astype(jnp.float32)]
    all_gather x1, blocking collectives: 11.7 us -> 9.24 us  [per_device(): hidden0 = lax.all_gather(tokens, feat_axes, axis=2, tiled=True)]
    ppermute x1, waiting for transfers between devices: 2.98 us -> 0.98 us  [per_device(): to_high.append(lax.ppermute(cols_high, feat_axes, pairs))]
    reduce_sum x1 -> x2, other arithmetic: 0.21 us -> 1.89 us  [attend_layer(): jnp.mean(hidden32 * hidden32, -1, keepdims=True) + 1e-06]
    dot_general x1 -> x2, matrix products: 0.7 us -> 2.25 us  [attend_layer(): jnp.einsum('bte,ed->btd', attended, out_w, preferred_element_type=jnp.flo...]
    unnamed x23 -> x25, local copies, waits for them, and re-layouts: 5.8 us -> 5.35 us
  transfers between devices with their start and end apart: 16 -> 14, of which waited for: 2 -> 3; matrix products, arithmetic and copies ran while one was open for 34% -> 12% of each run, Pallas kernels for 0% -> 0%
where the time goes in v9:
time: 104 us; the launch traced here: 102 us
  starting transfers between devices  26.9 us (26%)
  waiting for transfers between devices  17.6 us (17%)
  other arithmetic  17.4 us (17%)
  matrix products  17 us (16%)
  local copies, waits for them, and re-layouts  13.1 us (13%)
  blocking collectives  9.24 us (9%)
  between operations  1.25 us (1%)
    ppermute x2, waiting for transfers between devices, per_device(): term = lax.ppermute(partial0, feat_axes, pairs).astype(jnp.float32)  15.5 us
    ppermute x6, starting transfers between devices, gather_causal(): pieces.append(lax.ppermute(value, ('tm', 'section'), pairs))  14 us
    all_gather x1, blocking collectives, per_device(): hidden0 = lax.all_gather(tokens, feat_axes, axis=2, tiled=True)  9.24 us
    conv_general_dilated x1, matrix products, per_device(): lax.conv_general_dilated(chunks, kernel, window_strides=(STRIDE,), paddin...  6.23 us
    unnamed x25, local copies, waits for them, and re-layouts  5.35 us
    ppermute x3, starting transfers between devices, shift_from(): return lax.ppermute(value, axis, pairs)  4.66 us
    another operation x2, local copies, waits for them, and re-layouts, per_device(): jnp.stack([normed[:, :, q * chunk_tok * STRIDE:(q + 1) * chunk_tok * STRI...  3.55 us
    ppermute x1, starting transfers between devices, per_device(): to_high.append(lax.ppermute(cols_high, feat_axes, pairs))  3.12 us
  transfers between devices with their start and end apart: 14, of which 3 were waited for; matrix products, arithmetic and copies ran while one was open for 12% of the time, Pallas kernels for 0%

profile of v9, /device:TPU:1, one launch (start us, length us, event | category | flops | bytes accessed | tf_op | source)
XLA Modules:
  0.0 102.5 jit_solution(13647355518313941249)
XLA Ops:
  2.7 1.5 %multiply_reduce_fusion.1 = f32[2,64]{1,0:T(2,128)S(1)} fusion(f32[2,4096]{1,0:T(2,128)S(1)} %compare_convert_fusion, bf16[2,64,4096]{2,1,0:T(8,128)(2,1)} %param.8), kind=kLoop, calls=%fused_computation.28 | loop fusion | flops 1572736 | bytes 1081856 | tf_op jit(solution)/shard_map/reduce_sum | solution.py:151
  4.9 4.2 %collective-permute-start.2 = (f32[2,64,34]{1,0,2:T(2,128)S(1)}, f32[2,64,34]{1,0,2:T(2,128)S(1)}, u32[]{:S(2)}, u32[]{:S(2)}) collective-permute-start(f32[2,64,34]{1,0,2:T(2,128)S(1)} %pad_maximum_fusion.3), channel_id=1, source_target_pairs={{0,12},{4,0},{8,4},{12,8},{1,13},{5,1},{9,5},{13,9},{2,14},{6,2},{... | collective-permute-start | bytes 52232 | tf_op jit(solution)/shard_map/ppermute | solution.py:13
  10.4 1.6 %convert_element_type.167 = f32[2,64,4096]{2,1,0:T(8,128)} convert(bf16[2,64,4096]{2,1,0:T(8,128)(2,1)S(1)} %copy-done.1) | non-fusion elementwise | flops 524288 | bytes 3145728 | tf_op jit(solution)/shard_map/convert_element_type | solution.py:149
  12.0 4.5 %copy.39 = bf16[4096,320]{1,0:T(8,128)(2,1)} copy(bf16[4096,320]{0,1:T(8,128)(2,1)} %param.10) | data formatting | bytes 5242880 | tf_op args[2]
  17.6 2.3 %fusion.12 = bf16[2,64,4128]{2,1,0:T(8,128)(2,1)S(1)} fusion(f32[2,64,4096]{2,1,0:T(8,128)} %convert_element_type.167, f32[2,64,32]{2,1,0:T(8,128)S(1)} %copy.36, f32[2,64]{1,0:T(2,128)S(1)} %add_rsqrt_fusion.2, f32[2,64]{1,0:T(2,128)S(1)} %broadcast_divide_fusion, f32[2,4128]{1,0:T(2,128)S(1)} %and_convert_fusion), kind=kLoop, calls=%fused_computation.20 | loop fusion | flops 3170304 | bytes 3204352 | tf_op jit(solution)/shard_map/convert_element_type | solution.py:192
  20.2 3.5 %copy.38 = bf16[2,8,64,544]{2,1,0,3:T(8,128)(2,1)} copy(bf16[2,8,64,544]{3,2,0,1:T(8,128)(2,1)S(1)} %fusion.92) | data formatting | bytes 2228224 | tf_op jit(solution)/shard_map/stack | solution.py:196
  23.7 6.2 %fusion.60 = bf16[16,16,320]{2,0,1:T(8,128)(2,1)S(1)} fusion(bf16[64,64,320]{2,1,0:T(8,128)(2,1)} %bitcast.236, bf16[2,8,64,544]{2,1,0,3:T(8,128)(2,1)} %copy.38), kind=kOutput, calls=%fused_computation.57 | convolution fusion | flops 671170560 | bytes 3899392 | tf_op jit(solution)/shard_map/conv_general_dilated | solution.py:203
  30.1 9.2 %all_gather.3 = bf16[2,128,1280]{1,0,2:T(2,128)(2,1)S(1)} all-gather(bf16[2,128,320]{1,0,2:T(2,128)(2,1)S(1)} %copy.42), channel_id=1, replica_groups=mesh['groups'=2,'tm'=4,'mp'=2,'section'=2] {'mp','section'}, dimensions={2}, use_global_device_ids=true | all-gather | bytes 819200 | tf_op jit(solution)/shard_map/all_gather | solution.py:213
  40.5 1.5 %convolution_convert_fusion.4 = bf16[2,128,160]{1,2,0:T(8,128)(2,1)S(1)} fusion(bf16[1,1280,160]{1,2,0:T(8,128)(2,1)} %param.14, bf16[2,128,1280]{2,1,0:T(8,128)(2,1)S(1)} %copy.43, f32[1280]{0:T(1024)S(1)} %convert_reduce_fusion, f32[2,128]{1,0:T(2,128)S(1)} %add_rsqrt_fusion.1), kind=kOutput, calls=%fused_computation.60 | convolution fusion | flops 106209280 | bytes 1153024 | tf_op jit(solution)/shard_map/btd,de->bet/dot_general | solution.py:78
  43.8 1.3 %collective-permute-start.4 = (bf16[2,2,2,80,128]{4,3,2,1,0:T(8,128)(2,1)}, bf16[2,2,2,80,128]{4,3,2,1,0:T(8,128)(2,1)}, u32[]{:S(2)}, u32[]{:S(2)}) collective-permute-start(bf16[2,2,2,80,128]{4,3,2,1,0:T(8,128)(2,1)} %pad_maximum_fusion.1), channel_id=1, source_target_pairs={{0,8},{4,12},{2,10},{6,14},{16,24},{20,28},{18,26},{22,30}} | collective-permute-start | bytes 491528 | tf_op jit(solution)/shard_map/ppermute | solution.py:34
  45.2 1.3 %collective-permute-start.3 = (bf16[2,2,2,80,128]{4,3,2,1,0:T(8,128)(2,1)}, bf16[2,2,2,80,128]{4,3,2,1,0:T(8,128)(2,1)}, u32[]{:S(2)}, u32[]{:S(2)}) collective-permute-start(bf16[2,2,2,80,128]{4,3,2,1,0:T(8,128)(2,1)} %pad_maximum_fusion.1), channel_id=1, source_target_pairs={{0,12},{2,14},{16,28},{18,30}} | collective-permute-start | bytes 491528 | tf_op jit(solution)/shard_map/ppermute | solution.py:34
  51.1 1.5 %convolution_convert_fusion.1 = bf16[2,128,1280]{2,1,0:T(8,128)(2,1)} fusion(bf16[2,128,640]{1,2,0:T(8,128)(2,1)S(1)} %bitcast.253, bf16[1,640,1280]{2,1,0:T(8,128)(2,1)S(1)} %copy-done), kind=kOutput, calls=%fused_computation.14 | convolution fusion | flops 419758080 | bytes 2621440 | tf_op jit(solution)/shard_map/bte,ed->btd/dot_general | solution.py:128
  52.6 1.3 %collective-permute-start.7 = (bf16[2,128,1280]{2,1,0:T(8,128)(2,1)}, bf16[2,128,1280]{2,1,0:T(8,128)(2,1)}, u32[]{:S(2)}, u32[]{:S(2)}) collective-permute-start(bf16[2,128,1280]{2,1,0:T(8,128)(2,1)} %convolution_convert_fusion.1), channel_id=1, source_target_pairs={{0,3},{2,1},{4,7},{6,5},{8,11},{10,9},{12,15},{14,13},{16,19},{18,... | collective-permute-start | bytes 1966088 | tf_op jit(solution)/shard_map/ppermute | solution.py:225
  53.9 1.3 %collective-permute-start.6 = (bf16[2,128,1280]{2,1,0:T(8,128)(2,1)}, bf16[2,128,1280]{2,1,0:T(8,128)(2,1)}, u32[]{:S(2)}, u32[]{:S(2)}) collective-permute-start(bf16[2,128,1280]{2,1,0:T(8,128)(2,1)} %convolution_convert_fusion.1), channel_id=1, source_target_pairs={{0,1},{2,3},{4,5},{6,7},{8,9},{10,11},{12,13},{14,15},{16,17},{18,... | collective-permute-start | bytes 1966088 | tf_op jit(solution)/shard_map/ppermute | solution.py:225
  55.2 15.5 %collective-permute-done.7 = bf16[2,128,1280]{2,1,0:T(8,128)(2,1)} collective-permute-done((bf16[2,128,1280]{2,1,0:T(8,128)(2,1)}, bf16[2,128,1280]{2,1,0:T(8,128)(2,1)}, u32[]{:S(2)}, u32[]{:S(2)}) %collective-permute-start.7) | collective-permute-done | bytes 655392 | tf_op jit(solution)/shard_map/ppermute | solution.py:225
  70.8 1.7 %fusion.29 = (f32[2,128]{1,0:T(2,128)S(1)}, bf16[2,128,1280]{2,1,0:T(8,128)(2,1)S(1)}) fusion(bf16[2,128,1280]{2,1,0:T(8,128)(2,1)} %collective-permute-done.7, bf16[2,128,1280]{2,1,0:T(8,128)(2,1)} %collective-permute-done.6, bf16[2,128,1280]{2,1,0:T(8,128)(2,1)S(1)} %copy.43), kind=kLoop, calls=%fused_computation.42 | loop fusion | flops 2948864 | bytes 2622464 | tf_op jit(solution)/shard_map/reduce_sum | solution.py:69
  74.6 1.3 %collective-permute-start.10 = (bf16[2,2,2,80,128]{4,3,2,1,0:T(8,128)(2,1)}, bf16[2,2,2,80,128]{4,3,2,1,0:T(8,128)(2,1)S(1)}, u32[]{:S(2)}, u32[]{:S(2)}) collective-permute-start(bf16[2,2,2,80,128]{4,3,2,1,0:T(8,128)(2,1)} %pad_maximum_fusion.2), channel_id=1, source_target_pairs={{1,5},{5,9},{9,13},{3,7},{7,11},{11,15},{17,21},{21,25},{25,29},{1... | collective-permute-start | bytes 491528 | tf_op jit(solution)/shard_map/ppermute | solution.py:34
  75.9 7.5 %collective-permute-start.9 = (bf16[2,2,2,80,128]{4,3,2,1,0:T(8,128)(2,1)}, bf16[2,2,2,80,128]{4,3,2,1,0:T(8,128)(2,1)}, u32[]{:S(2)}, u32[]{:S(2)}) collective-permute-start(bf16[2,2,2,80,128]{4,3,2,1,0:T(8,128)(2,1)} %pad_maximum_fusion.2), channel_id=1, source_target_pairs={{1,9},{5,13},{3,11},{7,15},{17,25},{21,29},{19,27},{23,31}} | collective-permute-start | bytes 491528 | tf_op jit(solution)/shard_map/ppermute | solution.py:34
  83.3 1.9 %collective-permute-start.8 = (bf16[2,2,2,80,128]{4,3,2,1,0:T(8,128)(2,1)}, bf16[2,2,2,80,128]{4,3,2,1,0:T(8,128)(2,1)}, u32[]{:S(2)}, u32[]{:S(2)}) collective-permute-start(bf16[2,2,2,80,128]{4,3,2,1,0:T(8,128)(2,1)} %pad_maximum_fusion.2), channel_id=1, source_target_pairs={{1,13},{3,15},{17,29},{19,31}} | collective-permute-start | bytes 491528 | tf_op jit(solution)/shard_map/ppermute | solution.py:34
  85.3 1.4 %fusion.54 = bf16[2,128,640]{2,1,0:T(8,128)(2,1)} fusion(bf16[1,1280,640]{2,1,0:T(8,128)(2,1)S(1)} %copy-done.4, bf16[2,128,1280]{2,1,0:T(8,128)(2,1)S(1)} %get-tuple-element.4, f32[2,128]{1,0:T(2,128)S(1)} %add_rsqrt_fusion, f32[1280]{0:T(1024)S(1)} %convert_reduce_fusion), kind=kOutput, calls=%fused_computation.55 | convolution fusion | flops 421068800 | bytes 2627584 | tf_op jit(solution)/shard_map/btd,de->bte/dot_general | solution.py:72
  87.4 1.2 %copy.47 = bf16[2,128,640]{1,2,0:T(8,128)(2,1)S(1)} copy(bf16[2,128,640]{2,1,0:T(8,128)(2,1)} %fusion.54) | data formatting | bytes 655360 | tf_op jit(solution)/shard_map/convert_element_type | solution.py:74
  93.2 1.3 %collective-permute-start.11 = (bf16[2,1,128,640]{3,2,1,0:T(8,128)(2,1)S(1)}, bf16[2,1,128,640]{3,2,1,0:T(8,128)(2,1)S(1)}, u32[]{:S(2)}, u32[]{:S(2)}) collective-permute-start(bf16[2,1,128,640]{3,2,1,0:T(8,128)(2,1)S(1)} %pad_maximum_fusion), channel_id=1, source_target_pairs={{1,0},{3,2},{5,4},{7,6},{9,8},{11,10},{13,12},{15,14},{17,16},{19,... | collective-permute-start | bytes 983048 | tf_op jit(solution)/shard_map/ppermute | solution.py:251
  94.5 3.1 %collective-permute-start.13 = (bf16[1,128,640]{2,1,0:T(8,128)(2,1)S(1)}, bf16[1,128,640]{2,1,0:T(8,128)(2,1)S(1)}, u32[]{:S(2)}, u32[]{:S(2)}) collective-permute-start(bf16[1,128,640]{2,1,0:T(8,128)(2,1)S(1)} %constant_dynamic-slice_fusion), channel_id=1, source_target_pairs={{1,3},{3,1},{5,7},{7,5},{9,11},{11,9},{13,15},{15,13},{17,19},{19,... | collective-permute-start | bytes 491528 | tf_op jit(solution)/shard_map/ppermute | solution.py:255
  97.7 1.3 %collective-permute-start.12 = (bf16[1,128,640]{2,1,0:T(8,128)(2,1)S(1)}, bf16[1,128,640]{2,1,0:T(8,128)(2,1)S(1)}, u32[]{:S(2)}, u32[]{:S(2)}) collective-permute-start(bf16[1,128,640]{2,1,0:T(8,128)(2,1)S(1)} %get-tuple-element.10), channel_id=1, source_target_pairs={{1,2},{3,0},{5,6},{7,4},{9,10},{11,8},{13,14},{15,12},{17,18},{19,... | collective-permute-start | bytes 491528 | tf_op jit(solution)/shard_map/ppermute | solution.py:251
  (115 shorter events, 23.6 us)
Async XLA Ops:
  0.6 50.4 %copy-start = (bf16[1,640,1280]{2,1,0:T(8,128)(2,1)S(1)}, bf16[1,640,1280]{2,1,0:T(8,128)(2,1)}, u32[]{:S(2)}) copy-start(bf16[1,640,1280]{2,1,0:T(8,128)(2,1)} %param.15) | copy-start | bytes 4915204
  0.6 3.6 %copy-start.1 = (bf16[2,64,4096]{2,1,0:T(8,128)(2,1)S(1)}, bf16[2,64,4096]{2,1,0:T(8,128)(2,1)}, u32[]{:S(2)}) copy-start(bf16[2,64,4096]{2,1,0:T(8,128)(2,1)} %param.8) | copy-start | bytes 3145732
  1.8 8.3 %copy-start.2 = (bf16[1,1280]{1,0:T(2,128)(2,1)S(1)}, bf16[1,1280]{1,0:T(2,128)(2,1)}, u32[]{:S(2)}) copy-start(bf16[1,1280]{1,0:T(2,128)(2,1)} %param.11) | copy-start | bytes 7684
  4.9 11.6 %collective-permute-start.2 = (f32[2,64,34]{1,0,2:T(2,128)S(1)}, f32[2,64,34]{1,0,2:T(2,128)S(1)}, u32[]{:S(2)}, u32[]{:S(2)}) collective-permute-start(f32[2,64,34]{1,0,2:T(2,128)S(1)} %pad_maximum_fusion.3), channel_id=1, source_target_pairs={{0,12},{4,0},{8,4},{12,8},{1,13},{5,1},{9,5},{13,9},{2,14},{6,2},{... | collective-permute-start | bytes 52232 | tf_op jit(solution)/shard_map/ppermute | solution.py:13
  9.1 7.4 %collective-permute-start.1 = (f32[2,64,34]{1,0,2:T(2,128)S(1)}, f32[2,64,34]{1,0,2:T(2,128)S(1)}, u32[]{:S(2)}, u32[]{:S(2)}) collective-permute-start(f32[2,64,34]{1,0,2:T(2,128)S(1)} %pad_maximum_fusion.3), channel_id=1, source_target_pairs={{0,8},{4,12},{8,0},{12,4},{1,9},{5,13},{9,1},{13,5},{2,10},{6,14},... | collective-permute-start | bytes 52232 | tf_op jit(solution)/shard_map/ppermute | solution.py:13
  9.1 7.5 %collective-permute-start = (f32[2,64,34]{1,0,2:T(2,128)S(1)}, f32[2,64,34]{1,0,2:T(2,128)S(1)}, u32[]{:S(2)}, u32[]{:S(2)}) collective-permute-start(f32[2,64,34]{1,0,2:T(2,128)S(1)} %pad_maximum_fusion.3), channel_id=1, source_target_pairs={{0,4},{4,8},{8,12},{12,0},{1,5},{5,9},{9,13},{13,1},{2,6},{6,10},{... | collective-permute-start | bytes 52232 | tf_op jit(solution)/shard_map/ppermute | solution.py:13
  40.3 1.7 %copy-start.6 = (bf16[1,1280,160]{1,2,0:T(8,128)(2,1)S(1)}, bf16[1,1280,160]{1,2,0:T(8,128)(2,1)}, u32[]{:S(2)}) copy-start(bf16[1,1280,160]{1,2,0:T(8,128)(2,1)} %param.13) | copy-start | bytes 1228804
  42.0 4.5 %copy-start.3 = (bf16[1,1280,640]{2,1,0:T(8,128)(2,1)S(1)}, bf16[1,1280,640]{2,1,0:T(8,128)(2,1)}, u32[]{:S(2)}) copy-start(bf16[1,1280,640]{2,1,0:T(8,128)(2,1)} %param.12) | copy-start | bytes 4915204
  43.2 4.3 %collective-permute-start.5 = (bf16[2,2,2,80,128]{4,3,2,1,0:T(8,128)(2,1)}, bf16[2,2,2,80,128]{4,3,2,1,0:T(8,128)(2,1)S(1)}, u32[]{:S(2)}, u32[]{:S(2)}) collective-permute-start(bf16[2,2,2,80,128]{4,3,2,1,0:T(8,128)(2,1)} %pad_maximum_fusion.1), channel_id=1, source_target_pairs={{0,4},{4,8},{8,12},{2,6},{6,10},{10,14},{16,20},{20,24},{24,28},{1... | collective-permute-start | bytes 491528 | tf_op jit(solution)/shard_map/ppermute | solution.py:34
  43.8 3.6 %collective-permute-start.4 = (bf16[2,2,2,80,128]{4,3,2,1,0:T(8,128)(2,1)}, bf16[2,2,2,80,128]{4,3,2,1,0:T(8,128)(2,1)}, u32[]{:S(2)}, u32[]{:S(2)}) collective-permute-start(bf16[2,2,2,80,128]{4,3,2,1,0:T(8,128)(2,1)} %pad_maximum_fusion.1), channel_id=1, source_target_pairs={{0,8},{4,12},{2,10},{6,14},{16,24},{20,28},{18,26},{22,30}} | collective-permute-start | bytes 491528 | tf_op jit(solution)/shard_map/ppermute | solution.py:34
  45.2 2.3 %collective-permute-start.3 = (bf16[2,2,2,80,128]{4,3,2,1,0:T(8,128)(2,1)}, bf16[2,2,2,80,128]{4,3,2,1,0:T(8,128)(2,1)}, u32[]{:S(2)}, u32[]{:S(2)}) collective-permute-start(bf16[2,2,2,80,128]{4,3,2,1,0:T(8,128)(2,1)} %pad_maximum_fusion.1), channel_id=1, source_target_pairs={{0,12},{2,14},{16,28},{18,30}} | collective-permute-start | bytes 491528 | tf_op jit(solution)/shard_map/ppermute | solution.py:34
  52.6 18.1 %collective-permute-start.7 = (bf16[2,128,1280]{2,1,0:T(8,128)(2,1)}, bf16[2,128,1280]{2,1,0:T(8,128)(2,1)}, u32[]{:S(2)}, u32[]{:S(2)}) collective-permute-start(bf16[2,128,1280]{2,1,0:T(8,128)(2,1)} %convolution_convert_fusion.1), channel_id=1, source_target_pairs={{0,3},{2,1},{4,7},{6,5},{8,11},{10,9},{12,15},{14,13},{16,19},{18,... | collective-permute-start | bytes 1966088 | tf_op jit(solution)/shard_map/ppermute | solution.py:225
  53.9 16.9 %collective-permute-start.6 = (bf16[2,128,1280]{2,1,0:T(8,128)(2,1)}, bf16[2,128,1280]{2,1,0:T(8,128)(2,1)}, u32[]{:S(2)}, u32[]{:S(2)}) collective-permute-start(bf16[2,128,1280]{2,1,0:T(8,128)(2,1)} %convolution_convert_fusion.1), channel_id=1, source_target_pairs={{0,1},{2,3},{4,5},{6,7},{8,9},{10,11},{12,13},{14,15},{16,17},{18,... | collective-permute-start | bytes 1966088 | tf_op jit(solution)/shard_map/ppermute | solution.py:225
  55.2 17.2 %copy-start.5 = (bf16[1,1280,160]{1,2,0:T(8,128)(2,1)S(1)}, bf16[1,1280,160]{1,2,0:T(8,128)(2,1)}, u32[]{:S(2)}) copy-start(bf16[1,1280,160]{1,2,0:T(8,128)(2,1)} %param.14) | copy-start | bytes 1228804
  72.4 1.0 copy-start.7
  73.4 11.9 %copy-start.4 = (bf16[1,1280,640]{2,1,0:T(8,128)(2,1)S(1)}, bf16[1,1280,640]{2,1,0:T(8,128)(2,1)}, u32[]{:S(2)}) copy-start(bf16[1,1280,640]{2,1,0:T(8,128)(2,1)} %param.12) | copy-start | bytes 4915204
  74.6 14.1 %collective-permute-start.10 = (bf16[2,2,2,80,128]{4,3,2,1,0:T(8,128)(2,1)}, bf16[2,2,2,80,128]{4,3,2,1,0:T(8,128)(2,1)S(1)}, u32[]{:S(2)}, u32[]{:S(2)}) collective-permute-start(bf16[2,2,2,80,128]{4,3,2,1,0:T(8,128)(2,1)} %pad_maximum_fusion.2), channel_id=1, source_target_pairs={{1,5},{5,9},{9,13},{3,7},{7,11},{11,15},{17,21},{21,25},{25,29},{1... | collective-permute-start | bytes 491528 | tf_op jit(solution)/shard_map/ppermute | solution.py:34
  75.9 12.8 %collective-permute-start.9 = (bf16[2,2,2,80,128]{4,3,2,1,0:T(8,128)(2,1)}, bf16[2,2,2,80,128]{4,3,2,1,0:T(8,128)(2,1)}, u32[]{:S(2)}, u32[]{:S(2)}) collective-permute-start(bf16[2,2,2,80,128]{4,3,2,1,0:T(8,128)(2,1)} %pad_maximum_fusion.2), channel_id=1, source_target_pairs={{1,9},{5,13},{3,11},{7,15},{17,25},{21,29},{19,27},{23,31}} | collective-permute-start | bytes 491528 | tf_op jit(solution)/shard_map/ppermute | solution.py:34
  83.3 5.3 %collective-permute-start.8 = (bf16[2,2,2,80,128]{4,3,2,1,0:T(8,128)(2,1)}, bf16[2,2,2,80,128]{4,3,2,1,0:T(8,128)(2,1)}, u32[]{:S(2)}, u32[]{:S(2)}) collective-permute-start(bf16[2,2,2,80,128]{4,3,2,1,0:T(8,128)(2,1)} %pad_maximum_fusion.2), channel_id=1, source_target_pairs={{1,13},{3,15},{17,29},{19,31}} | collective-permute-start | bytes 491528 | tf_op jit(solution)/shard_map/ppermute | solution.py:34
  93.2 8.5 %collective-permute-start.11 = (bf16[2,1,128,640]{3,2,1,0:T(8,128)(2,1)S(1)}, bf16[2,1,128,640]{3,2,1,0:T(8,128)(2,1)S(1)}, u32[]{:S(2)}, u32[]{:S(2)}) collective-permute-start(bf16[2,1,128,640]{3,2,1,0:T(8,128)(2,1)S(1)} %pad_maximum_fusion), channel_id=1, source_target_pairs={{1,0},{3,2},{5,4},{7,6},{9,8},{11,10},{13,12},{15,14},{17,16},{19,... | collective-permute-start | bytes 983048 | tf_op jit(solution)/shard_map/ppermute | solution.py:251
  94.5 6.1 %collective-permute-start.13 = (bf16[1,128,640]{2,1,0:T(8,128)(2,1)S(1)}, bf16[1,128,640]{2,1,0:T(8,128)(2,1)S(1)}, u32[]{:S(2)}, u32[]{:S(2)}) collective-permute-start(bf16[1,128,640]{2,1,0:T(8,128)(2,1)S(1)} %constant_dynamic-slice_fusion), channel_id=1, source_target_pairs={{1,3},{3,1},{5,7},{7,5},{9,11},{11,9},{13,15},{15,13},{17,19},{19,... | collective-permute-start | bytes 491528 | tf_op jit(solution)/shard_map/ppermute | solution.py:255
  97.7 4.0 %collective-permute-start.12 = (bf16[1,128,640]{2,1,0:T(8,128)(2,1)S(1)}, bf16[1,128,640]{2,1,0:T(8,128)(2,1)S(1)}, u32[]{:S(2)}, u32[]{:S(2)}) collective-permute-start(bf16[1,128,640]{2,1,0:T(8,128)(2,1)S(1)} %get-tuple-element.10), channel_id=1, source_target_pairs={{1,2},{3,0},{5,6},{7,4},{9,10},{11,8},{13,14},{15,12},{17,18},{19,... | collective-permute-start | bytes 491528 | tf_op jit(solution)/shard_map/ppermute | solution.py:251

commit v10 on v9

--- a/solution.py
+++ b/solution.py
@@ -126,7 +126,7 @@
     if out_w is None:
         return attended, key_t, value_t
     partial_value = jnp.einsum("bte,ed->btd", attended, out_w, preferred_element_type=jnp.float32)
-    return partial_value.astype(jnp.bfloat16), key_t, value_t
+    return partial_value, key_t, value_t
 
 
 def per_device(
@@ -219,12 +219,30 @@
         hidden0, lengths, norm_gain[0], query_weight[0], key_weight[0], value_weight[0],
         out_weight[0], sizes, 0,
     )
-    head_sum = None
+    head_cols = feature_count // mp_n
+    own_cols = mp_at * head_cols
+    summed = lax.dynamic_slice_in_dim(partial0, own_cols, head_cols, 2)
+    for by in range(1, mp_n):
+        target_cols = ((mp_at + by) % mp_n) * head_cols
+        piece = lax.dynamic_slice_in_dim(partial0, target_cols, head_cols, 2).astype(jnp.bfloat16)
+        pairs = [(m * sec_n, ((m + by) % mp_n) * sec_n) for m in range(mp_n)]
+        summed = summed + lax.ppermute(piece, feat_axes, pairs).astype(jnp.float32)
+    own_hidden0 = lax.dynamic_slice_in_dim(hidden0, own_cols, head_cols, 2)
+    hidden1_cols = (own_hidden0.astype(jnp.float32) + summed).astype(jnp.bfloat16)
+    arrivals = []
     for by in range(mp_n):
         pairs = [(m * sec_n, ((m + by) % mp_n) * sec_n + 1) for m in range(mp_n)]
-        term = lax.ppermute(partial0, feat_axes, pairs).astype(jnp.float32)
-        head_sum = term if head_sum is None else head_sum + term
-    hidden1 = (hidden0.astype(jnp.float32) + head_sum).astype(jnp.bfloat16)
+        arrivals.append(lax.ppermute(hidden1_cols, feat_axes, pairs))
+    if mp_n == 2:
+        hidden1 = jnp.where(
+            mp_at == 0,
+            jnp.concatenate([arrivals[0], arrivals[1]], 2),
+            jnp.concatenate([arrivals[1], arrivals[0]], 2),
+        )
+    else:
+        order = (mp_at - jnp.arange(mp_n, dtype=jnp.int32)) % mp_n
+        blocks = jnp.take(jnp.stack(arrivals, 0), order, axis=0)
+        hidden1 = jnp.moveaxis(blocks, 0, 2).reshape(hidden0.shape)
 
     partial1, key1, value1 = attend_layer(
         hidden1, lengths, norm_gain[0], query_weight[0], key_weight[0], value_weight[0],
@@ -235,8 +253,8 @@
     value_store = jnp.where(is_first, value0, value1)[None]
 
     per_section = seq_count // sec_n
-    low_rows = partial1[:per_section]
-    high_rows = partial1[per_section:]
+    low_rows = partial1[:per_section].astype(jnp.bfloat16)
+    high_rows = partial1[per_section:].astype(jnp.bfloat16)
     low_hidden = hidden1[:per_section]
     to_low = []
     to_high = []

time: 104 us -> 109 us (1.048)
  waiting for transfers between devices: 17.6 us -> 22 us
    ppermute x2 -> x3, waiting for transfers between devices: 15.5 us -> 20 us  [the longest x2 20 us: per_device(): arrivals.append(lax.ppermute(hidden1_cols, feat_axes, pairs))]
    reduce_sum x2, other arithmetic: 1.89 us -> 0.48 us  [attend_layer(): jnp.mean(hidden32 * hidden32, -1, keepdims=True) + 1e-06]
    convert_element_type x0 -> x1, other arithmetic: none -> 1.19 us  [per_device(): (own_hidden0.astype(jnp.float32) + summed).astype(jnp.bfloat16)]
    ppermute x2 -> x3, starting transfers between devices: 2.57 us -> 3.4 us  [the longest x2 2.72 us: per_device(): arrivals.append(lax.ppermute(hidden1_cols, feat_axes, pairs))]
    unnamed x25 -> x27, local copies, waits for them, and re-layouts: 5.35 us -> 5.9 us
  transfers between devices with their start and end apart: 14 -> 15, of which waited for: 3 -> 3; matrix products, arithmetic and copies ran while one was open for 12% -> 11% of each run, Pallas kernels for 0% -> 0%
where the time goes in v10:
time: 109 us; the launch traced here: 107 us
  starting transfers between devices  27.8 us (26%)
  waiting for transfers between devices  22 us (20%)
  other arithmetic  17.1 us (16%)
  matrix products  16.1 us (15%)
  local copies, waits for them, and re-layouts  13.7 us (13%)
  blocking collectives  9.24 us (8%)
  between operations  1.29 us (1%)
    ppermute x2, waiting for transfers between devices, per_device(): arrivals.append(lax.ppermute(hidden1_cols, feat_axes, pairs))  20 us
    ppermute x6, starting transfers between devices, gather_causal(): pieces.append(lax.ppermute(value, ('tm', 'section'), pairs))  14 us
    all_gather x1, blocking collectives, per_device(): hidden0 = lax.all_gather(tokens, feat_axes, axis=2, tiled=True)  9.24 us
    conv_general_dilated x1, matrix products, per_device(): lax.conv_general_dilated(chunks, kernel, window_strides=(STRIDE,), paddin...  6.22 us
    unnamed x27, local copies, waits for them, and re-layouts  5.9 us
    ppermute x3, starting transfers between devices, shift_from(): return lax.ppermute(value, axis, pairs)  4.66 us
    another operation x2, local copies, waits for them, and re-layouts, per_device(): jnp.stack([normed[:, :, q * chunk_tok * STRIDE:(q + 1) * chunk_tok * STRI...  3.55 us
    ppermute x1, starting transfers between devices, per_device(): to_high.append(lax.ppermute(cols_high, feat_axes, pairs))  3.11 us
  transfers between devices with their start and end apart: 15, of which 3 were waited for; matrix products, arithmetic and copies ran while one was open for 11% of the time, Pallas kernels for 0%

profile of v10, /device:TPU:1, one launch (start us, length us, event | category | flops | bytes accessed | tf_op | source)
XLA Modules:
  0.0 107.3 jit_solution(3843769788289962668)
XLA Ops:
  2.7 1.5 %multiply_reduce_fusion.1 = f32[2,64]{1,0:T(2,128)S(1)} fusion(f32[2,4096]{1,0:T(2,128)S(1)} %compare_convert_fusion, bf16[2,64,4096]{2,1,0:T(8,128)(2,1)} %param.8), kind=kLoop, calls=%fused_computation.27 | loop fusion | flops 1572736 | bytes 1081856 | tf_op jit(solution)/shard_map/reduce_sum | solution.py:151
  4.9 4.2 %collective-permute-start.2 = (f32[2,64,34]{1,0,2:T(2,128)S(1)}, f32[2,64,34]{1,0,2:T(2,128)S(1)}, u32[]{:S(2)}, u32[]{:S(2)}) collective-permute-start(f32[2,64,34]{1,0,2:T(2,128)S(1)} %pad_maximum_fusion.3), channel_id=1, source_target_pairs={{0,12},{4,0},{8,4},{12,8},{1,13},{5,1},{9,5},{13,9},{2,14},{6,2},{... | collective-permute-start | bytes 52232 | tf_op jit(solution)/shard_map/ppermute | solution.py:13
  10.5 1.6 %convert_element_type.165 = f32[2,64,4096]{2,1,0:T(8,128)} convert(bf16[2,64,4096]{2,1,0:T(8,128)(2,1)S(1)} %copy-done.1) | non-fusion elementwise | flops 524288 | bytes 3145728 | tf_op jit(solution)/shard_map/convert_element_type | solution.py:149
  12.0 4.5 %copy.39 = bf16[4096,320]{1,0:T(8,128)(2,1)} copy(bf16[4096,320]{0,1:T(8,128)(2,1)} %param.10) | data formatting | bytes 5242880 | tf_op args[2]
  17.6 2.3 %fusion.12 = bf16[2,64,4128]{2,1,0:T(8,128)(2,1)S(1)} fusion(f32[2,64,4096]{2,1,0:T(8,128)} %convert_element_type.165, f32[2,64,32]{2,1,0:T(8,128)S(1)} %copy.36, f32[2,64]{1,0:T(2,128)S(1)} %add_rsqrt_fusion.2, f32[2,64]{1,0:T(2,128)S(1)} %broadcast_divide_fusion, f32[2,4128]{1,0:T(2,128)S(1)} %and_convert_fusion), kind=kLoop, calls=%fused_computation.19 | loop fusion | flops 3170304 | bytes 3204352 | tf_op jit(solution)/shard_map/convert_element_type | solution.py:192
  20.2 3.5 %copy.38 = bf16[2,8,64,544]{2,1,0,3:T(8,128)(2,1)} copy(bf16[2,8,64,544]{3,2,0,1:T(8,128)(2,1)S(1)} %fusion.92) | data formatting | bytes 2228224 | tf_op jit(solution)/shard_map/stack | solution.py:196
  23.7 6.2 %fusion.60 = bf16[16,16,320]{2,0,1:T(8,128)(2,1)S(1)} fusion(bf16[64,64,320]{2,1,0:T(8,128)(2,1)} %bitcast.236, bf16[2,8,64,544]{2,1,0,3:T(8,128)(2,1)} %copy.38), kind=kOutput, calls=%fused_computation.55 | convolution fusion | flops 671170560 | bytes 3899392 | tf_op jit(solution)/shard_map/conv_general_dilated | solution.py:203
  30.1 9.2 %all_gather.3 = bf16[2,128,1280]{1,0,2:T(2,128)(2,1)S(1)} all-gather(bf16[2,128,320]{1,0,2:T(2,128)(2,1)S(1)} %copy.42), channel_id=1, replica_groups=mesh['groups'=2,'tm'=4,'mp'=2,'section'=2] {'mp','section'}, dimensions={2}, use_global_device_ids=true | all-gather | bytes 819200 | tf_op jit(solution)/shard_map/all_gather | solution.py:213
  40.5 1.5 %convolution_convert_fusion.3 = bf16[2,128,160]{1,2,0:T(8,128)(2,1)S(1)} fusion(bf16[1,1280,160]{1,2,0:T(8,128)(2,1)} %param.14, bf16[2,128,1280]{2,1,0:T(8,128)(2,1)S(1)} %copy.43, f32[1280]{0:T(1024)S(1)} %convert_reduce_fusion, f32[2,128]{1,0:T(2,128)S(1)} %add_rsqrt_fusion.1), kind=kOutput, calls=%fused_computation.58 | convolution fusion | flops 106209280 | bytes 1153024 | tf_op jit(solution)/shard_map/btd,de->bet/dot_general | solution.py:78
  43.8 1.3 %collective-permute-start.4 = (bf16[2,2,2,80,128]{4,3,2,1,0:T(8,128)(2,1)}, bf16[2,2,2,80,128]{4,3,2,1,0:T(8,128)(2,1)}, u32[]{:S(2)}, u32[]{:S(2)}) collective-permute-start(bf16[2,2,2,80,128]{4,3,2,1,0:T(8,128)(2,1)} %pad_maximum_fusion.1), channel_id=1, source_target_pairs={{0,8},{4,12},{2,10},{6,14},{16,24},{20,28},{18,26},{22,30}} | collective-permute-start | bytes 491528 | tf_op jit(solution)/shard_map/ppermute | solution.py:34
  45.1 1.3 %collective-permute-start.3 = (bf16[2,2,2,80,128]{4,3,2,1,0:T(8,128)(2,1)}, bf16[2,2,2,80,128]{4,3,2,1,0:T(8,128)(2,1)}, u32[]{:S(2)}, u32[]{:S(2)}) collective-permute-start(bf16[2,2,2,80,128]{4,3,2,1,0:T(8,128)(2,1)} %pad_maximum_fusion.1), channel_id=1, source_target_pairs={{0,12},{2,14},{16,28},{18,30}} | collective-permute-start | bytes 491528 | tf_op jit(solution)/shard_map/ppermute | solution.py:34
  47.4 1.1 %maximum_bitcast_fusion = bf16[1,2,2,2,80,512]{5,4,3,2,1,0:T(8,128)(2,1)S(1)} fusion(bf16[1,2,2,80,128]{4,3,2,1,0:T(8,128)(2,1)S(1)} %bitcast.244, bf16[1,2,2,80,128]{4,3,2,1,0:T(8,128)(2,1)S(1)} %bitcast.241, bf16[2,2,2,80,128]{4,3,2,1,0:T(8,128)(2,1)S(1)} %collective-permute-done.5, bf16[2,2,2,80,128]{4,3,2,1,0:T(8,128)(2,1)} %collective-permute-done.4, ...), kind=kLoop, calls=%fused_computation.64 | loop fusion | flops 3276800 | bytes 1310720 | tf_op jit(solution)/shard_map/transpose;reshape | solution.py:94
  53.6 1.2 %add_convert_fusion = bf16[2,128,640]{2,1,0:T(8,128)(2,1)S(1)} fusion(bf16[2,128,640]{2,1,0:T(8,128)(2,1)S(1)} %collective-permute-done.6, f32[2,128,1280]{2,1,0:T(8,128)} %copy-done.2, s32[]{:T(128)S(6)} %select_n.127, bf16[2,128,1280]{2,1,0:T(8,128)(2,1)S(1)} %copy.43), kind=kLoop, calls=%fused_computation.67 | loop fusion | flops 819200 | bytes 1638404 | tf_op jit(solution)/shard_map/convert_element_type | solution.py:231
  54.8 1.4 %collective-permute-start.8 = (bf16[2,128,640]{2,1,0:T(8,128)(2,1)S(1)}, bf16[2,128,640]{2,1,0:T(8,128)(2,1)S(1)}, u32[]{:S(2)}, u32[]{:S(2)}) collective-permute-start(bf16[2,128,640]{2,1,0:T(8,128)(2,1)S(1)} %add_convert_fusion), channel_id=1, source_target_pairs={{0,3},{2,1},{4,7},{6,5},{8,11},{10,9},{12,15},{14,13},{16,19},{18,... | collective-permute-start | bytes 983048 | tf_op jit(solution)/shard_map/ppermute | solution.py:235
  56.2 1.3 %collective-permute-start.7 = (bf16[2,128,640]{2,1,0:T(8,128)(2,1)S(1)}, bf16[2,128,640]{2,1,0:T(8,128)(2,1)S(1)}, u32[]{:S(2)}, u32[]{:S(2)}) collective-permute-start(bf16[2,128,640]{2,1,0:T(8,128)(2,1)S(1)} %add_convert_fusion), channel_id=1, source_target_pairs={{0,1},{2,3},{4,5},{6,7},{8,9},{10,11},{12,13},{14,15},{16,17},{18,... | collective-permute-start | bytes 983048 | tf_op jit(solution)/shard_map/ppermute | solution.py:235
  57.6 20.0 %collective-permute-done.8 = bf16[2,128,640]{2,1,0:T(8,128)(2,1)S(1)} collective-permute-done((bf16[2,128,640]{2,1,0:T(8,128)(2,1)S(1)}, bf16[2,128,640]{2,1,0:T(8,128)(2,1)S(1)}, u32[]{:S(2)}, u32[]{:S(2)}) %collective-permute-start.8) | collective-permute-done | bytes 327712 | tf_op jit(solution)/shard_map/ppermute | solution.py:235
  79.5 1.3 %collective-permute-start.11 = (bf16[2,2,2,80,128]{4,3,2,1,0:T(8,128)(2,1)}, bf16[2,2,2,80,128]{4,3,2,1,0:T(8,128)(2,1)S(1)}, u32[]{:S(2)}, u32[]{:S(2)}) collective-permute-start(bf16[2,2,2,80,128]{4,3,2,1,0:T(8,128)(2,1)} %pad_maximum_fusion.2), channel_id=1, source_target_pairs={{1,5},{5,9},{9,13},{3,7},{7,11},{11,15},{17,21},{21,25},{25,29},{1... | collective-permute-start | bytes 491528 | tf_op jit(solution)/shard_map/ppermute | solution.py:34
  80.8 7.5 %collective-permute-start.10 = (bf16[2,2,2,80,128]{4,3,2,1,0:T(8,128)(2,1)}, bf16[2,2,2,80,128]{4,3,2,1,0:T(8,128)(2,1)}, u32[]{:S(2)}, u32[]{:S(2)}) collective-permute-start(bf16[2,2,2,80,128]{4,3,2,1,0:T(8,128)(2,1)} %pad_maximum_fusion.2), channel_id=1, source_target_pairs={{1,9},{5,13},{3,11},{7,15},{17,25},{21,29},{19,27},{23,31}} | collective-permute-start | bytes 491528 | tf_op jit(solution)/shard_map/ppermute | solution.py:34
  88.2 2.0 %collective-permute-start.9 = (bf16[2,2,2,80,128]{4,3,2,1,0:T(8,128)(2,1)}, bf16[2,2,2,80,128]{4,3,2,1,0:T(8,128)(2,1)}, u32[]{:S(2)}, u32[]{:S(2)}) collective-permute-start(bf16[2,2,2,80,128]{4,3,2,1,0:T(8,128)(2,1)} %pad_maximum_fusion.2), channel_id=1, source_target_pairs={{1,13},{3,15},{17,29},{19,31}} | collective-permute-start | bytes 491528 | tf_op jit(solution)/shard_map/ppermute | solution.py:34
  90.2 1.5 %fusion.54 = bf16[2,128,640]{2,1,0:T(8,128)(2,1)} fusion(bf16[1,1280,640]{2,1,0:T(8,128)(2,1)S(1)} %copy-done.5, bf16[2,128,1280]{2,1,0:T(8,128)(2,1)S(1)} %get-tuple-element.4, f32[2,128]{1,0:T(2,128)S(1)} %add_rsqrt_fusion, f32[1280]{0:T(1024)S(1)} %convert_reduce_fusion), kind=kOutput, calls=%fused_computation.53 | convolution fusion | flops 421068800 | bytes 2627584 | tf_op jit(solution)/shard_map/btd,de->bte/dot_general | solution.py:72
  92.3 1.2 %copy.48 = bf16[2,128,640]{1,2,0:T(8,128)(2,1)S(1)} copy(bf16[2,128,640]{2,1,0:T(8,128)(2,1)} %fusion.54) | data formatting | bytes 655360 | tf_op jit(solution)/shard_map/convert_element_type | solution.py:74
  98.0 1.3 %collective-permute-start.12 = (bf16[2,1,128,640]{3,2,1,0:T(8,128)(2,1)S(1)}, bf16[2,1,128,640]{3,2,1,0:T(8,128)(2,1)S(1)}, u32[]{:S(2)}, u32[]{:S(2)}) collective-permute-start(bf16[2,1,128,640]{3,2,1,0:T(8,128)(2,1)S(1)} %pad_maximum_fusion), channel_id=1, source_target_pairs={{1,0},{3,2},{5,4},{7,6},{9,8},{11,10},{13,12},{15,14},{17,16},{19,... | collective-permute-start | bytes 983048 | tf_op jit(solution)/shard_map/ppermute | solution.py:269
  99.4 3.1 %collective-permute-start.14 = (bf16[1,128,640]{2,1,0:T(8,128)(2,1)S(1)}, bf16[1,128,640]{2,1,0:T(8,128)(2,1)S(1)}, u32[]{:S(2)}, u32[]{:S(2)}) collective-permute-start(bf16[1,128,640]{2,1,0:T(8,128)(2,1)S(1)} %constant_dynamic-slice_fusion), channel_id=1, source_target_pairs={{1,3},{3,1},{5,7},{7,5},{9,11},{11,9},{13,15},{15,13},{17,19},{19,... | collective-permute-start | bytes 491528 | tf_op jit(solution)/shard_map/ppermute | solution.py:273
  102.5 1.3 %collective-permute-start.13 = (bf16[1,128,640]{2,1,0:T(8,128)(2,1)S(1)}, bf16[1,128,640]{2,1,0:T(8,128)(2,1)S(1)}, u32[]{:S(2)}, u32[]{:S(2)}) collective-permute-start(bf16[1,128,640]{2,1,0:T(8,128)(2,1)S(1)} %get-tuple-element.10), channel_id=1, source_target_pairs={{1,2},{3,0},{5,6},{7,4},{9,10},{11,8},{13,14},{15,12},{17,18},{19,... | collective-permute-start | bytes 491528 | tf_op jit(solution)/shard_map/ppermute | solution.py:269
  (121 shorter events, 24.8 us)
Async XLA Ops:
  0.6 50.4 %copy-start = (bf16[1,640,1280]{2,1,0:T(8,128)(2,1)S(1)}, bf16[1,640,1280]{2,1,0:T(8,128)(2,1)}, u32[]{:S(2)}) copy-start(bf16[1,640,1280]{2,1,0:T(8,128)(2,1)} %param.15) | copy-start | bytes 4915204
  0.6 3.6 %copy-start.1 = (bf16[2,64,4096]{2,1,0:T(8,128)(2,1)S(1)}, bf16[2,64,4096]{2,1,0:T(8,128)(2,1)}, u32[]{:S(2)}) copy-start(bf16[2,64,4096]{2,1,0:T(8,128)(2,1)} %param.8) | copy-start | bytes 3145732
  1.8 8.3 %copy-start.3 = (bf16[1,1280]{1,0:T(2,128)(2,1)S(1)}, bf16[1,1280]{1,0:T(2,128)(2,1)}, u32[]{:S(2)}) copy-start(bf16[1,1280]{1,0:T(2,128)(2,1)} %param.11) | copy-start | bytes 7684
  4.9 11.6 %collective-permute-start.2 = (f32[2,64,34]{1,0,2:T(2,128)S(1)}, f32[2,64,34]{1,0,2:T(2,128)S(1)}, u32[]{:S(2)}, u32[]{:S(2)}) collective-permute-start(f32[2,64,34]{1,0,2:T(2,128)S(1)} %pad_maximum_fusion.3), channel_id=1, source_target_pairs={{0,12},{4,0},{8,4},{12,8},{1,13},{5,1},{9,5},{13,9},{2,14},{6,2},{... | collective-permute-start | bytes 52232 | tf_op jit(solution)/shard_map/ppermute | solution.py:13
  9.1 7.4 %collective-permute-start.1 = (f32[2,64,34]{1,0,2:T(2,128)S(1)}, f32[2,64,34]{1,0,2:T(2,128)S(1)}, u32[]{:S(2)}, u32[]{:S(2)}) collective-permute-start(f32[2,64,34]{1,0,2:T(2,128)S(1)} %pad_maximum_fusion.3), channel_id=1, source_target_pairs={{0,8},{4,12},{8,0},{12,4},{1,9},{5,13},{9,1},{13,5},{2,10},{6,14},... | collective-permute-start | bytes 52232 | tf_op jit(solution)/shard_map/ppermute | solution.py:13
  9.1 7.4 %collective-permute-start = (f32[2,64,34]{1,0,2:T(2,128)S(1)}, f32[2,64,34]{1,0,2:T(2,128)S(1)}, u32[]{:S(2)}, u32[]{:S(2)}) collective-permute-start(f32[2,64,34]{1,0,2:T(2,128)S(1)} %pad_maximum_fusion.3), channel_id=1, source_target_pairs={{0,4},{4,8},{8,12},{12,0},{1,5},{5,9},{9,13},{13,1},{2,6},{6,10},{... | collective-permute-start | bytes 52232 | tf_op jit(solution)/shard_map/ppermute | solution.py:13
  40.3 1.7 %copy-start.7 = (bf16[1,1280,160]{1,2,0:T(8,128)(2,1)S(1)}, bf16[1,1280,160]{1,2,0:T(8,128)(2,1)}, u32[]{:S(2)}) copy-start(bf16[1,1280,160]{1,2,0:T(8,128)(2,1)} %param.13) | copy-start | bytes 1228804
  42.0 4.5 %copy-start.4 = (bf16[1,1280,640]{2,1,0:T(8,128)(2,1)S(1)}, bf16[1,1280,640]{2,1,0:T(8,128)(2,1)}, u32[]{:S(2)}) copy-start(bf16[1,1280,640]{2,1,0:T(8,128)(2,1)} %param.12) | copy-start | bytes 4915204
  43.2 4.3 %collective-permute-start.5 = (bf16[2,2,2,80,128]{4,3,2,1,0:T(8,128)(2,1)}, bf16[2,2,2,80,128]{4,3,2,1,0:T(8,128)(2,1)S(1)}, u32[]{:S(2)}, u32[]{:S(2)}) collective-permute-start(bf16[2,2,2,80,128]{4,3,2,1,0:T(8,128)(2,1)} %pad_maximum_fusion.1), channel_id=1, source_target_pairs={{0,4},{4,8},{8,12},{2,6},{6,10},{10,14},{16,20},{20,24},{24,28},{1... | collective-permute-start | bytes 491528 | tf_op jit(solution)/shard_map/ppermute | solution.py:34
  43.8 3.6 %collective-permute-start.4 = (bf16[2,2,2,80,128]{4,3,2,1,0:T(8,128)(2,1)}, bf16[2,2,2,80,128]{4,3,2,1,0:T(8,128)(2,1)}, u32[]{:S(2)}, u32[]{:S(2)}) collective-permute-start(bf16[2,2,2,80,128]{4,3,2,1,0:T(8,128)(2,1)} %pad_maximum_fusion.1), channel_id=1, source_target_pairs={{0,8},{4,12},{2,10},{6,14},{16,24},{20,28},{18,26},{22,30}} | collective-permute-start | bytes 491528 | tf_op jit(solution)/shard_map/ppermute | solution.py:34
  45.1 2.3 %collective-permute-start.3 = (bf16[2,2,2,80,128]{4,3,2,1,0:T(8,128)(2,1)}, bf16[2,2,2,80,128]{4,3,2,1,0:T(8,128)(2,1)}, u32[]{:S(2)}, u32[]{:S(2)}) collective-permute-start(bf16[2,2,2,80,128]{4,3,2,1,0:T(8,128)(2,1)} %pad_maximum_fusion.1), channel_id=1, source_target_pairs={{0,12},{2,14},{16,28},{18,30}} | collective-permute-start | bytes 491528 | tf_op jit(solution)/shard_map/ppermute | solution.py:34
  51.8 1.1 copy-start.2
  52.9 0.7 collective-permute-start.6
  54.8 23.0 %copy-start.6 = (bf16[1,1280,160]{1,2,0:T(8,128)(2,1)S(1)}, bf16[1,1280,160]{1,2,0:T(8,128)(2,1)}, u32[]{:S(2)}) copy-start(bf16[1,1280,160]{1,2,0:T(8,128)(2,1)} %param.14) | copy-start | bytes 1228804
  54.8 22.7 %collective-permute-start.8 = (bf16[2,128,640]{2,1,0:T(8,128)(2,1)S(1)}, bf16[2,128,640]{2,1,0:T(8,128)(2,1)S(1)}, u32[]{:S(2)}, u32[]{:S(2)}) collective-permute-start(bf16[2,128,640]{2,1,0:T(8,128)(2,1)S(1)} %add_convert_fusion), channel_id=1, source_target_pairs={{0,3},{2,1},{4,7},{6,5},{8,11},{10,9},{12,15},{14,13},{16,19},{18,... | collective-permute-start | bytes 983048 | tf_op jit(solution)/shard_map/ppermute | solution.py:235
  56.2 21.3 %collective-permute-start.7 = (bf16[2,128,640]{2,1,0:T(8,128)(2,1)S(1)}, bf16[2,128,640]{2,1,0:T(8,128)(2,1)S(1)}, u32[]{:S(2)}, u32[]{:S(2)}) collective-permute-start(bf16[2,128,640]{2,1,0:T(8,128)(2,1)S(1)} %add_convert_fusion), channel_id=1, source_target_pairs={{0,1},{2,3},{4,5},{6,7},{8,9},{10,11},{12,13},{14,15},{16,17},{18,... | collective-permute-start | bytes 983048 | tf_op jit(solution)/shard_map/ppermute | solution.py:235
  57.5 20.7 %copy-start.8 = (bf16[1,1280,160]{1,2,0:T(8,128)(2,1)S(1)}, bf16[1,1280,160]{1,2,0:T(8,128)(2,1)}, u32[]{:S(2)}) copy-start(bf16[1,1280,160]{1,2,0:T(8,128)(2,1)} %param.13) | copy-start | bytes 1228804
  78.3 11.9 %copy-start.5 = (bf16[1,1280,640]{2,1,0:T(8,128)(2,1)S(1)}, bf16[1,1280,640]{2,1,0:T(8,128)(2,1)}, u32[]{:S(2)}) copy-start(bf16[1,1280,640]{2,1,0:T(8,128)(2,1)} %param.12) | copy-start | bytes 4915204
  79.5 14.1 %collective-permute-start.11 = (bf16[2,2,2,80,128]{4,3,2,1,0:T(8,128)(2,1)}, bf16[2,2,2,80,128]{4,3,2,1,0:T(8,128)(2,1)S(1)}, u32[]{:S(2)}, u32[]{:S(2)}) collective-permute-start(bf16[2,2,2,80,128]{4,3,2,1,0:T(8,128)(2,1)} %pad_maximum_fusion.2), channel_id=1, source_target_pairs={{1,5},{5,9},{9,13},{3,7},{7,11},{11,15},{17,21},{21,25},{25,29},{1... | collective-permute-start | bytes 491528 | tf_op jit(solution)/shard_map/ppermute | solution.py:34
  80.8 12.8 %collective-permute-start.10 = (bf16[2,2,2,80,128]{4,3,2,1,0:T(8,128)(2,1)}, bf16[2,2,2,80,128]{4,3,2,1,0:T(8,128)(2,1)}, u32[]{:S(2)}, u32[]{:S(2)}) collective-permute-start(bf16[2,2,2,80,128]{4,3,2,1,0:T(8,128)(2,1)} %pad_maximum_fusion.2), channel_id=1, source_target_pairs={{1,9},{5,13},{3,11},{7,15},{17,25},{21,29},{19,27},{23,31}} | collective-permute-start | bytes 491528 | tf_op jit(solution)/shard_map/ppermute | solution.py:34
  88.2 5.3 %collective-permute-start.9 = (bf16[2,2,2,80,128]{4,3,2,1,0:T(8,128)(2,1)}, bf16[2,2,2,80,128]{4,3,2,1,0:T(8,128)(2,1)}, u32[]{:S(2)}, u32[]{:S(2)}) collective-permute-start(bf16[2,2,2,80,128]{4,3,2,1,0:T(8,128)(2,1)} %pad_maximum_fusion.2), channel_id=1, source_target_pairs={{1,13},{3,15},{17,29},{19,31}} | collective-permute-start | bytes 491528 | tf_op jit(solution)/shard_map/ppermute | solution.py:34
  98.0 8.5 %collective-permute-start.12 = (bf16[2,1,128,640]{3,2,1,0:T(8,128)(2,1)S(1)}, bf16[2,1,128,640]{3,2,1,0:T(8,128)(2,1)S(1)}, u32[]{:S(2)}, u32[]{:S(2)}) collective-permute-start(bf16[2,1,128,640]{3,2,1,0:T(8,128)(2,1)S(1)} %pad_maximum_fusion), channel_id=1, source_target_pairs={{1,0},{3,2},{5,4},{7,6},{9,8},{11,10},{13,12},{15,14},{17,16},{19,... | collective-permute-start | bytes 983048 | tf_op jit(solution)/shard_map/ppermute | solution.py:269
  99.4 6.1 %collective-permute-start.14 = (bf16[1,128,640]{2,1,0:T(8,128)(2,1)S(1)}, bf16[1,128,640]{2,1,0:T(8,128)(2,1)S(1)}, u32[]{:S(2)}, u32[]{:S(2)}) collective-permute-start(bf16[1,128,640]{2,1,0:T(8,128)(2,1)S(1)} %constant_dynamic-slice_fusion), channel_id=1, source_target_pairs={{1,3},{3,1},{5,7},{7,5},{9,11},{11,9},{13,15},{15,13},{17,19},{19,... | collective-permute-start | bytes 491528 | tf_op jit(solution)/shard_map/ppermute | solution.py:273
  102.5 4.0 %collective-permute-start.13 = (bf16[1,128,640]{2,1,0:T(8,128)(2,1)S(1)}, bf16[1,128,640]{2,1,0:T(8,128)(2,1)S(1)}, u32[]{:S(2)}, u32[]{:S(2)}) collective-permute-start(bf16[1,128,640]{2,1,0:T(8,128)(2,1)S(1)} %get-tuple-element.10), channel_id=1, source_target_pairs={{1,2},{3,0},{5,6},{7,4},{9,10},{11,8},{13,14},{15,12},{17,18},{19,... | collective-permute-start | bytes 491528 | tf_op jit(solution)/shard_map/ppermute | solution.py:269

commit v11 on v9

--- a/solution.py
+++ b/solution.py
@@ -191,7 +191,7 @@
         (padded * padded_valid - channel_mean[..., None]) * padded_valid * inv_std
     ).astype(jnp.bfloat16)
     kernel = patch_weight.reshape(channels, 2 * STRIDE, patch_weight.shape[1])
-    chunk_tok = 16 if tok_count % 16 == 0 else tok_count
+    chunk_tok = 32 if tok_count % 32 == 0 else tok_count
     chunk_count = tok_count // chunk_tok
     chunks = jnp.stack(
         [

time: 104 us -> 103 us (level)
  waiting for transfers between devices: 17.6 us -> 16.3 us
    ppermute x2, waiting for transfers between devices: 15.5 us -> 14.2 us  [per_device(): term = lax.ppermute(partial0, feat_axes, pairs).astype(jnp.float32)]
    dot_general x2, matrix products: 0.92 us -> 2.04 us  [attend_layer(): jnp.einsum('btd,de->bet', layer_input, key_w, preferred_element_type=jnp....]
    unnamed x25 -> x18, local copies, waits for them, and re-layouts: 5.35 us -> 5.17 us
  transfers between devices with their start and end apart: 14 -> 14, of which waited for: 3 -> 3; matrix products, arithmetic and copies ran while one was open for 12% -> 10% of each run, Pallas kernels for 0% -> 0%
where the time goes in v11:
time: 103 us; the launch traced here: 101 us
  starting transfers between devices  27.7 us (27%)
  other arithmetic  17.5 us (17%)
  matrix products  16.5 us (16%)
  waiting for transfers between devices  16.3 us (16%)
  local copies, waits for them, and re-layouts  12.6 us (12%)
  blocking collectives  9.24 us (9%)
  between operations  1.22 us (1%)
    ppermute x6, starting transfers between devices, gather_causal(): pieces.append(lax.ppermute(value, ('tm', 'section'), pairs))  14.5 us
    ppermute x2, waiting for transfers between devices, per_device(): term = lax.ppermute(partial0, feat_axes, pairs).astype(jnp.float32)  14.2 us
    all_gather x1, blocking collectives, per_device(): hidden0 = lax.all_gather(tokens, feat_axes, axis=2, tiled=True)  9.24 us
    conv_general_dilated x1, matrix products, per_device(): lax.conv_general_dilated(chunks, kernel, window_strides=(STRIDE,), paddin...  5.66 us
    unnamed x18, local copies, waits for them, and re-layouts  5.17 us
    ppermute x3, starting transfers between devices, shift_from(): return lax.ppermute(value, axis, pairs)  4.66 us
    another operation x2, local copies, waits for them, and re-layouts, per_device(): jnp.stack([normed[:, :, q * chunk_tok * STRIDE:(q + 1) * chunk_tok * STRI...  3.28 us
    ppermute x1, starting transfers between devices, per_device(): to_high.append(lax.ppermute(cols_high, feat_axes, pairs))  3.19 us
  transfers between devices with their start and end apart: 14, of which 3 were waited for; matrix products, arithmetic and copies ran while one was open for 10% of the time, Pallas kernels for 0%

profile of v11, /device:TPU:1, one launch (start us, length us, event | category | flops | bytes accessed | tf_op | source)
XLA Modules:
  0.0 101.1 jit_solution(5736870472624368125)
XLA Ops:
  2.8 1.5 %multiply_reduce_fusion.1 = f32[2,64]{1,0:T(2,128)S(1)} fusion(f32[2,4096]{1,0:T(2,128)S(1)} %compare_convert_fusion, bf16[2,64,4096]{2,1,0:T(8,128)(2,1)} %param.8), kind=kLoop, calls=%fused_computation.27 | loop fusion | flops 1572736 | bytes 1081856 | tf_op jit(solution)/shard_map/reduce_sum | solution.py:151
  4.9 2.2 %collective-permute-start = (f32[2,64,34]{1,0,2:T(2,128)S(1)}, f32[2,64,34]{1,0,2:T(2,128)S(1)}, u32[]{:S(2)}, u32[]{:S(2)}) collective-permute-start(f32[2,64,34]{1,0,2:T(2,128)S(1)} %pad_maximum_fusion.4), channel_id=1, source_target_pairs={{0,4},{4,8},{8,12},{12,0},{1,5},{5,9},{9,13},{13,1},{2,6},{6,10},{... | collective-permute-start | bytes 52232 | tf_op jit(solution)/shard_map/ppermute | solution.py:13
  7.1 2.1 %collective-permute-start.2 = (f32[2,64,34]{1,0,2:T(2,128)S(1)}, f32[2,64,34]{1,0,2:T(2,128)S(1)}, u32[]{:S(2)}, u32[]{:S(2)}) collective-permute-start(f32[2,64,34]{1,0,2:T(2,128)S(1)} %pad_maximum_fusion.4), channel_id=1, source_target_pairs={{0,12},{4,0},{8,4},{12,8},{1,13},{5,1},{9,5},{13,9},{2,14},{6,2},{... | collective-permute-start | bytes 52232 | tf_op jit(solution)/shard_map/ppermute | solution.py:13
  10.4 1.6 %convert_element_type.167 = f32[2,64,4096]{2,1,0:T(8,128)} convert(bf16[2,64,4096]{2,1,0:T(8,128)(2,1)S(1)} %copy-done.1) | non-fusion elementwise | flops 524288 | bytes 3145728 | tf_op jit(solution)/shard_map/convert_element_type | solution.py:149
  12.0 4.5 %copy.39 = bf16[4096,320]{1,0:T(8,128)(2,1)} copy(bf16[4096,320]{0,1:T(8,128)(2,1)} %param.10) | data formatting | bytes 5242880 | tf_op args[2]
  17.6 2.3 %fusion.11 = bf16[2,64,4128]{2,1,0:T(8,128)(2,1)S(1)} fusion(f32[2,64,4096]{2,1,0:T(8,128)} %convert_element_type.167, f32[2,64,32]{2,1,0:T(8,128)S(1)} %copy.36, f32[2,64]{1,0:T(2,128)S(1)} %add_rsqrt_fusion.2, f32[2,64]{1,0:T(2,128)S(1)} %broadcast_divide_fusion, f32[2,4128]{1,0:T(2,128)S(1)} %and_convert_fusion), kind=kLoop, calls=%fused_computation.19 | loop fusion | flops 3170304 | bytes 3204352 | tf_op jit(solution)/shard_map/convert_element_type | solution.py:192
  20.2 3.2 %copy.38 = bf16[2,4,64,1056]{2,1,0,3:T(4,128)(2,1)} copy(bf16[2,4,64,1056]{3,2,0,1:T(8,128)(2,1)S(1)} %pad_maximum_fusion) | data formatting | bytes 2162688 | tf_op jit(solution)/shard_map/stack | solution.py:196
  23.4 5.7 %fusion.59 = bf16[8,32,320]{2,0,1:T(8,128)(2,1)S(1)} fusion(bf16[8,64,1056]{1,0,2:T(8,128)(2,1)} %bitcast.210, bf16[64,64,320]{2,1,0:T(8,128)(2,1)} %bitcast.209), kind=kOutput, calls=%fused_computation.57 | convolution fusion | flops 671170560 | bytes 3866624 | tf_op jit(solution)/shard_map/conv_general_dilated | solution.py:203
  29.3 9.2 %all_gather.3 = bf16[2,128,1280]{1,0,2:T(2,128)(2,1)S(1)} all-gather(bf16[2,128,320]{1,0,2:T(2,128)(2,1)S(1)} %copy.42), channel_id=1, replica_groups=mesh['groups'=2,'tm'=4,'mp'=2,'section'=2] {'mp','section'}, dimensions={2}, use_global_device_ids=true | all-gather | bytes 819200 | tf_op jit(solution)/shard_map/all_gather | solution.py:213
  39.7 1.6 %convolution_convert_fusion.5 = bf16[2,128,160]{1,2,0:T(8,128)(2,1)S(1)} fusion(bf16[1,1280,160]{1,2,0:T(8,128)(2,1)} %param.13, bf16[2,128,1280]{2,1,0:T(8,128)(2,1)S(1)} %copy.43, f32[1280]{0:T(1024)S(1)} %convert_reduce_fusion, f32[2,128]{1,0:T(2,128)S(1)} %add_rsqrt_fusion.1), kind=kOutput, calls=%fused_computation.61 | convolution fusion | flops 106209280 | bytes 1153024 | tf_op jit(solution)/shard_map/btd,de->bet/dot_general | solution.py:75
  43.1 1.3 %collective-permute-start.4 = (bf16[2,2,2,80,128]{4,3,2,1,0:T(8,128)(2,1)}, bf16[2,2,2,80,128]{4,3,2,1,0:T(8,128)(2,1)}, u32[]{:S(2)}, u32[]{:S(2)}) collective-permute-start(bf16[2,2,2,80,128]{4,3,2,1,0:T(8,128)(2,1)} %pad_maximum_fusion.2), channel_id=1, source_target_pairs={{0,8},{4,12},{2,10},{6,14},{16,24},{20,28},{18,26},{22,30}} | collective-permute-start | bytes 491528 | tf_op jit(solution)/shard_map/ppermute | solution.py:34
  44.4 1.3 %collective-permute-start.3 = (bf16[2,2,2,80,128]{4,3,2,1,0:T(8,128)(2,1)}, bf16[2,2,2,80,128]{4,3,2,1,0:T(8,128)(2,1)}, u32[]{:S(2)}, u32[]{:S(2)}) collective-permute-start(bf16[2,2,2,80,128]{4,3,2,1,0:T(8,128)(2,1)} %pad_maximum_fusion.2), channel_id=1, source_target_pairs={{0,12},{2,14},{16,28},{18,30}} | collective-permute-start | bytes 491528 | tf_op jit(solution)/shard_map/ppermute | solution.py:34
  50.3 1.6 %convolution_convert_fusion.1 = bf16[2,128,1280]{2,1,0:T(8,128)(2,1)} fusion(bf16[2,128,640]{1,2,0:T(8,128)(2,1)S(1)} %bitcast.227, bf16[1,640,1280]{2,1,0:T(8,128)(2,1)S(1)} %copy-done), kind=kOutput, calls=%fused_computation.14 | convolution fusion | flops 419758080 | bytes 2621440 | tf_op jit(solution)/shard_map/bte,ed->btd/dot_general | solution.py:128
  51.9 1.4 %collective-permute-start.7 = (bf16[2,128,1280]{2,1,0:T(8,128)(2,1)}, bf16[2,128,1280]{2,1,0:T(8,128)(2,1)}, u32[]{:S(2)}, u32[]{:S(2)}) collective-permute-start(bf16[2,128,1280]{2,1,0:T(8,128)(2,1)} %convolution_convert_fusion.1), channel_id=1, source_target_pairs={{0,3},{2,1},{4,7},{6,5},{8,11},{10,9},{12,15},{14,13},{16,19},{18,... | collective-permute-start | bytes 1966088 | tf_op jit(solution)/shard_map/ppermute | solution.py:225
  53.3 1.3 %collective-permute-start.6 = (bf16[2,128,1280]{2,1,0:T(8,128)(2,1)}, bf16[2,128,1280]{2,1,0:T(8,128)(2,1)}, u32[]{:S(2)}, u32[]{:S(2)}) collective-permute-start(bf16[2,128,1280]{2,1,0:T(8,128)(2,1)} %convolution_convert_fusion.1), channel_id=1, source_target_pairs={{0,1},{2,3},{4,5},{6,7},{8,9},{10,11},{12,13},{14,15},{16,17},{18,... | collective-permute-start | bytes 1966088 | tf_op jit(solution)/shard_map/ppermute | solution.py:225
  54.7 14.2 %collective-permute-done.7 = bf16[2,128,1280]{2,1,0:T(8,128)(2,1)} collective-permute-done((bf16[2,128,1280]{2,1,0:T(8,128)(2,1)}, bf16[2,128,1280]{2,1,0:T(8,128)(2,1)}, u32[]{:S(2)}, u32[]{:S(2)}) %collective-permute-start.7) | collective-permute-done | bytes 655392 | tf_op jit(solution)/shard_map/ppermute | solution.py:225
  68.9 1.7 %fusion.28 = (f32[2,128]{1,0:T(2,128)S(1)}, bf16[2,128,1280]{2,1,0:T(8,128)(2,1)S(1)}) fusion(bf16[2,128,1280]{2,1,0:T(8,128)(2,1)} %collective-permute-done.7, bf16[2,128,1280]{2,1,0:T(8,128)(2,1)} %collective-permute-done.6, bf16[2,128,1280]{2,1,0:T(8,128)(2,1)S(1)} %copy.43), kind=kLoop, calls=%fused_computation.41 | loop fusion | flops 2948864 | bytes 2622464 | tf_op jit(solution)/shard_map/reduce_sum | solution.py:69
  72.0 1.4 %fusion.53 = bf16[2,128,640]{2,1,0:T(8,128)(2,1)} fusion(bf16[1,1280,640]{2,1,0:T(8,128)(2,1)S(1)} %copy-done.4, bf16[2,128,1280]{2,1,0:T(8,128)(2,1)S(1)} %get-tuple-element.4, f32[2,128]{1,0:T(2,128)S(1)} %add_rsqrt_fusion, f32[1280]{0:T(1024)S(1)} %convert_reduce_fusion), kind=kOutput, calls=%fused_computation.54 | convolution fusion | flops 421068800 | bytes 2627584 | tf_op jit(solution)/shard_map/btd,de->bte/dot_general | solution.py:72
  74.2 3.6 %collective-permute-start.10 = (bf16[2,2,2,80,128]{4,3,2,1,0:T(8,128)(2,1)}, bf16[2,2,2,80,128]{4,3,2,1,0:T(8,128)(2,1)S(1)}, u32[]{:S(2)}, u32[]{:S(2)}) collective-permute-start(bf16[2,2,2,80,128]{4,3,2,1,0:T(8,128)(2,1)} %pad_maximum_fusion.3), channel_id=1, source_target_pairs={{1,5},{5,9},{9,13},{3,7},{7,11},{11,15},{17,21},{21,25},{25,29},{1... | collective-permute-start | bytes 491528 | tf_op jit(solution)/shard_map/ppermute | solution.py:34
  77.8 5.6 %collective-permute-start.9 = (bf16[2,2,2,80,128]{4,3,2,1,0:T(8,128)(2,1)}, bf16[2,2,2,80,128]{4,3,2,1,0:T(8,128)(2,1)}, u32[]{:S(2)}, u32[]{:S(2)}) collective-permute-start(bf16[2,2,2,80,128]{4,3,2,1,0:T(8,128)(2,1)} %pad_maximum_fusion.3), channel_id=1, source_target_pairs={{1,9},{5,13},{3,11},{7,15},{17,25},{21,29},{19,27},{23,31}} | collective-permute-start | bytes 491528 | tf_op jit(solution)/shard_map/ppermute | solution.py:34
  83.4 2.0 %collective-permute-start.8 = (bf16[2,2,2,80,128]{4,3,2,1,0:T(8,128)(2,1)}, bf16[2,2,2,80,128]{4,3,2,1,0:T(8,128)(2,1)}, u32[]{:S(2)}, u32[]{:S(2)}) collective-permute-start(bf16[2,2,2,80,128]{4,3,2,1,0:T(8,128)(2,1)} %pad_maximum_fusion.3), channel_id=1, source_target_pairs={{1,13},{3,15},{17,29},{19,31}} | collective-permute-start | bytes 491528 | tf_op jit(solution)/shard_map/ppermute | solution.py:34
  91.8 1.3 %collective-permute-start.11 = (bf16[2,1,128,640]{3,2,1,0:T(8,128)(2,1)S(1)}, bf16[2,1,128,640]{3,2,1,0:T(8,128)(2,1)S(1)}, u32[]{:S(2)}, u32[]{:S(2)}) collective-permute-start(bf16[2,1,128,640]{3,2,1,0:T(8,128)(2,1)S(1)} %pad_maximum_fusion.1), channel_id=1, source_target_pairs={{1,0},{3,2},{5,4},{7,6},{9,8},{11,10},{13,12},{15,14},{17,16},{19,... | collective-permute-start | bytes 983048 | tf_op jit(solution)/shard_map/ppermute | solution.py:251
  93.1 3.2 %collective-permute-start.13 = (bf16[1,128,640]{2,1,0:T(8,128)(2,1)S(1)}, bf16[1,128,640]{2,1,0:T(8,128)(2,1)S(1)}, u32[]{:S(2)}, u32[]{:S(2)}) collective-permute-start(bf16[1,128,640]{2,1,0:T(8,128)(2,1)S(1)} %constant_dynamic-slice_fusion), channel_id=1, source_target_pairs={{1,3},{3,1},{5,7},{7,5},{9,11},{11,9},{13,15},{15,13},{17,19},{19,... | collective-permute-start | bytes 491528 | tf_op jit(solution)/shard_map/ppermute | solution.py:255
  96.3 1.3 %collective-permute-start.12 = (bf16[1,128,640]{2,1,0:T(8,128)(2,1)S(1)}, bf16[1,128,640]{2,1,0:T(8,128)(2,1)S(1)}, u32[]{:S(2)}, u32[]{:S(2)}) collective-permute-start(bf16[1,128,640]{2,1,0:T(8,128)(2,1)S(1)} %get-tuple-element.14), channel_id=1, source_target_pairs={{1,2},{3,0},{5,6},{7,4},{9,10},{11,8},{13,14},{15,12},{17,18},{19,... | collective-permute-start | bytes 491528 | tf_op jit(solution)/shard_map/ppermute | solution.py:251
  (109 shorter events, 24.8 us)
Async XLA Ops:
  0.6 49.7 %copy-start = (bf16[1,640,1280]{2,1,0:T(8,128)(2,1)S(1)}, bf16[1,640,1280]{2,1,0:T(8,128)(2,1)}, u32[]{:S(2)}) copy-start(bf16[1,640,1280]{2,1,0:T(8,128)(2,1)} %param.15) | copy-start | bytes 4915204
  0.6 3.7 %copy-start.1 = (bf16[2,64,4096]{2,1,0:T(8,128)(2,1)S(1)}, bf16[2,64,4096]{2,1,0:T(8,128)(2,1)}, u32[]{:S(2)}) copy-start(bf16[2,64,4096]{2,1,0:T(8,128)(2,1)} %param.8) | copy-start | bytes 3145732
  0.7 9.1 %copy-start.2 = (bf16[1,1280]{1,0:T(2,128)(2,1)S(1)}, bf16[1,1280]{1,0:T(2,128)(2,1)}, u32[]{:S(2)}) copy-start(bf16[1,1280]{1,0:T(2,128)(2,1)} %param.11) | copy-start | bytes 7684
  4.9 11.6 %collective-permute-start = (f32[2,64,34]{1,0,2:T(2,128)S(1)}, f32[2,64,34]{1,0,2:T(2,128)S(1)}, u32[]{:S(2)}, u32[]{:S(2)}) collective-permute-start(f32[2,64,34]{1,0,2:T(2,128)S(1)} %pad_maximum_fusion.4), channel_id=1, source_target_pairs={{0,4},{4,8},{8,12},{12,0},{1,5},{5,9},{9,13},{13,1},{2,6},{6,10},{... | collective-permute-start | bytes 52232 | tf_op jit(solution)/shard_map/ppermute | solution.py:13
  7.1 9.5 %collective-permute-start.2 = (f32[2,64,34]{1,0,2:T(2,128)S(1)}, f32[2,64,34]{1,0,2:T(2,128)S(1)}, u32[]{:S(2)}, u32[]{:S(2)}) collective-permute-start(f32[2,64,34]{1,0,2:T(2,128)S(1)} %pad_maximum_fusion.4), channel_id=1, source_target_pairs={{0,12},{4,0},{8,4},{12,8},{1,13},{5,1},{9,5},{13,9},{2,14},{6,2},{... | collective-permute-start | bytes 52232 | tf_op jit(solution)/shard_map/ppermute | solution.py:13
  9.2 7.5 %collective-permute-start.1 = (f32[2,64,34]{1,0,2:T(2,128)S(1)}, f32[2,64,34]{1,0,2:T(2,128)S(1)}, u32[]{:S(2)}, u32[]{:S(2)}) collective-permute-start(f32[2,64,34]{1,0,2:T(2,128)S(1)} %pad_maximum_fusion.4), channel_id=1, source_target_pairs={{0,8},{4,12},{8,0},{12,4},{1,9},{5,13},{9,1},{13,5},{2,10},{6,14},... | collective-permute-start | bytes 52232 | tf_op jit(solution)/shard_map/ppermute | solution.py:13
  39.5 1.8 %copy-start.6 = (bf16[1,1280,160]{1,2,0:T(8,128)(2,1)S(1)}, bf16[1,1280,160]{1,2,0:T(8,128)(2,1)}, u32[]{:S(2)}) copy-start(bf16[1,1280,160]{1,2,0:T(8,128)(2,1)} %param.14) | copy-start | bytes 1228804
  39.7 6.1 %copy-start.3 = (bf16[1,1280,640]{2,1,0:T(8,128)(2,1)S(1)}, bf16[1,1280,640]{2,1,0:T(8,128)(2,1)}, u32[]{:S(2)}) copy-start(bf16[1,1280,640]{2,1,0:T(8,128)(2,1)} %param.12) | copy-start | bytes 4915204
  42.4 4.3 %collective-permute-start.5 = (bf16[2,2,2,80,128]{4,3,2,1,0:T(8,128)(2,1)}, bf16[2,2,2,80,128]{4,3,2,1,0:T(8,128)(2,1)S(1)}, u32[]{:S(2)}, u32[]{:S(2)}) collective-permute-start(bf16[2,2,2,80,128]{4,3,2,1,0:T(8,128)(2,1)} %pad_maximum_fusion.2), channel_id=1, source_target_pairs={{0,4},{4,8},{8,12},{2,6},{6,10},{10,14},{16,20},{20,24},{24,28},{1... | collective-permute-start | bytes 491528 | tf_op jit(solution)/shard_map/ppermute | solution.py:34
  43.1 3.6 %collective-permute-start.4 = (bf16[2,2,2,80,128]{4,3,2,1,0:T(8,128)(2,1)}, bf16[2,2,2,80,128]{4,3,2,1,0:T(8,128)(2,1)}, u32[]{:S(2)}, u32[]{:S(2)}) collective-permute-start(bf16[2,2,2,80,128]{4,3,2,1,0:T(8,128)(2,1)} %pad_maximum_fusion.2), channel_id=1, source_target_pairs={{0,8},{4,12},{2,10},{6,14},{16,24},{20,28},{18,26},{22,30}} | collective-permute-start | bytes 491528 | tf_op jit(solution)/shard_map/ppermute | solution.py:34
  44.4 2.3 %collective-permute-start.3 = (bf16[2,2,2,80,128]{4,3,2,1,0:T(8,128)(2,1)}, bf16[2,2,2,80,128]{4,3,2,1,0:T(8,128)(2,1)}, u32[]{:S(2)}, u32[]{:S(2)}) collective-permute-start(bf16[2,2,2,80,128]{4,3,2,1,0:T(8,128)(2,1)} %pad_maximum_fusion.2), channel_id=1, source_target_pairs={{0,12},{2,14},{16,28},{18,30}} | collective-permute-start | bytes 491528 | tf_op jit(solution)/shard_map/ppermute | solution.py:34
  51.9 18.7 %copy-start.5 = (bf16[1,1280,160]{1,2,0:T(8,128)(2,1)S(1)}, bf16[1,1280,160]{1,2,0:T(8,128)(2,1)}, u32[]{:S(2)}) copy-start(bf16[1,1280,160]{1,2,0:T(8,128)(2,1)} %param.13) | copy-start | bytes 1228804
  51.9 17.0 %collective-permute-start.7 = (bf16[2,128,1280]{2,1,0:T(8,128)(2,1)}, bf16[2,128,1280]{2,1,0:T(8,128)(2,1)}, u32[]{:S(2)}, u32[]{:S(2)}) collective-permute-start(bf16[2,128,1280]{2,1,0:T(8,128)(2,1)} %convolution_convert_fusion.1), channel_id=1, source_target_pairs={{0,3},{2,1},{4,7},{6,5},{8,11},{10,9},{12,15},{14,13},{16,19},{18,... | collective-permute-start | bytes 1966088 | tf_op jit(solution)/shard_map/ppermute | solution.py:225
  53.3 15.6 %collective-permute-start.6 = (bf16[2,128,1280]{2,1,0:T(8,128)(2,1)}, bf16[2,128,1280]{2,1,0:T(8,128)(2,1)}, u32[]{:S(2)}, u32[]{:S(2)}) collective-permute-start(bf16[2,128,1280]{2,1,0:T(8,128)(2,1)} %convolution_convert_fusion.1), channel_id=1, source_target_pairs={{0,1},{2,3},{4,5},{6,7},{8,9},{10,11},{12,13},{14,15},{16,17},{18,... | collective-permute-start | bytes 1966088 | tf_op jit(solution)/shard_map/ppermute | solution.py:225
  54.7 16.4 %copy-start.7 = (bf16[1,1280,160]{1,2,0:T(8,128)(2,1)S(1)}, bf16[1,1280,160]{1,2,0:T(8,128)(2,1)}, u32[]{:S(2)}) copy-start(bf16[1,1280,160]{1,2,0:T(8,128)(2,1)} %param.14) | copy-start | bytes 1228804
  70.6 1.4 %copy-start.4 = (bf16[1,1280,640]{2,1,0:T(8,128)(2,1)S(1)}, bf16[1,1280,640]{2,1,0:T(8,128)(2,1)}, u32[]{:S(2)}) copy-start(bf16[1,1280,640]{2,1,0:T(8,128)(2,1)} %param.12) | copy-start | bytes 4915204
  74.2 13.1 %collective-permute-start.10 = (bf16[2,2,2,80,128]{4,3,2,1,0:T(8,128)(2,1)}, bf16[2,2,2,80,128]{4,3,2,1,0:T(8,128)(2,1)S(1)}, u32[]{:S(2)}, u32[]{:S(2)}) collective-permute-start(bf16[2,2,2,80,128]{4,3,2,1,0:T(8,128)(2,1)} %pad_maximum_fusion.3), channel_id=1, source_target_pairs={{1,5},{5,9},{9,13},{3,7},{7,11},{11,15},{17,21},{21,25},{25,29},{1... | collective-permute-start | bytes 491528 | tf_op jit(solution)/shard_map/ppermute | solution.py:34
  77.8 9.5 %collective-permute-start.9 = (bf16[2,2,2,80,128]{4,3,2,1,0:T(8,128)(2,1)}, bf16[2,2,2,80,128]{4,3,2,1,0:T(8,128)(2,1)}, u32[]{:S(2)}, u32[]{:S(2)}) collective-permute-start(bf16[2,2,2,80,128]{4,3,2,1,0:T(8,128)(2,1)} %pad_maximum_fusion.3), channel_id=1, source_target_pairs={{1,9},{5,13},{3,11},{7,15},{17,25},{21,29},{19,27},{23,31}} | collective-permute-start | bytes 491528 | tf_op jit(solution)/shard_map/ppermute | solution.py:34
  83.4 3.9 %collective-permute-start.8 = (bf16[2,2,2,80,128]{4,3,2,1,0:T(8,128)(2,1)}, bf16[2,2,2,80,128]{4,3,2,1,0:T(8,128)(2,1)}, u32[]{:S(2)}, u32[]{:S(2)}) collective-permute-start(bf16[2,2,2,80,128]{4,3,2,1,0:T(8,128)(2,1)} %pad_maximum_fusion.3), channel_id=1, source_target_pairs={{1,13},{3,15},{17,29},{19,31}} | collective-permute-start | bytes 491528 | tf_op jit(solution)/shard_map/ppermute | solution.py:34
  91.8 8.5 %collective-permute-start.11 = (bf16[2,1,128,640]{3,2,1,0:T(8,128)(2,1)S(1)}, bf16[2,1,128,640]{3,2,1,0:T(8,128)(2,1)S(1)}, u32[]{:S(2)}, u32[]{:S(2)}) collective-permute-start(bf16[2,1,128,640]{3,2,1,0:T(8,128)(2,1)S(1)} %pad_maximum_fusion.1), channel_id=1, source_target_pairs={{1,0},{3,2},{5,4},{7,6},{9,8},{11,10},{13,12},{15,14},{17,16},{19,... | collective-permute-start | bytes 983048 | tf_op jit(solution)/shard_map/ppermute | solution.py:251
  93.1 6.1 %collective-permute-start.13 = (bf16[1,128,640]{2,1,0:T(8,128)(2,1)S(1)}, bf16[1,128,640]{2,1,0:T(8,128)(2,1)S(1)}, u32[]{:S(2)}, u32[]{:S(2)}) collective-permute-start(bf16[1,128,640]{2,1,0:T(8,128)(2,1)S(1)} %constant_dynamic-slice_fusion), channel_id=1, source_target_pairs={{1,3},{3,1},{5,7},{7,5},{9,11},{11,9},{13,15},{15,13},{17,19},{19,... | collective-permute-start | bytes 491528 | tf_op jit(solution)/shard_map/ppermute | solution.py:255
  96.3 4.0 %collective-permute-start.12 = (bf16[1,128,640]{2,1,0:T(8,128)(2,1)S(1)}, bf16[1,128,640]{2,1,0:T(8,128)(2,1)S(1)}, u32[]{:S(2)}, u32[]{:S(2)}) collective-permute-start(bf16[1,128,640]{2,1,0:T(8,128)(2,1)S(1)} %get-tuple-element.14), channel_id=1, source_target_pairs={{1,2},{3,0},{5,6},{7,4},{9,10},{11,8},{13,14},{15,12},{17,18},{19,... | collective-permute-start | bytes 491528 | tf_op jit(solution)/shard_map/ppermute | solution.py:251

commit v12 on v11

--- a/solution.py
+++ b/solution.py
@@ -191,7 +191,7 @@
         (padded * padded_valid - channel_mean[..., None]) * padded_valid * inv_std
     ).astype(jnp.bfloat16)
     kernel = patch_weight.reshape(channels, 2 * STRIDE, patch_weight.shape[1])
-    chunk_tok = 32 if tok_count % 32 == 0 else tok_count
+    chunk_tok = 64 if tok_count % 64 == 0 else tok_count
     chunk_count = tok_count // chunk_tok
     chunks = jnp.stack(
         [

time: 103 us -> 113 us (1.097)
  local copies, waits for them, and re-layouts: 12.6 us -> 21.1 us
  waiting for transfers between devices: 16.3 us -> 18.5 us
  other arithmetic: 17.5 us -> 19 us
  starting transfers between devices: 27.7 us -> 26.2 us
    conv_general_dilated x0 -> x3, local copies, waits for them, and re-layouts: none -> 10.7 us  [per_device(): lax.conv_general_dilated(chunks, kernel, window_strides=(STRIDE,), paddin...]
    another operation x2 -> x1, local copies, waits for them, and re-layouts: 3.28 us -> 0.09 us  [per_device(): jnp.stack([normed[:, :, q * chunk_tok * STRIDE:(q + 1) * chunk_tok * STRI...]
    ppermute x2, waiting for transfers between devices: 14.2 us -> 16.2 us  [per_device(): term = lax.ppermute(partial0, feat_axes, pairs).astype(jnp.float32)]
    conv_general_dilated x0 -> x1, other arithmetic: none -> 1.57 us  [per_device(): lax.conv_general_dilated(chunks, kernel, window_strides=(STRIDE,), paddin...]
    ppermute x6, starting transfers between devices: 14.5 us -> 13 us  [gather_causal(): pieces.append(lax.ppermute(value, ('tm', 'section'), pairs))]
    ppermute x1, waiting for transfers between devices: 0.91 us -> 2.26 us  [per_device(): to_high.append(lax.ppermute(cols_high, feat_axes, pairs))]
    unnamed x18 -> x20, local copies, waits for them, and re-layouts: 5.17 us -> 4.68 us
  transfers between devices with their start and end apart: 14 -> 14, of which waited for: 3 -> 3; matrix products, arithmetic and copies ran while one was open for 10% -> 11% of each run, Pallas kernels for 0% -> 0%
where the time goes in v12:
time: 113 us; the launch traced here: 112 us
  starting transfers between devices  26.2 us (23%)
  local copies, waits for them, and re-layouts  21.1 us (19%)
  other arithmetic  19 us (17%)
  waiting for transfers between devices  18.5 us (16%)
  matrix products  16.6 us (15%)
  blocking collectives  9.25 us (8%)
  between operations  1.24 us (1%)
    ppermute x2, waiting for transfers between devices, per_device(): term = lax.ppermute(partial0, feat_axes, pairs).astype(jnp.float32)  16.2 us
    ppermute x6, starting transfers between devices, gather_causal(): pieces.append(lax.ppermute(value, ('tm', 'section'), pairs))  13 us
    conv_general_dilated x3, local copies, waits for them, and re-layouts, per_device(): lax.conv_general_dilated(chunks, kernel, window_strides=(STRIDE,), paddin...  10.7 us
    all_gather x1, blocking collectives, per_device(): hidden0 = lax.all_gather(tokens, feat_axes, axis=2, tiled=True)  9.25 us
    conv_general_dilated x1, matrix products, per_device(): lax.conv_general_dilated(chunks, kernel, window_strides=(STRIDE,), paddin...  5.74 us
    unnamed x20, local copies, waits for them, and re-layouts  4.68 us
    ppermute x3, starting transfers between devices, shift_from(): return lax.ppermute(value, axis, pairs)  4.66 us
    ppermute x1, starting transfers between devices, per_device(): to_high.append(lax.ppermute(cols_high, feat_axes, pairs))  3.14 us
  transfers between devices with their start and end apart: 14, of which 3 were waited for; matrix products, arithmetic and copies ran while one was open for 11% of the time, Pallas kernels for 0%

profile of v12, /device:TPU:1, one launch (start us, length us, event | category | flops | bytes accessed | tf_op | source)
XLA Modules:
  0.0 111.9 jit_solution(3282141993256011217)
XLA Ops:
  2.7 1.5 %multiply_reduce_fusion.1 = f32[2,64]{1,0:T(2,128)S(1)} fusion(f32[2,4096]{1,0:T(2,128)S(1)} %compare_convert_fusion, bf16[2,64,4096]{2,1,0:T(8,128)(2,1)} %param.8), kind=kLoop, calls=%fused_computation.30 | loop fusion | flops 1572736 | bytes 1081856 | tf_op jit(solution)/shard_map/reduce_sum | solution.py:151
  4.9 2.2 %collective-permute-start = (f32[2,64,34]{1,0,2:T(2,128)S(1)}, f32[2,64,34]{1,0,2:T(2,128)S(1)}, u32[]{:S(2)}, u32[]{:S(2)}) collective-permute-start(f32[2,64,34]{1,0,2:T(2,128)S(1)} %pad_maximum_fusion.4), channel_id=1, source_target_pairs={{0,4},{4,8},{8,12},{12,0},{1,5},{5,9},{9,13},{13,1},{2,6},{6,10},{... | collective-permute-start | bytes 52232 | tf_op jit(solution)/shard_map/ppermute | solution.py:13
  7.1 2.1 %collective-permute-start.2 = (f32[2,64,34]{1,0,2:T(2,128)S(1)}, f32[2,64,34]{1,0,2:T(2,128)S(1)}, u32[]{:S(2)}, u32[]{:S(2)}) collective-permute-start(f32[2,64,34]{1,0,2:T(2,128)S(1)} %pad_maximum_fusion.4), channel_id=1, source_target_pairs={{0,12},{4,0},{8,4},{12,8},{1,13},{5,1},{9,5},{13,9},{2,14},{6,2},{... | collective-permute-start | bytes 52232 | tf_op jit(solution)/shard_map/ppermute | solution.py:13
  10.4 1.6 %convert_element_type.167 = f32[2,64,4096]{2,1,0:T(8,128)} convert(bf16[2,64,4096]{2,1,0:T(8,128)(2,1)S(1)} %copy-done.1) | non-fusion elementwise | flops 524288 | bytes 3145728 | tf_op jit(solution)/shard_map/convert_element_type | solution.py:149
  12.0 4.5 %copy.40 = bf16[4096,320]{1,0:T(8,128)(2,1)} copy(bf16[4096,320]{0,1:T(8,128)(2,1)} %param.10) | data formatting | bytes 5242880 | tf_op args[2]
  17.6 2.3 %fusion.13 = bf16[2,64,4128]{2,1,0:T(8,128)(2,1)S(1)} fusion(f32[2,64,4096]{2,1,0:T(8,128)} %convert_element_type.167, f32[2,64,32]{2,1,0:T(8,128)S(1)} %copy.36, f32[2,64]{1,0:T(2,128)S(1)} %add_rsqrt_fusion.2, f32[2,64]{1,0:T(2,128)S(1)} %broadcast_divide_fusion, f32[2,4128]{1,0:T(2,128)S(1)} %and_convert_fusion), kind=kLoop, calls=%fused_computation.22 | loop fusion | flops 3170304 | bytes 3204352 | tf_op jit(solution)/shard_map/convert_element_type | solution.py:192
  21.2 3.6 %reshape.534 = bf16[64,4,8,288]{3,2,0,1:T(8,128)(2,1)S(1)} reshape(bf16[64,4,2304]{2,0,1:T(8,128)(2,1)} %pad) | data formatting | bytes 2359296 | tf_op jit(solution)/shard_map/conv_general_dilated | solution.py:203
  25.0 1.6 %fusion.30 = bf16[64,4,8,351]{3,2,0,1:T(8,128)(2,1)} fusion(bf16[64,4,7,63]{3,2,0,1:T(8,128)(2,1)S(1)} %slice.88, bf16[64,4,8,288]{3,2,0,1:T(8,128)(2,1)S(1)} %reshape.534), kind=kLoop, calls=%fused_computation.44 | loop fusion | flops 4313088 | bytes 2843136 | tf_op jit(solution)/shard_map/conv_general_dilated | solution.py:203
  26.6 7.0 %copy.39 = bf16[64,4,8,351]{0,2,1,3:T(8,128)(2,1)} copy(bf16[64,4,8,351]{3,2,0,1:T(8,128)(2,1)} %fusion.30) | data formatting | bytes 2875392 | tf_op jit(solution)/shard_map/conv_general_dilated | solution.py:203
  33.6 5.7 %fusion.67 = bf16[32,9,320]{2,0,1:T(8,128)(2,1)S(1)} fusion(bf16[64,64,320]{2,1,0:T(8,128)(2,1)} %bitcast.218, bf16[64,4,8,351]{0,2,1,3:T(8,128)(2,1)} %copy.39, pred[32,9]{0,1:T(8,128)(4,1)S(1)} %copy-done.8), kind=kOutput, calls=%fused_computation.61 | convolution fusion | flops 755159040 | bytes 4243744 | tf_op jit(solution)/shard_map/conv_general_dilated | solution.py:203
  39.8 9.2 %all_gather.3 = bf16[2,128,1280]{1,0,2:T(2,128)(2,1)S(1)} all-gather(bf16[2,128,320]{1,0,2:T(2,128)(2,1)S(1)} %copy.43), channel_id=1, replica_groups=mesh['groups'=2,'tm'=4,'mp'=2,'section'=2] {'mp','section'}, dimensions={2}, use_global_device_ids=true | all-gather | bytes 819200 | tf_op jit(solution)/shard_map/all_gather | solution.py:213
  50.2 1.6 %convolution_convert_fusion.4 = bf16[2,128,160]{1,2,0:T(8,128)(2,1)S(1)} fusion(bf16[1,1280,160]{1,2,0:T(8,128)(2,1)} %param.14, bf16[2,128,1280]{2,1,0:T(8,128)(2,1)S(1)} %copy.44, f32[1280]{0:T(1024)S(1)} %convert_reduce_fusion, f32[2,128]{1,0:T(2,128)S(1)} %add_rsqrt_fusion.1), kind=kOutput, calls=%fused_computation.64 | convolution fusion | flops 106209280 | bytes 1153024 | tf_op jit(solution)/shard_map/btd,de->bet/dot_general | solution.py:78
  53.6 1.3 %collective-permute-start.4 = (bf16[2,2,2,80,128]{4,3,2,1,0:T(8,128)(2,1)}, bf16[2,2,2,80,128]{4,3,2,1,0:T(8,128)(2,1)}, u32[]{:S(2)}, u32[]{:S(2)}) collective-permute-start(bf16[2,2,2,80,128]{4,3,2,1,0:T(8,128)(2,1)} %pad_maximum_fusion.2), channel_id=1, source_target_pairs={{0,8},{4,12},{2,10},{6,14},{16,24},{20,28},{18,26},{22,30}} | collective-permute-start | bytes 491528 | tf_op jit(solution)/shard_map/ppermute | solution.py:34
  60.8 1.6 %convolution_convert_fusion.1 = bf16[2,128,1280]{2,1,0:T(8,128)(2,1)} fusion(bf16[2,128,640]{1,2,0:T(8,128)(2,1)S(1)} %bitcast.235, bf16[1,640,1280]{2,1,0:T(8,128)(2,1)S(1)} %copy-done), kind=kOutput, calls=%fused_computation.17 | convolution fusion | flops 419758080 | bytes 2621440 | tf_op jit(solution)/shard_map/bte,ed->btd/dot_general | solution.py:128
  62.4 1.4 %collective-permute-start.6 = (bf16[2,128,1280]{2,1,0:T(8,128)(2,1)}, bf16[2,128,1280]{2,1,0:T(8,128)(2,1)}, u32[]{:S(2)}, u32[]{:S(2)}) collective-permute-start(bf16[2,128,1280]{2,1,0:T(8,128)(2,1)} %convolution_convert_fusion.1), channel_id=1, source_target_pairs={{0,1},{2,3},{4,5},{6,7},{8,9},{10,11},{12,13},{14,15},{16,17},{18,... | collective-permute-start | bytes 1966088 | tf_op jit(solution)/shard_map/ppermute | solution.py:225
  65.2 7.2 %collective-permute-done.6 = bf16[2,128,1280]{2,1,0:T(8,128)(2,1)} collective-permute-done((bf16[2,128,1280]{2,1,0:T(8,128)(2,1)}, bf16[2,128,1280]{2,1,0:T(8,128)(2,1)}, u32[]{:S(2)}, u32[]{:S(2)}) %collective-permute-start.6) | collective-permute-done | bytes 655392 | tf_op jit(solution)/shard_map/ppermute | solution.py:225
  72.4 8.9 %collective-permute-done.7 = bf16[2,128,1280]{2,1,0:T(8,128)(2,1)} collective-permute-done((bf16[2,128,1280]{2,1,0:T(8,128)(2,1)}, bf16[2,128,1280]{2,1,0:T(8,128)(2,1)}, u32[]{:S(2)}, u32[]{:S(2)}) %collective-permute-start.7) | collective-permute-done | bytes 655392 | tf_op jit(solution)/shard_map/ppermute | solution.py:225
  81.4 1.7 %fusion.31 = (f32[2,128]{1,0:T(2,128)S(1)}, bf16[2,128,1280]{2,1,0:T(8,128)(2,1)S(1)}) fusion(bf16[2,128,1280]{2,1,0:T(8,128)(2,1)} %collective-permute-done.7, bf16[2,128,1280]{2,1,0:T(8,128)(2,1)} %collective-permute-done.6, bf16[2,128,1280]{2,1,0:T(8,128)(2,1)S(1)} %copy.44), kind=kLoop, calls=%fused_computation.45 | loop fusion | flops 2948864 | bytes 2622464 | tf_op jit(solution)/shard_map/reduce_sum | solution.py:69
  84.7 4.1 %collective-permute-start.10 = (bf16[2,2,2,80,128]{4,3,2,1,0:T(8,128)(2,1)}, bf16[2,2,2,80,128]{4,3,2,1,0:T(8,128)(2,1)S(1)}, u32[]{:S(2)}, u32[]{:S(2)}) collective-permute-start(bf16[2,2,2,80,128]{4,3,2,1,0:T(8,128)(2,1)} %pad_maximum_fusion.3), channel_id=1, source_target_pairs={{1,5},{5,9},{9,13},{3,7},{7,11},{11,15},{17,21},{21,25},{25,29},{1... | collective-permute-start | bytes 491528 | tf_op jit(solution)/shard_map/ppermute | solution.py:34
  88.8 2.8 %collective-permute-start.8 = (bf16[2,2,2,80,128]{4,3,2,1,0:T(8,128)(2,1)}, bf16[2,2,2,80,128]{4,3,2,1,0:T(8,128)(2,1)}, u32[]{:S(2)}, u32[]{:S(2)}) collective-permute-start(bf16[2,2,2,80,128]{4,3,2,1,0:T(8,128)(2,1)} %pad_maximum_fusion.3), channel_id=1, source_target_pairs={{1,13},{3,15},{17,29},{19,31}} | collective-permute-start | bytes 491528 | tf_op jit(solution)/shard_map/ppermute | solution.py:34
  91.6 2.8 %collective-permute-start.9 = (bf16[2,2,2,80,128]{4,3,2,1,0:T(8,128)(2,1)}, bf16[2,2,2,80,128]{4,3,2,1,0:T(8,128)(2,1)}, u32[]{:S(2)}, u32[]{:S(2)}) collective-permute-start(bf16[2,2,2,80,128]{4,3,2,1,0:T(8,128)(2,1)} %pad_maximum_fusion.3), channel_id=1, source_target_pairs={{1,9},{5,13},{3,11},{7,15},{17,25},{21,29},{19,27},{23,31}} | collective-permute-start | bytes 491528 | tf_op jit(solution)/shard_map/ppermute | solution.py:34
  94.5 1.5 %fusion.56 = bf16[2,128,640]{2,1,0:T(8,128)(2,1)} fusion(bf16[1,1280,640]{2,1,0:T(8,128)(2,1)S(1)} %copy-done.4, bf16[2,128,1280]{2,1,0:T(8,128)(2,1)S(1)} %get-tuple-element.4, f32[2,128]{1,0:T(2,128)S(1)} %add_rsqrt_fusion, f32[1280]{0:T(1024)S(1)} %convert_reduce_fusion), kind=kOutput, calls=%fused_computation.58 | convolution fusion | flops 421068800 | bytes 2627584 | tf_op jit(solution)/shard_map/btd,de->bte/dot_general | solution.py:72
  105.0 3.1 %collective-permute-start.13 = (bf16[1,128,640]{2,1,0:T(8,128)(2,1)S(1)}, bf16[1,128,640]{2,1,0:T(8,128)(2,1)S(1)}, u32[]{:S(2)}, u32[]{:S(2)}) collective-permute-start(bf16[1,128,640]{2,1,0:T(8,128)(2,1)S(1)} %constant_dynamic-slice_fusion), channel_id=1, source_target_pairs={{1,3},{3,1},{5,7},{7,5},{9,11},{11,9},{13,15},{15,13},{17,19},{19,... | collective-permute-start | bytes 491528 | tf_op jit(solution)/shard_map/ppermute | solution.py:255
  108.8 2.3 %collective-permute-done.13 = bf16[1,128,640]{2,1,0:T(8,128)(2,1)S(1)} collective-permute-done((bf16[1,128,640]{2,1,0:T(8,128)(2,1)S(1)}, bf16[1,128,640]{2,1,0:T(8,128)(2,1)S(1)}, u32[]{:S(2)}, u32[]{:S(2)}) %collective-permute-start.13) | collective-permute-done | bytes 163872 | tf_op jit(solution)/shard_map/ppermute | solution.py:255
  (117 shorter events, 28.9 us)
Async XLA Ops:
  0.6 60.2 %copy-start = (bf16[1,640,1280]{2,1,0:T(8,128)(2,1)S(1)}, bf16[1,640,1280]{2,1,0:T(8,128)(2,1)}, u32[]{:S(2)}) copy-start(bf16[1,640,1280]{2,1,0:T(8,128)(2,1)} %param.15) | copy-start | bytes 4915204
  0.6 3.6 %copy-start.1 = (bf16[2,64,4096]{2,1,0:T(8,128)(2,1)S(1)}, bf16[2,64,4096]{2,1,0:T(8,128)(2,1)}, u32[]{:S(2)}) copy-start(bf16[2,64,4096]{2,1,0:T(8,128)(2,1)} %param.8) | copy-start | bytes 3145732
  0.7 9.1 %copy-start.2 = (bf16[1,1280]{1,0:T(2,128)(2,1)S(1)}, bf16[1,1280]{1,0:T(2,128)(2,1)}, u32[]{:S(2)}) copy-start(bf16[1,1280]{1,0:T(2,128)(2,1)} %param.11) | copy-start | bytes 7684
  4.9 11.6 %collective-permute-start = (f32[2,64,34]{1,0,2:T(2,128)S(1)}, f32[2,64,34]{1,0,2:T(2,128)S(1)}, u32[]{:S(2)}, u32[]{:S(2)}) collective-permute-start(f32[2,64,34]{1,0,2:T(2,128)S(1)} %pad_maximum_fusion.4), channel_id=1, source_target_pairs={{0,4},{4,8},{8,12},{12,0},{1,5},{5,9},{9,13},{13,1},{2,6},{6,10},{... | collective-permute-start | bytes 52232 | tf_op jit(solution)/shard_map/ppermute | solution.py:13
  7.1 9.4 %collective-permute-start.2 = (f32[2,64,34]{1,0,2:T(2,128)S(1)}, f32[2,64,34]{1,0,2:T(2,128)S(1)}, u32[]{:S(2)}, u32[]{:S(2)}) collective-permute-start(f32[2,64,34]{1,0,2:T(2,128)S(1)} %pad_maximum_fusion.4), channel_id=1, source_target_pairs={{0,12},{4,0},{8,4},{12,8},{1,13},{5,1},{9,5},{13,9},{2,14},{6,2},{... | collective-permute-start | bytes 52232 | tf_op jit(solution)/shard_map/ppermute | solution.py:13
  9.2 7.4 %collective-permute-start.1 = (f32[2,64,34]{1,0,2:T(2,128)S(1)}, f32[2,64,34]{1,0,2:T(2,128)S(1)}, u32[]{:S(2)}, u32[]{:S(2)}) collective-permute-start(f32[2,64,34]{1,0,2:T(2,128)S(1)} %pad_maximum_fusion.4), channel_id=1, source_target_pairs={{0,8},{4,12},{8,0},{12,4},{1,9},{5,13},{9,1},{13,5},{2,10},{6,14},... | collective-permute-start | bytes 52232 | tf_op jit(solution)/shard_map/ppermute | solution.py:13
  26.5 7.0 %copy-start.8 = (pred[32,9]{0,1:T(8,128)(4,1)S(1)}, pred[32,9]{0,1:T(8,128)(4,1)}, u32[]{:S(2)}) copy-start(pred[32,9]{0,1:T(8,128)(4,1)} %constant.128) | copy-start | bytes 868
  50.0 1.8 %copy-start.6 = (bf16[1,1280,160]{1,2,0:T(8,128)(2,1)S(1)}, bf16[1,1280,160]{1,2,0:T(8,128)(2,1)}, u32[]{:S(2)}) copy-start(bf16[1,1280,160]{1,2,0:T(8,128)(2,1)} %param.13) | copy-start | bytes 1228804
  50.2 6.1 %copy-start.3 = (bf16[1,1280,640]{2,1,0:T(8,128)(2,1)S(1)}, bf16[1,1280,640]{2,1,0:T(8,128)(2,1)}, u32[]{:S(2)}) copy-start(bf16[1,1280,640]{2,1,0:T(8,128)(2,1)} %param.12) | copy-start | bytes 4915204
  52.9 4.3 %collective-permute-start.3 = (bf16[2,2,2,80,128]{4,3,2,1,0:T(8,128)(2,1)}, bf16[2,2,2,80,128]{4,3,2,1,0:T(8,128)(2,1)S(1)}, u32[]{:S(2)}, u32[]{:S(2)}) collective-permute-start(bf16[2,2,2,80,128]{4,3,2,1,0:T(8,128)(2,1)} %pad_maximum_fusion.2), channel_id=1, source_target_pairs={{0,12},{2,14},{16,28},{18,30}} | collective-permute-start | bytes 491528 | tf_op jit(solution)/shard_map/ppermute | solution.py:34
  53.6 3.6 %collective-permute-start.4 = (bf16[2,2,2,80,128]{4,3,2,1,0:T(8,128)(2,1)}, bf16[2,2,2,80,128]{4,3,2,1,0:T(8,128)(2,1)}, u32[]{:S(2)}, u32[]{:S(2)}) collective-permute-start(bf16[2,2,2,80,128]{4,3,2,1,0:T(8,128)(2,1)} %pad_maximum_fusion.2), channel_id=1, source_target_pairs={{0,8},{4,12},{2,10},{6,14},{16,24},{20,28},{18,26},{22,30}} | collective-permute-start | bytes 491528 | tf_op jit(solution)/shard_map/ppermute | solution.py:34
  54.9 2.3 %collective-permute-start.5 = (bf16[2,2,2,80,128]{4,3,2,1,0:T(8,128)(2,1)}, bf16[2,2,2,80,128]{4,3,2,1,0:T(8,128)(2,1)}, u32[]{:S(2)}, u32[]{:S(2)}) collective-permute-start(bf16[2,2,2,80,128]{4,3,2,1,0:T(8,128)(2,1)} %pad_maximum_fusion.2), channel_id=1, source_target_pairs={{0,4},{4,8},{8,12},{2,6},{6,10},{10,14},{16,20},{20,24},{24,28},{1... | collective-permute-start | bytes 491528 | tf_op jit(solution)/shard_map/ppermute | solution.py:34
  62.4 20.7 %copy-start.5 = (bf16[1,1280,160]{1,2,0:T(8,128)(2,1)S(1)}, bf16[1,1280,160]{1,2,0:T(8,128)(2,1)}, u32[]{:S(2)}) copy-start(bf16[1,1280,160]{1,2,0:T(8,128)(2,1)} %param.14) | copy-start | bytes 1228804
  62.4 10.0 %collective-permute-start.6 = (bf16[2,128,1280]{2,1,0:T(8,128)(2,1)}, bf16[2,128,1280]{2,1,0:T(8,128)(2,1)}, u32[]{:S(2)}, u32[]{:S(2)}) collective-permute-start(bf16[2,128,1280]{2,1,0:T(8,128)(2,1)} %convolution_convert_fusion.1), channel_id=1, source_target_pairs={{0,1},{2,3},{4,5},{6,7},{8,9},{10,11},{12,13},{14,15},{16,17},{18,... | collective-permute-start | bytes 1966088 | tf_op jit(solution)/shard_map/ppermute | solution.py:225
  63.8 17.5 %collective-permute-start.7 = (bf16[2,128,1280]{2,1,0:T(8,128)(2,1)}, bf16[2,128,1280]{2,1,0:T(8,128)(2,1)}, u32[]{:S(2)}, u32[]{:S(2)}) collective-permute-start(bf16[2,128,1280]{2,1,0:T(8,128)(2,1)} %convolution_convert_fusion.1), channel_id=1, source_target_pairs={{0,3},{2,1},{4,7},{6,5},{8,11},{10,9},{12,15},{14,13},{16,19},{18,... | collective-permute-start | bytes 1966088 | tf_op jit(solution)/shard_map/ppermute | solution.py:225
  65.2 18.4 %copy-start.7 = (bf16[1,1280,160]{1,2,0:T(8,128)(2,1)S(1)}, bf16[1,1280,160]{1,2,0:T(8,128)(2,1)}, u32[]{:S(2)}) copy-start(bf16[1,1280,160]{1,2,0:T(8,128)(2,1)} %param.13) | copy-start | bytes 1228804
  83.1 11.4 %copy-start.4 = (bf16[1,1280,640]{2,1,0:T(8,128)(2,1)S(1)}, bf16[1,1280,640]{2,1,0:T(8,128)(2,1)}, u32[]{:S(2)}) copy-start(bf16[1,1280,640]{2,1,0:T(8,128)(2,1)} %param.12) | copy-start | bytes 4915204
  84.7 13.1 %collective-permute-start.10 = (bf16[2,2,2,80,128]{4,3,2,1,0:T(8,128)(2,1)}, bf16[2,2,2,80,128]{4,3,2,1,0:T(8,128)(2,1)S(1)}, u32[]{:S(2)}, u32[]{:S(2)}) collective-permute-start(bf16[2,2,2,80,128]{4,3,2,1,0:T(8,128)(2,1)} %pad_maximum_fusion.3), channel_id=1, source_target_pairs={{1,5},{5,9},{9,13},{3,7},{7,11},{11,15},{17,21},{21,25},{25,29},{1... | collective-permute-start | bytes 491528 | tf_op jit(solution)/shard_map/ppermute | solution.py:34
  88.8 9.0 %collective-permute-start.8 = (bf16[2,2,2,80,128]{4,3,2,1,0:T(8,128)(2,1)}, bf16[2,2,2,80,128]{4,3,2,1,0:T(8,128)(2,1)}, u32[]{:S(2)}, u32[]{:S(2)}) collective-permute-start(bf16[2,2,2,80,128]{4,3,2,1,0:T(8,128)(2,1)} %pad_maximum_fusion.3), channel_id=1, source_target_pairs={{1,13},{3,15},{17,29},{19,31}} | collective-permute-start | bytes 491528 | tf_op jit(solution)/shard_map/ppermute | solution.py:34
  91.6 6.2 %collective-permute-start.9 = (bf16[2,2,2,80,128]{4,3,2,1,0:T(8,128)(2,1)}, bf16[2,2,2,80,128]{4,3,2,1,0:T(8,128)(2,1)}, u32[]{:S(2)}, u32[]{:S(2)}) collective-permute-start(bf16[2,2,2,80,128]{4,3,2,1,0:T(8,128)(2,1)} %pad_maximum_fusion.3), channel_id=1, source_target_pairs={{1,9},{5,13},{3,11},{7,15},{17,25},{21,29},{19,27},{23,31}} | collective-permute-start | bytes 491528 | tf_op jit(solution)/shard_map/ppermute | solution.py:34
  102.3 8.7 %collective-permute-start.11 = (bf16[2,1,128,640]{3,2,1,0:T(8,128)(2,1)S(1)}, bf16[2,1,128,640]{3,2,1,0:T(8,128)(2,1)S(1)}, u32[]{:S(2)}, u32[]{:S(2)}) collective-permute-start(bf16[2,1,128,640]{3,2,1,0:T(8,128)(2,1)S(1)} %pad_maximum_fusion.1), channel_id=1, source_target_pairs={{1,0},{3,2},{5,4},{7,6},{9,8},{11,10},{13,12},{15,14},{17,16},{19,... | collective-permute-start | bytes 983048 | tf_op jit(solution)/shard_map/ppermute | solution.py:251
  103.6 5.1 %collective-permute-start.12 = (bf16[1,128,640]{2,1,0:T(8,128)(2,1)S(1)}, bf16[1,128,640]{2,1,0:T(8,128)(2,1)S(1)}, u32[]{:S(2)}, u32[]{:S(2)}) collective-permute-start(bf16[1,128,640]{2,1,0:T(8,128)(2,1)S(1)} %get-tuple-element.12), channel_id=1, source_target_pairs={{1,2},{3,0},{5,6},{7,4},{9,10},{11,8},{13,14},{15,12},{17,18},{19,... | collective-permute-start | bytes 491528 | tf_op jit(solution)/shard_map/ppermute | solution.py:251
  105.0 6.1 %collective-permute-start.13 = (bf16[1,128,640]{2,1,0:T(8,128)(2,1)S(1)}, bf16[1,128,640]{2,1,0:T(8,128)(2,1)S(1)}, u32[]{:S(2)}, u32[]{:S(2)}) collective-permute-start(bf16[1,128,640]{2,1,0:T(8,128)(2,1)S(1)} %constant_dynamic-slice_fusion), channel_id=1, source_target_pairs={{1,3},{3,1},{5,7},{7,5},{9,11},{11,9},{13,15},{15,13},{17,19},{19,... | collective-permute-start | bytes 491528 | tf_op jit(solution)/shard_map/ppermute | solution.py:255

commit v13 on v11

--- a/solution.py
+++ b/solution.py
@@ -219,25 +219,34 @@
         hidden0, lengths, norm_gain[0], query_weight[0], key_weight[0], value_weight[0],
         out_weight[0], sizes, 0,
     )
-    head_sum = None
-    for by in range(mp_n):
-        pairs = [(m * sec_n, ((m + by) % mp_n) * sec_n + 1) for m in range(mp_n)]
-        term = lax.ppermute(partial0, feat_axes, pairs).astype(jnp.float32)
-        head_sum = term if head_sum is None else head_sum + term
-    hidden1 = (hidden0.astype(jnp.float32) + head_sum).astype(jnp.bfloat16)
-
-    partial1, key1, value1 = attend_layer(
-        hidden1, lengths, norm_gain[0], query_weight[0], key_weight[0], value_weight[0],
-        out_weight[0], sizes, 1,
-    )
+    per_section = seq_count // sec_n
     is_first = sec_at == 0
+    partial0 = partial0.astype(jnp.bfloat16)
+    key_parts, value_parts, partial_parts, hidden_parts = [], [], [], []
+    for seq in range(seq_count):
+        head_sum = None
+        for by in range(mp_n):
+            pairs = [(m * sec_n, ((m + by) % mp_n) * sec_n + 1) for m in range(mp_n)]
+            term = lax.ppermute(partial0[seq : seq + 1], feat_axes, pairs).astype(jnp.float32)
+            head_sum = term if head_sum is None else head_sum + term
+        hidden_seq = (hidden0[seq : seq + 1].astype(jnp.float32) + head_sum).astype(jnp.bfloat16)
+        partial_seq, key_seq, value_seq = attend_layer(
+            hidden_seq, lengths[seq : seq + 1], norm_gain[0], query_weight[0], key_weight[0],
+            value_weight[0], out_weight[0], sizes, 1,
+        )
+        key_parts.append(key_seq)
+        value_parts.append(value_seq)
+        partial_parts.append(partial_seq.astype(jnp.bfloat16))
+        hidden_parts.append(hidden_seq)
+    key1 = jnp.concatenate(key_parts, 0)
+    value1 = jnp.concatenate(value_parts, 0)
     key_store = jnp.where(is_first, key0, key1)[None]
     value_store = jnp.where(is_first, value0, value1)[None]
 
-    per_section = seq_count // sec_n
-    low_rows = partial1[:per_section]
-    high_rows = partial1[per_section:]
-    low_hidden = hidden1[:per_section]
+    low_rows = jnp.concatenate(partial_parts[:per_section], 0)
+    high_rows = jnp.concatenate(partial_parts[per_section:], 0)
+    low_hidden = jnp.concatenate(hidden_parts[:per_section], 0)
+    high_hidden = jnp.concatenate(hidden_parts[per_section:], 0)
     to_low = []
     to_high = []
     for by in range(mp_n):
@@ -258,7 +267,7 @@
         + sum(piece.astype(jnp.float32) for piece in to_low[1:])
     )
     own_high = lax.dynamic_slice_in_dim(high_rows, mp_at * head_cols, head_cols, 2)
-    own_hidden = lax.dynamic_slice_in_dim(hidden1[per_section:], mp_at * head_cols, head_cols, 2)
+    own_hidden = lax.dynamic_slice_in_dim(high_hidden, mp_at * head_cols, head_cols, 2)
     high_total = own_hidden.astype(jnp.float32) + (
         own_high.astype(jnp.float32) + sum(piece.astype(jnp.float32) for piece in to_high)
     )

time: 103 us -> 112 us (1.087); the launches traced: 101 us -> 112 us
  between operations: 1.22 us -> 6.63 us
  starting transfers between devices: 27.7 us -> 32.1 us
  waiting for transfers between devices: 16.3 us -> 12.8 us
  other arithmetic: 17.5 us -> 19.4 us
  local copies, waits for them, and re-layouts: 12.6 us -> 14.4 us
    ppermute x2 -> x4, waiting for transfers between devices: 14.2 us -> 10.5 us  [per_device(): lax.ppermute(partial0[seq:seq + 1], feat_axes, pairs).astype(jnp.float32)]
    ppermute x2 -> x4, starting transfers between devices: 2.7 us -> 5.16 us  [per_device(): lax.ppermute(partial0[seq:seq + 1], feat_axes, pairs).astype(jnp.float32)]
    ppermute x6 -> x9, starting transfers between devices: 14.5 us -> 16.6 us  [gather_causal(): pieces.append(lax.ppermute(value, ('tm', 'section'), pairs))]
    ppermute x1, waiting for transfers between devices: 0.91 us -> 2.28 us  [per_device(): to_high.append(lax.ppermute(cols_high, feat_axes, pairs))]
    slice x2, local copies, waits for them, and re-layouts: 0.09 us -> 1.45 us  [the longest x1 0.87 us: per_device(): partial0[seq:seq + 1]]
    dot_general x2 -> x3, matrix products: 0.92 us -> 2.27 us  [attend_layer(): jnp.einsum('btd,de->bet', layer_input, value_w, preferred_element_type=jn...]
    reduce_sum x1, other arithmetic: 0.5 us -> 1.73 us  [per_device(): local_m2 = jnp.sum(local_dev * local_dev, -1)]
    ppermute x2, waiting for transfers between devices: 1.13 us -> 0.01 us  [per_device(): to_low.append(lax.ppermute(cols, feat_axes, pairs))]
  transfers between devices with their start and end apart: 14 -> 19, of which waited for: 3 -> 4; matrix products, arithmetic and copies ran while one was open for 10% -> 17% of each run, Pallas kernels for 0% -> 0%
where the time goes in v13:
time: 112 us
  starting transfers between devices  32.1 us (29%)
  other arithmetic  19.4 us (17%)
  matrix products  16.9 us (15%)
  local copies, waits for them, and re-layouts  14.4 us (13%)
  waiting for transfers between devices  12.8 us (11%)
  blocking collectives  9.24 us (8%)
  between operations  6.63 us (6%)
    ppermute x9, starting transfers between devices, gather_causal(): pieces.append(lax.ppermute(value, ('tm', 'section'), pairs))  16.6 us
    ppermute x4, waiting for transfers between devices, per_device(): lax.ppermute(partial0[seq:seq + 1], feat_axes, pairs).astype(jnp.float32)  10.5 us
    all_gather x1, blocking collectives, per_device(): hidden0 = lax.all_gather(tokens, feat_axes, axis=2, tiled=True)  9.24 us
    conv_general_dilated x1, matrix products, per_device(): lax.conv_general_dilated(chunks, kernel, window_strides=(STRIDE,), paddin...  5.67 us
    unnamed x24, local copies, waits for them, and re-layouts  5.42 us
    ppermute x4, starting transfers between devices, per_device(): lax.ppermute(partial0[seq:seq + 1], feat_axes, pairs).astype(jnp.float32)  5.16 us
    ppermute x3, starting transfers between devices, shift_from(): return lax.ppermute(value, axis, pairs)  4.66 us
    another operation x2, local copies, waits for them, and re-layouts, per_device(): jnp.stack([normed[:, :, q * chunk_tok * STRIDE:(q + 1) * chunk_tok * STRI...  3.28 us
  transfers between devices with their start and end apart: 19, of which 4 were waited for; matrix products, arithmetic and copies ran while one was open for 17% of the time, Pallas kernels for 0%

profile of v13, /device:TPU:1, one launch (start us, length us, event | category | flops | bytes accessed | tf_op | source)
XLA Modules:
  0.0 111.5 jit_solution(1343083430031157514)
XLA Ops:
  2.7 1.5 %multiply_reduce_fusion.1 = f32[2,64]{1,0:T(2,128)S(1)} fusion(f32[2,4096]{1,0:T(2,128)S(1)} %compare_convert_fusion, bf16[2,64,4096]{2,1,0:T(8,128)(2,1)} %param.8), kind=kLoop, calls=%fused_computation.24 | loop fusion | flops 1572736 | bytes 1081856 | tf_op jit(solution)/shard_map/reduce_sum | solution.py:151
  4.3 1.7 %multiply_reduce_fusion = f32[2,64]{1,0:T(2,128)S(1)} fusion(f32[2,64]{1,0:T(2,128)S(1)} %broadcast_divide_fusion.1, f32[2,4096]{1,0:T(2,128)S(1)} %compare_convert_fusion, bf16[2,64,4096]{2,1,0:T(8,128)(2,1)} %param.8), kind=kLoop, calls=%fused_computation.23 | loop fusion | flops 2621312 | bytes 1082368 | tf_op jit(solution)/shard_map/reduce_sum | solution.py:161
  6.1 2.2 %collective-permute-start = (f32[2,64,34]{1,0,2:T(2,128)S(1)}, f32[2,64,34]{1,0,2:T(2,128)S(1)}, u32[]{:S(2)}, u32[]{:S(2)}) collective-permute-start(f32[2,64,34]{1,0,2:T(2,128)S(1)} %pad_maximum_fusion.5), channel_id=1, source_target_pairs={{0,4},{4,8},{8,12},{12,0},{1,5},{5,9},{9,13},{13,1},{2,6},{6,10},{... | collective-permute-start | bytes 52232 | tf_op jit(solution)/shard_map/ppermute | solution.py:13
  8.3 2.1 %collective-permute-start.2 = (f32[2,64,34]{1,0,2:T(2,128)S(1)}, f32[2,64,34]{1,0,2:T(2,128)S(1)}, u32[]{:S(2)}, u32[]{:S(2)}) collective-permute-start(f32[2,64,34]{1,0,2:T(2,128)S(1)} %pad_maximum_fusion.5), channel_id=1, source_target_pairs={{0,12},{4,0},{8,4},{12,8},{1,13},{5,1},{9,5},{13,9},{2,14},{6,2},{... | collective-permute-start | bytes 52232 | tf_op jit(solution)/shard_map/ppermute | solution.py:13
  17.6 1.6 %convert_element_type.226 = f32[2,64,4096]{2,1,0:T(8,128)} convert(bf16[2,64,4096]{2,1,0:T(8,128)(2,1)S(1)} %copy-done.1) | non-fusion elementwise | flops 524288 | bytes 3145728 | tf_op jit(solution)/shard_map/convert_element_type | solution.py:149
  19.2 4.6 %copy.61 = bf16[4096,320]{1,0:T(8,128)(2,1)} copy(bf16[4096,320]{0,1:T(8,128)(2,1)} %param.10) | data formatting | bytes 5242880 | tf_op args[2]
  24.8 2.3 %fusion.8 = bf16[2,64,4128]{2,1,0:T(8,128)(2,1)S(1)} fusion(f32[2,64,4096]{2,1,0:T(8,128)} %convert_element_type.226, f32[2,64,32]{2,1,0:T(8,128)S(1)} %copy.58, f32[2,64]{1,0:T(2,128)S(1)} %add_rsqrt_fusion.1, f32[2,64]{1,0:T(2,128)S(1)} %broadcast_divide_fusion, f32[2,4128]{1,0:T(2,128)S(1)} %and_convert_fusion), kind=kLoop, calls=%fused_computation.15 | loop fusion | flops 3170304 | bytes 3204352 | tf_op jit(solution)/shard_map/convert_element_type | solution.py:192
  27.4 3.2 %copy.60 = bf16[2,4,64,1056]{2,1,0,3:T(4,128)(2,1)} copy(bf16[2,4,64,1056]{3,2,0,1:T(8,128)(2,1)S(1)} %pad_maximum_fusion) | data formatting | bytes 2162688 | tf_op jit(solution)/shard_map/stack | solution.py:196
  30.6 5.7 %fusion.52 = bf16[8,32,320]{2,0,1:T(8,128)(2,1)S(1)} fusion(bf16[8,64,1056]{1,0,2:T(8,128)(2,1)} %bitcast.280, bf16[64,64,320]{2,1,0:T(8,128)(2,1)} %bitcast.279), kind=kOutput, calls=%fused_computation.57 | convolution fusion | flops 671170560 | bytes 3866624 | tf_op jit(solution)/shard_map/conv_general_dilated | solution.py:203
  36.5 9.2 %all_gather.3 = bf16[2,128,1280]{1,0,2:T(2,128)(2,1)S(1)} all-gather(bf16[2,128,320]{1,0,2:T(2,128)(2,1)S(1)} %copy.64), channel_id=1, replica_groups=mesh['groups'=2,'tm'=4,'mp'=2,'section'=2] {'mp','section'}, dimensions={2}, use_global_device_ids=true | all-gather | bytes 819200 | tf_op jit(solution)/shard_map/all_gather | solution.py:213
  46.9 1.6 %convolution_convert_fusion.3 = bf16[2,128,160]{1,2,0:T(8,128)(2,1)S(1)} fusion(bf16[1,1280,160]{1,2,0:T(8,128)(2,1)} %param.14, bf16[2,128,1280]{2,1,0:T(8,128)(2,1)S(1)} %copy.65, f32[1280]{0:T(1024)S(1)} %convert_reduce_fusion, f32[2,128]{1,0:T(2,128)S(1)} %add_rsqrt_fusion), kind=kOutput, calls=%fused_computation.62 | convolution fusion | flops 106209280 | bytes 1153024 | tf_op jit(solution)/shard_map/btd,de->bet/dot_general | solution.py:78
  51.0 1.3 %collective-permute-start.5 = (bf16[2,2,2,80,128]{4,3,2,1,0:T(8,128)(2,1)}, bf16[2,2,2,80,128]{4,3,2,1,0:T(8,128)(2,1)}, u32[]{:S(2)}, u32[]{:S(2)}) collective-permute-start(bf16[2,2,2,80,128]{4,3,2,1,0:T(8,128)(2,1)} %pad_maximum_fusion.2), channel_id=1, source_target_pairs={{0,4},{4,8},{8,12},{2,6},{6,10},{10,14},{16,20},{20,24},{24,28},{1... | collective-permute-start | bytes 491528 | tf_op jit(solution)/shard_map/ppermute | solution.py:34
  52.3 1.4 %fusion.41 = bf16[2,128,640]{2,1,0:T(8,128)(2,1)} fusion(bf16[1,1280,640]{2,1,0:T(8,128)(2,1)S(1)} %copy-done.6, bf16[2,128,1280]{2,1,0:T(8,128)(2,1)S(1)} %copy.65, f32[1280]{0:T(1024)S(1)} %convert_reduce_fusion, f32[2,128]{1,0:T(2,128)S(1)} %add_rsqrt_fusion), kind=kOutput, calls=%fused_computation.49 | convolution fusion | flops 421068800 | bytes 2627584 | tf_op jit(solution)/shard_map/btd,de->bte/dot_general | solution.py:72
  65.4 2.5 %collective-permute-done.6 = bf16[1,128,1280]{2,1,0:T(8,128)(2,1)S(1)} collective-permute-done((bf16[1,128,1280]{2,1,0:T(8,128)(2,1)}, bf16[1,128,1280]{2,1,0:T(8,128)(2,1)S(1)}, u32[]{:S(2)}, u32[]{:S(2)}) %collective-permute-start.6) | collective-permute-done | bytes 327712 | tf_op jit(solution)/shard_map/ppermute | solution.py:230
  67.9 5.1 %collective-permute-done.7 = bf16[1,128,1280]{2,1,0:T(8,128)(2,1)S(1)} collective-permute-done((bf16[1,128,1280]{2,1,0:T(8,128)(2,1)}, bf16[1,128,1280]{2,1,0:T(8,128)(2,1)S(1)}, u32[]{:S(2)}, u32[]{:S(2)}) %collective-permute-start.7) | collective-permute-done | bytes 327712 | tf_op jit(solution)/shard_map/ppermute | solution.py:230
  73.7 2.9 %collective-permute-done.9 = bf16[1,128,1280]{2,1,0:T(8,128)(2,1)} collective-permute-done((bf16[1,128,1280]{2,1,0:T(8,128)(2,1)}, bf16[1,128,1280]{2,1,0:T(8,128)(2,1)}, u32[]{:S(2)}, u32[]{:S(2)}) %collective-permute-start.9) | collective-permute-done | bytes 327712 | tf_op jit(solution)/shard_map/ppermute | solution.py:230
  76.6 1.7 %fusion.79 = (f32[128]{0:T(128)S(1)}, bf16[1,128,1280]{2,1,0:T(8,128)(2,1)S(1)}, f32[128]{0:T(128)S(1)}, bf16[1,128,1280]{2,1,0:T(8,128)(2,1)S(1)}) fusion(bf16[1,128,1280]{2,1,0:T(8,128)(2,1)} %copy-done.3, bf16[1,128,1280]{2,1,0:T(8,128)(2,1)} %copy-done.2, bf16[2,128,1280]{2,1,0:T(8,128)(2,1)S(1)} %copy.65, ...), kind=kLoop, calls=%fused_computation.82 | loop fusion | flops 2948864 | bytes 2622464 | tf_op jit(solution)/shard_map/reduce_sum | solution.py:69
  79.7 5.3 %collective-permute-start.10 = (bf16[2,1,2,80,128]{4,3,2,1,0:T(8,128)(2,1)}, bf16[2,1,2,80,128]{4,3,2,1,0:T(8,128)(2,1)S(1)}, u32[]{:S(2)}, u32[]{:S(2)}) collective-permute-start(bf16[2,1,2,80,128]{4,3,2,1,0:T(8,128)(2,1)} %pad_maximum_fusion.3), channel_id=1, source_target_pairs={{1,13},{3,15},{17,29},{19,31}} | collective-permute-start | bytes 245768 | tf_op jit(solution)/shard_map/ppermute | solution.py:34
  85.0 2.3 %collective-permute-start.11 = (bf16[2,1,2,80,128]{4,3,2,1,0:T(8,128)(2,1)}, bf16[2,1,2,80,128]{4,3,2,1,0:T(8,128)(2,1)}, u32[]{:S(2)}, u32[]{:S(2)}) collective-permute-start(bf16[2,1,2,80,128]{4,3,2,1,0:T(8,128)(2,1)} %pad_maximum_fusion.3), channel_id=1, source_target_pairs={{1,9},{5,13},{3,11},{7,15},{17,25},{21,29},{19,27},{23,31}} | collective-permute-start | bytes 245768 | tf_op jit(solution)/shard_map/ppermute | solution.py:34
  87.3 2.5 %collective-permute-start.12 = (bf16[2,1,2,80,128]{4,3,2,1,0:T(8,128)(2,1)}, bf16[2,1,2,80,128]{4,3,2,1,0:T(8,128)(2,1)}, u32[]{:S(2)}, u32[]{:S(2)}) collective-permute-start(bf16[2,1,2,80,128]{4,3,2,1,0:T(8,128)(2,1)} %pad_maximum_fusion.3), channel_id=1, source_target_pairs={{1,5},{5,9},{9,13},{3,7},{7,11},{11,15},{17,21},{21,25},{25,29},{1... | collective-permute-start | bytes 245768 | tf_op jit(solution)/shard_map/ppermute | solution.py:34
  100.0 1.3 %collective-permute-start.13 = (bf16[2,1,128,640]{3,2,1,0:T(8,128)(2,1)S(1)}, bf16[2,1,128,640]{3,2,1,0:T(8,128)(2,1)S(1)}, u32[]{:S(2)}, u32[]{:S(2)}) collective-permute-start(bf16[2,1,128,640]{3,2,1,0:T(8,128)(2,1)S(1)} %pad_maximum_fusion.1), channel_id=1, source_target_pairs={{1,0},{3,2},{5,4},{7,6},{9,8},{11,10},{13,12},{15,14},{17,16},{19,... | collective-permute-start | bytes 983048 | tf_op jit(solution)/shard_map/ppermute | solution.py:260
  101.3 1.3 %collective-permute-start.14 = (bf16[1,128,640]{2,1,0:T(8,128)(2,1)S(1)}, bf16[1,128,640]{2,1,0:T(8,128)(2,1)S(1)}, u32[]{:S(2)}, u32[]{:S(2)}) collective-permute-start(bf16[1,128,640]{2,1,0:T(8,128)(2,1)S(1)} %get-tuple-element.18), channel_id=1, source_target_pairs={{1,2},{3,0},{5,6},{7,4},{9,10},{11,8},{13,14},{15,12},{17,18},{19,... | collective-permute-start | bytes 491528 | tf_op jit(solution)/shard_map/ppermute | solution.py:260
  104.6 3.1 %collective-permute-start.18 = (bf16[1,128,640]{2,1,0:T(8,128)(2,1)S(1)}, bf16[1,128,640]{2,1,0:T(8,128)(2,1)S(1)}, u32[]{:S(2)}, u32[]{:S(2)}) collective-permute-start(bf16[1,128,640]{2,1,0:T(8,128)(2,1)S(1)} %dynamic-slice_bitcast_fusion), channel_id=1, source_target_pairs={{1,3},{3,1},{5,7},{7,5},{9,11},{11,9},{13,15},{15,13},{17,19},{19,... | collective-permute-start | bytes 491528 | tf_op jit(solution)/shard_map/ppermute | solution.py:264
  108.4 2.3 %collective-permute-done.18 = bf16[1,128,640]{2,1,0:T(8,128)(2,1)S(1)} collective-permute-done((bf16[1,128,640]{2,1,0:T(8,128)(2,1)S(1)}, bf16[1,128,640]{2,1,0:T(8,128)(2,1)S(1)}, u32[]{:S(2)}, u32[]{:S(2)}) %collective-permute-start.18) | collective-permute-done | bytes 163872 | tf_op jit(solution)/shard_map/ppermute | solution.py:264
  (139 shorter events, 36.3 us)
Async XLA Ops:
  0.6 57.9 %copy-start = (bf16[1,640,1280]{2,1,0:T(8,128)(2,1)S(1)}, bf16[1,640,1280]{2,1,0:T(8,128)(2,1)}, u32[]{:S(2)}) copy-start(bf16[1,640,1280]{2,1,0:T(8,128)(2,1)} %param.15) | copy-start | bytes 4915204
  0.7 17.0 %copy-start.1 = (bf16[2,64,4096]{2,1,0:T(8,128)(2,1)S(1)}, bf16[2,64,4096]{2,1,0:T(8,128)(2,1)}, u32[]{:S(2)}) copy-start(bf16[2,64,4096]{2,1,0:T(8,128)(2,1)} %param.8) | copy-start | bytes 3145732
  0.7 16.1 %copy-start.4 = (bf16[1,1280]{1,0:T(2,128)(2,1)S(1)}, bf16[1,1280]{1,0:T(2,128)(2,1)}, u32[]{:S(2)}) copy-start(bf16[1,1280]{1,0:T(2,128)(2,1)} %param.11) | copy-start | bytes 7684
  6.1 17.6 %collective-permute-start = (f32[2,64,34]{1,0,2:T(2,128)S(1)}, f32[2,64,34]{1,0,2:T(2,128)S(1)}, u32[]{:S(2)}, u32[]{:S(2)}) collective-permute-start(f32[2,64,34]{1,0,2:T(2,128)S(1)} %pad_maximum_fusion.5), channel_id=1, source_target_pairs={{0,4},{4,8},{8,12},{12,0},{1,5},{5,9},{9,13},{13,1},{2,6},{6,10},{... | collective-permute-start | bytes 52232 | tf_op jit(solution)/shard_map/ppermute | solution.py:13
  8.3 15.4 %collective-permute-start.2 = (f32[2,64,34]{1,0,2:T(2,128)S(1)}, f32[2,64,34]{1,0,2:T(2,128)S(1)}, u32[]{:S(2)}, u32[]{:S(2)}) collective-permute-start(f32[2,64,34]{1,0,2:T(2,128)S(1)} %pad_maximum_fusion.5), channel_id=1, source_target_pairs={{0,12},{4,0},{8,4},{12,8},{1,13},{5,1},{9,5},{13,9},{2,14},{6,2},{... | collective-permute-start | bytes 52232 | tf_op jit(solution)/shard_map/ppermute | solution.py:13
  10.4 13.4 %collective-permute-start.1 = (f32[2,64,34]{1,0,2:T(2,128)S(1)}, f32[2,64,34]{1,0,2:T(2,128)S(1)}, u32[]{:S(2)}, u32[]{:S(2)}) collective-permute-start(f32[2,64,34]{1,0,2:T(2,128)S(1)} %pad_maximum_fusion.5), channel_id=1, source_target_pairs={{0,8},{4,12},{8,0},{12,4},{1,9},{5,13},{9,1},{13,5},{2,10},{6,14},... | collective-permute-start | bytes 52232 | tf_op jit(solution)/shard_map/ppermute | solution.py:13
  49.7 5.3 %collective-permute-start.3 = (bf16[2,2,2,80,128]{4,3,2,1,0:T(8,128)(2,1)}, bf16[2,2,2,80,128]{4,3,2,1,0:T(8,128)(2,1)S(1)}, u32[]{:S(2)}, u32[]{:S(2)}) collective-permute-start(bf16[2,2,2,80,128]{4,3,2,1,0:T(8,128)(2,1)} %pad_maximum_fusion.2), channel_id=1, source_target_pairs={{0,12},{2,14},{16,28},{18,30}} | collective-permute-start | bytes 491528 | tf_op jit(solution)/shard_map/ppermute | solution.py:34
  50.3 4.7 %collective-permute-start.4 = (bf16[2,2,2,80,128]{4,3,2,1,0:T(8,128)(2,1)}, bf16[2,2,2,80,128]{4,3,2,1,0:T(8,128)(2,1)S(1)}, u32[]{:S(2)}, u32[]{:S(2)}) collective-permute-start(bf16[2,2,2,80,128]{4,3,2,1,0:T(8,128)(2,1)} %pad_maximum_fusion.2), channel_id=1, source_target_pairs={{0,8},{4,12},{2,10},{6,14},{16,24},{20,28},{18,26},{22,30}} | collective-permute-start | bytes 491528 | tf_op jit(solution)/shard_map/ppermute | solution.py:34
  51.0 4.0 %collective-permute-start.5 = (bf16[2,2,2,80,128]{4,3,2,1,0:T(8,128)(2,1)}, bf16[2,2,2,80,128]{4,3,2,1,0:T(8,128)(2,1)}, u32[]{:S(2)}, u32[]{:S(2)}) collective-permute-start(bf16[2,2,2,80,128]{4,3,2,1,0:T(8,128)(2,1)} %pad_maximum_fusion.2), channel_id=1, source_target_pairs={{0,4},{4,8},{8,12},{2,6},{6,10},{10,14},{16,20},{20,24},{24,28},{1... | collective-permute-start | bytes 491528 | tf_op jit(solution)/shard_map/ppermute | solution.py:34
  60.1 7.8 %collective-permute-start.6 = (bf16[1,128,1280]{2,1,0:T(8,128)(2,1)}, bf16[1,128,1280]{2,1,0:T(8,128)(2,1)S(1)}, u32[]{:S(2)}, u32[]{:S(2)}) collective-permute-start(bf16[1,128,1280]{2,1,0:T(8,128)(2,1)} %get-tuple-element.15), channel_id=1, source_target_pairs={{0,1},{2,3},{4,5},{6,7},{8,9},{10,11},{12,13},{14,15},{16,17},{18,... | collective-permute-start | bytes 983048 | tf_op jit(solution)/shard_map/ppermute | solution.py:230
  61.4 11.6 %collective-permute-start.7 = (bf16[1,128,1280]{2,1,0:T(8,128)(2,1)}, bf16[1,128,1280]{2,1,0:T(8,128)(2,1)S(1)}, u32[]{:S(2)}, u32[]{:S(2)}) collective-permute-start(bf16[1,128,1280]{2,1,0:T(8,128)(2,1)} %get-tuple-element.15), channel_id=1, source_target_pairs={{0,3},{2,1},{4,7},{6,5},{8,11},{10,9},{12,15},{14,13},{16,19},{18,... | collective-permute-start | bytes 983048 | tf_op jit(solution)/shard_map/ppermute | solution.py:230
  62.7 10.3 %collective-permute-start.8 = (bf16[1,128,1280]{2,1,0:T(8,128)(2,1)}, bf16[1,128,1280]{2,1,0:T(8,128)(2,1)}, u32[]{:S(2)}, u32[]{:S(2)}) collective-permute-start(bf16[1,128,1280]{2,1,0:T(8,128)(2,1)} %get-tuple-element.16), channel_id=1, source_target_pairs={{0,1},{2,3},{4,5},{6,7},{8,9},{10,11},{12,13},{14,15},{16,17},{18,... | collective-permute-start | bytes 983048 | tf_op jit(solution)/shard_map/ppermute | solution.py:230
  64.0 12.6 %collective-permute-start.9 = (bf16[1,128,1280]{2,1,0:T(8,128)(2,1)}, bf16[1,128,1280]{2,1,0:T(8,128)(2,1)}, u32[]{:S(2)}, u32[]{:S(2)}) collective-permute-start(bf16[1,128,1280]{2,1,0:T(8,128)(2,1)} %get-tuple-element.16), channel_id=1, source_target_pairs={{0,3},{2,1},{4,7},{6,5},{8,11},{10,9},{12,15},{14,13},{16,19},{18,... | collective-permute-start | bytes 983048 | tf_op jit(solution)/shard_map/ppermute | solution.py:230
  65.4 13.3 %copy-start.10 = (bf16[1,1280,160]{1,2,0:T(8,128)(2,1)S(1)}, bf16[1,1280,160]{1,2,0:T(8,128)(2,1)}, u32[]{:S(2)}) copy-start(bf16[1,1280,160]{1,2,0:T(8,128)(2,1)} %param.13) | copy-start | bytes 1228804
  65.4 24.4 %copy-start.7 = (bf16[1,1280,640]{2,1,0:T(8,128)(2,1)S(1)}, bf16[1,1280,640]{2,1,0:T(8,128)(2,1)}, u32[]{:S(2)}) copy-start(bf16[1,1280,640]{2,1,0:T(8,128)(2,1)} %param.12) | copy-start | bytes 4915204
  79.7 16.0 %collective-permute-start.10 = (bf16[2,1,2,80,128]{4,3,2,1,0:T(8,128)(2,1)}, bf16[2,1,2,80,128]{4,3,2,1,0:T(8,128)(2,1)S(1)}, u32[]{:S(2)}, u32[]{:S(2)}) collective-permute-start(bf16[2,1,2,80,128]{4,3,2,1,0:T(8,128)(2,1)} %pad_maximum_fusion.3), channel_id=1, source_target_pairs={{1,13},{3,15},{17,29},{19,31}} | collective-permute-start | bytes 245768 | tf_op jit(solution)/shard_map/ppermute | solution.py:34
  85.0 12.0 %collective-permute-start.11 = (bf16[2,1,2,80,128]{4,3,2,1,0:T(8,128)(2,1)}, bf16[2,1,2,80,128]{4,3,2,1,0:T(8,128)(2,1)}, u32[]{:S(2)}, u32[]{:S(2)}) collective-permute-start(bf16[2,1,2,80,128]{4,3,2,1,0:T(8,128)(2,1)} %pad_maximum_fusion.3), channel_id=1, source_target_pairs={{1,9},{5,13},{3,11},{7,15},{17,25},{21,29},{19,27},{23,31}} | collective-permute-start | bytes 245768 | tf_op jit(solution)/shard_map/ppermute | solution.py:34
  87.3 9.7 %collective-permute-start.12 = (bf16[2,1,2,80,128]{4,3,2,1,0:T(8,128)(2,1)}, bf16[2,1,2,80,128]{4,3,2,1,0:T(8,128)(2,1)}, u32[]{:S(2)}, u32[]{:S(2)}) collective-permute-start(bf16[2,1,2,80,128]{4,3,2,1,0:T(8,128)(2,1)} %pad_maximum_fusion.3), channel_id=1, source_target_pairs={{1,5},{5,9},{9,13},{3,7},{7,11},{11,15},{17,21},{21,25},{25,29},{1... | collective-permute-start | bytes 245768 | tf_op jit(solution)/shard_map/ppermute | solution.py:34
  91.6 11.0 %collective-permute-start.15 = (bf16[2,1,2,80,128]{4,3,2,1,0:T(8,128)(2,1)}, bf16[2,1,2,80,128]{4,3,2,1,0:T(8,128)(2,1)S(1)}, u32[]{:S(2)}, u32[]{:S(2)}) collective-permute-start(bf16[2,1,2,80,128]{4,3,2,1,0:T(8,128)(2,1)} %pad_maximum_fusion.4), channel_id=1, source_target_pairs={{1,13},{3,15},{17,29},{19,31}} | collective-permute-start | bytes 245768 | tf_op jit(solution)/shard_map/ppermute | solution.py:34
  92.9 9.7 %collective-permute-start.16 = (bf16[2,1,2,80,128]{4,3,2,1,0:T(8,128)(2,1)}, bf16[2,1,2,80,128]{4,3,2,1,0:T(8,128)(2,1)S(1)}, u32[]{:S(2)}, u32[]{:S(2)}) collective-permute-start(bf16[2,1,2,80,128]{4,3,2,1,0:T(8,128)(2,1)} %pad_maximum_fusion.4), channel_id=1, source_target_pairs={{1,9},{5,13},{3,11},{7,15},{17,25},{21,29},{19,27},{23,31}} | collective-permute-start | bytes 245768 | tf_op jit(solution)/shard_map/ppermute | solution.py:34
  95.7 7.0 %collective-permute-start.17 = (bf16[2,1,2,80,128]{4,3,2,1,0:T(8,128)(2,1)}, bf16[2,1,2,80,128]{4,3,2,1,0:T(8,128)(2,1)S(1)}, u32[]{:S(2)}, u32[]{:S(2)}) collective-permute-start(bf16[2,1,2,80,128]{4,3,2,1,0:T(8,128)(2,1)} %pad_maximum_fusion.4), channel_id=1, source_target_pairs={{1,5},{5,9},{9,13},{3,7},{7,11},{11,15},{17,21},{21,25},{25,29},{1... | collective-permute-start | bytes 245768 | tf_op jit(solution)/shard_map/ppermute | solution.py:34
  100.0 10.7 %collective-permute-start.13 = (bf16[2,1,128,640]{3,2,1,0:T(8,128)(2,1)S(1)}, bf16[2,1,128,640]{3,2,1,0:T(8,128)(2,1)S(1)}, u32[]{:S(2)}, u32[]{:S(2)}) collective-permute-start(bf16[2,1,128,640]{3,2,1,0:T(8,128)(2,1)S(1)} %pad_maximum_fusion.1), channel_id=1, source_target_pairs={{1,0},{3,2},{5,4},{7,6},{9,8},{11,10},{13,12},{15,14},{17,16},{19,... | collective-permute-start | bytes 983048 | tf_op jit(solution)/shard_map/ppermute | solution.py:260
  101.3 7.1 %collective-permute-start.14 = (bf16[1,128,640]{2,1,0:T(8,128)(2,1)S(1)}, bf16[1,128,640]{2,1,0:T(8,128)(2,1)S(1)}, u32[]{:S(2)}, u32[]{:S(2)}) collective-permute-start(bf16[1,128,640]{2,1,0:T(8,128)(2,1)S(1)} %get-tuple-element.18), channel_id=1, source_target_pairs={{1,2},{3,0},{5,6},{7,4},{9,10},{11,8},{13,14},{15,12},{17,18},{19,... | collective-permute-start | bytes 491528 | tf_op jit(solution)/shard_map/ppermute | solution.py:260
  104.6 6.1 %collective-permute-start.18 = (bf16[1,128,640]{2,1,0:T(8,128)(2,1)S(1)}, bf16[1,128,640]{2,1,0:T(8,128)(2,1)S(1)}, u32[]{:S(2)}, u32[]{:S(2)}) collective-permute-start(bf16[1,128,640]{2,1,0:T(8,128)(2,1)S(1)} %dynamic-slice_bitcast_fusion), channel_id=1, source_target_pairs={{1,3},{3,1},{5,7},{7,5},{9,11},{11,9},{13,15},{15,13},{17,19},{19,... | collective-permute-start | bytes 491528 | tf_op jit(solution)/shard_map/ppermute | solution.py:264
  (6 other events, 36.6 us)

commit v14 on v11

--- a/solution.py
+++ b/solution.py
@@ -126,7 +126,7 @@
     if out_w is None:
         return attended, key_t, value_t
     partial_value = jnp.einsum("bte,ed->btd", attended, out_w, preferred_element_type=jnp.float32)
-    return partial_value.astype(jnp.bfloat16), key_t, value_t
+    return partial_value, key_t, value_t
 
 
 def per_device(
@@ -222,7 +222,7 @@
     head_sum = None
     for by in range(mp_n):
         pairs = [(m * sec_n, ((m + by) % mp_n) * sec_n + 1) for m in range(mp_n)]
-        term = lax.ppermute(partial0, feat_axes, pairs).astype(jnp.float32)
+        term = lax.ppermute(partial0.astype(jnp.bfloat16), feat_axes, pairs).astype(jnp.float32)
         head_sum = term if head_sum is None else head_sum + term
     hidden1 = (hidden0.astype(jnp.float32) + head_sum).astype(jnp.bfloat16)
 
@@ -244,23 +244,21 @@
         target_mp = (mp_at + by) % mp_n
         cols = lax.dynamic_slice_in_dim(low_rows, target_mp * head_cols, head_cols, 2)
         if by == 0:
-            cols = jnp.stack(
-                [lax.dynamic_slice_in_dim(low_hidden, target_mp * head_cols, head_cols, 2), cols], 0
-            )
+            residual = lax.dynamic_slice_in_dim(low_hidden, target_mp * head_cols, head_cols, 2)
+            cols = residual.astype(jnp.float32) + cols
         pairs = [(m * sec_n + 1, ((m + by) % mp_n) * sec_n) for m in range(mp_n)]
-        to_low.append(lax.ppermute(cols, feat_axes, pairs))
+        to_low.append(lax.ppermute(cols.astype(jnp.bfloat16), feat_axes, pairs))
         if by > 0:
             cols_high = lax.dynamic_slice_in_dim(high_rows, target_mp * head_cols, head_cols, 2)
             pairs = [(m * sec_n + 1, ((m + by) % mp_n) * sec_n + 1) for m in range(mp_n)]
-            to_high.append(lax.ppermute(cols_high, feat_axes, pairs))
-    low_total = to_low[0][0].astype(jnp.float32) + (
-        to_low[0][1].astype(jnp.float32)
-        + sum(piece.astype(jnp.float32) for piece in to_low[1:])
+            to_high.append(lax.ppermute(cols_high.astype(jnp.bfloat16), feat_axes, pairs))
+    low_total = to_low[0].astype(jnp.float32) + sum(
+        piece.astype(jnp.float32) for piece in to_low[1:]
     )
     own_high = lax.dynamic_slice_in_dim(high_rows, mp_at * head_cols, head_cols, 2)
     own_hidden = lax.dynamic_slice_in_dim(hidden1[per_section:], mp_at * head_cols, head_cols, 2)
-    high_total = own_hidden.astype(jnp.float32) + (
-        own_high.astype(jnp.float32) + sum(piece.astype(jnp.float32) for piece in to_high)
+    high_total = own_hidden.astype(jnp.float32) + own_high + sum(
+        piece.astype(jnp.float32) for piece in to_high
     )
     final_cols = jnp.where(is_first, low_total, high_total).astype(jnp.bfloat16)
     return (key_store, value_store, final_cols)

time: 103 us -> 101 us (0.981)
    ppermute x5, waiting for transfers between devices: 16.3 us -> 14.9 us  [the longest x2 14.2 us: per_device(): lax.ppermute(partial0.astype(jnp.bfloat16), feat_axes, pairs)]
  transfers between devices with their start and end apart: 14 -> 14, of which waited for: 3 -> 3; matrix products, arithmetic and copies ran while one was open for 10% -> 11% of each run, Pallas kernels for 0% -> 0%
where the time goes in v14:
time: 101 us; the launch traced here: 99.4 us
  starting transfers between devices  27 us (27%)
  other arithmetic  17.4 us (17%)
  matrix products  16.5 us (16%)
  waiting for transfers between devices  15.4 us (15%)
  local copies, waits for them, and re-layouts  12.6 us (12%)
  blocking collectives  9.24 us (9%)
  between operations  1.2 us (1%)
    ppermute x2, waiting for transfers between devices, per_device(): lax.ppermute(partial0.astype(jnp.bfloat16), feat_axes, pairs)  14.2 us
    ppermute x6, starting transfers between devices, gather_causal(): pieces.append(lax.ppermute(value, ('tm', 'section'), pairs))  13.8 us
    all_gather x1, blocking collectives, per_device(): hidden0 = lax.all_gather(tokens, feat_axes, axis=2, tiled=True)  9.24 us
    conv_general_dilated x1, matrix products, per_device(): lax.conv_general_dilated(chunks, kernel, window_strides=(STRIDE,), paddin...  5.67 us
    unnamed x18, local copies, waits for them, and re-layouts  5.17 us
    ppermute x3, starting transfers between devices, shift_from(): return lax.ppermute(value, axis, pairs)  4.66 us
    another operation x2, local copies, waits for them, and re-layouts, per_device(): jnp.stack([normed[:, :, q * chunk_tok * STRIDE:(q + 1) * chunk_tok * STRI...  3.27 us
    ppermute x1, starting transfers between devices, per_device(): lax.ppermute(cols_high.astype(jnp.bfloat16), feat_axes, pairs)  3.17 us
  transfers between devices with their start and end apart: 14, of which 3 were waited for; matrix products, arithmetic and copies ran while one was open for 11% of the time, Pallas kernels for 0%

profile of v14, /device:TPU:1, one launch (start us, length us, event | category | flops | bytes accessed | tf_op | source)
XLA Modules:
  0.0 99.4 jit_solution(11252732540037949764)
XLA Ops:
  2.8 1.5 %multiply_reduce_fusion.1 = f32[2,64]{1,0:T(2,128)S(1)} fusion(f32[2,4096]{1,0:T(2,128)S(1)} %compare_convert_fusion, bf16[2,64,4096]{2,1,0:T(8,128)(2,1)} %param.8), kind=kLoop, calls=%fused_computation.26 | loop fusion | flops 1572736 | bytes 1081856 | tf_op jit(solution)/shard_map/reduce_sum | solution.py:151
  4.9 2.2 %collective-permute-start = (f32[2,64,34]{1,0,2:T(2,128)S(1)}, f32[2,64,34]{1,0,2:T(2,128)S(1)}, u32[]{:S(2)}, u32[]{:S(2)}) collective-permute-start(f32[2,64,34]{1,0,2:T(2,128)S(1)} %pad_maximum_fusion.3), channel_id=1, source_target_pairs={{0,4},{4,8},{8,12},{12,0},{1,5},{5,9},{9,13},{13,1},{2,6},{6,10},{... | collective-permute-start | bytes 52232 | tf_op jit(solution)/shard_map/ppermute | solution.py:13
  7.1 2.1 %collective-permute-start.2 = (f32[2,64,34]{1,0,2:T(2,128)S(1)}, f32[2,64,34]{1,0,2:T(2,128)S(1)}, u32[]{:S(2)}, u32[]{:S(2)}) collective-permute-start(f32[2,64,34]{1,0,2:T(2,128)S(1)} %pad_maximum_fusion.3), channel_id=1, source_target_pairs={{0,12},{4,0},{8,4},{12,8},{1,13},{5,1},{9,5},{13,9},{2,14},{6,2},{... | collective-permute-start | bytes 52232 | tf_op jit(solution)/shard_map/ppermute | solution.py:13
  10.4 1.6 %convert_element_type.149 = f32[2,64,4096]{2,1,0:T(8,128)} convert(bf16[2,64,4096]{2,1,0:T(8,128)(2,1)S(1)} %copy-done.1) | non-fusion elementwise | flops 524288 | bytes 3145728 | tf_op jit(solution)/shard_map/convert_element_type | solution.py:149
  12.0 4.5 %copy.39 = bf16[4096,320]{1,0:T(8,128)(2,1)} copy(bf16[4096,320]{0,1:T(8,128)(2,1)} %param.10) | data formatting | bytes 5242880 | tf_op args[2]
  17.6 2.3 %fusion.11 = bf16[2,64,4128]{2,1,0:T(8,128)(2,1)S(1)} fusion(f32[2,64,4096]{2,1,0:T(8,128)} %convert_element_type.149, f32[2,64,32]{2,1,0:T(8,128)S(1)} %copy.36, f32[2,64]{1,0:T(2,128)S(1)} %add_rsqrt_fusion.2, f32[2,64]{1,0:T(2,128)S(1)} %broadcast_divide_fusion, f32[2,4128]{1,0:T(2,128)S(1)} %and_convert_fusion), kind=kLoop, calls=%fused_computation.18 | loop fusion | flops 3170304 | bytes 3204352 | tf_op jit(solution)/shard_map/convert_element_type | solution.py:192
  20.2 3.2 %copy.38 = bf16[2,4,64,1056]{2,1,0,3:T(4,128)(2,1)} copy(bf16[2,4,64,1056]{3,2,0,1:T(8,128)(2,1)S(1)} %pad_maximum_fusion) | data formatting | bytes 2162688 | tf_op jit(solution)/shard_map/stack | solution.py:196
  23.4 5.7 %fusion.60 = bf16[8,32,320]{2,0,1:T(8,128)(2,1)S(1)} fusion(bf16[8,64,1056]{1,0,2:T(8,128)(2,1)} %bitcast.196, bf16[64,64,320]{2,1,0:T(8,128)(2,1)} %bitcast.195), kind=kOutput, calls=%fused_computation.57 | convolution fusion | flops 671170560 | bytes 3866624 | tf_op jit(solution)/shard_map/conv_general_dilated | solution.py:203
  29.3 9.2 %all_gather.3 = bf16[2,128,1280]{1,0,2:T(2,128)(2,1)S(1)} all-gather(bf16[2,128,320]{1,0,2:T(2,128)(2,1)S(1)} %copy.42), channel_id=1, replica_groups=mesh['groups'=2,'tm'=4,'mp'=2,'section'=2] {'mp','section'}, dimensions={2}, use_global_device_ids=true | all-gather | bytes 819200 | tf_op jit(solution)/shard_map/all_gather | solution.py:213
  39.7 1.6 %convolution_convert_fusion.4 = bf16[2,128,160]{1,2,0:T(8,128)(2,1)S(1)} fusion(bf16[1,1280,160]{1,2,0:T(8,128)(2,1)} %param.13, bf16[2,128,1280]{2,1,0:T(8,128)(2,1)S(1)} %copy.43, f32[1280]{0:T(1024)S(1)} %convert_reduce_fusion, f32[2,128]{1,0:T(2,128)S(1)} %add_rsqrt_fusion.1), kind=kOutput, calls=%fused_computation.61 | convolution fusion | flops 106209280 | bytes 1153024 | tf_op jit(solution)/shard_map/btd,de->bet/dot_general | solution.py:75
  43.1 1.3 %collective-permute-start.4 = (bf16[2,2,2,80,128]{4,3,2,1,0:T(8,128)(2,1)}, bf16[2,2,2,80,128]{4,3,2,1,0:T(8,128)(2,1)}, u32[]{:S(2)}, u32[]{:S(2)}) collective-permute-start(bf16[2,2,2,80,128]{4,3,2,1,0:T(8,128)(2,1)} %pad_maximum_fusion.1), channel_id=1, source_target_pairs={{0,8},{4,12},{2,10},{6,14},{16,24},{20,28},{18,26},{22,30}} | collective-permute-start | bytes 491528 | tf_op jit(solution)/shard_map/ppermute | solution.py:34
  44.4 1.3 %collective-permute-start.3 = (bf16[2,2,2,80,128]{4,3,2,1,0:T(8,128)(2,1)}, bf16[2,2,2,80,128]{4,3,2,1,0:T(8,128)(2,1)}, u32[]{:S(2)}, u32[]{:S(2)}) collective-permute-start(bf16[2,2,2,80,128]{4,3,2,1,0:T(8,128)(2,1)} %pad_maximum_fusion.1), channel_id=1, source_target_pairs={{0,12},{2,14},{16,28},{18,30}} | collective-permute-start | bytes 491528 | tf_op jit(solution)/shard_map/ppermute | solution.py:34
  50.3 1.5 %convolution_convert_fusion = bf16[2,128,1280]{2,1,0:T(8,128)(2,1)} fusion(bf16[2,128,640]{1,2,0:T(8,128)(2,1)S(1)} %bitcast.213, bf16[1,640,1280]{2,1,0:T(8,128)(2,1)S(1)} %copy-done), kind=kOutput, calls=%fused_computation.13 | convolution fusion | flops 419758080 | bytes 2621440 | tf_op jit(solution)/shard_map/bte,ed->btd/dot_general | solution.py:128
  51.9 1.4 %collective-permute-start.7 = (bf16[2,128,1280]{2,1,0:T(8,128)(2,1)}, bf16[2,128,1280]{2,1,0:T(8,128)(2,1)}, u32[]{:S(2)}, u32[]{:S(2)}) collective-permute-start(bf16[2,128,1280]{2,1,0:T(8,128)(2,1)} %convolution_convert_fusion), channel_id=1, source_target_pairs={{0,3},{2,1},{4,7},{6,5},{8,11},{10,9},{12,15},{14,13},{16,19},{18,... | collective-permute-start | bytes 1966088 | tf_op jit(solution)/shard_map/ppermute | solution.py:225
  53.3 1.3 %collective-permute-start.6 = (bf16[2,128,1280]{2,1,0:T(8,128)(2,1)}, bf16[2,128,1280]{2,1,0:T(8,128)(2,1)}, u32[]{:S(2)}, u32[]{:S(2)}) collective-permute-start(bf16[2,128,1280]{2,1,0:T(8,128)(2,1)} %convolution_convert_fusion), channel_id=1, source_target_pairs={{0,1},{2,3},{4,5},{6,7},{8,9},{10,11},{12,13},{14,15},{16,17},{18,... | collective-permute-start | bytes 1966088 | tf_op jit(solution)/shard_map/ppermute | solution.py:225
  54.6 14.2 %collective-permute-done.7 = bf16[2,128,1280]{2,1,0:T(8,128)(2,1)} collective-permute-done((bf16[2,128,1280]{2,1,0:T(8,128)(2,1)}, bf16[2,128,1280]{2,1,0:T(8,128)(2,1)}, u32[]{:S(2)}, u32[]{:S(2)}) %collective-permute-start.7) | collective-permute-done | bytes 655392 | tf_op jit(solution)/shard_map/ppermute | solution.py:225
  68.9 1.7 %fusion.29 = (f32[2,128]{1,0:T(2,128)S(1)}, bf16[2,128,1280]{2,1,0:T(8,128)(2,1)S(1)}) fusion(bf16[2,128,1280]{2,1,0:T(8,128)(2,1)} %collective-permute-done.7, bf16[2,128,1280]{2,1,0:T(8,128)(2,1)} %collective-permute-done.6, bf16[2,128,1280]{2,1,0:T(8,128)(2,1)S(1)} %copy.43), kind=kLoop, calls=%fused_computation.41 | loop fusion | flops 2948864 | bytes 2622464 | tf_op jit(solution)/shard_map/reduce_sum | solution.py:69
  72.0 1.4 %fusion.54 = bf16[2,128,640]{2,1,0:T(8,128)(2,1)} fusion(bf16[1,1280,640]{2,1,0:T(8,128)(2,1)S(1)} %copy-done.4, bf16[2,128,1280]{2,1,0:T(8,128)(2,1)S(1)} %get-tuple-element.4, f32[2,128]{1,0:T(2,128)S(1)} %add_rsqrt_fusion, f32[1280]{0:T(1024)S(1)} %convert_reduce_fusion), kind=kOutput, calls=%fused_computation.54 | convolution fusion | flops 421068800 | bytes 2627584 | tf_op jit(solution)/shard_map/btd,de->bte/dot_general | solution.py:72
  74.1 3.6 %collective-permute-start.10 = (bf16[2,2,2,80,128]{4,3,2,1,0:T(8,128)(2,1)}, bf16[2,2,2,80,128]{4,3,2,1,0:T(8,128)(2,1)S(1)}, u32[]{:S(2)}, u32[]{:S(2)}) collective-permute-start(bf16[2,2,2,80,128]{4,3,2,1,0:T(8,128)(2,1)} %pad_maximum_fusion.2), channel_id=1, source_target_pairs={{1,5},{5,9},{9,13},{3,7},{7,11},{11,15},{17,21},{21,25},{25,29},{1... | collective-permute-start | bytes 491528 | tf_op jit(solution)/shard_map/ppermute | solution.py:34
  77.8 5.0 %collective-permute-start.9 = (bf16[2,2,2,80,128]{4,3,2,1,0:T(8,128)(2,1)}, bf16[2,2,2,80,128]{4,3,2,1,0:T(8,128)(2,1)S(1)}, u32[]{:S(2)}, u32[]{:S(2)}) collective-permute-start(bf16[2,2,2,80,128]{4,3,2,1,0:T(8,128)(2,1)} %pad_maximum_fusion.2), channel_id=1, source_target_pairs={{1,9},{5,13},{3,11},{7,15},{17,25},{21,29},{19,27},{23,31}} | collective-permute-start | bytes 491528 | tf_op jit(solution)/shard_map/ppermute | solution.py:34
  82.7 2.0 %collective-permute-start.8 = (bf16[2,2,2,80,128]{4,3,2,1,0:T(8,128)(2,1)}, bf16[2,2,2,80,128]{4,3,2,1,0:T(8,128)(2,1)}, u32[]{:S(2)}, u32[]{:S(2)}) collective-permute-start(bf16[2,2,2,80,128]{4,3,2,1,0:T(8,128)(2,1)} %pad_maximum_fusion.2), channel_id=1, source_target_pairs={{1,13},{3,15},{17,29},{19,31}} | collective-permute-start | bytes 491528 | tf_op jit(solution)/shard_map/ppermute | solution.py:34
  91.4 3.2 %collective-permute-start.13 = (bf16[1,128,640]{2,1,0:T(8,128)(2,1)S(1)}, bf16[1,128,640]{2,1,0:T(8,128)(2,1)S(1)}, u32[]{:S(2)}, u32[]{:S(2)}) collective-permute-start(bf16[1,128,640]{2,1,0:T(8,128)(2,1)S(1)} %dynamic-slice_convert_fusion), channel_id=1, source_target_pairs={{1,3},{3,1},{5,7},{7,5},{9,11},{11,9},{13,15},{15,13},{17,19},{19,... | collective-permute-start | bytes 491528 | tf_op jit(solution)/shard_map/ppermute | solution.py:254
  94.6 1.3 %collective-permute-start.12 = (bf16[1,128,640]{2,1,0:T(8,128)(2,1)S(1)}, bf16[1,128,640]{2,1,0:T(8,128)(2,1)S(1)}, u32[]{:S(2)}, u32[]{:S(2)}) collective-permute-start(bf16[1,128,640]{2,1,0:T(8,128)(2,1)S(1)} %dynamic-slice_convert_fusion.1), channel_id=1, source_target_pairs={{1,2},{3,0},{5,6},{7,4},{9,10},{11,8},{13,14},{15,12},{17,18},{19,... | collective-permute-start | bytes 491528 | tf_op jit(solution)/shard_map/ppermute | solution.py:250
  96.0 1.3 %collective-permute-start.11 = (bf16[1,128,640]{2,1,0:T(8,128)(2,1)S(1)}, bf16[1,128,640]{2,1,0:T(8,128)(2,1)S(1)}, u32[]{:S(2)}, u32[]{:S(2)}) collective-permute-start(bf16[1,128,640]{2,1,0:T(8,128)(2,1)S(1)} %add_convert_fusion), channel_id=1, source_target_pairs={{1,0},{3,2},{5,4},{7,6},{9,8},{11,10},{13,12},{15,14},{17,16},{19,... | collective-permute-start | bytes 491528 | tf_op jit(solution)/shard_map/ppermute | solution.py:250
  (108 shorter events, 23.8 us)
Async XLA Ops:
  0.6 49.7 %copy-start = (bf16[1,640,1280]{2,1,0:T(8,128)(2,1)S(1)}, bf16[1,640,1280]{2,1,0:T(8,128)(2,1)}, u32[]{:S(2)}) copy-start(bf16[1,640,1280]{2,1,0:T(8,128)(2,1)} %param.15) | copy-start | bytes 4915204
  0.6 3.7 %copy-start.1 = (bf16[2,64,4096]{2,1,0:T(8,128)(2,1)S(1)}, bf16[2,64,4096]{2,1,0:T(8,128)(2,1)}, u32[]{:S(2)}) copy-start(bf16[2,64,4096]{2,1,0:T(8,128)(2,1)} %param.8) | copy-start | bytes 3145732
  0.7 9.1 %copy-start.2 = (bf16[1,1280]{1,0:T(2,128)(2,1)S(1)}, bf16[1,1280]{1,0:T(2,128)(2,1)}, u32[]{:S(2)}) copy-start(bf16[1,1280]{1,0:T(2,128)(2,1)} %param.11) | copy-start | bytes 7684
  4.9 11.6 %collective-permute-start = (f32[2,64,34]{1,0,2:T(2,128)S(1)}, f32[2,64,34]{1,0,2:T(2,128)S(1)}, u32[]{:S(2)}, u32[]{:S(2)}) collective-permute-start(f32[2,64,34]{1,0,2:T(2,128)S(1)} %pad_maximum_fusion.3), channel_id=1, source_target_pairs={{0,4},{4,8},{8,12},{12,0},{1,5},{5,9},{9,13},{13,1},{2,6},{6,10},{... | collective-permute-start | bytes 52232 | tf_op jit(solution)/shard_map/ppermute | solution.py:13
  7.1 9.5 %collective-permute-start.2 = (f32[2,64,34]{1,0,2:T(2,128)S(1)}, f32[2,64,34]{1,0,2:T(2,128)S(1)}, u32[]{:S(2)}, u32[]{:S(2)}) collective-permute-start(f32[2,64,34]{1,0,2:T(2,128)S(1)} %pad_maximum_fusion.3), channel_id=1, source_target_pairs={{0,12},{4,0},{8,4},{12,8},{1,13},{5,1},{9,5},{13,9},{2,14},{6,2},{... | collective-permute-start | bytes 52232 | tf_op jit(solution)/shard_map/ppermute | solution.py:13
  9.2 7.5 %collective-permute-start.1 = (f32[2,64,34]{1,0,2:T(2,128)S(1)}, f32[2,64,34]{1,0,2:T(2,128)S(1)}, u32[]{:S(2)}, u32[]{:S(2)}) collective-permute-start(f32[2,64,34]{1,0,2:T(2,128)S(1)} %pad_maximum_fusion.3), channel_id=1, source_target_pairs={{0,8},{4,12},{8,0},{12,4},{1,9},{5,13},{9,1},{13,5},{2,10},{6,14},... | collective-permute-start | bytes 52232 | tf_op jit(solution)/shard_map/ppermute | solution.py:13
  39.5 1.8 %copy-start.6 = (bf16[1,1280,160]{1,2,0:T(8,128)(2,1)S(1)}, bf16[1,1280,160]{1,2,0:T(8,128)(2,1)}, u32[]{:S(2)}) copy-start(bf16[1,1280,160]{1,2,0:T(8,128)(2,1)} %param.14) | copy-start | bytes 1228804
  39.7 6.0 %copy-start.3 = (bf16[1,1280,640]{2,1,0:T(8,128)(2,1)S(1)}, bf16[1,1280,640]{2,1,0:T(8,128)(2,1)}, u32[]{:S(2)}) copy-start(bf16[1,1280,640]{2,1,0:T(8,128)(2,1)} %param.12) | copy-start | bytes 4915204
  42.4 4.2 %collective-permute-start.5 = (bf16[2,2,2,80,128]{4,3,2,1,0:T(8,128)(2,1)}, bf16[2,2,2,80,128]{4,3,2,1,0:T(8,128)(2,1)S(1)}, u32[]{:S(2)}, u32[]{:S(2)}) collective-permute-start(bf16[2,2,2,80,128]{4,3,2,1,0:T(8,128)(2,1)} %pad_maximum_fusion.1), channel_id=1, source_target_pairs={{0,4},{4,8},{8,12},{2,6},{6,10},{10,14},{16,20},{20,24},{24,28},{1... | collective-permute-start | bytes 491528 | tf_op jit(solution)/shard_map/ppermute | solution.py:34
  43.1 3.6 %collective-permute-start.4 = (bf16[2,2,2,80,128]{4,3,2,1,0:T(8,128)(2,1)}, bf16[2,2,2,80,128]{4,3,2,1,0:T(8,128)(2,1)}, u32[]{:S(2)}, u32[]{:S(2)}) collective-permute-start(bf16[2,2,2,80,128]{4,3,2,1,0:T(8,128)(2,1)} %pad_maximum_fusion.1), channel_id=1, source_target_pairs={{0,8},{4,12},{2,10},{6,14},{16,24},{20,28},{18,26},{22,30}} | collective-permute-start | bytes 491528 | tf_op jit(solution)/shard_map/ppermute | solution.py:34
  44.4 2.3 %collective-permute-start.3 = (bf16[2,2,2,80,128]{4,3,2,1,0:T(8,128)(2,1)}, bf16[2,2,2,80,128]{4,3,2,1,0:T(8,128)(2,1)}, u32[]{:S(2)}, u32[]{:S(2)}) collective-permute-start(bf16[2,2,2,80,128]{4,3,2,1,0:T(8,128)(2,1)} %pad_maximum_fusion.1), channel_id=1, source_target_pairs={{0,12},{2,14},{16,28},{18,30}} | collective-permute-start | bytes 491528 | tf_op jit(solution)/shard_map/ppermute | solution.py:34
  51.9 18.7 %copy-start.5 = (bf16[1,1280,160]{1,2,0:T(8,128)(2,1)S(1)}, bf16[1,1280,160]{1,2,0:T(8,128)(2,1)}, u32[]{:S(2)}) copy-start(bf16[1,1280,160]{1,2,0:T(8,128)(2,1)} %param.13) | copy-start | bytes 1228804
  51.9 17.0 %collective-permute-start.7 = (bf16[2,128,1280]{2,1,0:T(8,128)(2,1)}, bf16[2,128,1280]{2,1,0:T(8,128)(2,1)}, u32[]{:S(2)}, u32[]{:S(2)}) collective-permute-start(bf16[2,128,1280]{2,1,0:T(8,128)(2,1)} %convolution_convert_fusion), channel_id=1, source_target_pairs={{0,3},{2,1},{4,7},{6,5},{8,11},{10,9},{12,15},{14,13},{16,19},{18,... | collective-permute-start | bytes 1966088 | tf_op jit(solution)/shard_map/ppermute | solution.py:225
  53.3 15.6 %collective-permute-start.6 = (bf16[2,128,1280]{2,1,0:T(8,128)(2,1)}, bf16[2,128,1280]{2,1,0:T(8,128)(2,1)}, u32[]{:S(2)}, u32[]{:S(2)}) collective-permute-start(bf16[2,128,1280]{2,1,0:T(8,128)(2,1)} %convolution_convert_fusion), channel_id=1, source_target_pairs={{0,1},{2,3},{4,5},{6,7},{8,9},{10,11},{12,13},{14,15},{16,17},{18,... | collective-permute-start | bytes 1966088 | tf_op jit(solution)/shard_map/ppermute | solution.py:225
  54.6 16.4 %copy-start.7 = (bf16[1,1280,160]{1,2,0:T(8,128)(2,1)S(1)}, bf16[1,1280,160]{1,2,0:T(8,128)(2,1)}, u32[]{:S(2)}) copy-start(bf16[1,1280,160]{1,2,0:T(8,128)(2,1)} %param.14) | copy-start | bytes 1228804
  70.6 1.4 %copy-start.4 = (bf16[1,1280,640]{2,1,0:T(8,128)(2,1)S(1)}, bf16[1,1280,640]{2,1,0:T(8,128)(2,1)}, u32[]{:S(2)}) copy-start(bf16[1,1280,640]{2,1,0:T(8,128)(2,1)} %param.12) | copy-start | bytes 4915204
  74.1 12.4 %collective-permute-start.10 = (bf16[2,2,2,80,128]{4,3,2,1,0:T(8,128)(2,1)}, bf16[2,2,2,80,128]{4,3,2,1,0:T(8,128)(2,1)S(1)}, u32[]{:S(2)}, u32[]{:S(2)}) collective-permute-start(bf16[2,2,2,80,128]{4,3,2,1,0:T(8,128)(2,1)} %pad_maximum_fusion.2), channel_id=1, source_target_pairs={{1,5},{5,9},{9,13},{3,7},{7,11},{11,15},{17,21},{21,25},{25,29},{1... | collective-permute-start | bytes 491528 | tf_op jit(solution)/shard_map/ppermute | solution.py:34
  77.8 8.8 %collective-permute-start.9 = (bf16[2,2,2,80,128]{4,3,2,1,0:T(8,128)(2,1)}, bf16[2,2,2,80,128]{4,3,2,1,0:T(8,128)(2,1)S(1)}, u32[]{:S(2)}, u32[]{:S(2)}) collective-permute-start(bf16[2,2,2,80,128]{4,3,2,1,0:T(8,128)(2,1)} %pad_maximum_fusion.2), channel_id=1, source_target_pairs={{1,9},{5,13},{3,11},{7,15},{17,25},{21,29},{19,27},{23,31}} | collective-permute-start | bytes 491528 | tf_op jit(solution)/shard_map/ppermute | solution.py:34
  82.7 4.3 %collective-permute-start.8 = (bf16[2,2,2,80,128]{4,3,2,1,0:T(8,128)(2,1)}, bf16[2,2,2,80,128]{4,3,2,1,0:T(8,128)(2,1)}, u32[]{:S(2)}, u32[]{:S(2)}) collective-permute-start(bf16[2,2,2,80,128]{4,3,2,1,0:T(8,128)(2,1)} %pad_maximum_fusion.2), channel_id=1, source_target_pairs={{1,13},{3,15},{17,29},{19,31}} | collective-permute-start | bytes 491528 | tf_op jit(solution)/shard_map/ppermute | solution.py:34
  91.4 6.5 %collective-permute-start.13 = (bf16[1,128,640]{2,1,0:T(8,128)(2,1)S(1)}, bf16[1,128,640]{2,1,0:T(8,128)(2,1)S(1)}, u32[]{:S(2)}, u32[]{:S(2)}) collective-permute-start(bf16[1,128,640]{2,1,0:T(8,128)(2,1)S(1)} %dynamic-slice_convert_fusion), channel_id=1, source_target_pairs={{1,3},{3,1},{5,7},{7,5},{9,11},{11,9},{13,15},{15,13},{17,19},{19,... | collective-permute-start | bytes 491528 | tf_op jit(solution)/shard_map/ppermute | solution.py:254
  94.6 4.0 %collective-permute-start.12 = (bf16[1,128,640]{2,1,0:T(8,128)(2,1)S(1)}, bf16[1,128,640]{2,1,0:T(8,128)(2,1)S(1)}, u32[]{:S(2)}, u32[]{:S(2)}) collective-permute-start(bf16[1,128,640]{2,1,0:T(8,128)(2,1)S(1)} %dynamic-slice_convert_fusion.1), channel_id=1, source_target_pairs={{1,2},{3,0},{5,6},{7,4},{9,10},{11,8},{13,14},{15,12},{17,18},{19,... | collective-permute-start | bytes 491528 | tf_op jit(solution)/shard_map/ppermute | solution.py:250
  96.0 2.6 %collective-permute-start.11 = (bf16[1,128,640]{2,1,0:T(8,128)(2,1)S(1)}, bf16[1,128,640]{2,1,0:T(8,128)(2,1)S(1)}, u32[]{:S(2)}, u32[]{:S(2)}) collective-permute-start(bf16[1,128,640]{2,1,0:T(8,128)(2,1)S(1)} %add_convert_fusion), channel_id=1, source_target_pairs={{1,0},{3,2},{5,4},{7,6},{9,8},{11,10},{13,12},{15,14},{17,16},{19,... | collective-permute-start | bytes 491528 | tf_op jit(solution)/shard_map/ppermute | solution.py:250

commit v15 on v14

--- a/solution.py
+++ b/solution.py
@@ -126,7 +126,7 @@
     if out_w is None:
         return attended, key_t, value_t
     partial_value = jnp.einsum("bte,ed->btd", attended, out_w, preferred_element_type=jnp.float32)
-    return partial_value, key_t, value_t
+    return partial_value, key_t, value_t, attended
 
 
 def per_device(
@@ -210,23 +210,27 @@
     ).astype(jnp.bfloat16)
     tokens = tokens.reshape(seq_count, tok_count, tokens.shape[2])
     column_count = patch_weight.shape[1]
+    rows_out, tokens = lax.optimization_barrier((out_weight[0], tokens))
+    on_chip = [(m * sec_n, m * sec_n + 1) for m in range(mp_n)]
+    partner_rows = lax.ppermute(rows_out, feat_axes, on_chip)
     hidden0 = lax.all_gather(tokens, feat_axes, axis=2, tiled=True)
     feature_count = hidden0.shape[2]
     head_cols = feature_count // mp_n
     sizes = (tm_n, sec_n, tm_at, total_tokens)
 
-    partial0, key0, value0 = attend_layer(
+    partial0, key0, value0, attended0 = attend_layer(
         hidden0, lengths, norm_gain[0], query_weight[0], key_weight[0], value_weight[0],
         out_weight[0], sizes, 0,
     )
-    head_sum = None
-    for by in range(mp_n):
+    arrived = lax.ppermute(attended0, feat_axes, on_chip)
+    head_sum = jnp.einsum("bte,ed->btd", arrived, partner_rows, preferred_element_type=jnp.float32)
+    for by in range(1, mp_n):
         pairs = [(m * sec_n, ((m + by) % mp_n) * sec_n + 1) for m in range(mp_n)]
         term = lax.ppermute(partial0.astype(jnp.bfloat16), feat_axes, pairs).astype(jnp.float32)
-        head_sum = term if head_sum is None else head_sum + term
+        head_sum = head_sum + term
     hidden1 = (hidden0.astype(jnp.float32) + head_sum).astype(jnp.bfloat16)
 
-    partial1, key1, value1 = attend_layer(
+    partial1, key1, value1, _ = attend_layer(
         hidden1, lengths, norm_gain[0], query_weight[0], key_weight[0], value_weight[0],
         out_weight[0], sizes, 1,
     )

time: 101 us -> 107 us (1.059)
  local copies, waits for them, and re-layouts: 12.6 us -> 19.2 us
  matrix products: 16.5 us -> 20.9 us
  waiting for transfers between devices: 15.4 us -> 11.9 us
  starting transfers between devices: 27 us -> 25.5 us
    ppermute x2 -> x1, waiting for transfers between devices: 14.2 us -> 3.22 us  [per_device(): lax.ppermute(partial0.astype(jnp.bfloat16), feat_axes, pairs)]
    ppermute x0 -> x2, waiting for transfers between devices: none -> 8 us  [the longest x1 8 us: per_device(): arrived = lax.ppermute(attended0, feat_axes, on_chip)]
    ppermute x6, starting transfers between devices: 13.8 us -> 10.9 us  [gather_causal(): pieces.append(lax.ppermute(value, ('tm', 'section'), pairs))]
    ppermute x0 -> x2, starting transfers between devices: none -> 2.74 us  [the longest x1 1.46 us: per_device(): partner_rows = lax.ppermute(rows_out, feat_axes, on_chip)]
    dot_general x0 -> x1, matrix products: none -> 2.72 us  [per_device(): jnp.einsum('bte,ed->btd', arrived, partner_rows, preferred_element_type=j...]
    convert_element_type x2, local copies, waits for them, and re-layouts: 1.39 us -> 3.73 us  [attend_layer(): queries = (jnp.einsum('btd,de->bte', layer_input, query_w, preferred_elem...]
    dot_general x2, matrix products: 2.17 us -> 3.98 us  [attend_layer(): jnp.einsum('btd,de->bte', layer_input, query_w, preferred_element_type=jn...]
    reshape x1, local copies, waits for them, and re-layouts: 0.17 us -> 1.85 us  [attend_layer(): attended.transpose(0, 3, 1, 2, 4)]
  transfers between devices with their start and end apart: 14 -> 15, of which waited for: 3 -> 3; matrix products, arithmetic and copies ran while one was open for 11% -> 23% of each run, Pallas kernels for 0% -> 0%
where the time goes in v15:
time: 107 us; the launch traced here: 105 us
  starting transfers between devices  25.5 us (24%)
  matrix products  20.9 us (20%)
  local copies, waits for them, and re-layouts  19.2 us (18%)
  other arithmetic  17 us (16%)
  waiting for transfers between devices  11.9 us (11%)
  blocking collectives  9.24 us (9%)
  between operations  1.25 us (1%)
    ppermute x6, starting transfers between devices, gather_causal(): pieces.append(lax.ppermute(value, ('tm', 'section'), pairs))  10.9 us
    all_gather x1, blocking collectives, per_device(): hidden0 = lax.all_gather(tokens, feat_axes, axis=2, tiled=True)  9.24 us
    ppermute x1, waiting for transfers between devices, per_device(): arrived = lax.ppermute(attended0, feat_axes, on_chip)  8 us
    unnamed x36, local copies, waits for them, and re-layouts  6.64 us
    conv_general_dilated x1, matrix products, per_device(): lax.conv_general_dilated(chunks, kernel, window_strides=(STRIDE,), paddin...  5.66 us
    ppermute x3, starting transfers between devices, shift_from(): return lax.ppermute(value, axis, pairs)  4.66 us
    dot_general x2, matrix products, attend_layer(): jnp.einsum('btd,de->bte', layer_input, query_w, preferred_element_type=jn...  3.98 us
    convert_element_type x2, local copies, waits for them, and re-layouts, attend_layer(): queries = (jnp.einsum('btd,de->bte', layer_input, query_w, preferred_elem...  3.73 us
  transfers between devices with their start and end apart: 15, of which 3 were waited for; matrix products, arithmetic and copies ran while one was open for 23% of the time, Pallas kernels for 0%

profile of v15, /device:TPU:1, one launch (start us, length us, event | category | flops | bytes accessed | tf_op | source)
XLA Modules:
  0.0 104.9 jit_solution(11372613523089560107)
XLA Ops:
  2.8 1.5 %multiply_reduce_fusion.1 = f32[2,64]{1,0:T(2,128)S(1)} fusion(f32[2,4096]{1,0:T(2,128)S(1)} %compare_convert_fusion, bf16[2,64,4096]{2,1,0:T(8,128)(2,1)} %param.8), kind=kLoop, calls=%fused_computation.29 | loop fusion | flops 1572736 | bytes 1081856 | tf_op jit(solution)/shard_map/reduce_sum | solution.py:151
  4.9 2.2 %collective-permute-start = (f32[2,64,34]{1,0,2:T(2,128)S(1)}, f32[2,64,34]{1,0,2:T(2,128)S(1)}, u32[]{:S(2)}, u32[]{:S(2)}) collective-permute-start(f32[2,64,34]{1,0,2:T(2,128)S(1)} %pad_maximum_fusion.3), channel_id=1, source_target_pairs={{0,4},{4,8},{8,12},{12,0},{1,5},{5,9},{9,13},{13,1},{2,6},{6,10},{... | collective-permute-start | bytes 52232 | tf_op jit(solution)/shard_map/ppermute | solution.py:13
  7.1 2.1 %collective-permute-start.2 = (f32[2,64,34]{1,0,2:T(2,128)S(1)}, f32[2,64,34]{1,0,2:T(2,128)S(1)}, u32[]{:S(2)}, u32[]{:S(2)}) collective-permute-start(f32[2,64,34]{1,0,2:T(2,128)S(1)} %pad_maximum_fusion.3), channel_id=1, source_target_pairs={{0,12},{4,0},{8,4},{12,8},{1,13},{5,1},{9,5},{13,9},{2,14},{6,2},{... | collective-permute-start | bytes 52232 | tf_op jit(solution)/shard_map/ppermute | solution.py:13
  10.4 1.5 %convert_element_type.145 = f32[2,64,4096]{2,1,0:T(8,128)} convert(bf16[2,64,4096]{2,1,0:T(8,128)(2,1)S(1)} %copy-done.1) | non-fusion elementwise | flops 524288 | bytes 3145728 | tf_op jit(solution)/shard_map/convert_element_type | solution.py:149
  12.0 4.5 %copy.41 = bf16[4096,320]{1,0:T(8,128)(2,1)} copy(bf16[4096,320]{0,1:T(8,128)(2,1)} %param.10) | data formatting | bytes 5242880 | tf_op args[2]
  17.6 2.3 %fusion.13 = bf16[2,64,4128]{2,1,0:T(8,128)(2,1)S(1)} fusion(f32[2,64,4096]{2,1,0:T(8,128)} %convert_element_type.145, f32[2,64,32]{2,1,0:T(8,128)S(1)} %copy.38, f32[2,64]{1,0:T(2,128)S(1)} %add_rsqrt_fusion.2, f32[2,64]{1,0:T(2,128)S(1)} %broadcast_divide_fusion, f32[2,4128]{1,0:T(2,128)S(1)} %and_convert_fusion), kind=kLoop, calls=%fused_computation.21 | loop fusion | flops 3170304 | bytes 3204352 | tf_op jit(solution)/shard_map/convert_element_type | solution.py:192
  20.2 3.2 %copy.40 = bf16[2,4,64,1056]{2,1,0,3:T(4,128)(2,1)} copy(bf16[2,4,64,1056]{3,2,0,1:T(8,128)(2,1)S(1)} %pad_maximum_fusion) | data formatting | bytes 2162688 | tf_op jit(solution)/shard_map/stack | solution.py:196
  23.4 5.7 %fusion.62 = bf16[8,32,320]{2,0,1:T(8,128)(2,1)S(1)} fusion(bf16[8,64,1056]{1,0,2:T(8,128)(2,1)} %bitcast.203, bf16[64,64,320]{2,1,0:T(8,128)(2,1)} %bitcast.202), kind=kOutput, calls=%fused_computation.59 | convolution fusion | flops 671170560 | bytes 3866624 | tf_op jit(solution)/shard_map/conv_general_dilated | solution.py:203
  29.3 9.2 %all_gather.3 = bf16[2,128,1280]{1,0,2:T(2,128)(2,1)S(1)} all-gather(bf16[2,128,320]{1,0,2:T(2,128)(2,1)S(1)} %copy.44), channel_id=1, replica_groups=mesh['groups'=2,'tm'=4,'mp'=2,'section'=2] {'mp','section'}, dimensions={2}, use_global_device_ids=true | all-gather | bytes 819200 | tf_op jit(solution)/shard_map/all_gather | solution.py:216
  46.1 2.5 %fusion.59 = bf16[2,128,640]{2,1,0:T(8,128)(2,1)} fusion(bf16[1,1280,640]{2,1,0:T(8,128)(2,1)S(1)} %copy-done, bf16[2,128,1280]{2,1,0:T(8,128)(2,1)} %copy-done.3, f32[1280]{0:T(1024)S(1)} %convert_reduce_fusion, f32[2,128]{1,0:T(2,128)S(1)} %add_rsqrt_fusion.1), kind=kOutput, calls=%fused_computation.57 | convolution fusion | flops 421068800 | bytes 2627584 | tf_op jit(solution)/shard_map/btd,de->bte/dot_general | solution.py:72
  48.6 1.9 %copy.46 = bf16[2,128,640]{1,2,0:T(8,128)(2,1)} copy(bf16[2,128,640]{2,1,0:T(8,128)(2,1)} %fusion.59) | data formatting | bytes 655360 | tf_op jit(solution)/shard_map/convert_element_type | solution.py:74
  50.5 1.5 %collective-permute-start.7 = (bf16[640,1280]{1,0:T(8,128)(2,1)S(1)}, bf16[640,1280]{1,0:T(8,128)(2,1)}, u32[]{:S(2)}, u32[]{:S(2)}) collective-permute-start(bf16[640,1280]{1,0:T(8,128)(2,1)S(1)} %bitcast.201), channel_id=1, source_target_pairs={{0,1},{2,3},{4,5},{6,7},{8,9},{10,11},{12,13},{14,15},{16,17},{18,... | collective-permute-start | bytes 4915208 | tf_op jit(solution)/shard_map/ppermute | solution.py:215
  53.2 1.8 %fusion = (f32[2,2,4,128]{3,2,1,0:T(4,128)S(1)}, f32[2,2,512,128,4]{3,2,4,1,0:T(8,128)S(1)}) fusion(pred[2,128,512]{1,2,0:T(8,128)(4,1)S(1)} %or_and_fusion, bf16[2,128,2,4,80]{1,4,3,2,0:T(8,128)(2,1)} %bitcast.204, bf16[1,2,2,2,80,512]{5,4,3,2,1,0:T(8,128)(2,1)S(1)} %maximum_bitcast_fusion), kind=kOutput, calls=%fused_computation.5 | convolution fusion | flops 169867264 | bytes 4988928 | tf_op jit(solution)/shard_map/btkgh,bkhn->bkgtn/dot_general | solution.py:47
  57.4 1.5 %convolution_convert_fusion = bf16[2,128,1280]{2,1,0:T(8,128)(2,1)} fusion(bf16[2,128,640]{1,2,0:T(8,128)(2,1)S(1)} %bitcast.206, bf16[1,640,1280]{2,1,0:T(8,128)(2,1)S(1)} %copy-done.2), kind=kOutput, calls=%fused_computation.15 | convolution fusion | flops 419758080 | bytes 2621440 | tf_op jit(solution)/shard_map/bte,ed->btd/dot_general | solution.py:128
  60.3 1.9 %copy.48 = bf16[2,128,640]{2,1,0:T(8,128)(2,1)} copy(bf16[2,128,640]{1,2,0:T(8,128)(2,1)} %bitcast.207) | data formatting | bytes 655360 | tf_op jit(solution)/shard_map/reshape | solution.py:123
  63.4 8.0 %collective-permute-done.6 = bf16[2,128,640]{2,1,0:T(8,128)(2,1)} collective-permute-done((bf16[2,128,640]{2,1,0:T(8,128)(2,1)}, bf16[2,128,640]{2,1,0:T(8,128)(2,1)}, u32[]{:S(2)}, u32[]{:S(2)}) %collective-permute-start.6) | collective-permute-done | bytes 327712 | tf_op jit(solution)/shard_map/ppermute | solution.py:225
  71.5 3.2 %collective-permute-done.8 = bf16[2,128,1280]{2,1,0:T(8,128)(2,1)} collective-permute-done((bf16[2,128,1280]{2,1,0:T(8,128)(2,1)}, bf16[2,128,1280]{2,1,0:T(8,128)(2,1)}, u32[]{:S(2)}, u32[]{:S(2)}) %collective-permute-start.8) | collective-permute-done | bytes 655392 | tf_op jit(solution)/shard_map/ppermute | solution.py:229
  74.7 2.7 %fusion.32 = (f32[2,128]{1,0:T(2,128)S(1)}, bf16[2,128,1280]{2,1,0:T(8,128)(2,1)S(1)}) fusion(bf16[2,128,1280]{2,1,0:T(8,128)(2,1)} %collective-permute-done.8, bf16[2,128,640]{2,1,0:T(8,128)(2,1)} %collective-permute-done.6, bf16[640,1280]{1,0:T(8,128)(2,1)} %collective-permute-done.7, bf16[2,128,1280]{2,1,0:T(8,128)(2,1)} %copy-done.3), kind=kOutput, calls=%fused_computation.44 | convolution fusion | flops 422051584 | bytes 3933184 | tf_op jit(solution)/shard_map/bte,ed->btd/dot_general | solution.py:226
  81.0 2.0 %collective-permute-start.11 = (bf16[2,2,2,80,128]{4,3,2,1,0:T(8,128)(2,1)}, bf16[2,2,2,80,128]{4,3,2,1,0:T(8,128)(2,1)}, u32[]{:S(2)}, u32[]{:S(2)}) collective-permute-start(bf16[2,2,2,80,128]{4,3,2,1,0:T(8,128)(2,1)} %pad_maximum_fusion.2), channel_id=1, source_target_pairs={{1,5},{5,9},{9,13},{3,7},{7,11},{11,15},{17,21},{21,25},{25,29},{1... | collective-permute-start | bytes 491528 | tf_op jit(solution)/shard_map/ppermute | solution.py:34
  83.0 2.9 %collective-permute-start.10 = (bf16[2,2,2,80,128]{4,3,2,1,0:T(8,128)(2,1)}, bf16[2,2,2,80,128]{4,3,2,1,0:T(8,128)(2,1)}, u32[]{:S(2)}, u32[]{:S(2)}) collective-permute-start(bf16[2,2,2,80,128]{4,3,2,1,0:T(8,128)(2,1)} %pad_maximum_fusion.2), channel_id=1, source_target_pairs={{1,9},{5,13},{3,11},{7,15},{17,25},{21,29},{19,27},{23,31}} | collective-permute-start | bytes 491528 | tf_op jit(solution)/shard_map/ppermute | solution.py:34
  85.8 1.9 %collective-permute-start.9 = (bf16[2,2,2,80,128]{4,3,2,1,0:T(8,128)(2,1)}, bf16[2,2,2,80,128]{4,3,2,1,0:T(8,128)(2,1)}, u32[]{:S(2)}, u32[]{:S(2)}) collective-permute-start(bf16[2,2,2,80,128]{4,3,2,1,0:T(8,128)(2,1)} %pad_maximum_fusion.2), channel_id=1, source_target_pairs={{1,13},{3,15},{17,29},{19,31}} | collective-permute-start | bytes 491528 | tf_op jit(solution)/shard_map/ppermute | solution.py:34
  88.7 1.9 %copy.50 = bf16[2,128,640]{1,2,0:T(8,128)(2,1)} copy(bf16[2,128,640]{2,1,0:T(8,128)(2,1)} %fusion.56) | data formatting | bytes 655360 | tf_op jit(solution)/shard_map/convert_element_type | solution.py:74
  90.5 1.6 %broadcast_select_fusion.1 = bf16[1,2,2,80,128]{4,3,2,1,0:T(8,128)(2,1)} fusion(bf16[1,2,2,80,128]{4,3,2,1,0:T(8,128)(2,1)} %bitcast.214, bf16[1,2,2,80,128]{4,3,2,1,0:T(8,128)(2,1)} %bitcast.219, pred[]{:T(512)S(6)} %eq.13), kind=kLoop, calls=%fused_computation.94 | loop fusion | flops 40960 | bytes 245761 | tf_op jit(solution)/shard_map/jit(_where)/select_n | solution.py:238
  96.8 3.3 %collective-permute-start.14 = (bf16[1,128,640]{2,1,0:T(8,128)(2,1)S(1)}, bf16[1,128,640]{2,1,0:T(8,128)(2,1)S(1)}, u32[]{:S(2)}, u32[]{:S(2)}) collective-permute-start(bf16[1,128,640]{2,1,0:T(8,128)(2,1)S(1)} %dynamic-slice_convert_fusion), channel_id=1, source_target_pairs={{1,3},{3,1},{5,7},{7,5},{9,11},{11,9},{13,15},{15,13},{17,19},{19,... | collective-permute-start | bytes 491528 | tf_op jit(solution)/shard_map/ppermute | solution.py:258
  (129 shorter events, 32.9 us)
Async XLA Ops:
  0.6 45.5 %copy-start = (bf16[1,1280,640]{2,1,0:T(8,128)(2,1)S(1)}, bf16[1,1280,640]{2,1,0:T(8,128)(2,1)}, u32[]{:S(2)}) copy-start(bf16[1,1280,640]{2,1,0:T(8,128)(2,1)} %param.12) | copy-start | bytes 4915204
  0.6 3.7 %copy-start.1 = (bf16[2,64,4096]{2,1,0:T(8,128)(2,1)S(1)}, bf16[2,64,4096]{2,1,0:T(8,128)(2,1)}, u32[]{:S(2)}) copy-start(bf16[2,64,4096]{2,1,0:T(8,128)(2,1)} %param.8) | copy-start | bytes 3145732
  0.7 9.1 %copy-start.12 = (bf16[1,1280]{1,0:T(2,128)(2,1)S(1)}, bf16[1,1280]{1,0:T(2,128)(2,1)}, u32[]{:S(2)}) copy-start(bf16[1,1280]{1,0:T(2,128)(2,1)} %param.11) | copy-start | bytes 7684
  4.9 11.6 %collective-permute-start = (f32[2,64,34]{1,0,2:T(2,128)S(1)}, f32[2,64,34]{1,0,2:T(2,128)S(1)}, u32[]{:S(2)}, u32[]{:S(2)}) collective-permute-start(f32[2,64,34]{1,0,2:T(2,128)S(1)} %pad_maximum_fusion.3), channel_id=1, source_target_pairs={{0,4},{4,8},{8,12},{12,0},{1,5},{5,9},{9,13},{13,1},{2,6},{6,10},{... | collective-permute-start | bytes 52232 | tf_op jit(solution)/shard_map/ppermute | solution.py:13
  7.1 9.4 %collective-permute-start.2 = (f32[2,64,34]{1,0,2:T(2,128)S(1)}, f32[2,64,34]{1,0,2:T(2,128)S(1)}, u32[]{:S(2)}, u32[]{:S(2)}) collective-permute-start(f32[2,64,34]{1,0,2:T(2,128)S(1)} %pad_maximum_fusion.3), channel_id=1, source_target_pairs={{0,12},{4,0},{8,4},{12,8},{1,13},{5,1},{9,5},{13,9},{2,14},{6,2},{... | collective-permute-start | bytes 52232 | tf_op jit(solution)/shard_map/ppermute | solution.py:13
  9.2 7.4 %collective-permute-start.1 = (f32[2,64,34]{1,0,2:T(2,128)S(1)}, f32[2,64,34]{1,0,2:T(2,128)S(1)}, u32[]{:S(2)}, u32[]{:S(2)}) collective-permute-start(f32[2,64,34]{1,0,2:T(2,128)S(1)} %pad_maximum_fusion.3), channel_id=1, source_target_pairs={{0,8},{4,12},{8,0},{12,4},{1,9},{5,13},{9,1},{13,5},{2,10},{6,14},... | collective-permute-start | bytes 52232 | tf_op jit(solution)/shard_map/ppermute | solution.py:13
  29.1 10.6 %copy-start.13 = (bf16[1,1280,160]{1,2,0:T(8,128)(2,1)S(1)}, bf16[1,1280,160]{1,2,0:T(8,128)(2,1)}, u32[]{:S(2)}) copy-start(bf16[1,1280,160]{1,2,0:T(8,128)(2,1)} %param.13) | copy-start | bytes 1228804
  42.0 8.5 %copy-start.2 = (bf16[1,640,1280]{2,1,0:T(8,128)(2,1)S(1)}, bf16[1,640,1280]{2,1,0:T(8,128)(2,1)}, u32[]{:S(2)}) copy-start(bf16[1,640,1280]{2,1,0:T(8,128)(2,1)} %param.15) | copy-start | bytes 4915204
  42.0 10.0 %collective-permute-start.5 = (bf16[2,2,2,80,128]{4,3,2,1,0:T(8,128)(2,1)}, bf16[2,2,2,80,128]{4,3,2,1,0:T(8,128)(2,1)}, u32[]{:S(2)}, u32[]{:S(2)}) collective-permute-start(bf16[2,2,2,80,128]{4,3,2,1,0:T(8,128)(2,1)} %pad_maximum_fusion.1), channel_id=1, source_target_pairs={{0,4},{4,8},{8,12},{2,6},{6,10},{10,14},{16,20},{20,24},{24,28},{1... | collective-permute-start | bytes 491528 | tf_op jit(solution)/shard_map/ppermute | solution.py:34
  43.5 8.5 %collective-permute-start.4 = (bf16[2,2,2,80,128]{4,3,2,1,0:T(8,128)(2,1)}, bf16[2,2,2,80,128]{4,3,2,1,0:T(8,128)(2,1)}, u32[]{:S(2)}, u32[]{:S(2)}) collective-permute-start(bf16[2,2,2,80,128]{4,3,2,1,0:T(8,128)(2,1)} %pad_maximum_fusion.1), channel_id=1, source_target_pairs={{0,8},{4,12},{2,10},{6,14},{16,24},{20,28},{18,26},{22,30}} | collective-permute-start | bytes 491528 | tf_op jit(solution)/shard_map/ppermute | solution.py:34
  44.8 7.2 %collective-permute-start.3 = (bf16[2,2,2,80,128]{4,3,2,1,0:T(8,128)(2,1)}, bf16[2,2,2,80,128]{4,3,2,1,0:T(8,128)(2,1)}, u32[]{:S(2)}, u32[]{:S(2)}) collective-permute-start(bf16[2,2,2,80,128]{4,3,2,1,0:T(8,128)(2,1)} %pad_maximum_fusion.1), channel_id=1, source_target_pairs={{0,12},{2,14},{16,28},{18,30}} | collective-permute-start | bytes 491528 | tf_op jit(solution)/shard_map/ppermute | solution.py:34
  50.5 24.2 %collective-permute-start.7 = (bf16[640,1280]{1,0:T(8,128)(2,1)S(1)}, bf16[640,1280]{1,0:T(8,128)(2,1)}, u32[]{:S(2)}, u32[]{:S(2)}) collective-permute-start(bf16[640,1280]{1,0:T(8,128)(2,1)S(1)} %bitcast.201), channel_id=1, source_target_pairs={{0,1},{2,3},{4,5},{6,7},{8,9},{10,11},{12,13},{14,15},{16,17},{18,... | collective-permute-start | bytes 4915208 | tf_op jit(solution)/shard_map/ppermute | solution.py:215
  59.0 15.7 %collective-permute-start.8 = (bf16[2,128,1280]{2,1,0:T(8,128)(2,1)}, bf16[2,128,1280]{2,1,0:T(8,128)(2,1)}, u32[]{:S(2)}, u32[]{:S(2)}) collective-permute-start(bf16[2,128,1280]{2,1,0:T(8,128)(2,1)} %convolution_convert_fusion), channel_id=1, source_target_pairs={{0,3},{2,1},{4,7},{6,5},{8,11},{10,9},{12,15},{14,13},{16,19},{18,... | collective-permute-start | bytes 1966088 | tf_op jit(solution)/shard_map/ppermute | solution.py:229
  62.1 9.3 %collective-permute-start.6 = (bf16[2,128,640]{2,1,0:T(8,128)(2,1)}, bf16[2,128,640]{2,1,0:T(8,128)(2,1)}, u32[]{:S(2)}, u32[]{:S(2)}) collective-permute-start(bf16[2,128,640]{2,1,0:T(8,128)(2,1)} %copy.48), channel_id=1, source_target_pairs={{0,1},{2,3},{4,5},{6,7},{8,9},{10,11},{12,13},{14,15},{16,17},{18,... | collective-permute-start | bytes 983048 | tf_op jit(solution)/shard_map/ppermute | solution.py:225
  63.4 14.0 %copy-start.14 = (bf16[1,1280,160]{1,2,0:T(8,128)(2,1)S(1)}, bf16[1,1280,160]{1,2,0:T(8,128)(2,1)}, u32[]{:S(2)}) copy-start(bf16[1,1280,160]{1,2,0:T(8,128)(2,1)} %param.13) | copy-start | bytes 1228804
  81.0 11.1 %collective-permute-start.11 = (bf16[2,2,2,80,128]{4,3,2,1,0:T(8,128)(2,1)}, bf16[2,2,2,80,128]{4,3,2,1,0:T(8,128)(2,1)}, u32[]{:S(2)}, u32[]{:S(2)}) collective-permute-start(bf16[2,2,2,80,128]{4,3,2,1,0:T(8,128)(2,1)} %pad_maximum_fusion.2), channel_id=1, source_target_pairs={{1,5},{5,9},{9,13},{3,7},{7,11},{11,15},{17,21},{21,25},{25,29},{1... | collective-permute-start | bytes 491528 | tf_op jit(solution)/shard_map/ppermute | solution.py:34
  83.0 9.2 %collective-permute-start.10 = (bf16[2,2,2,80,128]{4,3,2,1,0:T(8,128)(2,1)}, bf16[2,2,2,80,128]{4,3,2,1,0:T(8,128)(2,1)}, u32[]{:S(2)}, u32[]{:S(2)}) collective-permute-start(bf16[2,2,2,80,128]{4,3,2,1,0:T(8,128)(2,1)} %pad_maximum_fusion.2), channel_id=1, source_target_pairs={{1,9},{5,13},{3,11},{7,15},{17,25},{21,29},{19,27},{23,31}} | collective-permute-start | bytes 491528 | tf_op jit(solution)/shard_map/ppermute | solution.py:34
  85.8 6.3 %collective-permute-start.9 = (bf16[2,2,2,80,128]{4,3,2,1,0:T(8,128)(2,1)}, bf16[2,2,2,80,128]{4,3,2,1,0:T(8,128)(2,1)}, u32[]{:S(2)}, u32[]{:S(2)}) collective-permute-start(bf16[2,2,2,80,128]{4,3,2,1,0:T(8,128)(2,1)} %pad_maximum_fusion.2), channel_id=1, source_target_pairs={{1,13},{3,15},{17,29},{19,31}} | collective-permute-start | bytes 491528 | tf_op jit(solution)/shard_map/ppermute | solution.py:34
  96.6 4.8 %copy-start.10 = (bf16[1,128,1280]{2,1,0:T(8,128)(2,1)S(1)}, bf16[1,128,1280]{2,1,0:T(8,128)(2,1)}, u32[]{:S(2)}) copy-start(bf16[1,128,1280]{2,1,0:T(8,128)(2,1)} %get-tuple-element.14) | copy-start | bytes 983044
  96.6 6.2 %copy-start.8 = (bf16[2,128,160]{1,2,0:T(8,128)(2,1)S(1)}, bf16[2,128,160]{1,2,0:T(8,128)(2,1)}, u32[]{:S(2)}) copy-start(bf16[2,128,160]{1,2,0:T(8,128)(2,1)} %copy-done.7) | copy-start | bytes 245764
  96.6 7.5 %copy-start.11 = (bf16[1,128,1280]{2,1,0:T(8,128)(2,1)S(1)}, bf16[1,128,1280]{2,1,0:T(8,128)(2,1)}, u32[]{:S(2)}) copy-start(bf16[1,128,1280]{2,1,0:T(8,128)(2,1)} %get-tuple-element.13) | copy-start | bytes 983044
  96.8 6.7 %collective-permute-start.14 = (bf16[1,128,640]{2,1,0:T(8,128)(2,1)S(1)}, bf16[1,128,640]{2,1,0:T(8,128)(2,1)S(1)}, u32[]{:S(2)}, u32[]{:S(2)}) collective-permute-start(bf16[1,128,640]{2,1,0:T(8,128)(2,1)S(1)} %dynamic-slice_convert_fusion), channel_id=1, source_target_pairs={{1,3},{3,1},{5,7},{7,5},{9,11},{11,9},{13,15},{15,13},{17,19},{19,... | collective-permute-start | bytes 491528 | tf_op jit(solution)/shard_map/ppermute | solution.py:258
  100.1 4.0 %collective-permute-start.13 = (bf16[1,128,640]{2,1,0:T(8,128)(2,1)S(1)}, bf16[1,128,640]{2,1,0:T(8,128)(2,1)S(1)}, u32[]{:S(2)}, u32[]{:S(2)}) collective-permute-start(bf16[1,128,640]{2,1,0:T(8,128)(2,1)S(1)} %dynamic-slice_convert_fusion.1), channel_id=1, source_target_pairs={{1,2},{3,0},{5,6},{7,4},{9,10},{11,8},{13,14},{15,12},{17,18},{19,... | collective-permute-start | bytes 491528 | tf_op jit(solution)/shard_map/ppermute | solution.py:254
  101.5 2.6 %collective-permute-start.12 = (bf16[1,128,640]{2,1,0:T(8,128)(2,1)S(1)}, bf16[1,128,640]{2,1,0:T(8,128)(2,1)S(1)}, u32[]{:S(2)}, u32[]{:S(2)}) collective-permute-start(bf16[1,128,640]{2,1,0:T(8,128)(2,1)S(1)} %add_convert_fusion), channel_id=1, source_target_pairs={{1,0},{3,2},{5,4},{7,6},{9,8},{11,10},{13,12},{15,14},{17,16},{19,... | collective-permute-start | bytes 491528 | tf_op jit(solution)/shard_map/ppermute | solution.py:254
  (8 other events, 11.5 us)

commit v16 on v14

--- a/solution.py
+++ b/solution.py
@@ -72,27 +72,24 @@
         jnp.einsum("btd,de->bte", layer_input, query_w, preferred_element_type=jnp.float32)
         * HD ** (-0.5)
     ).astype(jnp.bfloat16)
-    key_t = jnp.einsum(
-        "btd,de->bet", layer_input, key_w, preferred_element_type=jnp.float32
-    ).astype(jnp.bfloat16)
-    value_t = jnp.einsum(
-        "btd,de->bet", layer_input, value_w, preferred_element_type=jnp.float32
-    ).astype(jnp.bfloat16)
     kv_local = key_w.shape[1] // HD
     group_size = query_w.shape[1] // key_w.shape[1]
-    key_t = key_t.reshape(batch_count, kv_local, HD, tok_count)
-    value_t = value_t.reshape(batch_count, kv_local, HD, tok_count)
+    kv_t = jnp.einsum(
+        "btd,de->bet", layer_input, jnp.concatenate([key_w, value_w], 1),
+        preferred_element_type=jnp.float32,
+    ).astype(jnp.bfloat16)
+    kv_t = kv_t.reshape(batch_count, 2, kv_local, HD, tok_count)
+    key_t = kv_t[:, 0]
+    value_t = kv_t[:, 1]
     query_rows = queries.reshape(batch_count, tok_count, kv_local, group_size, HD)
     query_pos = tm_at * tok_count + jnp.arange(tok_count, dtype=jnp.int32)
     first_valid = total_tokens - seq_lens // STRIDE
-    both, key_pos = gather_causal(
-        jnp.stack([key_t, value_t], 0), tm_n, sec_n, tm_at, phase, tok_count
-    )
+    both, key_pos = gather_causal(kv_t, tm_n, sec_n, tm_at, phase, tok_count)
     key_count = both.shape[-1]
     block_width = 1024 if key_count % 1024 == 0 else key_count
     rounds = key_count // block_width
     blocks = jnp.moveaxis(
-        both.reshape(2, batch_count, kv_local, HD, rounds, block_width), 4, 0
+        both.reshape(batch_count, 2, kv_local, HD, rounds, block_width), 4, 0
     )
     pos_blocks = key_pos.reshape(rounds, block_width)
     start_state = (
@@ -102,7 +99,7 @@
     )
     if rounds == 1:
         result = absorb_block(
-            start_state, blocks[0, 0], blocks[0, 1], pos_blocks[0], query_rows, query_pos,
+            start_state, blocks[0][:, 0], blocks[0][:, 1], pos_blocks[0], query_rows, query_pos,
             first_valid,
         )
     else:
@@ -111,7 +108,7 @@
             kv_block, pos_block = block_item
             return (
                 absorb_block(
-                    state, kv_block[0], kv_block[1], pos_block, query_rows, query_pos,
+                    state, kv_block[:, 0], kv_block[:, 1], pos_block, query_rows, query_pos,
                     first_valid,
                 ),
                 None,

time: 101 us -> 97.9 us (0.969)
  the two profiles are of different devices: /device:TPU:1 before, /device:TPU:0 now
where the time goes in v16:
time: 97.9 us; the launch traced here: 97.2 us
  starting transfers between devices  25.3 us (26%)
  local copies, waits for them, and re-layouts  17.1 us (17%)
  waiting for transfers between devices  16.2 us (17%)
  matrix products  15 us (15%)
  other arithmetic  14.6 us (15%)
  blocking collectives  7.89 us (8%)
  between operations  1.2 us (1%)
    ppermute x6, starting transfers between devices, gather_causal(): pieces.append(lax.ppermute(value, ('tm', 'section'), pairs))  11.6 us
    ppermute x2, waiting for transfers between devices, per_device(): to_low.append(lax.ppermute(cols.astype(jnp.bfloat16), feat_axes, pairs))  11 us
    unnamed x22, local copies, waits for them, and re-layouts  9.47 us
    all_gather x1, blocking collectives, per_device(): hidden0 = lax.all_gather(tokens, feat_axes, axis=2, tiled=True)  7.89 us
    ppermute x3, starting transfers between devices, shift_from(): return lax.ppermute(value, axis, pairs)  6.11 us
    conv_general_dilated x1, matrix products, per_device(): lax.conv_general_dilated(chunks, kernel, window_strides=(STRIDE,), paddin...  5.66 us
    ppermute x2, waiting for transfers between devices, per_device(): lax.ppermute(partial0.astype(jnp.bfloat16), feat_axes, pairs)  5.11 us
    ppermute x2, starting transfers between devices, per_device(): lax.ppermute(partial0.astype(jnp.bfloat16), feat_axes, pairs)  4.28 us
  transfers between devices with their start and end apart: 14, of which 2 were waited for; matrix products, arithmetic and copies ran while one was open for 16% of the time, Pallas kernels for 0%

profile of v16, /device:TPU:0, one launch (start us, length us, event | category | flops | bytes accessed | tf_op | source)
XLA Modules:
  0.0 97.2 jit_solution(3991931336786180583)
XLA Ops:
  2.8 1.5 %multiply_reduce_fusion.1 = f32[2,64]{1,0:T(2,128)S(1)} fusion(f32[2,4096]{1,0:T(2,128)S(1)} %compare_convert_fusion, bf16[2,64,4096]{2,1,0:T(8,128)(2,1)} %param.8), kind=kLoop, calls=%fused_computation.26 | loop fusion | flops 1572736 | bytes 1081856 | tf_op jit(solution)/shard_map/reduce_sum | solution.py:148
  4.4 1.7 %multiply_reduce_fusion = f32[2,64]{1,0:T(2,128)S(1)} fusion(f32[2,64]{1,0:T(2,128)S(1)} %broadcast_divide_fusion.1, f32[2,4096]{1,0:T(2,128)S(1)} %compare_convert_fusion, bf16[2,64,4096]{2,1,0:T(8,128)(2,1)} %param.8), kind=kLoop, calls=%fused_computation.25 | loop fusion | flops 2621312 | bytes 1082368 | tf_op jit(solution)/shard_map/reduce_sum | solution.py:158
  6.1 3.1 %collective-permute-start = (f32[2,64,34]{1,0,2:T(2,128)S(1)}, f32[2,64,34]{1,0,2:T(2,128)S(1)}, u32[]{:S(2)}, u32[]{:S(2)}) collective-permute-start(f32[2,64,34]{1,0,2:T(2,128)S(1)} %pad_maximum_fusion.1), channel_id=1, source_target_pairs={{0,4},{4,8},{8,12},{12,0},{1,5},{5,9},{9,13},{13,1},{2,6},{6,10},{... | collective-permute-start | bytes 52232 | tf_op jit(solution)/shard_map/ppermute | solution.py:13
  9.2 2.1 %collective-permute-start.2 = (f32[2,64,34]{1,0,2:T(2,128)S(1)}, f32[2,64,34]{1,0,2:T(2,128)S(1)}, u32[]{:S(2)}, u32[]{:S(2)}) collective-permute-start(f32[2,64,34]{1,0,2:T(2,128)S(1)} %pad_maximum_fusion.1), channel_id=1, source_target_pairs={{0,12},{4,0},{8,4},{12,8},{1,13},{5,1},{9,5},{13,9},{2,14},{6,2},{... | collective-permute-start | bytes 52232 | tf_op jit(solution)/shard_map/ppermute | solution.py:13
  13.1 1.6 %convert_element_type.137 = f32[2,64,4096]{2,1,0:T(8,128)} convert(bf16[2,64,4096]{2,1,0:T(8,128)(2,1)S(1)} %copy-done.1) | non-fusion elementwise | flops 524288 | bytes 3145728 | tf_op jit(solution)/shard_map/convert_element_type | solution.py:146
  14.7 4.5 %copy.63 = bf16[4096,320]{1,0:T(8,128)(2,1)} copy(bf16[4096,320]{0,1:T(8,128)(2,1)} %param.10) | data formatting | bytes 5242880 | tf_op args[2]
  20.3 2.3 %fusion.11 = bf16[2,64,4128]{2,1,0:T(8,128)(2,1)S(1)} fusion(f32[2,64,4096]{2,1,0:T(8,128)} %convert_element_type.137, f32[2,64,32]{2,1,0:T(8,128)S(1)} %copy.60, f32[2,64]{1,0:T(2,128)S(1)} %add_rsqrt_fusion.2, f32[2,64]{1,0:T(2,128)S(1)} %broadcast_divide_fusion, f32[2,4128]{1,0:T(2,128)S(1)} %and_convert_fusion), kind=kLoop, calls=%fused_computation.18 | loop fusion | flops 3170304 | bytes 3204352 | tf_op jit(solution)/shard_map/convert_element_type | solution.py:189
  22.9 3.2 %copy.62 = bf16[2,4,64,1056]{2,1,0,3:T(4,128)(2,1)} copy(bf16[2,4,64,1056]{3,2,0,1:T(8,128)(2,1)S(1)} %pad_maximum_fusion) | data formatting | bytes 2162688 | tf_op jit(solution)/shard_map/stack | solution.py:193
  26.1 5.7 %fusion.60 = bf16[8,32,320]{2,0,1:T(8,128)(2,1)S(1)} fusion(bf16[8,64,1056]{1,0,2:T(8,128)(2,1)} %bitcast.180, bf16[64,64,320]{2,1,0:T(8,128)(2,1)} %bitcast.179), kind=kOutput, calls=%fused_computation.57 | convolution fusion | flops 671170560 | bytes 3866624 | tf_op jit(solution)/shard_map/conv_general_dilated | solution.py:200
  31.9 7.9 %all_gather.3 = bf16[2,128,1280]{1,0,2:T(2,128)(2,1)S(1)} all-gather(bf16[2,128,320]{1,0,2:T(2,128)(2,1)S(1)} %copy.66), channel_id=1, replica_groups=mesh['groups'=2,'tm'=4,'mp'=2,'section'=2] {'mp','section'}, dimensions={2}, use_global_device_ids=true | all-gather | bytes 819200 | tf_op jit(solution)/shard_map/all_gather | solution.py:210
  41.0 1.7 %convolution_convert_fusion.2 = bf16[320,2,128]{2,0,1:T(8,128)(2,1)S(1)} fusion(bf16[1280,160]{0,1:T(8,128)(2,1)} %bitcast.196, bf16[1280,160]{0,1:T(8,128)(2,1)} %bitcast.198, bf16[2,128,1280]{2,1,0:T(8,128)(2,1)S(1)} %copy.67, f32[1280]{0:T(1024)S(1)} %convert_reduce_fusion, f32[2,128]{1,0:T(2,128)S(1)} %add_rsqrt_fusion.1), kind=kOutput, calls=%fused_computation.59 | convolution fusion | flops 212746240 | bytes 1644544 | tf_op jit(solution)/shard_map/btd,de->bet/dot_general | solution.py:77
  42.8 3.9 %collective-permute-start.3 = (bf16[2,2,2,80,128]{4,3,2,0,1:T(8,128)(2,1)S(1)}, bf16[2,2,2,80,128]{4,3,2,0,1:T(8,128)(2,1)}, u32[]{:S(2)}, u32[]{:S(2)}) collective-permute-start(bf16[2,2,2,80,128]{4,3,2,0,1:T(8,128)(2,1)S(1)} %copy.68), channel_id=1, source_target_pairs={{0,12},{2,14},{16,28},{18,30}} | collective-permute-start | bytes 491528 | tf_op jit(solution)/shard_map/ppermute | solution.py:34
  46.7 2.1 %collective-permute-start.4 = (bf16[2,2,2,80,128]{4,3,2,0,1:T(8,128)(2,1)S(1)}, bf16[2,2,2,80,128]{4,3,2,0,1:T(8,128)(2,1)}, u32[]{:S(2)}, u32[]{:S(2)}) collective-permute-start(bf16[2,2,2,80,128]{4,3,2,0,1:T(8,128)(2,1)S(1)} %copy.68), channel_id=1, source_target_pairs={{0,8},{4,12},{2,10},{6,14},{16,24},{20,28},{18,26},{22,30}} | collective-permute-start | bytes 491528 | tf_op jit(solution)/shard_map/ppermute | solution.py:34
  48.8 2.3 %collective-permute-start.5 = (bf16[2,2,2,80,128]{4,3,2,0,1:T(8,128)(2,1)S(1)}, bf16[2,2,2,80,128]{4,3,2,0,1:T(8,128)(2,1)}, u32[]{:S(2)}, u32[]{:S(2)}) collective-permute-start(bf16[2,2,2,80,128]{4,3,2,0,1:T(8,128)(2,1)S(1)} %copy.68), channel_id=1, source_target_pairs={{0,4},{4,8},{8,12},{2,6},{6,10},{10,14},{16,20},{20,24},{24,28},{1... | collective-permute-start | bytes 491528 | tf_op jit(solution)/shard_map/ppermute | solution.py:34
  58.3 2.1 %collective-permute-start.7 = (bf16[2,128,1280]{2,1,0:T(8,128)(2,1)S(1)}, bf16[2,128,1280]{2,1,0:T(8,128)(2,1)}, u32[]{:S(2)}, u32[]{:S(2)}) collective-permute-start(bf16[2,128,1280]{2,1,0:T(8,128)(2,1)S(1)} %convolution_convert_fusion), channel_id=1, source_target_pairs={{0,3},{2,1},{4,7},{6,5},{8,11},{10,9},{12,15},{14,13},{16,19},{18,... | collective-permute-start | bytes 1966088 | tf_op jit(solution)/shard_map/ppermute | solution.py:222
  60.4 2.1 %collective-permute-start.6 = (bf16[2,128,1280]{2,1,0:T(8,128)(2,1)S(1)}, bf16[2,128,1280]{2,1,0:T(8,128)(2,1)}, u32[]{:S(2)}, u32[]{:S(2)}) collective-permute-start(bf16[2,128,1280]{2,1,0:T(8,128)(2,1)S(1)} %convolution_convert_fusion), channel_id=1, source_target_pairs={{0,1},{2,3},{4,5},{6,7},{8,9},{10,11},{12,13},{14,15},{16,17},{18,... | collective-permute-start | bytes 1966088 | tf_op jit(solution)/shard_map/ppermute | solution.py:222
  62.5 5.1 %collective-permute-done.7 = bf16[2,128,1280]{2,1,0:T(8,128)(2,1)} collective-permute-done((bf16[2,128,1280]{2,1,0:T(8,128)(2,1)S(1)}, bf16[2,128,1280]{2,1,0:T(8,128)(2,1)}, u32[]{:S(2)}, u32[]{:S(2)}) %collective-permute-start.7) | collective-permute-done | bytes 655392 | tf_op jit(solution)/shard_map/ppermute | solution.py:222
  67.6 1.7 %fusion.29 = (f32[2,128]{1,0:T(2,128)S(1)}, bf16[2,128,1280]{2,1,0:T(8,128)(2,1)S(1)}) fusion(bf16[2,128,1280]{2,1,0:T(8,128)(2,1)} %collective-permute-done.7, bf16[2,128,1280]{2,1,0:T(8,128)(2,1)} %collective-permute-done.6, bf16[2,128,1280]{2,1,0:T(8,128)(2,1)S(1)} %copy.67), kind=kLoop, calls=%fused_computation.41 | loop fusion | flops 2948864 | bytes 2622464 | tf_op jit(solution)/shard_map/reduce_sum | solution.py:69
  69.9 1.3 %collective-permute-start.8 = (bf16[2,2,2,80,128]{4,3,2,0,1:T(8,128)(2,1)S(1)}, bf16[2,2,2,80,128]{4,3,2,0,1:T(8,128)(2,1)}, u32[]{:S(2)}, u32[]{:S(2)}) collective-permute-start(bf16[2,2,2,80,128]{4,3,2,0,1:T(8,128)(2,1)S(1)} %copy.76), channel_id=1, source_target_pairs={{1,13},{3,15},{17,29},{19,31}} | collective-permute-start | bytes 491528 | tf_op jit(solution)/shard_map/ppermute | solution.py:34
  71.2 1.3 %collective-permute-start.9 = (bf16[2,2,2,80,128]{4,3,2,0,1:T(8,128)(2,1)S(1)}, bf16[2,2,2,80,128]{4,3,2,0,1:T(8,128)(2,1)}, u32[]{:S(2)}, u32[]{:S(2)}) collective-permute-start(bf16[2,2,2,80,128]{4,3,2,0,1:T(8,128)(2,1)S(1)} %copy.76), channel_id=1, source_target_pairs={{1,9},{5,13},{3,11},{7,15},{17,25},{21,29},{19,27},{23,31}} | collective-permute-start | bytes 491528 | tf_op jit(solution)/shard_map/ppermute | solution.py:34
  73.3 1.4 %fusion.54 = bf16[2,128,640]{2,1,0:T(8,128)(2,1)} fusion(bf16[1,1280,640]{2,1,0:T(8,128)(2,1)S(1)} %copy-done.4, bf16[2,128,1280]{2,1,0:T(8,128)(2,1)S(1)} %get-tuple-element.4, f32[2,128]{1,0:T(2,128)S(1)} %add_rsqrt_fusion, f32[1280]{0:T(1024)S(1)} %convert_reduce_fusion), kind=kOutput, calls=%fused_computation.54 | convolution fusion | flops 421068800 | bytes 2627584 | tf_op jit(solution)/shard_map/btd,de->bte/dot_general | solution.py:72
  82.0 1.3 %collective-permute-start.12 = (bf16[1,128,640]{2,1,0:T(8,128)(2,1)S(1)}, bf16[1,128,640]{2,1,0:T(8,128)(2,1)S(1)}, u32[]{:S(2)}, u32[]{:S(2)}) collective-permute-start(bf16[1,128,640]{2,1,0:T(8,128)(2,1)S(1)} %dynamic-slice_convert_fusion.1), channel_id=1, source_target_pairs={{1,2},{3,0},{5,6},{7,4},{9,10},{11,8},{13,14},{15,12},{17,18},{19,... | collective-permute-start | bytes 491528 | tf_op jit(solution)/shard_map/ppermute | solution.py:247
  83.4 1.3 %collective-permute-start.11 = (bf16[1,128,640]{2,1,0:T(8,128)(2,1)S(1)}, bf16[1,128,640]{2,1,0:T(8,128)(2,1)S(1)}, u32[]{:S(2)}, u32[]{:S(2)}) collective-permute-start(bf16[1,128,640]{2,1,0:T(8,128)(2,1)S(1)} %add_convert_fusion), channel_id=1, source_target_pairs={{1,0},{3,2},{5,4},{7,6},{9,8},{11,10},{13,12},{15,14},{17,16},{19,... | collective-permute-start | bytes 491528 | tf_op jit(solution)/shard_map/ppermute | solution.py:247
  85.4 11.0 %collective-permute-done.12 = bf16[1,128,640]{2,1,0:T(8,128)(2,1)S(1)} collective-permute-done((bf16[1,128,640]{2,1,0:T(8,128)(2,1)S(1)}, bf16[1,128,640]{2,1,0:T(8,128)(2,1)S(1)}, u32[]{:S(2)}, u32[]{:S(2)}) %collective-permute-start.12) | collective-permute-done | bytes 163872 | tf_op jit(solution)/shard_map/ppermute | solution.py:247
  (109 shorter events, 23.6 us)
Async XLA Ops:
  0.6 56.9 %copy-start = (bf16[1,640,1280]{2,1,0:T(8,128)(2,1)S(1)}, bf16[1,640,1280]{2,1,0:T(8,128)(2,1)}, u32[]{:S(2)}) copy-start(bf16[1,640,1280]{2,1,0:T(8,128)(2,1)} %param.15) | copy-start | bytes 4915204
  0.6 12.4 %copy-start.1 = (bf16[2,64,4096]{2,1,0:T(8,128)(2,1)S(1)}, bf16[2,64,4096]{2,1,0:T(8,128)(2,1)}, u32[]{:S(2)}) copy-start(bf16[2,64,4096]{2,1,0:T(8,128)(2,1)} %param.8) | copy-start | bytes 3145732
  0.7 12.1 %copy-start.2 = (bf16[1,1280]{1,0:T(2,128)(2,1)S(1)}, bf16[1,1280]{1,0:T(2,128)(2,1)}, u32[]{:S(2)}) copy-start(bf16[1,1280]{1,0:T(2,128)(2,1)} %param.11) | copy-start | bytes 7684
  6.1 13.1 %collective-permute-start = (f32[2,64,34]{1,0,2:T(2,128)S(1)}, f32[2,64,34]{1,0,2:T(2,128)S(1)}, u32[]{:S(2)}, u32[]{:S(2)}) collective-permute-start(f32[2,64,34]{1,0,2:T(2,128)S(1)} %pad_maximum_fusion.1), channel_id=1, source_target_pairs={{0,4},{4,8},{8,12},{12,0},{1,5},{5,9},{9,13},{13,1},{2,6},{6,10},{... | collective-permute-start | bytes 52232 | tf_op jit(solution)/shard_map/ppermute | solution.py:13
  9.2 10.0 %collective-permute-start.2 = (f32[2,64,34]{1,0,2:T(2,128)S(1)}, f32[2,64,34]{1,0,2:T(2,128)S(1)}, u32[]{:S(2)}, u32[]{:S(2)}) collective-permute-start(f32[2,64,34]{1,0,2:T(2,128)S(1)} %pad_maximum_fusion.1), channel_id=1, source_target_pairs={{0,12},{4,0},{8,4},{12,8},{1,13},{5,1},{9,5},{13,9},{2,14},{6,2},{... | collective-permute-start | bytes 52232 | tf_op jit(solution)/shard_map/ppermute | solution.py:13
  11.3 8.0 %collective-permute-start.1 = (f32[2,64,34]{1,0,2:T(2,128)S(1)}, f32[2,64,34]{1,0,2:T(2,128)S(1)}, u32[]{:S(2)}, u32[]{:S(2)}) collective-permute-start(f32[2,64,34]{1,0,2:T(2,128)S(1)} %pad_maximum_fusion.1), channel_id=1, source_target_pairs={{0,8},{4,12},{8,0},{12,4},{1,9},{5,13},{9,1},{13,5},{2,10},{6,14},... | collective-permute-start | bytes 52232 | tf_op jit(solution)/shard_map/ppermute | solution.py:13
  40.8 10.3 %copy-start.3 = (bf16[1,1280,640]{2,1,0:T(8,128)(2,1)S(1)}, bf16[1,1280,640]{2,1,0:T(8,128)(2,1)}, u32[]{:S(2)}) copy-start(bf16[1,1280,640]{2,1,0:T(8,128)(2,1)} %param.12) | copy-start | bytes 4915204
  42.8 9.3 %collective-permute-start.3 = (bf16[2,2,2,80,128]{4,3,2,0,1:T(8,128)(2,1)S(1)}, bf16[2,2,2,80,128]{4,3,2,0,1:T(8,128)(2,1)}, u32[]{:S(2)}, u32[]{:S(2)}) collective-permute-start(bf16[2,2,2,80,128]{4,3,2,0,1:T(8,128)(2,1)S(1)} %copy.68), channel_id=1, source_target_pairs={{0,12},{2,14},{16,28},{18,30}} | collective-permute-start | bytes 491528 | tf_op jit(solution)/shard_map/ppermute | solution.py:34
  46.7 6.3 %collective-permute-start.4 = (bf16[2,2,2,80,128]{4,3,2,0,1:T(8,128)(2,1)S(1)}, bf16[2,2,2,80,128]{4,3,2,0,1:T(8,128)(2,1)}, u32[]{:S(2)}, u32[]{:S(2)}) collective-permute-start(bf16[2,2,2,80,128]{4,3,2,0,1:T(8,128)(2,1)S(1)} %copy.68), channel_id=1, source_target_pairs={{0,8},{4,12},{2,10},{6,14},{16,24},{20,28},{18,26},{22,30}} | collective-permute-start | bytes 491528 | tf_op jit(solution)/shard_map/ppermute | solution.py:34
  48.8 5.2 %collective-permute-start.5 = (bf16[2,2,2,80,128]{4,3,2,0,1:T(8,128)(2,1)S(1)}, bf16[2,2,2,80,128]{4,3,2,0,1:T(8,128)(2,1)}, u32[]{:S(2)}, u32[]{:S(2)}) collective-permute-start(bf16[2,2,2,80,128]{4,3,2,0,1:T(8,128)(2,1)S(1)} %copy.68), channel_id=1, source_target_pairs={{0,4},{4,8},{8,12},{2,6},{6,10},{10,14},{16,20},{20,24},{24,28},{1... | collective-permute-start | bytes 491528 | tf_op jit(solution)/shard_map/ppermute | solution.py:34
  58.3 9.4 %collective-permute-start.7 = (bf16[2,128,1280]{2,1,0:T(8,128)(2,1)S(1)}, bf16[2,128,1280]{2,1,0:T(8,128)(2,1)}, u32[]{:S(2)}, u32[]{:S(2)}) collective-permute-start(bf16[2,128,1280]{2,1,0:T(8,128)(2,1)S(1)} %convolution_convert_fusion), channel_id=1, source_target_pairs={{0,3},{2,1},{4,7},{6,5},{8,11},{10,9},{12,15},{14,13},{16,19},{18,... | collective-permute-start | bytes 1966088 | tf_op jit(solution)/shard_map/ppermute | solution.py:222
  60.4 7.3 %collective-permute-start.6 = (bf16[2,128,1280]{2,1,0:T(8,128)(2,1)S(1)}, bf16[2,128,1280]{2,1,0:T(8,128)(2,1)}, u32[]{:S(2)}, u32[]{:S(2)}) collective-permute-start(bf16[2,128,1280]{2,1,0:T(8,128)(2,1)S(1)} %convolution_convert_fusion), channel_id=1, source_target_pairs={{0,1},{2,3},{4,5},{6,7},{8,9},{10,11},{12,13},{14,15},{16,17},{18,... | collective-permute-start | bytes 1966088 | tf_op jit(solution)/shard_map/ppermute | solution.py:222
  62.5 6.8 %copy-start.5 = (bf16[1,1280,160]{1,2,0:T(8,128)(2,1)S(1)}, bf16[1,1280,160]{1,2,0:T(8,128)(2,1)}, u32[]{:S(2)}) copy-start(bf16[1,1280,160]{1,2,0:T(8,128)(2,1)} %param.14) | copy-start | bytes 1228804
  62.5 6.8 %copy-start.6 = (bf16[1,1280,160]{1,2,0:T(8,128)(2,1)S(1)}, bf16[1,1280,160]{1,2,0:T(8,128)(2,1)}, u32[]{:S(2)}) copy-start(bf16[1,1280,160]{1,2,0:T(8,128)(2,1)} %param.13) | copy-start | bytes 1228804
  69.4 3.9 %copy-start.4 = (bf16[1,1280,640]{2,1,0:T(8,128)(2,1)S(1)}, bf16[1,1280,640]{2,1,0:T(8,128)(2,1)}, u32[]{:S(2)}) copy-start(bf16[1,1280,640]{2,1,0:T(8,128)(2,1)} %param.12) | copy-start | bytes 4915204
  69.9 6.0 %collective-permute-start.8 = (bf16[2,2,2,80,128]{4,3,2,0,1:T(8,128)(2,1)S(1)}, bf16[2,2,2,80,128]{4,3,2,0,1:T(8,128)(2,1)}, u32[]{:S(2)}, u32[]{:S(2)}) collective-permute-start(bf16[2,2,2,80,128]{4,3,2,0,1:T(8,128)(2,1)S(1)} %copy.76), channel_id=1, source_target_pairs={{1,13},{3,15},{17,29},{19,31}} | collective-permute-start | bytes 491528 | tf_op jit(solution)/shard_map/ppermute | solution.py:34
  71.2 5.6 %collective-permute-start.9 = (bf16[2,2,2,80,128]{4,3,2,0,1:T(8,128)(2,1)S(1)}, bf16[2,2,2,80,128]{4,3,2,0,1:T(8,128)(2,1)}, u32[]{:S(2)}, u32[]{:S(2)}) collective-permute-start(bf16[2,2,2,80,128]{4,3,2,0,1:T(8,128)(2,1)S(1)} %copy.76), channel_id=1, source_target_pairs={{1,9},{5,13},{3,11},{7,15},{17,25},{21,29},{19,27},{23,31}} | collective-permute-start | bytes 491528 | tf_op jit(solution)/shard_map/ppermute | solution.py:34
  72.5 5.3 %collective-permute-start.10 = (bf16[2,2,2,80,128]{4,3,2,0,1:T(8,128)(2,1)S(1)}, bf16[2,2,2,80,128]{4,3,2,0,1:T(8,128)(2,1)S(1)}, u32[]{:S(2)}, u32[]{:S(2)}) collective-permute-start(bf16[2,2,2,80,128]{4,3,2,0,1:T(8,128)(2,1)S(1)} %copy.76), channel_id=1, source_target_pairs={{1,5},{5,9},{9,13},{3,7},{7,11},{11,15},{17,21},{21,25},{25,29},{1... | collective-permute-start | bytes 491528 | tf_op jit(solution)/shard_map/ppermute | solution.py:34
  81.3 4.1 %collective-permute-start.13 = (bf16[1,128,640]{2,1,0:T(8,128)(2,1)S(1)}, bf16[1,128,640]{2,1,0:T(8,128)(2,1)S(1)}, u32[]{:S(2)}, u32[]{:S(2)}) collective-permute-start(bf16[1,128,640]{2,1,0:T(8,128)(2,1)S(1)} %dynamic-slice_convert_fusion), channel_id=1, source_target_pairs={{1,3},{3,1},{5,7},{7,5},{9,11},{11,9},{13,15},{15,13},{17,19},{19,... | collective-permute-start | bytes 491528 | tf_op jit(solution)/shard_map/ppermute | solution.py:251
  82.0 14.4 %collective-permute-start.12 = (bf16[1,128,640]{2,1,0:T(8,128)(2,1)S(1)}, bf16[1,128,640]{2,1,0:T(8,128)(2,1)S(1)}, u32[]{:S(2)}, u32[]{:S(2)}) collective-permute-start(bf16[1,128,640]{2,1,0:T(8,128)(2,1)S(1)} %dynamic-slice_convert_fusion.1), channel_id=1, source_target_pairs={{1,2},{3,0},{5,6},{7,4},{9,10},{11,8},{13,14},{15,12},{17,18},{19,... | collective-permute-start | bytes 491528 | tf_op jit(solution)/shard_map/ppermute | solution.py:247
  83.4 13.1 %collective-permute-start.11 = (bf16[1,128,640]{2,1,0:T(8,128)(2,1)S(1)}, bf16[1,128,640]{2,1,0:T(8,128)(2,1)S(1)}, u32[]{:S(2)}, u32[]{:S(2)}) collective-permute-start(bf16[1,128,640]{2,1,0:T(8,128)(2,1)S(1)} %add_convert_fusion), channel_id=1, source_target_pairs={{1,0},{3,2},{5,4},{7,6},{9,8},{11,10},{13,12},{15,14},{17,16},{19,... | collective-permute-start | bytes 491528 | tf_op jit(solution)/shard_map/ppermute | solution.py:247

commit v17 on v16

--- a/solution.py
+++ b/solution.py
@@ -75,12 +75,12 @@
     kv_local = key_w.shape[1] // HD
     group_size = query_w.shape[1] // key_w.shape[1]
     kv_t = jnp.einsum(
-        "btd,de->bet", layer_input, jnp.concatenate([key_w, value_w], 1),
+        "btd,de->ebt", layer_input, jnp.concatenate([key_w, value_w], 1),
         preferred_element_type=jnp.float32,
     ).astype(jnp.bfloat16)
-    kv_t = kv_t.reshape(batch_count, 2, kv_local, HD, tok_count)
-    key_t = kv_t[:, 0]
-    value_t = kv_t[:, 1]
+    kv_t = kv_t.reshape(2, kv_local, HD, batch_count, tok_count).transpose(0, 3, 1, 2, 4)
+    key_t = kv_t[0]
+    value_t = kv_t[1]
     query_rows = queries.reshape(batch_count, tok_count, kv_local, group_size, HD)
     query_pos = tm_at * tok_count + jnp.arange(tok_count, dtype=jnp.int32)
     first_valid = total_tokens - seq_lens // STRIDE
@@ -89,7 +89,7 @@
     block_width = 1024 if key_count % 1024 == 0 else key_count
     rounds = key_count // block_width
     blocks = jnp.moveaxis(
-        both.reshape(batch_count, 2, kv_local, HD, rounds, block_width), 4, 0
+        both.reshape(2, batch_count, kv_local, HD, rounds, block_width), 4, 0
     )
     pos_blocks = key_pos.reshape(rounds, block_width)
     start_state = (
@@ -99,7 +99,7 @@
     )
     if rounds == 1:
         result = absorb_block(
-            start_state, blocks[0][:, 0], blocks[0][:, 1], pos_blocks[0], query_rows, query_pos,
+            start_state, blocks[0, 0], blocks[0, 1], pos_blocks[0], query_rows, query_pos,
             first_valid,
         )
     else:
@@ -108,7 +108,7 @@
             kv_block, pos_block = block_item
             return (
                 absorb_block(
-                    state, kv_block[:, 0], kv_block[:, 1], pos_block, query_rows, query_pos,
+                    state, kv_block[0], kv_block[1], pos_block, query_rows, query_pos,
                     first_valid,
                 ),
                 None,

time: 97.9 us -> 96.3 us (0.984)
  the two profiles are of different devices: /device:TPU:0 before, /device:TPU:1 now
where the time goes in v17:
time: 96.3 us; the launch traced here: 94.4 us
  starting transfers between devices  27 us (28%)
  other arithmetic  15.5 us (16%)
  matrix products  15 us (16%)
  waiting for transfers between devices  14.3 us (15%)
  local copies, waits for them, and re-layouts  12.2 us (13%)
  blocking collectives  9.24 us (10%)
  between operations  1.23 us (1%)
    ppermute x6, starting transfers between devices, gather_causal(): pieces.append(lax.ppermute(value, ('tm', 'section'), pairs))  14 us
    ppermute x2, waiting for transfers between devices, per_device(): lax.ppermute(partial0.astype(jnp.bfloat16), feat_axes, pairs)  13.7 us
    all_gather x1, blocking collectives, per_device(): hidden0 = lax.all_gather(tokens, feat_axes, axis=2, tiled=True)  9.24 us
    conv_general_dilated x1, matrix products, per_device(): lax.conv_general_dilated(chunks, kernel, window_strides=(STRIDE,), paddin...  5.67 us
    unnamed x16, local copies, waits for them, and re-layouts  4.67 us
    ppermute x3, starting transfers between devices, shift_from(): return lax.ppermute(value, axis, pairs)  4.66 us
    another operation x2, local copies, waits for them, and re-layouts, per_device(): jnp.stack([normed[:, :, q * chunk_tok * STRIDE:(q + 1) * chunk_tok * STRI...  3.27 us
    ppermute x1, starting transfers between devices, per_device(): lax.ppermute(cols_high.astype(jnp.bfloat16), feat_axes, pairs)  3.18 us
  transfers between devices with their start and end apart: 14, of which 2 were waited for; matrix products, arithmetic and copies ran while one was open for 12% of the time, Pallas kernels for 0%

profile of v17, /device:TPU:1, one launch (start us, length us, event | category | flops | bytes accessed | tf_op | source)
XLA Modules:
  0.0 94.4 jit_solution(8525588700261035830)
XLA Ops:
  2.8 1.5 %multiply_reduce_fusion.1 = f32[2,64]{1,0:T(2,128)S(1)} fusion(f32[2,4096]{1,0:T(2,128)S(1)} %compare_convert_fusion, bf16[2,64,4096]{2,1,0:T(8,128)(2,1)} %param.8), kind=kLoop, calls=%fused_computation.26 | loop fusion | flops 1572736 | bytes 1081856 | tf_op jit(solution)/shard_map/reduce_sum | solution.py:148
  4.9 2.2 %collective-permute-start = (f32[2,64,34]{1,0,2:T(2,128)S(1)}, f32[2,64,34]{1,0,2:T(2,128)S(1)}, u32[]{:S(2)}, u32[]{:S(2)}) collective-permute-start(f32[2,64,34]{1,0,2:T(2,128)S(1)} %pad_maximum_fusion.1), channel_id=1, source_target_pairs={{0,4},{4,8},{8,12},{12,0},{1,5},{5,9},{9,13},{13,1},{2,6},{6,10},{... | collective-permute-start | bytes 52232 | tf_op jit(solution)/shard_map/ppermute | solution.py:13
  7.1 2.1 %collective-permute-start.2 = (f32[2,64,34]{1,0,2:T(2,128)S(1)}, f32[2,64,34]{1,0,2:T(2,128)S(1)}, u32[]{:S(2)}, u32[]{:S(2)}) collective-permute-start(f32[2,64,34]{1,0,2:T(2,128)S(1)} %pad_maximum_fusion.1), channel_id=1, source_target_pairs={{0,12},{4,0},{8,4},{12,8},{1,13},{5,1},{9,5},{13,9},{2,14},{6,2},{... | collective-permute-start | bytes 52232 | tf_op jit(solution)/shard_map/ppermute | solution.py:13
  10.4 1.6 %convert_element_type.131 = f32[2,64,4096]{2,1,0:T(8,128)} convert(bf16[2,64,4096]{2,1,0:T(8,128)(2,1)S(1)} %copy-done.1) | non-fusion elementwise | flops 524288 | bytes 3145728 | tf_op jit(solution)/shard_map/convert_element_type | solution.py:146
  12.0 4.5 %copy.42 = bf16[4096,320]{1,0:T(8,128)(2,1)} copy(bf16[4096,320]{0,1:T(8,128)(2,1)} %param.10) | data formatting | bytes 5242880 | tf_op args[2]
  17.6 2.3 %fusion.11 = bf16[2,64,4128]{2,1,0:T(8,128)(2,1)S(1)} fusion(f32[2,64,4096]{2,1,0:T(8,128)} %convert_element_type.131, f32[2,64,32]{2,1,0:T(8,128)S(1)} %copy.39, f32[2,64]{1,0:T(2,128)S(1)} %add_rsqrt_fusion.2, f32[2,64]{1,0:T(2,128)S(1)} %broadcast_divide_fusion, f32[2,4128]{1,0:T(2,128)S(1)} %and_convert_fusion), kind=kLoop, calls=%fused_computation.18 | loop fusion | flops 3170304 | bytes 3204352 | tf_op jit(solution)/shard_map/convert_element_type | solution.py:189
  20.2 3.2 %copy.41 = bf16[2,4,64,1056]{2,1,0,3:T(4,128)(2,1)} copy(bf16[2,4,64,1056]{3,2,0,1:T(8,128)(2,1)S(1)} %pad_maximum_fusion) | data formatting | bytes 2162688 | tf_op jit(solution)/shard_map/stack | solution.py:193
  23.4 5.7 %fusion.60 = bf16[8,32,320]{2,0,1:T(8,128)(2,1)S(1)} fusion(bf16[8,64,1056]{1,0,2:T(8,128)(2,1)} %bitcast.186, bf16[64,64,320]{2,1,0:T(8,128)(2,1)} %bitcast.185), kind=kOutput, calls=%fused_computation.57 | convolution fusion | flops 671170560 | bytes 3866624 | tf_op jit(solution)/shard_map/conv_general_dilated | solution.py:200
  29.3 9.2 %all_gather.3 = bf16[2,128,1280]{1,0,2:T(2,128)(2,1)S(1)} all-gather(bf16[2,128,320]{1,0,2:T(2,128)(2,1)S(1)} %copy.45), channel_id=1, replica_groups=mesh['groups'=2,'tm'=4,'mp'=2,'section'=2] {'mp','section'}, dimensions={2}, use_global_device_ids=true | all-gather | bytes 819200 | tf_op jit(solution)/shard_map/all_gather | solution.py:210
  39.7 1.7 %convolution_convert_fusion.2 = bf16[320,2,128]{2,0,1:T(8,128)(2,1)S(1)} fusion(bf16[1280,160]{0,1:T(8,128)(2,1)} %bitcast.208, bf16[1280,160]{0,1:T(8,128)(2,1)} %bitcast.210, bf16[2,128,1280]{2,1,0:T(8,128)(2,1)S(1)} %copy.46, f32[1280]{0:T(1024)S(1)} %convert_reduce_fusion, f32[2,128]{1,0:T(2,128)S(1)} %add_rsqrt_fusion.1), kind=kOutput, calls=%fused_computation.59 | convolution fusion | flops 212746240 | bytes 1644544 | tf_op jit(solution)/shard_map/btd,de->ebt/dot_general | solution.py:77
  42.1 1.3 %collective-permute-start.4 = (bf16[2,2,2,80,128]{4,3,2,1,0:T(8,128)(2,1)S(1)}, bf16[2,2,2,80,128]{4,3,2,1,0:T(8,128)(2,1)}, u32[]{:S(2)}, u32[]{:S(2)}) collective-permute-start(bf16[2,2,2,80,128]{4,3,2,1,0:T(8,128)(2,1)S(1)} %bitcast.188), channel_id=1, source_target_pairs={{0,8},{4,12},{2,10},{6,14},{16,24},{20,28},{18,26},{22,30}} | collective-permute-start | bytes 491528 | tf_op jit(solution)/shard_map/ppermute | solution.py:34
  43.4 1.3 %collective-permute-start.3 = (bf16[2,2,2,80,128]{4,3,2,1,0:T(8,128)(2,1)S(1)}, bf16[2,2,2,80,128]{4,3,2,1,0:T(8,128)(2,1)}, u32[]{:S(2)}, u32[]{:S(2)}) collective-permute-start(bf16[2,2,2,80,128]{4,3,2,1,0:T(8,128)(2,1)S(1)} %bitcast.189), channel_id=1, source_target_pairs={{0,12},{2,14},{16,28},{18,30}} | collective-permute-start | bytes 491528 | tf_op jit(solution)/shard_map/ppermute | solution.py:34
  50.1 1.3 %collective-permute-start.7 = (bf16[2,128,1280]{2,1,0:T(8,128)(2,1)S(1)}, bf16[2,128,1280]{2,1,0:T(8,128)(2,1)}, u32[]{:S(2)}, u32[]{:S(2)}) collective-permute-start(bf16[2,128,1280]{2,1,0:T(8,128)(2,1)S(1)} %convolution_convert_fusion), channel_id=1, source_target_pairs={{0,3},{2,1},{4,7},{6,5},{8,11},{10,9},{12,15},{14,13},{16,19},{18,... | collective-permute-start | bytes 1966088 | tf_op jit(solution)/shard_map/ppermute | solution.py:222
  51.4 1.3 %collective-permute-start.6 = (bf16[2,128,1280]{2,1,0:T(8,128)(2,1)S(1)}, bf16[2,128,1280]{2,1,0:T(8,128)(2,1)}, u32[]{:S(2)}, u32[]{:S(2)}) collective-permute-start(bf16[2,128,1280]{2,1,0:T(8,128)(2,1)S(1)} %convolution_convert_fusion), channel_id=1, source_target_pairs={{0,1},{2,3},{4,5},{6,7},{8,9},{10,11},{12,13},{14,15},{16,17},{18,... | collective-permute-start | bytes 1966088 | tf_op jit(solution)/shard_map/ppermute | solution.py:222
  52.7 13.7 %collective-permute-done.7 = bf16[2,128,1280]{2,1,0:T(8,128)(2,1)} collective-permute-done((bf16[2,128,1280]{2,1,0:T(8,128)(2,1)S(1)}, bf16[2,128,1280]{2,1,0:T(8,128)(2,1)}, u32[]{:S(2)}, u32[]{:S(2)}) %collective-permute-start.7) | collective-permute-done | bytes 655392 | tf_op jit(solution)/shard_map/ppermute | solution.py:222
  66.4 1.7 %fusion.29 = (f32[2,128]{1,0:T(2,128)S(1)}, bf16[2,128,1280]{2,1,0:T(8,128)(2,1)S(1)}) fusion(bf16[2,128,1280]{2,1,0:T(8,128)(2,1)} %collective-permute-done.7, bf16[2,128,1280]{2,1,0:T(8,128)(2,1)} %collective-permute-done.6, bf16[2,128,1280]{2,1,0:T(8,128)(2,1)S(1)} %copy.46), kind=kLoop, calls=%fused_computation.41 | loop fusion | flops 2948864 | bytes 2622464 | tf_op jit(solution)/shard_map/reduce_sum | solution.py:69
  68.7 3.6 %collective-permute-start.10 = (bf16[2,2,2,80,128]{4,3,2,1,0:T(8,128)(2,1)S(1)}, bf16[2,2,2,80,128]{4,3,2,1,0:T(8,128)(2,1)S(1)}, u32[]{:S(2)}, u32[]{:S(2)}) collective-permute-start(bf16[2,2,2,80,128]{4,3,2,1,0:T(8,128)(2,1)S(1)} %bitcast.192), channel_id=1, source_target_pairs={{1,5},{5,9},{9,13},{3,7},{7,11},{11,15},{17,21},{21,25},{25,29},{1... | collective-permute-start | bytes 491528 | tf_op jit(solution)/shard_map/ppermute | solution.py:34
  72.3 5.1 %collective-permute-start.9 = (bf16[2,2,2,80,128]{4,3,2,1,0:T(8,128)(2,1)S(1)}, bf16[2,2,2,80,128]{4,3,2,1,0:T(8,128)(2,1)S(1)}, u32[]{:S(2)}, u32[]{:S(2)}) collective-permute-start(bf16[2,2,2,80,128]{4,3,2,1,0:T(8,128)(2,1)S(1)} %bitcast.193), channel_id=1, source_target_pairs={{1,9},{5,13},{3,11},{7,15},{17,25},{21,29},{19,27},{23,31}} | collective-permute-start | bytes 491528 | tf_op jit(solution)/shard_map/ppermute | solution.py:34
  77.4 2.0 %collective-permute-start.8 = (bf16[2,2,2,80,128]{4,3,2,1,0:T(8,128)(2,1)S(1)}, bf16[2,2,2,80,128]{4,3,2,1,0:T(8,128)(2,1)}, u32[]{:S(2)}, u32[]{:S(2)}) collective-permute-start(bf16[2,2,2,80,128]{4,3,2,1,0:T(8,128)(2,1)S(1)} %bitcast.194), channel_id=1, source_target_pairs={{1,13},{3,15},{17,29},{19,31}} | collective-permute-start | bytes 491528 | tf_op jit(solution)/shard_map/ppermute | solution.py:34
  79.4 1.4 %fusion.54 = bf16[2,128,640]{2,1,0:T(8,128)(2,1)} fusion(bf16[1,1280,640]{2,1,0:T(8,128)(2,1)S(1)} %copy-done.4, bf16[2,128,1280]{2,1,0:T(8,128)(2,1)S(1)} %get-tuple-element.4, f32[2,128]{1,0:T(2,128)S(1)} %add_rsqrt_fusion, f32[1280]{0:T(1024)S(1)} %convert_reduce_fusion), kind=kOutput, calls=%fused_computation.54 | convolution fusion | flops 421068800 | bytes 2627584 | tf_op jit(solution)/shard_map/btd,de->bte/dot_general | solution.py:72
  80.8 1.2 %copy.52 = bf16[2,128,640]{1,2,0:T(8,128)(2,1)S(1)} copy(bf16[2,128,640]{2,1,0:T(8,128)(2,1)} %fusion.54) | data formatting | bytes 655360 | tf_op jit(solution)/shard_map/convert_element_type | solution.py:74
  86.4 3.2 %collective-permute-start.13 = (bf16[1,128,640]{2,1,0:T(8,128)(2,1)S(1)}, bf16[1,128,640]{2,1,0:T(8,128)(2,1)S(1)}, u32[]{:S(2)}, u32[]{:S(2)}) collective-permute-start(bf16[1,128,640]{2,1,0:T(8,128)(2,1)S(1)} %dynamic-slice_convert_fusion), channel_id=1, source_target_pairs={{1,3},{3,1},{5,7},{7,5},{9,11},{11,9},{13,15},{15,13},{17,19},{19,... | collective-permute-start | bytes 491528 | tf_op jit(solution)/shard_map/ppermute | solution.py:251
  89.6 1.3 %collective-permute-start.12 = (bf16[1,128,640]{2,1,0:T(8,128)(2,1)S(1)}, bf16[1,128,640]{2,1,0:T(8,128)(2,1)S(1)}, u32[]{:S(2)}, u32[]{:S(2)}) collective-permute-start(bf16[1,128,640]{2,1,0:T(8,128)(2,1)S(1)} %dynamic-slice_convert_fusion.1), channel_id=1, source_target_pairs={{1,2},{3,0},{5,6},{7,4},{9,10},{11,8},{13,14},{15,12},{17,18},{19,... | collective-permute-start | bytes 491528 | tf_op jit(solution)/shard_map/ppermute | solution.py:247
  91.0 1.3 %collective-permute-start.11 = (bf16[1,128,640]{2,1,0:T(8,128)(2,1)S(1)}, bf16[1,128,640]{2,1,0:T(8,128)(2,1)S(1)}, u32[]{:S(2)}, u32[]{:S(2)}) collective-permute-start(bf16[1,128,640]{2,1,0:T(8,128)(2,1)S(1)} %add_convert_fusion), channel_id=1, source_target_pairs={{1,0},{3,2},{5,4},{7,6},{9,8},{11,10},{13,12},{15,14},{17,16},{19,... | collective-permute-start | bytes 491528 | tf_op jit(solution)/shard_map/ppermute | solution.py:247
  (103 shorter events, 19.5 us)
Async XLA Ops:
  0.6 48.7 %copy-start = (bf16[1,640,1280]{2,1,0:T(8,128)(2,1)S(1)}, bf16[1,640,1280]{2,1,0:T(8,128)(2,1)}, u32[]{:S(2)}) copy-start(bf16[1,640,1280]{2,1,0:T(8,128)(2,1)} %param.15) | copy-start | bytes 4915204
  0.6 3.7 %copy-start.1 = (bf16[2,64,4096]{2,1,0:T(8,128)(2,1)S(1)}, bf16[2,64,4096]{2,1,0:T(8,128)(2,1)}, u32[]{:S(2)}) copy-start(bf16[2,64,4096]{2,1,0:T(8,128)(2,1)} %param.8) | copy-start | bytes 3145732
  0.7 9.4 %copy-start.2 = (bf16[1,1280]{1,0:T(2,128)(2,1)S(1)}, bf16[1,1280]{1,0:T(2,128)(2,1)}, u32[]{:S(2)}) copy-start(bf16[1,1280]{1,0:T(2,128)(2,1)} %param.11) | copy-start | bytes 7684
  4.9 11.6 %collective-permute-start = (f32[2,64,34]{1,0,2:T(2,128)S(1)}, f32[2,64,34]{1,0,2:T(2,128)S(1)}, u32[]{:S(2)}, u32[]{:S(2)}) collective-permute-start(f32[2,64,34]{1,0,2:T(2,128)S(1)} %pad_maximum_fusion.1), channel_id=1, source_target_pairs={{0,4},{4,8},{8,12},{12,0},{1,5},{5,9},{9,13},{13,1},{2,6},{6,10},{... | collective-permute-start | bytes 52232 | tf_op jit(solution)/shard_map/ppermute | solution.py:13
  7.1 9.4 %collective-permute-start.2 = (f32[2,64,34]{1,0,2:T(2,128)S(1)}, f32[2,64,34]{1,0,2:T(2,128)S(1)}, u32[]{:S(2)}, u32[]{:S(2)}) collective-permute-start(f32[2,64,34]{1,0,2:T(2,128)S(1)} %pad_maximum_fusion.1), channel_id=1, source_target_pairs={{0,12},{4,0},{8,4},{12,8},{1,13},{5,1},{9,5},{13,9},{2,14},{6,2},{... | collective-permute-start | bytes 52232 | tf_op jit(solution)/shard_map/ppermute | solution.py:13
  9.2 7.5 %collective-permute-start.1 = (f32[2,64,34]{1,0,2:T(2,128)S(1)}, f32[2,64,34]{1,0,2:T(2,128)S(1)}, u32[]{:S(2)}, u32[]{:S(2)}) collective-permute-start(f32[2,64,34]{1,0,2:T(2,128)S(1)} %pad_maximum_fusion.1), channel_id=1, source_target_pairs={{0,8},{4,12},{8,0},{12,4},{1,9},{5,13},{9,1},{13,5},{2,10},{6,14},... | collective-permute-start | bytes 52232 | tf_op jit(solution)/shard_map/ppermute | solution.py:13
  39.7 5.1 %copy-start.3 = (bf16[1,1280,640]{2,1,0:T(8,128)(2,1)S(1)}, bf16[1,1280,640]{2,1,0:T(8,128)(2,1)}, u32[]{:S(2)}) copy-start(bf16[1,1280,640]{2,1,0:T(8,128)(2,1)} %param.12) | copy-start | bytes 4915204
  41.4 4.3 %collective-permute-start.5 = (bf16[2,2,2,80,128]{4,3,2,1,0:T(8,128)(2,1)S(1)}, bf16[2,2,2,80,128]{4,3,2,1,0:T(8,128)(2,1)S(1)}, u32[]{:S(2)}, u32[]{:S(2)}) collective-permute-start(bf16[2,2,2,80,128]{4,3,2,1,0:T(8,128)(2,1)S(1)} %bitcast.187), channel_id=1, source_target_pairs={{0,4},{4,8},{8,12},{2,6},{6,10},{10,14},{16,20},{20,24},{24,28},{1... | collective-permute-start | bytes 491528 | tf_op jit(solution)/shard_map/ppermute | solution.py:34
  42.1 3.6 %collective-permute-start.4 = (bf16[2,2,2,80,128]{4,3,2,1,0:T(8,128)(2,1)S(1)}, bf16[2,2,2,80,128]{4,3,2,1,0:T(8,128)(2,1)}, u32[]{:S(2)}, u32[]{:S(2)}) collective-permute-start(bf16[2,2,2,80,128]{4,3,2,1,0:T(8,128)(2,1)S(1)} %bitcast.188), channel_id=1, source_target_pairs={{0,8},{4,12},{2,10},{6,14},{16,24},{20,28},{18,26},{22,30}} | collective-permute-start | bytes 491528 | tf_op jit(solution)/shard_map/ppermute | solution.py:34
  43.4 2.3 %collective-permute-start.3 = (bf16[2,2,2,80,128]{4,3,2,1,0:T(8,128)(2,1)S(1)}, bf16[2,2,2,80,128]{4,3,2,1,0:T(8,128)(2,1)}, u32[]{:S(2)}, u32[]{:S(2)}) collective-permute-start(bf16[2,2,2,80,128]{4,3,2,1,0:T(8,128)(2,1)S(1)} %bitcast.189), channel_id=1, source_target_pairs={{0,12},{2,14},{16,28},{18,30}} | collective-permute-start | bytes 491528 | tf_op jit(solution)/shard_map/ppermute | solution.py:34
  50.1 16.3 %collective-permute-start.7 = (bf16[2,128,1280]{2,1,0:T(8,128)(2,1)S(1)}, bf16[2,128,1280]{2,1,0:T(8,128)(2,1)}, u32[]{:S(2)}, u32[]{:S(2)}) collective-permute-start(bf16[2,128,1280]{2,1,0:T(8,128)(2,1)S(1)} %convolution_convert_fusion), channel_id=1, source_target_pairs={{0,3},{2,1},{4,7},{6,5},{8,11},{10,9},{12,15},{14,13},{16,19},{18,... | collective-permute-start | bytes 1966088 | tf_op jit(solution)/shard_map/ppermute | solution.py:222
  51.4 15.0 %collective-permute-start.6 = (bf16[2,128,1280]{2,1,0:T(8,128)(2,1)S(1)}, bf16[2,128,1280]{2,1,0:T(8,128)(2,1)}, u32[]{:S(2)}, u32[]{:S(2)}) collective-permute-start(bf16[2,128,1280]{2,1,0:T(8,128)(2,1)S(1)} %convolution_convert_fusion), channel_id=1, source_target_pairs={{0,1},{2,3},{4,5},{6,7},{8,9},{10,11},{12,13},{14,15},{16,17},{18,... | collective-permute-start | bytes 1966088 | tf_op jit(solution)/shard_map/ppermute | solution.py:222
  52.7 15.4 %copy-start.5 = (bf16[1,1280,160]{1,2,0:T(8,128)(2,1)S(1)}, bf16[1,1280,160]{1,2,0:T(8,128)(2,1)}, u32[]{:S(2)}) copy-start(bf16[1,1280,160]{1,2,0:T(8,128)(2,1)} %param.14) | copy-start | bytes 1228804
  52.7 15.4 %copy-start.6 = (bf16[1,1280,160]{1,2,0:T(8,128)(2,1)S(1)}, bf16[1,1280,160]{1,2,0:T(8,128)(2,1)}, u32[]{:S(2)}) copy-start(bf16[1,1280,160]{1,2,0:T(8,128)(2,1)} %param.13) | copy-start | bytes 1228804
  68.1 11.3 %copy-start.4 = (bf16[1,1280,640]{2,1,0:T(8,128)(2,1)S(1)}, bf16[1,1280,640]{2,1,0:T(8,128)(2,1)}, u32[]{:S(2)}) copy-start(bf16[1,1280,640]{2,1,0:T(8,128)(2,1)} %param.12) | copy-start | bytes 4915204
  68.7 13.4 %collective-permute-start.10 = (bf16[2,2,2,80,128]{4,3,2,1,0:T(8,128)(2,1)S(1)}, bf16[2,2,2,80,128]{4,3,2,1,0:T(8,128)(2,1)S(1)}, u32[]{:S(2)}, u32[]{:S(2)}) collective-permute-start(bf16[2,2,2,80,128]{4,3,2,1,0:T(8,128)(2,1)S(1)} %bitcast.192), channel_id=1, source_target_pairs={{1,5},{5,9},{9,13},{3,7},{7,11},{11,15},{17,21},{21,25},{25,29},{1... | collective-permute-start | bytes 491528 | tf_op jit(solution)/shard_map/ppermute | solution.py:34
  72.3 9.7 %collective-permute-start.9 = (bf16[2,2,2,80,128]{4,3,2,1,0:T(8,128)(2,1)S(1)}, bf16[2,2,2,80,128]{4,3,2,1,0:T(8,128)(2,1)S(1)}, u32[]{:S(2)}, u32[]{:S(2)}) collective-permute-start(bf16[2,2,2,80,128]{4,3,2,1,0:T(8,128)(2,1)S(1)} %bitcast.193), channel_id=1, source_target_pairs={{1,9},{5,13},{3,11},{7,15},{17,25},{21,29},{19,27},{23,31}} | collective-permute-start | bytes 491528 | tf_op jit(solution)/shard_map/ppermute | solution.py:34
  77.4 4.7 %collective-permute-start.8 = (bf16[2,2,2,80,128]{4,3,2,1,0:T(8,128)(2,1)S(1)}, bf16[2,2,2,80,128]{4,3,2,1,0:T(8,128)(2,1)}, u32[]{:S(2)}, u32[]{:S(2)}) collective-permute-start(bf16[2,2,2,80,128]{4,3,2,1,0:T(8,128)(2,1)S(1)} %bitcast.194), channel_id=1, source_target_pairs={{1,13},{3,15},{17,29},{19,31}} | collective-permute-start | bytes 491528 | tf_op jit(solution)/shard_map/ppermute | solution.py:34
  86.4 6.6 %collective-permute-start.13 = (bf16[1,128,640]{2,1,0:T(8,128)(2,1)S(1)}, bf16[1,128,640]{2,1,0:T(8,128)(2,1)S(1)}, u32[]{:S(2)}, u32[]{:S(2)}) collective-permute-start(bf16[1,128,640]{2,1,0:T(8,128)(2,1)S(1)} %dynamic-slice_convert_fusion), channel_id=1, source_target_pairs={{1,3},{3,1},{5,7},{7,5},{9,11},{11,9},{13,15},{15,13},{17,19},{19,... | collective-permute-start | bytes 491528 | tf_op jit(solution)/shard_map/ppermute | solution.py:251
  89.6 4.0 %collective-permute-start.12 = (bf16[1,128,640]{2,1,0:T(8,128)(2,1)S(1)}, bf16[1,128,640]{2,1,0:T(8,128)(2,1)S(1)}, u32[]{:S(2)}, u32[]{:S(2)}) collective-permute-start(bf16[1,128,640]{2,1,0:T(8,128)(2,1)S(1)} %dynamic-slice_convert_fusion.1), channel_id=1, source_target_pairs={{1,2},{3,0},{5,6},{7,4},{9,10},{11,8},{13,14},{15,12},{17,18},{19,... | collective-permute-start | bytes 491528 | tf_op jit(solution)/shard_map/ppermute | solution.py:247
  91.0 2.6 %collective-permute-start.11 = (bf16[1,128,640]{2,1,0:T(8,128)(2,1)S(1)}, bf16[1,128,640]{2,1,0:T(8,128)(2,1)S(1)}, u32[]{:S(2)}, u32[]{:S(2)}) collective-permute-start(bf16[1,128,640]{2,1,0:T(8,128)(2,1)S(1)} %add_convert_fusion), channel_id=1, source_target_pairs={{1,0},{3,2},{5,4},{7,6},{9,8},{11,10},{13,12},{15,14},{17,16},{19,... | collective-permute-start | bytes 491528 | tf_op jit(solution)/shard_map/ppermute | solution.py:247

commit v18 on v17

--- a/solution.py
+++ b/solution.py
@@ -98,9 +98,25 @@
         jnp.zeros((batch_count, kv_local, group_size, tok_count, HD), jnp.float32),
     )
     if rounds == 1:
-        result = absorb_block(
-            start_state, blocks[0, 0], blocks[0, 1], pos_blocks[0], query_rows, query_pos,
-            first_valid,
+        key_pos1 = pos_blocks[0]
+        allowed = (key_pos1[None, None, :] <= query_pos[None, :, None]) & (
+            (key_pos1[None, None, :] >= first_valid[:, None, None])
+            | (key_pos1[None, None, :] == query_pos[None, :, None])
+        )
+        scores = jnp.einsum(
+            "btkgh,bkhn->bkgtn", query_rows, blocks[0, 0], preferred_element_type=jnp.float32
+        )
+        scores = jnp.where(allowed[:, None, None], scores, -jnp.inf)
+        exp_scores = jnp.exp(scores - jnp.max(scores, -1, keepdims=True))
+        result = (
+            None,
+            jnp.sum(exp_scores, -1),
+            jnp.einsum(
+                "bkgtn,bkhn->bkgth",
+                exp_scores.astype(jnp.bfloat16),
+                blocks[0, 1],
+                preferred_element_type=jnp.float32,
+            ),
         )
     else:
 

time: 96.3 us -> 96.1 us (level)
  no operation moved by 1% of the time
where the time goes in v18:
time: 96.1 us; the launch traced here: 94.3 us
  starting transfers between devices  27 us (28%)
  other arithmetic  15.4 us (16%)
  matrix products  14.9 us (16%)
  waiting for transfers between devices  14.3 us (15%)
  local copies, waits for them, and re-layouts  12.2 us (13%)
  blocking collectives  9.24 us (10%)
  between operations  1.2 us (1%)
    ppermute x6, starting transfers between devices, gather_causal(): pieces.append(lax.ppermute(value, ('tm', 'section'), pairs))  14 us
    ppermute x2, waiting for transfers between devices, per_device(): lax.ppermute(partial0.astype(jnp.bfloat16), feat_axes, pairs)  13.7 us
    all_gather x1, blocking collectives, per_device(): hidden0 = lax.all_gather(tokens, feat_axes, axis=2, tiled=True)  9.24 us
    conv_general_dilated x1, matrix products, per_device(): lax.conv_general_dilated(chunks, kernel, window_strides=(STRIDE,), paddin...  5.67 us
    unnamed x16, local copies, waits for them, and re-layouts  4.67 us
    ppermute x3, starting transfers between devices, shift_from(): return lax.ppermute(value, axis, pairs)  4.66 us
    another operation x2, local copies, waits for them, and re-layouts, per_device(): jnp.stack([normed[:, :, q * chunk_tok * STRIDE:(q + 1) * chunk_tok * STRI...  3.27 us
    ppermute x1, starting transfers between devices, per_device(): lax.ppermute(cols_high.astype(jnp.bfloat16), feat_axes, pairs)  3.18 us
  transfers between devices with their start and end apart: 14, of which 2 were waited for; matrix products, arithmetic and copies ran while one was open for 12% of the time, Pallas kernels for 0%

profile of v18, /device:TPU:1, one launch (start us, length us, event | category | flops | bytes accessed | tf_op | source)
XLA Modules:
  0.0 94.3 jit_solution(9141657204066236478)
XLA Ops:
  2.8 1.5 %multiply_reduce_fusion.1 = f32[2,64]{1,0:T(2,128)S(1)} fusion(f32[2,4096]{1,0:T(2,128)S(1)} %compare_convert_fusion, bf16[2,64,4096]{2,1,0:T(8,128)(2,1)} %param.8), kind=kLoop, calls=%fused_computation.26 | loop fusion | flops 1572736 | bytes 1081856 | tf_op jit(solution)/shard_map/reduce_sum | solution.py:164
  4.9 2.2 %collective-permute-start = (f32[2,64,34]{1,0,2:T(2,128)S(1)}, f32[2,64,34]{1,0,2:T(2,128)S(1)}, u32[]{:S(2)}, u32[]{:S(2)}) collective-permute-start(f32[2,64,34]{1,0,2:T(2,128)S(1)} %pad_maximum_fusion.1), channel_id=1, source_target_pairs={{0,4},{4,8},{8,12},{12,0},{1,5},{5,9},{9,13},{13,1},{2,6},{6,10},{... | collective-permute-start | bytes 52232 | tf_op jit(solution)/shard_map/ppermute | solution.py:13
  7.1 2.1 %collective-permute-start.2 = (f32[2,64,34]{1,0,2:T(2,128)S(1)}, f32[2,64,34]{1,0,2:T(2,128)S(1)}, u32[]{:S(2)}, u32[]{:S(2)}) collective-permute-start(f32[2,64,34]{1,0,2:T(2,128)S(1)} %pad_maximum_fusion.1), channel_id=1, source_target_pairs={{0,12},{4,0},{8,4},{12,8},{1,13},{5,1},{9,5},{13,9},{2,14},{6,2},{... | collective-permute-start | bytes 52232 | tf_op jit(solution)/shard_map/ppermute | solution.py:13
  10.4 1.6 %convert_element_type.131 = f32[2,64,4096]{2,1,0:T(8,128)} convert(bf16[2,64,4096]{2,1,0:T(8,128)(2,1)S(1)} %copy-done.1) | non-fusion elementwise | flops 524288 | bytes 3145728 | tf_op jit(solution)/shard_map/convert_element_type | solution.py:162
  12.0 4.5 %copy.42 = bf16[4096,320]{1,0:T(8,128)(2,1)} copy(bf16[4096,320]{0,1:T(8,128)(2,1)} %param.10) | data formatting | bytes 5242880 | tf_op args[2]
  17.6 2.3 %fusion.11 = bf16[2,64,4128]{2,1,0:T(8,128)(2,1)S(1)} fusion(f32[2,64,4096]{2,1,0:T(8,128)} %convert_element_type.131, f32[2,64,32]{2,1,0:T(8,128)S(1)} %copy.39, f32[2,64]{1,0:T(2,128)S(1)} %add_rsqrt_fusion.2, f32[2,64]{1,0:T(2,128)S(1)} %broadcast_divide_fusion, f32[2,4128]{1,0:T(2,128)S(1)} %and_convert_fusion), kind=kLoop, calls=%fused_computation.18 | loop fusion | flops 3170304 | bytes 3204352 | tf_op jit(solution)/shard_map/convert_element_type | solution.py:205
  20.2 3.2 %copy.41 = bf16[2,4,64,1056]{2,1,0,3:T(4,128)(2,1)} copy(bf16[2,4,64,1056]{3,2,0,1:T(8,128)(2,1)S(1)} %pad_maximum_fusion) | data formatting | bytes 2162688 | tf_op jit(solution)/shard_map/stack | solution.py:209
  23.4 5.7 %fusion.54 = bf16[8,32,320]{2,0,1:T(8,128)(2,1)S(1)} fusion(bf16[8,64,1056]{1,0,2:T(8,128)(2,1)} %bitcast.168, bf16[64,64,320]{2,1,0:T(8,128)(2,1)} %bitcast.167), kind=kOutput, calls=%fused_computation.55 | convolution fusion | flops 671170560 | bytes 3866624 | tf_op jit(solution)/shard_map/conv_general_dilated | solution.py:216
  29.3 9.2 %all_gather.3 = bf16[2,128,1280]{1,0,2:T(2,128)(2,1)S(1)} all-gather(bf16[2,128,320]{1,0,2:T(2,128)(2,1)S(1)} %copy.45), channel_id=1, replica_groups=mesh['groups'=2,'tm'=4,'mp'=2,'section'=2] {'mp','section'}, dimensions={2}, use_global_device_ids=true | all-gather | bytes 819200 | tf_op jit(solution)/shard_map/all_gather | solution.py:226
  39.7 1.7 %convolution_convert_fusion.2 = bf16[320,2,128]{2,0,1:T(8,128)(2,1)S(1)} fusion(bf16[1280,160]{0,1:T(8,128)(2,1)} %bitcast.192, bf16[1280,160]{0,1:T(8,128)(2,1)} %bitcast.194, bf16[2,128,1280]{2,1,0:T(8,128)(2,1)S(1)} %copy.46, f32[1280]{0:T(1024)S(1)} %convert_reduce_fusion, f32[2,128]{1,0:T(2,128)S(1)} %add_rsqrt_fusion.1), kind=kOutput, calls=%fused_computation.57 | convolution fusion | flops 212746240 | bytes 1644544 | tf_op jit(solution)/shard_map/btd,de->ebt/dot_general | solution.py:77
  42.1 1.3 %collective-permute-start.4 = (bf16[2,2,2,80,128]{4,3,2,1,0:T(8,128)(2,1)S(1)}, bf16[2,2,2,80,128]{4,3,2,1,0:T(8,128)(2,1)}, u32[]{:S(2)}, u32[]{:S(2)}) collective-permute-start(bf16[2,2,2,80,128]{4,3,2,1,0:T(8,128)(2,1)S(1)} %bitcast.170), channel_id=1, source_target_pairs={{0,8},{4,12},{2,10},{6,14},{16,24},{20,28},{18,26},{22,30}} | collective-permute-start | bytes 491528 | tf_op jit(solution)/shard_map/ppermute | solution.py:34
  43.4 1.3 %collective-permute-start.3 = (bf16[2,2,2,80,128]{4,3,2,1,0:T(8,128)(2,1)S(1)}, bf16[2,2,2,80,128]{4,3,2,1,0:T(8,128)(2,1)}, u32[]{:S(2)}, u32[]{:S(2)}) collective-permute-start(bf16[2,2,2,80,128]{4,3,2,1,0:T(8,128)(2,1)S(1)} %bitcast.171), channel_id=1, source_target_pairs={{0,12},{2,14},{16,28},{18,30}} | collective-permute-start | bytes 491528 | tf_op jit(solution)/shard_map/ppermute | solution.py:34
  50.0 1.3 %collective-permute-start.7 = (bf16[2,128,1280]{2,1,0:T(8,128)(2,1)S(1)}, bf16[2,128,1280]{2,1,0:T(8,128)(2,1)}, u32[]{:S(2)}, u32[]{:S(2)}) collective-permute-start(bf16[2,128,1280]{2,1,0:T(8,128)(2,1)S(1)} %convolution_convert_fusion), channel_id=1, source_target_pairs={{0,3},{2,1},{4,7},{6,5},{8,11},{10,9},{12,15},{14,13},{16,19},{18,... | collective-permute-start | bytes 1966088 | tf_op jit(solution)/shard_map/ppermute | solution.py:238
  51.3 1.3 %collective-permute-start.6 = (bf16[2,128,1280]{2,1,0:T(8,128)(2,1)S(1)}, bf16[2,128,1280]{2,1,0:T(8,128)(2,1)}, u32[]{:S(2)}, u32[]{:S(2)}) collective-permute-start(bf16[2,128,1280]{2,1,0:T(8,128)(2,1)S(1)} %convolution_convert_fusion), channel_id=1, source_target_pairs={{0,1},{2,3},{4,5},{6,7},{8,9},{10,11},{12,13},{14,15},{16,17},{18,... | collective-permute-start | bytes 1966088 | tf_op jit(solution)/shard_map/ppermute | solution.py:238
  52.7 13.7 %collective-permute-done.7 = bf16[2,128,1280]{2,1,0:T(8,128)(2,1)} collective-permute-done((bf16[2,128,1280]{2,1,0:T(8,128)(2,1)S(1)}, bf16[2,128,1280]{2,1,0:T(8,128)(2,1)}, u32[]{:S(2)}, u32[]{:S(2)}) %collective-permute-start.7) | collective-permute-done | bytes 655392 | tf_op jit(solution)/shard_map/ppermute | solution.py:238
  66.3 1.7 %fusion.29 = (f32[2,128]{1,0:T(2,128)S(1)}, bf16[2,128,1280]{2,1,0:T(8,128)(2,1)S(1)}) fusion(bf16[2,128,1280]{2,1,0:T(8,128)(2,1)} %collective-permute-done.7, bf16[2,128,1280]{2,1,0:T(8,128)(2,1)} %collective-permute-done.6, bf16[2,128,1280]{2,1,0:T(8,128)(2,1)S(1)} %copy.46), kind=kLoop, calls=%fused_computation.41 | loop fusion | flops 2948864 | bytes 2622464 | tf_op jit(solution)/shard_map/reduce_sum | solution.py:69
  68.6 3.6 %collective-permute-start.10 = (bf16[2,2,2,80,128]{4,3,2,1,0:T(8,128)(2,1)S(1)}, bf16[2,2,2,80,128]{4,3,2,1,0:T(8,128)(2,1)S(1)}, u32[]{:S(2)}, u32[]{:S(2)}) collective-permute-start(bf16[2,2,2,80,128]{4,3,2,1,0:T(8,128)(2,1)S(1)} %bitcast.174), channel_id=1, source_target_pairs={{1,5},{5,9},{9,13},{3,7},{7,11},{11,15},{17,21},{21,25},{25,29},{1... | collective-permute-start | bytes 491528 | tf_op jit(solution)/shard_map/ppermute | solution.py:34
  72.2 5.1 %collective-permute-start.9 = (bf16[2,2,2,80,128]{4,3,2,1,0:T(8,128)(2,1)S(1)}, bf16[2,2,2,80,128]{4,3,2,1,0:T(8,128)(2,1)S(1)}, u32[]{:S(2)}, u32[]{:S(2)}) collective-permute-start(bf16[2,2,2,80,128]{4,3,2,1,0:T(8,128)(2,1)S(1)} %bitcast.175), channel_id=1, source_target_pairs={{1,9},{5,13},{3,11},{7,15},{17,25},{21,29},{19,27},{23,31}} | collective-permute-start | bytes 491528 | tf_op jit(solution)/shard_map/ppermute | solution.py:34
  77.3 2.0 %collective-permute-start.8 = (bf16[2,2,2,80,128]{4,3,2,1,0:T(8,128)(2,1)S(1)}, bf16[2,2,2,80,128]{4,3,2,1,0:T(8,128)(2,1)}, u32[]{:S(2)}, u32[]{:S(2)}) collective-permute-start(bf16[2,2,2,80,128]{4,3,2,1,0:T(8,128)(2,1)S(1)} %bitcast.176), channel_id=1, source_target_pairs={{1,13},{3,15},{17,29},{19,31}} | collective-permute-start | bytes 491528 | tf_op jit(solution)/shard_map/ppermute | solution.py:34
  79.3 1.4 %fusion.48 = bf16[2,128,640]{2,1,0:T(8,128)(2,1)} fusion(bf16[1,1280,640]{2,1,0:T(8,128)(2,1)S(1)} %copy-done.4, bf16[2,128,1280]{2,1,0:T(8,128)(2,1)S(1)} %get-tuple-element.4, f32[2,128]{1,0:T(2,128)S(1)} %add_rsqrt_fusion, f32[1280]{0:T(1024)S(1)} %convert_reduce_fusion), kind=kOutput, calls=%fused_computation.52 | convolution fusion | flops 421068800 | bytes 2627584 | tf_op jit(solution)/shard_map/btd,de->bte/dot_general | solution.py:72
  80.8 1.2 %copy.52 = bf16[2,128,640]{1,2,0:T(8,128)(2,1)S(1)} copy(bf16[2,128,640]{2,1,0:T(8,128)(2,1)} %fusion.48) | data formatting | bytes 655360 | tf_op jit(solution)/shard_map/convert_element_type | solution.py:74
  86.3 3.2 %collective-permute-start.13 = (bf16[1,128,640]{2,1,0:T(8,128)(2,1)S(1)}, bf16[1,128,640]{2,1,0:T(8,128)(2,1)S(1)}, u32[]{:S(2)}, u32[]{:S(2)}) collective-permute-start(bf16[1,128,640]{2,1,0:T(8,128)(2,1)S(1)} %dynamic-slice_convert_fusion), channel_id=1, source_target_pairs={{1,3},{3,1},{5,7},{7,5},{9,11},{11,9},{13,15},{15,13},{17,19},{19,... | collective-permute-start | bytes 491528 | tf_op jit(solution)/shard_map/ppermute | solution.py:267
  89.5 1.3 %collective-permute-start.12 = (bf16[1,128,640]{2,1,0:T(8,128)(2,1)S(1)}, bf16[1,128,640]{2,1,0:T(8,128)(2,1)S(1)}, u32[]{:S(2)}, u32[]{:S(2)}) collective-permute-start(bf16[1,128,640]{2,1,0:T(8,128)(2,1)S(1)} %dynamic-slice_convert_fusion.1), channel_id=1, source_target_pairs={{1,2},{3,0},{5,6},{7,4},{9,10},{11,8},{13,14},{15,12},{17,18},{19,... | collective-permute-start | bytes 491528 | tf_op jit(solution)/shard_map/ppermute | solution.py:263
  90.9 1.3 %collective-permute-start.11 = (bf16[1,128,640]{2,1,0:T(8,128)(2,1)S(1)}, bf16[1,128,640]{2,1,0:T(8,128)(2,1)S(1)}, u32[]{:S(2)}, u32[]{:S(2)}) collective-permute-start(bf16[1,128,640]{2,1,0:T(8,128)(2,1)S(1)} %add_convert_fusion), channel_id=1, source_target_pairs={{1,0},{3,2},{5,4},{7,6},{9,8},{11,10},{13,12},{15,14},{17,16},{19,... | collective-permute-start | bytes 491528 | tf_op jit(solution)/shard_map/ppermute | solution.py:263
  (99 shorter events, 19.4 us)
Async XLA Ops:
  0.6 48.6 %copy-start = (bf16[1,640,1280]{2,1,0:T(8,128)(2,1)S(1)}, bf16[1,640,1280]{2,1,0:T(8,128)(2,1)}, u32[]{:S(2)}) copy-start(bf16[1,640,1280]{2,1,0:T(8,128)(2,1)} %param.15) | copy-start | bytes 4915204
  0.6 3.7 %copy-start.1 = (bf16[2,64,4096]{2,1,0:T(8,128)(2,1)S(1)}, bf16[2,64,4096]{2,1,0:T(8,128)(2,1)}, u32[]{:S(2)}) copy-start(bf16[2,64,4096]{2,1,0:T(8,128)(2,1)} %param.8) | copy-start | bytes 3145732
  0.7 9.4 %copy-start.2 = (bf16[1,1280]{1,0:T(2,128)(2,1)S(1)}, bf16[1,1280]{1,0:T(2,128)(2,1)}, u32[]{:S(2)}) copy-start(bf16[1,1280]{1,0:T(2,128)(2,1)} %param.11) | copy-start | bytes 7684
  4.9 11.6 %collective-permute-start = (f32[2,64,34]{1,0,2:T(2,128)S(1)}, f32[2,64,34]{1,0,2:T(2,128)S(1)}, u32[]{:S(2)}, u32[]{:S(2)}) collective-permute-start(f32[2,64,34]{1,0,2:T(2,128)S(1)} %pad_maximum_fusion.1), channel_id=1, source_target_pairs={{0,4},{4,8},{8,12},{12,0},{1,5},{5,9},{9,13},{13,1},{2,6},{6,10},{... | collective-permute-start | bytes 52232 | tf_op jit(solution)/shard_map/ppermute | solution.py:13
  7.1 9.4 %collective-permute-start.2 = (f32[2,64,34]{1,0,2:T(2,128)S(1)}, f32[2,64,34]{1,0,2:T(2,128)S(1)}, u32[]{:S(2)}, u32[]{:S(2)}) collective-permute-start(f32[2,64,34]{1,0,2:T(2,128)S(1)} %pad_maximum_fusion.1), channel_id=1, source_target_pairs={{0,12},{4,0},{8,4},{12,8},{1,13},{5,1},{9,5},{13,9},{2,14},{6,2},{... | collective-permute-start | bytes 52232 | tf_op jit(solution)/shard_map/ppermute | solution.py:13
  9.2 7.5 %collective-permute-start.1 = (f32[2,64,34]{1,0,2:T(2,128)S(1)}, f32[2,64,34]{1,0,2:T(2,128)S(1)}, u32[]{:S(2)}, u32[]{:S(2)}) collective-permute-start(f32[2,64,34]{1,0,2:T(2,128)S(1)} %pad_maximum_fusion.1), channel_id=1, source_target_pairs={{0,8},{4,12},{8,0},{12,4},{1,9},{5,13},{9,1},{13,5},{2,10},{6,14},... | collective-permute-start | bytes 52232 | tf_op jit(solution)/shard_map/ppermute | solution.py:13
  39.7 5.1 %copy-start.3 = (bf16[1,1280,640]{2,1,0:T(8,128)(2,1)S(1)}, bf16[1,1280,640]{2,1,0:T(8,128)(2,1)}, u32[]{:S(2)}) copy-start(bf16[1,1280,640]{2,1,0:T(8,128)(2,1)} %param.12) | copy-start | bytes 4915204
  41.4 4.3 %collective-permute-start.5 = (bf16[2,2,2,80,128]{4,3,2,1,0:T(8,128)(2,1)S(1)}, bf16[2,2,2,80,128]{4,3,2,1,0:T(8,128)(2,1)S(1)}, u32[]{:S(2)}, u32[]{:S(2)}) collective-permute-start(bf16[2,2,2,80,128]{4,3,2,1,0:T(8,128)(2,1)S(1)} %bitcast.169), channel_id=1, source_target_pairs={{0,4},{4,8},{8,12},{2,6},{6,10},{10,14},{16,20},{20,24},{24,28},{1... | collective-permute-start | bytes 491528 | tf_op jit(solution)/shard_map/ppermute | solution.py:34
  42.1 3.6 %collective-permute-start.4 = (bf16[2,2,2,80,128]{4,3,2,1,0:T(8,128)(2,1)S(1)}, bf16[2,2,2,80,128]{4,3,2,1,0:T(8,128)(2,1)}, u32[]{:S(2)}, u32[]{:S(2)}) collective-permute-start(bf16[2,2,2,80,128]{4,3,2,1,0:T(8,128)(2,1)S(1)} %bitcast.170), channel_id=1, source_target_pairs={{0,8},{4,12},{2,10},{6,14},{16,24},{20,28},{18,26},{22,30}} | collective-permute-start | bytes 491528 | tf_op jit(solution)/shard_map/ppermute | solution.py:34
  43.4 2.3 %collective-permute-start.3 = (bf16[2,2,2,80,128]{4,3,2,1,0:T(8,128)(2,1)S(1)}, bf16[2,2,2,80,128]{4,3,2,1,0:T(8,128)(2,1)}, u32[]{:S(2)}, u32[]{:S(2)}) collective-permute-start(bf16[2,2,2,80,128]{4,3,2,1,0:T(8,128)(2,1)S(1)} %bitcast.171), channel_id=1, source_target_pairs={{0,12},{2,14},{16,28},{18,30}} | collective-permute-start | bytes 491528 | tf_op jit(solution)/shard_map/ppermute | solution.py:34
  50.0 16.3 %collective-permute-start.7 = (bf16[2,128,1280]{2,1,0:T(8,128)(2,1)S(1)}, bf16[2,128,1280]{2,1,0:T(8,128)(2,1)}, u32[]{:S(2)}, u32[]{:S(2)}) collective-permute-start(bf16[2,128,1280]{2,1,0:T(8,128)(2,1)S(1)} %convolution_convert_fusion), channel_id=1, source_target_pairs={{0,3},{2,1},{4,7},{6,5},{8,11},{10,9},{12,15},{14,13},{16,19},{18,... | collective-permute-start | bytes 1966088 | tf_op jit(solution)/shard_map/ppermute | solution.py:238
  51.3 15.0 %collective-permute-start.6 = (bf16[2,128,1280]{2,1,0:T(8,128)(2,1)S(1)}, bf16[2,128,1280]{2,1,0:T(8,128)(2,1)}, u32[]{:S(2)}, u32[]{:S(2)}) collective-permute-start(bf16[2,128,1280]{2,1,0:T(8,128)(2,1)S(1)} %convolution_convert_fusion), channel_id=1, source_target_pairs={{0,1},{2,3},{4,5},{6,7},{8,9},{10,11},{12,13},{14,15},{16,17},{18,... | collective-permute-start | bytes 1966088 | tf_op jit(solution)/shard_map/ppermute | solution.py:238
  52.6 15.4 %copy-start.5 = (bf16[1,1280,160]{1,2,0:T(8,128)(2,1)S(1)}, bf16[1,1280,160]{1,2,0:T(8,128)(2,1)}, u32[]{:S(2)}) copy-start(bf16[1,1280,160]{1,2,0:T(8,128)(2,1)} %param.14) | copy-start | bytes 1228804
  52.6 15.4 %copy-start.6 = (bf16[1,1280,160]{1,2,0:T(8,128)(2,1)S(1)}, bf16[1,1280,160]{1,2,0:T(8,128)(2,1)}, u32[]{:S(2)}) copy-start(bf16[1,1280,160]{1,2,0:T(8,128)(2,1)} %param.13) | copy-start | bytes 1228804
  68.0 11.3 %copy-start.4 = (bf16[1,1280,640]{2,1,0:T(8,128)(2,1)S(1)}, bf16[1,1280,640]{2,1,0:T(8,128)(2,1)}, u32[]{:S(2)}) copy-start(bf16[1,1280,640]{2,1,0:T(8,128)(2,1)} %param.12) | copy-start | bytes 4915204
  68.6 13.4 %collective-permute-start.10 = (bf16[2,2,2,80,128]{4,3,2,1,0:T(8,128)(2,1)S(1)}, bf16[2,2,2,80,128]{4,3,2,1,0:T(8,128)(2,1)S(1)}, u32[]{:S(2)}, u32[]{:S(2)}) collective-permute-start(bf16[2,2,2,80,128]{4,3,2,1,0:T(8,128)(2,1)S(1)} %bitcast.174), channel_id=1, source_target_pairs={{1,5},{5,9},{9,13},{3,7},{7,11},{11,15},{17,21},{21,25},{25,29},{1... | collective-permute-start | bytes 491528 | tf_op jit(solution)/shard_map/ppermute | solution.py:34
  72.2 9.7 %collective-permute-start.9 = (bf16[2,2,2,80,128]{4,3,2,1,0:T(8,128)(2,1)S(1)}, bf16[2,2,2,80,128]{4,3,2,1,0:T(8,128)(2,1)S(1)}, u32[]{:S(2)}, u32[]{:S(2)}) collective-permute-start(bf16[2,2,2,80,128]{4,3,2,1,0:T(8,128)(2,1)S(1)} %bitcast.175), channel_id=1, source_target_pairs={{1,9},{5,13},{3,11},{7,15},{17,25},{21,29},{19,27},{23,31}} | collective-permute-start | bytes 491528 | tf_op jit(solution)/shard_map/ppermute | solution.py:34
  77.3 4.7 %collective-permute-start.8 = (bf16[2,2,2,80,128]{4,3,2,1,0:T(8,128)(2,1)S(1)}, bf16[2,2,2,80,128]{4,3,2,1,0:T(8,128)(2,1)}, u32[]{:S(2)}, u32[]{:S(2)}) collective-permute-start(bf16[2,2,2,80,128]{4,3,2,1,0:T(8,128)(2,1)S(1)} %bitcast.176), channel_id=1, source_target_pairs={{1,13},{3,15},{17,29},{19,31}} | collective-permute-start | bytes 491528 | tf_op jit(solution)/shard_map/ppermute | solution.py:34
  86.3 6.6 %collective-permute-start.13 = (bf16[1,128,640]{2,1,0:T(8,128)(2,1)S(1)}, bf16[1,128,640]{2,1,0:T(8,128)(2,1)S(1)}, u32[]{:S(2)}, u32[]{:S(2)}) collective-permute-start(bf16[1,128,640]{2,1,0:T(8,128)(2,1)S(1)} %dynamic-slice_convert_fusion), channel_id=1, source_target_pairs={{1,3},{3,1},{5,7},{7,5},{9,11},{11,9},{13,15},{15,13},{17,19},{19,... | collective-permute-start | bytes 491528 | tf_op jit(solution)/shard_map/ppermute | solution.py:267
  89.5 4.0 %collective-permute-start.12 = (bf16[1,128,640]{2,1,0:T(8,128)(2,1)S(1)}, bf16[1,128,640]{2,1,0:T(8,128)(2,1)S(1)}, u32[]{:S(2)}, u32[]{:S(2)}) collective-permute-start(bf16[1,128,640]{2,1,0:T(8,128)(2,1)S(1)} %dynamic-slice_convert_fusion.1), channel_id=1, source_target_pairs={{1,2},{3,0},{5,6},{7,4},{9,10},{11,8},{13,14},{15,12},{17,18},{19,... | collective-permute-start | bytes 491528 | tf_op jit(solution)/shard_map/ppermute | solution.py:263
  90.9 2.6 %collective-permute-start.11 = (bf16[1,128,640]{2,1,0:T(8,128)(2,1)S(1)}, bf16[1,128,640]{2,1,0:T(8,128)(2,1)S(1)}, u32[]{:S(2)}, u32[]{:S(2)}) collective-permute-start(bf16[1,128,640]{2,1,0:T(8,128)(2,1)S(1)} %add_convert_fusion), channel_id=1, source_target_pairs={{1,0},{3,2},{5,4},{7,6},{9,8},{11,10},{13,12},{15,14},{17,16},{19,... | collective-permute-start | bytes 491528 | tf_op jit(solution)/shard_map/ppermute | solution.py:263

commit v19 on v18

--- a/solution.py
+++ b/solution.py
@@ -68,20 +68,20 @@
     gain32 = gain.astype(jnp.float32)
     scaled = hidden32 * lax.rsqrt(jnp.mean(hidden32 * hidden32, -1, keepdims=True) + 1e-06)
     layer_input = (scaled * gain32).astype(jnp.bfloat16)
-    queries = (
-        jnp.einsum("btd,de->bte", layer_input, query_w, preferred_element_type=jnp.float32)
-        * HD ** (-0.5)
-    ).astype(jnp.bfloat16)
     kv_local = key_w.shape[1] // HD
     group_size = query_w.shape[1] // key_w.shape[1]
-    kv_t = jnp.einsum(
-        "btd,de->ebt", layer_input, jnp.concatenate([key_w, value_w], 1),
+    q_width = query_w.shape[1]
+    projected = jnp.einsum(
+        "btd,de->ebt", layer_input, jnp.concatenate([query_w, key_w, value_w], 1),
         preferred_element_type=jnp.float32,
-    ).astype(jnp.bfloat16)
+    )
+    queries = (projected[:q_width] * HD ** (-0.5)).astype(jnp.bfloat16)
+    queries = queries.reshape(kv_local, group_size, HD, batch_count, tok_count)
+    kv_t = projected[q_width:].astype(jnp.bfloat16)
     kv_t = kv_t.reshape(2, kv_local, HD, batch_count, tok_count).transpose(0, 3, 1, 2, 4)
     key_t = kv_t[0]
     value_t = kv_t[1]
-    query_rows = queries.reshape(batch_count, tok_count, kv_local, group_size, HD)
+    query_rows = queries.transpose(3, 4, 0, 1, 2)
     query_pos = tm_at * tok_count + jnp.arange(tok_count, dtype=jnp.int32)
     first_valid = total_tokens - seq_lens // STRIDE
     both, key_pos = gather_causal(kv_t, tm_n, sec_n, tm_at, phase, tok_count)

time: 96.1 us -> 101 us (1.051)
  waiting for transfers between devices: 14.3 us -> 21.3 us
  starting transfers between devices: 27 us -> 24.2 us
  local copies, waits for them, and re-layouts: 12.2 us -> 14.5 us
    ppermute x2, waiting for transfers between devices: 13.7 us -> 16.9 us  [per_device(): lax.ppermute(partial0.astype(jnp.bfloat16), feat_axes, pairs)]
    ppermute x6, starting transfers between devices: 14 us -> 11.3 us  [gather_causal(): pieces.append(lax.ppermute(value, ('tm', 'section'), pairs))]
    unnamed x16 -> x19, local copies, waits for them, and re-layouts: 4.67 us -> 7.01 us
    ppermute x1, waiting for transfers between devices: 0.01 us -> 2.24 us  [per_device(): lax.ppermute(cols_high.astype(jnp.bfloat16), feat_axes, pairs)]
    ppermute x6, waiting for transfers between devices: 0.02 us -> 2.09 us  [gather_causal(): pieces.append(lax.ppermute(value, ('tm', 'section'), pairs))]
    another operation x2, other arithmetic: 2.07 us -> 0.17 us  [attend_layer(): jnp.moveaxis(both.reshape(2, batch_count, kv_local, HD, rounds, block_wid...]
    convert_element_type x2 -> x0, local copies, waits for them, and re-layouts: 1.39 us -> none  [attend_layer(): queries = (jnp.einsum('btd,de->bte', layer_input, query_w, preferred_elem...]
    another operation x3, local copies, waits for them, and re-layouts: 0.01 us -> 1.34 us  [per_device(): jnp.stack([piece[..., :2] for piece in received], 0)]
  transfers between devices with their start and end apart: 14 -> 14, of which waited for: 2 -> 4; matrix products, arithmetic and copies ran while one was open for 12% -> 11% of each run, Pallas kernels for 0% -> 0%
where the time goes in v19:
time: 101 us; the launch traced here: 99.4 us
  starting transfers between devices  24.2 us (24%)
  waiting for transfers between devices  21.3 us (21%)
  other arithmetic  14.9 us (15%)
  local copies, waits for them, and re-layouts  14.5 us (14%)
  matrix products  13.9 us (14%)
  blocking collectives  9.24 us (9%)
  between operations  1.24 us (1%)
    ppermute x2, waiting for transfers between devices, per_device(): lax.ppermute(partial0.astype(jnp.bfloat16), feat_axes, pairs)  16.9 us
    ppermute x6, starting transfers between devices, gather_causal(): pieces.append(lax.ppermute(value, ('tm', 'section'), pairs))  11.3 us
    all_gather x1, blocking collectives, per_device(): hidden0 = lax.all_gather(tokens, feat_axes, axis=2, tiled=True)  9.24 us
    unnamed x19, local copies, waits for them, and re-layouts  7.01 us
    conv_general_dilated x1, matrix products, per_device(): lax.conv_general_dilated(chunks, kernel, window_strides=(STRIDE,), paddin...  5.67 us
    ppermute x3, starting transfers between devices, shift_from(): return lax.ppermute(value, axis, pairs)  4.66 us
    dot_general x2, matrix products, attend_layer(): jnp.einsum('btd,de->ebt', layer_input, jnp.concatenate([query_w, key_w, v...  3.41 us
    another operation x2, local copies, waits for them, and re-layouts, per_device(): jnp.stack([normed[:, :, q * chunk_tok * STRIDE:(q + 1) * chunk_tok * STRI...  3.29 us
  transfers between devices with their start and end apart: 14, of which 4 were waited for; matrix products, arithmetic and copies ran while one was open for 11% of the time, Pallas kernels for 0%

profile of v19, /device:TPU:1, one launch (start us, length us, event | category | flops | bytes accessed | tf_op | source)
XLA Modules:
  0.0 99.4 jit_solution(6727055653135362269)
XLA Ops:
  2.7 1.5 %multiply_reduce_fusion.1 = f32[2,64]{1,0:T(2,128)S(1)} fusion(f32[2,4096]{1,0:T(2,128)S(1)} %compare_convert_fusion, bf16[2,64,4096]{2,1,0:T(8,128)(2,1)} %param.8), kind=kLoop, calls=%fused_computation.27 | loop fusion | flops 1572736 | bytes 1081856 | tf_op jit(solution)/shard_map/reduce_sum | solution.py:164
  4.3 1.7 %multiply_reduce_fusion = f32[2,64]{1,0:T(2,128)S(1)} fusion(f32[2,64]{1,0:T(2,128)S(1)} %broadcast_divide_fusion.1, f32[2,4096]{1,0:T(2,128)S(1)} %compare_convert_fusion, bf16[2,64,4096]{2,1,0:T(8,128)(2,1)} %param.8), kind=kLoop, calls=%fused_computation.26 | loop fusion | flops 2621312 | bytes 1082368 | tf_op jit(solution)/shard_map/reduce_sum | solution.py:174
  6.1 2.2 %collective-permute-start = (f32[2,64,34]{1,0,2:T(2,128)S(1)}, f32[2,64,34]{1,0,2:T(2,128)S(1)}, u32[]{:S(2)}, u32[]{:S(2)}) collective-permute-start(f32[2,64,34]{1,0,2:T(2,128)S(1)} %pad_maximum_fusion.1), channel_id=1, source_target_pairs={{0,4},{4,8},{8,12},{12,0},{1,5},{5,9},{9,13},{13,1},{2,6},{6,10},{... | collective-permute-start | bytes 52232 | tf_op jit(solution)/shard_map/ppermute | solution.py:13
  8.3 2.1 %collective-permute-start.2 = (f32[2,64,34]{1,0,2:T(2,128)S(1)}, f32[2,64,34]{1,0,2:T(2,128)}, u32[]{:S(2)}, u32[]{:S(2)}) collective-permute-start(f32[2,64,34]{1,0,2:T(2,128)S(1)} %pad_maximum_fusion.1), channel_id=1, source_target_pairs={{0,12},{4,0},{8,4},{12,8},{1,13},{5,1},{9,5},{13,9},{2,14},{6,2},{... | collective-permute-start | bytes 52232 | tf_op jit(solution)/shard_map/ppermute | solution.py:13
  11.7 1.6 %convert_element_type.127 = f32[2,64,4096]{2,1,0:T(8,128)} convert(bf16[2,64,4096]{2,1,0:T(8,128)(2,1)S(1)} %copy-done.1) | non-fusion elementwise | flops 524288 | bytes 3145728 | tf_op jit(solution)/shard_map/convert_element_type | solution.py:162
  13.2 4.7 %copy.41 = bf16[4096,320]{1,0:T(8,128)(2,1)} copy(bf16[4096,320]{0,1:T(8,128)(2,1)} %param.10) | data formatting | bytes 5242880 | tf_op args[2]
  17.9 2.2 %copy.36 = bf16[1,1280,640]{1,2,0:T(8,128)(2,1)} copy(bf16[1,1280,640]{2,1,0:T(8,128)(2,1)S(1)} %copy-done.2) | data formatting | bytes 3276800 | tf_op args[4]
  22.5 2.3 %fusion.11 = bf16[2,64,4128]{2,1,0:T(8,128)(2,1)S(1)} fusion(f32[2,64,4096]{2,1,0:T(8,128)} %convert_element_type.127, f32[2,64,32]{2,1,0:T(8,128)S(1)} %copy.38, f32[2,64]{1,0:T(2,128)S(1)} %add_rsqrt_fusion.2, f32[2,64]{1,0:T(2,128)S(1)} %broadcast_divide_fusion, f32[2,4128]{1,0:T(2,128)S(1)} %and_convert_fusion), kind=kLoop, calls=%fused_computation.19 | loop fusion | flops 3170304 | bytes 3204352 | tf_op jit(solution)/shard_map/convert_element_type | solution.py:205
  25.1 3.2 %copy.40 = bf16[2,4,64,1056]{2,1,0,3:T(4,128)(2,1)} copy(bf16[2,4,64,1056]{3,2,0,1:T(8,128)(2,1)S(1)} %pad_maximum_fusion) | data formatting | bytes 2162688 | tf_op jit(solution)/shard_map/stack | solution.py:209
  28.3 5.7 %fusion.40 = bf16[8,32,320]{2,0,1:T(8,128)(2,1)S(1)} fusion(bf16[8,64,1056]{1,0,2:T(8,128)(2,1)} %bitcast.159, bf16[64,64,320]{2,1,0:T(8,128)(2,1)} %bitcast.158), kind=kOutput, calls=%fused_computation.50 | convolution fusion | flops 671170560 | bytes 3866624 | tf_op jit(solution)/shard_map/conv_general_dilated | solution.py:216
  34.2 9.2 %all_gather.3 = bf16[2,128,1280]{1,0,2:T(2,128)(2,1)S(1)} all-gather(bf16[2,128,320]{1,0,2:T(2,128)(2,1)S(1)} %copy.44), channel_id=1, replica_groups=mesh['groups'=2,'tm'=4,'mp'=2,'section'=2] {'mp','section'}, dimensions={2}, use_global_device_ids=true | all-gather | bytes 819200 | tf_op jit(solution)/shard_map/all_gather | solution.py:226
  44.6 2.5 %fusion.33 = f32[960,2,128]{2,0,1:T(8,128)S(1)} fusion(bf16[1280,160]{0,1:T(8,128)(2,1)S(1)} %bitcast.185, bf16[1280,160]{0,1:T(8,128)(2,1)} %bitcast.187, bf16[1280,640]{0,1:T(8,128)(2,1)} %bitcast.160, bf16[2,128,1280]{2,1,0:T(8,128)(2,1)S(1)} %copy.45, f32[1280]{0:T(1024)S(1)} %convert_reduce_fusion, f32[2,128]{1,0:T(2,128)S(1)} %add_rsqrt_fusion.1), kind=kOutput, calls=%fused_computation.46 | convolution fusion | flops 637829120 | bytes 4102144 | tf_op jit(solution)/shard_map/btd,de->ebt/dot_general | solution.py:74
  52.7 1.3 %collective-permute-start.6 = (bf16[2,128,1280]{2,1,0:T(8,128)(2,1)S(1)}, bf16[2,128,1280]{2,1,0:T(8,128)(2,1)}, u32[]{:S(2)}, u32[]{:S(2)}) collective-permute-start(bf16[2,128,1280]{2,1,0:T(8,128)(2,1)S(1)} %convolution_convert_fusion), channel_id=1, source_target_pairs={{0,1},{2,3},{4,5},{6,7},{8,9},{10,11},{12,13},{14,15},{16,17},{18,... | collective-permute-start | bytes 1966088 | tf_op jit(solution)/shard_map/ppermute | solution.py:238
  55.4 8.0 %collective-permute-done.6 = bf16[2,128,1280]{2,1,0:T(8,128)(2,1)} collective-permute-done((bf16[2,128,1280]{2,1,0:T(8,128)(2,1)S(1)}, bf16[2,128,1280]{2,1,0:T(8,128)(2,1)}, u32[]{:S(2)}, u32[]{:S(2)}) %collective-permute-start.6) | collective-permute-done | bytes 655392 | tf_op jit(solution)/shard_map/ppermute | solution.py:238
  63.4 8.9 %collective-permute-done.7 = bf16[2,128,1280]{2,1,0:T(8,128)(2,1)} collective-permute-done((bf16[2,128,1280]{2,1,0:T(8,128)(2,1)S(1)}, bf16[2,128,1280]{2,1,0:T(8,128)(2,1)}, u32[]{:S(2)}, u32[]{:S(2)}) %collective-permute-start.7) | collective-permute-done | bytes 655392 | tf_op jit(solution)/shard_map/ppermute | solution.py:238
  72.3 1.7 %fusion.25 = (f32[2,128]{1,0:T(2,128)S(1)}, bf16[2,128,1280]{2,1,0:T(8,128)(2,1)S(1)}) fusion(bf16[2,128,1280]{2,1,0:T(8,128)(2,1)} %collective-permute-done.7, bf16[2,128,1280]{2,1,0:T(8,128)(2,1)} %collective-permute-done.6, bf16[2,128,1280]{2,1,0:T(8,128)(2,1)S(1)} %copy.45), kind=kLoop, calls=%fused_computation.38 | loop fusion | flops 2948864 | bytes 2622464 | tf_op jit(solution)/shard_map/reduce_sum | solution.py:69
  75.0 4.6 %collective-permute-start.10 = (bf16[2,2,2,80,128]{4,3,2,1,0:T(8,128)(2,1)S(1)}, bf16[2,2,2,80,128]{4,3,2,1,0:T(8,128)(2,1)S(1)}, u32[]{:S(2)}, u32[]{:S(2)}) collective-permute-start(bf16[2,2,2,80,128]{4,3,2,1,0:T(8,128)(2,1)S(1)} %bitcast.167), channel_id=1, source_target_pairs={{1,5},{5,9},{9,13},{3,7},{7,11},{11,15},{17,21},{21,25},{25,29},{1... | collective-permute-start | bytes 491528 | tf_op jit(solution)/shard_map/ppermute | solution.py:34
  79.6 2.4 %collective-permute-start.8 = (bf16[2,2,2,80,128]{4,3,2,1,0:T(8,128)(2,1)S(1)}, bf16[2,2,2,80,128]{4,3,2,1,0:T(8,128)(2,1)S(1)}, u32[]{:S(2)}, u32[]{:S(2)}) collective-permute-start(bf16[2,2,2,80,128]{4,3,2,1,0:T(8,128)(2,1)S(1)} %bitcast.168), channel_id=1, source_target_pairs={{1,13},{3,15},{17,29},{19,31}} | collective-permute-start | bytes 491528 | tf_op jit(solution)/shard_map/ppermute | solution.py:34
  82.0 2.2 %collective-permute-start.9 = (bf16[2,2,2,80,128]{4,3,2,1,0:T(8,128)(2,1)S(1)}, bf16[2,2,2,80,128]{4,3,2,1,0:T(8,128)(2,1)S(1)}, u32[]{:S(2)}, u32[]{:S(2)}) collective-permute-start(bf16[2,2,2,80,128]{4,3,2,1,0:T(8,128)(2,1)S(1)} %bitcast.169), channel_id=1, source_target_pairs={{1,9},{5,13},{3,11},{7,15},{17,25},{21,29},{19,27},{23,31}} | collective-permute-start | bytes 491528 | tf_op jit(solution)/shard_map/ppermute | solution.py:34
  84.3 2.1 %collective-permute-done.9 = bf16[2,2,2,80,128]{4,3,2,1,0:T(8,128)(2,1)S(1)} collective-permute-done((bf16[2,2,2,80,128]{4,3,2,1,0:T(8,128)(2,1)S(1)}, bf16[2,2,2,80,128]{4,3,2,1,0:T(8,128)(2,1)S(1)}, u32[]{:S(2)}, u32[]{:S(2)}) %collective-permute-start.9) | collective-permute-done | bytes 163872 | tf_op jit(solution)/shard_map/ppermute | solution.py:34
  89.8 1.3 %collective-permute-start.11 = (bf16[1,128,640]{2,1,0:T(8,128)(2,1)S(1)}, bf16[1,128,640]{2,1,0:T(8,128)(2,1)S(1)}, u32[]{:S(2)}, u32[]{:S(2)}) collective-permute-start(bf16[1,128,640]{2,1,0:T(8,128)(2,1)S(1)} %add_convert_fusion), channel_id=1, source_target_pairs={{1,0},{3,2},{5,4},{7,6},{9,8},{11,10},{13,12},{15,14},{17,16},{19,... | collective-permute-start | bytes 491528 | tf_op jit(solution)/shard_map/ppermute | solution.py:263
  91.2 1.3 %collective-permute-start.12 = (bf16[1,128,640]{2,1,0:T(8,128)(2,1)S(1)}, bf16[1,128,640]{2,1,0:T(8,128)(2,1)S(1)}, u32[]{:S(2)}, u32[]{:S(2)}) collective-permute-start(bf16[1,128,640]{2,1,0:T(8,128)(2,1)S(1)} %dynamic-slice_convert_fusion.1), channel_id=1, source_target_pairs={{1,2},{3,0},{5,6},{7,4},{9,10},{11,8},{13,14},{15,12},{17,18},{19,... | collective-permute-start | bytes 491528 | tf_op jit(solution)/shard_map/ppermute | solution.py:263
  92.5 3.1 %collective-permute-start.13 = (bf16[1,128,640]{2,1,0:T(8,128)(2,1)S(1)}, bf16[1,128,640]{2,1,0:T(8,128)(2,1)S(1)}, u32[]{:S(2)}, u32[]{:S(2)}) collective-permute-start(bf16[1,128,640]{2,1,0:T(8,128)(2,1)S(1)} %dynamic-slice_convert_fusion), channel_id=1, source_target_pairs={{1,3},{3,1},{5,7},{7,5},{9,11},{11,9},{13,15},{15,13},{17,19},{19,... | collective-permute-start | bytes 491528 | tf_op jit(solution)/shard_map/ppermute | solution.py:267
  96.3 2.2 %collective-permute-done.13 = bf16[1,128,640]{2,1,0:T(8,128)(2,1)S(1)} collective-permute-done((bf16[1,128,640]{2,1,0:T(8,128)(2,1)S(1)}, bf16[1,128,640]{2,1,0:T(8,128)(2,1)S(1)}, u32[]{:S(2)}, u32[]{:S(2)}) %collective-permute-start.13) | collective-permute-done | bytes 163872 | tf_op jit(solution)/shard_map/ppermute | solution.py:267
  (102 shorter events, 20.2 us)
Async XLA Ops:
  0.6 51.4 %copy-start = (bf16[1,640,1280]{2,1,0:T(8,128)(2,1)S(1)}, bf16[1,640,1280]{2,1,0:T(8,128)(2,1)}, u32[]{:S(2)}) copy-start(bf16[1,640,1280]{2,1,0:T(8,128)(2,1)} %param.15) | copy-start | bytes 4915204
  0.6 11.0 %copy-start.1 = (bf16[2,64,4096]{2,1,0:T(8,128)(2,1)S(1)}, bf16[2,64,4096]{2,1,0:T(8,128)(2,1)}, u32[]{:S(2)}) copy-start(bf16[2,64,4096]{2,1,0:T(8,128)(2,1)} %param.8) | copy-start | bytes 3145732
  0.7 10.4 %copy-start.4 = (bf16[1,1280]{1,0:T(2,128)(2,1)S(1)}, bf16[1,1280]{1,0:T(2,128)(2,1)}, u32[]{:S(2)}) copy-start(bf16[1,1280]{1,0:T(2,128)(2,1)} %param.11) | copy-start | bytes 7684
  6.1 14.0 %collective-permute-start = (f32[2,64,34]{1,0,2:T(2,128)S(1)}, f32[2,64,34]{1,0,2:T(2,128)S(1)}, u32[]{:S(2)}, u32[]{:S(2)}) collective-permute-start(f32[2,64,34]{1,0,2:T(2,128)S(1)} %pad_maximum_fusion.1), channel_id=1, source_target_pairs={{0,4},{4,8},{8,12},{12,0},{1,5},{5,9},{9,13},{13,1},{2,6},{6,10},{... | collective-permute-start | bytes 52232 | tf_op jit(solution)/shard_map/ppermute | solution.py:13
  8.3 11.8 %collective-permute-start.2 = (f32[2,64,34]{1,0,2:T(2,128)S(1)}, f32[2,64,34]{1,0,2:T(2,128)}, u32[]{:S(2)}, u32[]{:S(2)}) collective-permute-start(f32[2,64,34]{1,0,2:T(2,128)S(1)} %pad_maximum_fusion.1), channel_id=1, source_target_pairs={{0,12},{4,0},{8,4},{12,8},{1,13},{5,1},{9,5},{13,9},{2,14},{6,2},{... | collective-permute-start | bytes 52232 | tf_op jit(solution)/shard_map/ppermute | solution.py:13
  10.4 10.4 %collective-permute-start.1 = (f32[2,64,34]{1,0,2:T(2,128)S(1)}, f32[2,64,34]{1,0,2:T(2,128)}, u32[]{:S(2)}, u32[]{:S(2)}) collective-permute-start(f32[2,64,34]{1,0,2:T(2,128)S(1)} %pad_maximum_fusion.1), channel_id=1, source_target_pairs={{0,8},{4,12},{8,0},{12,4},{1,9},{5,13},{9,1},{13,5},{2,10},{6,14},... | collective-permute-start | bytes 52232 | tf_op jit(solution)/shard_map/ppermute | solution.py:13
  13.2 4.7 %copy-start.2 = (bf16[1,1280,640]{2,1,0:T(8,128)(2,1)S(1)}, bf16[1,1280,640]{2,1,0:T(8,128)(2,1)}, u32[]{:S(2)}) copy-start(bf16[1,1280,640]{2,1,0:T(8,128)(2,1)} %param.12) | copy-start | bytes 4915204
  34.0 10.6 %copy-start.5 = (bf16[1,1280,160]{1,2,0:T(8,128)(2,1)S(1)}, bf16[1,1280,160]{1,2,0:T(8,128)(2,1)}, u32[]{:S(2)}) copy-start(bf16[1,1280,160]{1,2,0:T(8,128)(2,1)} %param.14) | copy-start | bytes 1228804
  47.1 2.3 %collective-permute-start.3 = (bf16[2,2,2,80,128]{4,3,2,1,0:T(8,128)(2,1)S(1)}, bf16[2,2,2,80,128]{4,3,2,1,0:T(8,128)(2,1)S(1)}, u32[]{:S(2)}, u32[]{:S(2)}) collective-permute-start(bf16[2,2,2,80,128]{4,3,2,1,0:T(8,128)(2,1)S(1)} %bitcast.162), channel_id=1, source_target_pairs={{0,12},{2,14},{16,28},{18,30}} | collective-permute-start | bytes 491528 | tf_op jit(solution)/shard_map/ppermute | solution.py:34
  47.8 1.6 %collective-permute-start.4 = (bf16[2,2,2,80,128]{4,3,2,1,0:T(8,128)(2,1)S(1)}, bf16[2,2,2,80,128]{4,3,2,1,0:T(8,128)(2,1)S(1)}, u32[]{:S(2)}, u32[]{:S(2)}) collective-permute-start(bf16[2,2,2,80,128]{4,3,2,1,0:T(8,128)(2,1)S(1)} %bitcast.163), channel_id=1, source_target_pairs={{0,8},{4,12},{2,10},{6,14},{16,24},{20,28},{18,26},{22,30}} | collective-permute-start | bytes 491528 | tf_op jit(solution)/shard_map/ppermute | solution.py:34
  48.5 1.0 collective-permute-start.5
  52.7 10.7 %collective-permute-start.6 = (bf16[2,128,1280]{2,1,0:T(8,128)(2,1)S(1)}, bf16[2,128,1280]{2,1,0:T(8,128)(2,1)}, u32[]{:S(2)}, u32[]{:S(2)}) collective-permute-start(bf16[2,128,1280]{2,1,0:T(8,128)(2,1)S(1)} %convolution_convert_fusion), channel_id=1, source_target_pairs={{0,1},{2,3},{4,5},{6,7},{8,9},{10,11},{12,13},{14,15},{16,17},{18,... | collective-permute-start | bytes 1966088 | tf_op jit(solution)/shard_map/ppermute | solution.py:238
  54.0 18.3 %collective-permute-start.7 = (bf16[2,128,1280]{2,1,0:T(8,128)(2,1)S(1)}, bf16[2,128,1280]{2,1,0:T(8,128)(2,1)}, u32[]{:S(2)}, u32[]{:S(2)}) collective-permute-start(bf16[2,128,1280]{2,1,0:T(8,128)(2,1)S(1)} %convolution_convert_fusion), channel_id=1, source_target_pairs={{0,3},{2,1},{4,7},{6,5},{8,11},{10,9},{12,15},{14,13},{16,19},{18,... | collective-permute-start | bytes 1966088 | tf_op jit(solution)/shard_map/ppermute | solution.py:238
  55.4 18.7 %copy-start.3 = (bf16[1,1280,640]{1,2,0:T(8,128)(2,1)S(1)}, bf16[1,1280,640]{1,2,0:T(8,128)(2,1)}, u32[]{:S(2)}) copy-start(bf16[1,1280,640]{1,2,0:T(8,128)(2,1)} %copy.36) | copy-start | bytes 4915204
  55.4 18.7 %copy-start.6 = (bf16[1,1280,160]{1,2,0:T(8,128)(2,1)S(1)}, bf16[1,1280,160]{1,2,0:T(8,128)(2,1)}, u32[]{:S(2)}) copy-start(bf16[1,1280,160]{1,2,0:T(8,128)(2,1)} %param.14) | copy-start | bytes 1228804
  55.4 18.7 %copy-start.7 = (bf16[1,1280,160]{1,2,0:T(8,128)(2,1)S(1)}, bf16[1,1280,160]{1,2,0:T(8,128)(2,1)}, u32[]{:S(2)}) copy-start(bf16[1,1280,160]{1,2,0:T(8,128)(2,1)} %param.13) | copy-start | bytes 1228804
  75.0 9.3 %collective-permute-start.10 = (bf16[2,2,2,80,128]{4,3,2,1,0:T(8,128)(2,1)S(1)}, bf16[2,2,2,80,128]{4,3,2,1,0:T(8,128)(2,1)S(1)}, u32[]{:S(2)}, u32[]{:S(2)}) collective-permute-start(bf16[2,2,2,80,128]{4,3,2,1,0:T(8,128)(2,1)S(1)} %bitcast.167), channel_id=1, source_target_pairs={{1,5},{5,9},{9,13},{3,7},{7,11},{11,15},{17,21},{21,25},{25,29},{1... | collective-permute-start | bytes 491528 | tf_op jit(solution)/shard_map/ppermute | solution.py:34
  79.6 4.7 %collective-permute-start.8 = (bf16[2,2,2,80,128]{4,3,2,1,0:T(8,128)(2,1)S(1)}, bf16[2,2,2,80,128]{4,3,2,1,0:T(8,128)(2,1)S(1)}, u32[]{:S(2)}, u32[]{:S(2)}) collective-permute-start(bf16[2,2,2,80,128]{4,3,2,1,0:T(8,128)(2,1)S(1)} %bitcast.168), channel_id=1, source_target_pairs={{1,13},{3,15},{17,29},{19,31}} | collective-permute-start | bytes 491528 | tf_op jit(solution)/shard_map/ppermute | solution.py:34
  82.0 4.4 %collective-permute-start.9 = (bf16[2,2,2,80,128]{4,3,2,1,0:T(8,128)(2,1)S(1)}, bf16[2,2,2,80,128]{4,3,2,1,0:T(8,128)(2,1)S(1)}, u32[]{:S(2)}, u32[]{:S(2)}) collective-permute-start(bf16[2,2,2,80,128]{4,3,2,1,0:T(8,128)(2,1)S(1)} %bitcast.169), channel_id=1, source_target_pairs={{1,9},{5,13},{3,11},{7,15},{17,25},{21,29},{19,27},{23,31}} | collective-permute-start | bytes 491528 | tf_op jit(solution)/shard_map/ppermute | solution.py:34
  89.8 6.5 %collective-permute-start.11 = (bf16[1,128,640]{2,1,0:T(8,128)(2,1)S(1)}, bf16[1,128,640]{2,1,0:T(8,128)(2,1)S(1)}, u32[]{:S(2)}, u32[]{:S(2)}) collective-permute-start(bf16[1,128,640]{2,1,0:T(8,128)(2,1)S(1)} %add_convert_fusion), channel_id=1, source_target_pairs={{1,0},{3,2},{5,4},{7,6},{9,8},{11,10},{13,12},{15,14},{17,16},{19,... | collective-permute-start | bytes 491528 | tf_op jit(solution)/shard_map/ppermute | solution.py:263
  91.2 5.2 %collective-permute-start.12 = (bf16[1,128,640]{2,1,0:T(8,128)(2,1)S(1)}, bf16[1,128,640]{2,1,0:T(8,128)(2,1)S(1)}, u32[]{:S(2)}, u32[]{:S(2)}) collective-permute-start(bf16[1,128,640]{2,1,0:T(8,128)(2,1)S(1)} %dynamic-slice_convert_fusion.1), channel_id=1, source_target_pairs={{1,2},{3,0},{5,6},{7,4},{9,10},{11,8},{13,14},{15,12},{17,18},{19,... | collective-permute-start | bytes 491528 | tf_op jit(solution)/shard_map/ppermute | solution.py:263
  92.5 6.1 %collective-permute-start.13 = (bf16[1,128,640]{2,1,0:T(8,128)(2,1)S(1)}, bf16[1,128,640]{2,1,0:T(8,128)(2,1)S(1)}, u32[]{:S(2)}, u32[]{:S(2)}) collective-permute-start(bf16[1,128,640]{2,1,0:T(8,128)(2,1)S(1)} %dynamic-slice_convert_fusion), channel_id=1, source_target_pairs={{1,3},{3,1},{5,7},{7,5},{9,11},{11,9},{13,15},{15,13},{17,19},{19,... | collective-permute-start | bytes 491528 | tf_op jit(solution)/shard_map/ppermute | solution.py:267

commit v20 on v17

--- a/solution.py
+++ b/solution.py
@@ -45,7 +45,7 @@
         | (key_pos[None, None, :] == query_pos[None, :, None])
     )
     scores = jnp.einsum(
-        "btkgh,bkhn->bkgtn", query_rows, key_block, preferred_element_type=jnp.float32
+        "bkght,bkhn->bkgtn", query_rows, key_block, preferred_element_type=jnp.float32
     )
     scores = jnp.where(allowed[:, None, None], scores, -jnp.inf)
     new_max = jnp.maximum(run_max, jnp.max(scores, -1))
@@ -69,7 +69,7 @@
     scaled = hidden32 * lax.rsqrt(jnp.mean(hidden32 * hidden32, -1, keepdims=True) + 1e-06)
     layer_input = (scaled * gain32).astype(jnp.bfloat16)
     queries = (
-        jnp.einsum("btd,de->bte", layer_input, query_w, preferred_element_type=jnp.float32)
+        jnp.einsum("btd,de->bet", layer_input, query_w, preferred_element_type=jnp.float32)
         * HD ** (-0.5)
     ).astype(jnp.bfloat16)
     kv_local = key_w.shape[1] // HD
@@ -81,7 +81,7 @@
     kv_t = kv_t.reshape(2, kv_local, HD, batch_count, tok_count).transpose(0, 3, 1, 2, 4)
     key_t = kv_t[0]
     value_t = kv_t[1]
-    query_rows = queries.reshape(batch_count, tok_count, kv_local, group_size, HD)
+    query_rows = queries.reshape(batch_count, kv_local, group_size, HD, tok_count)
     query_pos = tm_at * tok_count + jnp.arange(tok_count, dtype=jnp.int32)
     first_valid = total_tokens - seq_lens // STRIDE
     both, key_pos = gather_causal(kv_t, tm_n, sec_n, tm_at, phase, tok_count)

time: 96.3 us -> 97.5 us (1.012)
  no operation moved by 1% of the time
where the time goes in v20:
time: 97.5 us; the launch traced here: 95.6 us
  starting transfers between devices  27 us (28%)
  other arithmetic  16.2 us (17%)
  matrix products  15.4 us (16%)
  waiting for transfers between devices  14.3 us (15%)
  local copies, waits for them, and re-layouts  12.2 us (13%)
  blocking collectives  9.24 us (9%)
  between operations  1.23 us (1%)
    ppermute x6, starting transfers between devices, gather_causal(): pieces.append(lax.ppermute(value, ('tm', 'section'), pairs))  14 us
    ppermute x2, waiting for transfers between devices, per_device(): lax.ppermute(partial0.astype(jnp.bfloat16), feat_axes, pairs)  13.7 us
    all_gather x1, blocking collectives, per_device(): hidden0 = lax.all_gather(tokens, feat_axes, axis=2, tiled=True)  9.24 us
    conv_general_dilated x1, matrix products, per_device(): lax.conv_general_dilated(chunks, kernel, window_strides=(STRIDE,), paddin...  5.67 us
    unnamed x16, local copies, waits for them, and re-layouts  4.67 us
    ppermute x3, starting transfers between devices, shift_from(): return lax.ppermute(value, axis, pairs)  4.66 us
    another operation x2, local copies, waits for them, and re-layouts, per_device(): jnp.stack([normed[:, :, q * chunk_tok * STRIDE:(q + 1) * chunk_tok * STRI...  3.27 us
    ppermute x1, starting transfers between devices, per_device(): lax.ppermute(cols_high.astype(jnp.bfloat16), feat_axes, pairs)  3.18 us
  transfers between devices with their start and end apart: 14, of which 2 were waited for; matrix products, arithmetic and copies ran while one was open for 12% of the time, Pallas kernels for 0%

profile of v20, /device:TPU:1, one launch (start us, length us, event | category | flops | bytes accessed | tf_op | source)
XLA Modules:
  0.0 95.6 jit_solution(13988772723462272165)
XLA Ops:
  2.8 1.5 %multiply_reduce_fusion.1 = f32[2,64]{1,0:T(2,128)S(1)} fusion(f32[2,4096]{1,0:T(2,128)S(1)} %compare_convert_fusion, bf16[2,64,4096]{2,1,0:T(8,128)(2,1)} %param.8), kind=kLoop, calls=%fused_computation.24 | loop fusion | flops 1572736 | bytes 1081856 | tf_op jit(solution)/shard_map/reduce_sum | solution.py:148
  4.9 2.2 %collective-permute-start = (f32[2,64,34]{1,0,2:T(2,128)S(1)}, f32[2,64,34]{1,0,2:T(2,128)S(1)}, u32[]{:S(2)}, u32[]{:S(2)}) collective-permute-start(f32[2,64,34]{1,0,2:T(2,128)S(1)} %pad_maximum_fusion.1), channel_id=1, source_target_pairs={{0,4},{4,8},{8,12},{12,0},{1,5},{5,9},{9,13},{13,1},{2,6},{6,10},{... | collective-permute-start | bytes 52232 | tf_op jit(solution)/shard_map/ppermute | solution.py:13
  7.1 2.1 %collective-permute-start.2 = (f32[2,64,34]{1,0,2:T(2,128)S(1)}, f32[2,64,34]{1,0,2:T(2,128)S(1)}, u32[]{:S(2)}, u32[]{:S(2)}) collective-permute-start(f32[2,64,34]{1,0,2:T(2,128)S(1)} %pad_maximum_fusion.1), channel_id=1, source_target_pairs={{0,12},{4,0},{8,4},{12,8},{1,13},{5,1},{9,5},{13,9},{2,14},{6,2},{... | collective-permute-start | bytes 52232 | tf_op jit(solution)/shard_map/ppermute | solution.py:13
  10.3 1.6 %convert_element_type.137 = f32[2,64,4096]{2,1,0:T(8,128)} convert(bf16[2,64,4096]{2,1,0:T(8,128)(2,1)S(1)} %copy-done.1) | non-fusion elementwise | flops 524288 | bytes 3145728 | tf_op jit(solution)/shard_map/convert_element_type | solution.py:146
  11.9 4.5 %copy.38 = bf16[4096,320]{1,0:T(8,128)(2,1)} copy(bf16[4096,320]{0,1:T(8,128)(2,1)} %param.10) | data formatting | bytes 5242880 | tf_op args[2]
  17.5 2.3 %fusion.9 = bf16[2,64,4128]{2,1,0:T(8,128)(2,1)S(1)} fusion(f32[2,64,4096]{2,1,0:T(8,128)} %convert_element_type.137, f32[2,64,32]{2,1,0:T(8,128)S(1)} %copy.35, f32[2,64]{1,0:T(2,128)S(1)} %add_rsqrt_fusion.2, f32[2,64]{1,0:T(2,128)S(1)} %broadcast_divide_fusion, f32[2,4128]{1,0:T(2,128)S(1)} %and_convert_fusion), kind=kLoop, calls=%fused_computation.16 | loop fusion | flops 3170304 | bytes 3204352 | tf_op jit(solution)/shard_map/convert_element_type | solution.py:189
  20.1 3.2 %copy.37 = bf16[2,4,64,1056]{2,1,0,3:T(4,128)(2,1)} copy(bf16[2,4,64,1056]{3,2,0,1:T(8,128)(2,1)S(1)} %pad_maximum_fusion) | data formatting | bytes 2162688 | tf_op jit(solution)/shard_map/stack | solution.py:193
  23.3 5.7 %fusion.64 = bf16[8,32,320]{2,0,1:T(8,128)(2,1)S(1)} fusion(bf16[8,64,1056]{1,0,2:T(8,128)(2,1)} %bitcast.156, bf16[64,64,320]{2,1,0:T(8,128)(2,1)} %bitcast.155), kind=kOutput, calls=%fused_computation.57 | convolution fusion | flops 671170560 | bytes 3866624 | tf_op jit(solution)/shard_map/conv_general_dilated | solution.py:200
  29.2 9.2 %all_gather.3 = bf16[2,128,1280]{1,0,2:T(2,128)(2,1)S(1)} all-gather(bf16[2,128,320]{1,0,2:T(2,128)(2,1)S(1)} %copy.41), channel_id=1, replica_groups=mesh['groups'=2,'tm'=4,'mp'=2,'section'=2] {'mp','section'}, dimensions={2}, use_global_device_ids=true | all-gather | bytes 819200 | tf_op jit(solution)/shard_map/all_gather | solution.py:210
  39.6 1.7 %convolution_convert_fusion.2 = bf16[320,2,128]{2,0,1:T(8,128)(2,1)S(1)} fusion(bf16[1280,160]{0,1:T(8,128)(2,1)} %bitcast.178, bf16[1280,160]{0,1:T(8,128)(2,1)} %bitcast.180, bf16[2,128,1280]{2,1,0:T(8,128)(2,1)S(1)} %copy.42, f32[1280]{0:T(1024)S(1)} %convert_reduce_fusion, f32[2,128]{1,0:T(2,128)S(1)} %add_rsqrt_fusion.1), kind=kOutput, calls=%fused_computation.59 | convolution fusion | flops 212746240 | bytes 1644544 | tf_op jit(solution)/shard_map/btd,de->ebt/dot_general | solution.py:77
  42.0 1.3 %collective-permute-start.4 = (bf16[2,2,2,80,128]{4,3,2,1,0:T(8,128)(2,1)S(1)}, bf16[2,2,2,80,128]{4,3,2,1,0:T(8,128)(2,1)}, u32[]{:S(2)}, u32[]{:S(2)}) collective-permute-start(bf16[2,2,2,80,128]{4,3,2,1,0:T(8,128)(2,1)S(1)} %bitcast.158), channel_id=1, source_target_pairs={{0,8},{4,12},{2,10},{6,14},{16,24},{20,28},{18,26},{22,30}} | collective-permute-start | bytes 491528 | tf_op jit(solution)/shard_map/ppermute | solution.py:34
  43.3 1.3 %collective-permute-start.3 = (bf16[2,2,2,80,128]{4,3,2,1,0:T(8,128)(2,1)S(1)}, bf16[2,2,2,80,128]{4,3,2,1,0:T(8,128)(2,1)}, u32[]{:S(2)}, u32[]{:S(2)}) collective-permute-start(bf16[2,2,2,80,128]{4,3,2,1,0:T(8,128)(2,1)S(1)} %bitcast.159), channel_id=1, source_target_pairs={{0,12},{2,14},{16,28},{18,30}} | collective-permute-start | bytes 491528 | tf_op jit(solution)/shard_map/ppermute | solution.py:34
  50.6 1.3 %collective-permute-start.7 = (bf16[2,128,1280]{2,1,0:T(8,128)(2,1)S(1)}, bf16[2,128,1280]{2,1,0:T(8,128)(2,1)}, u32[]{:S(2)}, u32[]{:S(2)}) collective-permute-start(bf16[2,128,1280]{2,1,0:T(8,128)(2,1)S(1)} %convolution_convert_fusion), channel_id=1, source_target_pairs={{0,3},{2,1},{4,7},{6,5},{8,11},{10,9},{12,15},{14,13},{16,19},{18,... | collective-permute-start | bytes 1966088 | tf_op jit(solution)/shard_map/ppermute | solution.py:222
  51.9 1.3 %collective-permute-start.6 = (bf16[2,128,1280]{2,1,0:T(8,128)(2,1)S(1)}, bf16[2,128,1280]{2,1,0:T(8,128)(2,1)}, u32[]{:S(2)}, u32[]{:S(2)}) collective-permute-start(bf16[2,128,1280]{2,1,0:T(8,128)(2,1)S(1)} %convolution_convert_fusion), channel_id=1, source_target_pairs={{0,1},{2,3},{4,5},{6,7},{8,9},{10,11},{12,13},{14,15},{16,17},{18,... | collective-permute-start | bytes 1966088 | tf_op jit(solution)/shard_map/ppermute | solution.py:222
  53.2 13.7 %collective-permute-done.7 = bf16[2,128,1280]{2,1,0:T(8,128)(2,1)} collective-permute-done((bf16[2,128,1280]{2,1,0:T(8,128)(2,1)S(1)}, bf16[2,128,1280]{2,1,0:T(8,128)(2,1)}, u32[]{:S(2)}, u32[]{:S(2)}) %collective-permute-start.7) | collective-permute-done | bytes 655392 | tf_op jit(solution)/shard_map/ppermute | solution.py:222
  66.9 1.7 %fusion.27 = (f32[2,128]{1,0:T(2,128)S(1)}, bf16[2,128,1280]{2,1,0:T(8,128)(2,1)S(1)}) fusion(bf16[2,128,1280]{2,1,0:T(8,128)(2,1)} %collective-permute-done.7, bf16[2,128,1280]{2,1,0:T(8,128)(2,1)} %collective-permute-done.6, bf16[2,128,1280]{2,1,0:T(8,128)(2,1)S(1)} %copy.42), kind=kLoop, calls=%fused_computation.39 | loop fusion | flops 2948864 | bytes 2622464 | tf_op jit(solution)/shard_map/reduce_sum | solution.py:69
  69.2 3.6 %collective-permute-start.10 = (bf16[2,2,2,80,128]{4,3,2,1,0:T(8,128)(2,1)S(1)}, bf16[2,2,2,80,128]{4,3,2,1,0:T(8,128)(2,1)S(1)}, u32[]{:S(2)}, u32[]{:S(2)}) collective-permute-start(bf16[2,2,2,80,128]{4,3,2,1,0:T(8,128)(2,1)S(1)} %bitcast.162), channel_id=1, source_target_pairs={{1,5},{5,9},{9,13},{3,7},{7,11},{11,15},{17,21},{21,25},{25,29},{1... | collective-permute-start | bytes 491528 | tf_op jit(solution)/shard_map/ppermute | solution.py:34
  72.8 5.1 %collective-permute-start.9 = (bf16[2,2,2,80,128]{4,3,2,1,0:T(8,128)(2,1)S(1)}, bf16[2,2,2,80,128]{4,3,2,1,0:T(8,128)(2,1)S(1)}, u32[]{:S(2)}, u32[]{:S(2)}) collective-permute-start(bf16[2,2,2,80,128]{4,3,2,1,0:T(8,128)(2,1)S(1)} %bitcast.163), channel_id=1, source_target_pairs={{1,9},{5,13},{3,11},{7,15},{17,25},{21,29},{19,27},{23,31}} | collective-permute-start | bytes 491528 | tf_op jit(solution)/shard_map/ppermute | solution.py:34
  77.9 2.0 %collective-permute-start.8 = (bf16[2,2,2,80,128]{4,3,2,1,0:T(8,128)(2,1)S(1)}, bf16[2,2,2,80,128]{4,3,2,1,0:T(8,128)(2,1)}, u32[]{:S(2)}, u32[]{:S(2)}) collective-permute-start(bf16[2,2,2,80,128]{4,3,2,1,0:T(8,128)(2,1)S(1)} %bitcast.164), channel_id=1, source_target_pairs={{1,13},{3,15},{17,29},{19,31}} | collective-permute-start | bytes 491528 | tf_op jit(solution)/shard_map/ppermute | solution.py:34
  79.9 1.5 %fusion.61 = bf16[2,640,128]{1,2,0:T(8,128)(2,1)} fusion(bf16[1,1280,640]{2,1,0:T(8,128)(2,1)S(1)} %copy-done.4, bf16[2,128,1280]{2,1,0:T(8,128)(2,1)S(1)} %get-tuple-element.4, f32[2,128]{1,0:T(2,128)S(1)} %add_rsqrt_fusion, f32[1280]{0:T(1024)S(1)} %convert_reduce_fusion), kind=kOutput, calls=%fused_computation.55 | convolution fusion | flops 421068800 | bytes 2627584 | tf_op jit(solution)/shard_map/btd,de->bet/dot_general | solution.py:72
  84.5 1.2 %fusion.2 = f32[2,2,4,128]{3,2,1,0:T(4,128)S(1)} fusion(f32[2,2,4,128,512]{4,3,2,1,0:T(8,128)S(1)} %get-tuple-element.27, f32[2,2,4,128]{3,2,1,0:T(4,128)S(1)} %get-tuple-element.16, pred[2,128,512]{2,1,0:T(8,128)(4,1)S(1)} %or_and_fusion), kind=kLoop, calls=%fused_computation.7 | loop fusion | flops 3143680 | bytes 4341760 | tf_op jit(solution)/shard_map/reduce_sum | solution.py:54
  87.6 3.2 %collective-permute-start.13 = (bf16[1,128,640]{2,1,0:T(8,128)(2,1)S(1)}, bf16[1,128,640]{2,1,0:T(8,128)(2,1)S(1)}, u32[]{:S(2)}, u32[]{:S(2)}) collective-permute-start(bf16[1,128,640]{2,1,0:T(8,128)(2,1)S(1)} %dynamic-slice_convert_fusion), channel_id=1, source_target_pairs={{1,3},{3,1},{5,7},{7,5},{9,11},{11,9},{13,15},{15,13},{17,19},{19,... | collective-permute-start | bytes 491528 | tf_op jit(solution)/shard_map/ppermute | solution.py:251
  90.8 1.3 %collective-permute-start.12 = (bf16[1,128,640]{2,1,0:T(8,128)(2,1)S(1)}, bf16[1,128,640]{2,1,0:T(8,128)(2,1)S(1)}, u32[]{:S(2)}, u32[]{:S(2)}) collective-permute-start(bf16[1,128,640]{2,1,0:T(8,128)(2,1)S(1)} %dynamic-slice_convert_fusion.1), channel_id=1, source_target_pairs={{1,2},{3,0},{5,6},{7,4},{9,10},{11,8},{13,14},{15,12},{17,18},{19,... | collective-permute-start | bytes 491528 | tf_op jit(solution)/shard_map/ppermute | solution.py:247
  92.2 1.3 %collective-permute-start.11 = (bf16[1,128,640]{2,1,0:T(8,128)(2,1)S(1)}, bf16[1,128,640]{2,1,0:T(8,128)(2,1)S(1)}, u32[]{:S(2)}, u32[]{:S(2)}) collective-permute-start(bf16[1,128,640]{2,1,0:T(8,128)(2,1)S(1)} %add_convert_fusion), channel_id=1, source_target_pairs={{1,0},{3,2},{5,4},{7,6},{9,8},{11,10},{13,12},{15,14},{17,16},{19,... | collective-permute-start | bytes 491528 | tf_op jit(solution)/shard_map/ppermute | solution.py:247
  (103 shorter events, 20.7 us)
Async XLA Ops:
  0.6 49.2 %copy-start = (bf16[1,640,1280]{2,1,0:T(8,128)(2,1)S(1)}, bf16[1,640,1280]{2,1,0:T(8,128)(2,1)}, u32[]{:S(2)}) copy-start(bf16[1,640,1280]{2,1,0:T(8,128)(2,1)} %param.15) | copy-start | bytes 4915204
  0.6 3.7 %copy-start.1 = (bf16[2,64,4096]{2,1,0:T(8,128)(2,1)S(1)}, bf16[2,64,4096]{2,1,0:T(8,128)(2,1)}, u32[]{:S(2)}) copy-start(bf16[2,64,4096]{2,1,0:T(8,128)(2,1)} %param.8) | copy-start | bytes 3145732
  0.7 9.4 %copy-start.2 = (bf16[1,1280]{1,0:T(2,128)(2,1)S(1)}, bf16[1,1280]{1,0:T(2,128)(2,1)}, u32[]{:S(2)}) copy-start(bf16[1,1280]{1,0:T(2,128)(2,1)} %param.11) | copy-start | bytes 7684
  4.9 11.5 %collective-permute-start = (f32[2,64,34]{1,0,2:T(2,128)S(1)}, f32[2,64,34]{1,0,2:T(2,128)S(1)}, u32[]{:S(2)}, u32[]{:S(2)}) collective-permute-start(f32[2,64,34]{1,0,2:T(2,128)S(1)} %pad_maximum_fusion.1), channel_id=1, source_target_pairs={{0,4},{4,8},{8,12},{12,0},{1,5},{5,9},{9,13},{13,1},{2,6},{6,10},{... | collective-permute-start | bytes 52232 | tf_op jit(solution)/shard_map/ppermute | solution.py:13
  7.1 9.3 %collective-permute-start.2 = (f32[2,64,34]{1,0,2:T(2,128)S(1)}, f32[2,64,34]{1,0,2:T(2,128)S(1)}, u32[]{:S(2)}, u32[]{:S(2)}) collective-permute-start(f32[2,64,34]{1,0,2:T(2,128)S(1)} %pad_maximum_fusion.1), channel_id=1, source_target_pairs={{0,12},{4,0},{8,4},{12,8},{1,13},{5,1},{9,5},{13,9},{2,14},{6,2},{... | collective-permute-start | bytes 52232 | tf_op jit(solution)/shard_map/ppermute | solution.py:13
  9.2 7.4 %collective-permute-start.1 = (f32[2,64,34]{1,0,2:T(2,128)S(1)}, f32[2,64,34]{1,0,2:T(2,128)S(1)}, u32[]{:S(2)}, u32[]{:S(2)}) collective-permute-start(f32[2,64,34]{1,0,2:T(2,128)S(1)} %pad_maximum_fusion.1), channel_id=1, source_target_pairs={{0,8},{4,12},{8,0},{12,4},{1,9},{5,13},{9,1},{13,5},{2,10},{6,14},... | collective-permute-start | bytes 52232 | tf_op jit(solution)/shard_map/ppermute | solution.py:13
  39.5 5.1 %copy-start.3 = (bf16[1,1280,640]{2,1,0:T(8,128)(2,1)S(1)}, bf16[1,1280,640]{2,1,0:T(8,128)(2,1)}, u32[]{:S(2)}) copy-start(bf16[1,1280,640]{2,1,0:T(8,128)(2,1)} %param.12) | copy-start | bytes 4915204
  41.3 4.3 %collective-permute-start.5 = (bf16[2,2,2,80,128]{4,3,2,1,0:T(8,128)(2,1)S(1)}, bf16[2,2,2,80,128]{4,3,2,1,0:T(8,128)(2,1)S(1)}, u32[]{:S(2)}, u32[]{:S(2)}) collective-permute-start(bf16[2,2,2,80,128]{4,3,2,1,0:T(8,128)(2,1)S(1)} %bitcast.157), channel_id=1, source_target_pairs={{0,4},{4,8},{8,12},{2,6},{6,10},{10,14},{16,20},{20,24},{24,28},{1... | collective-permute-start | bytes 491528 | tf_op jit(solution)/shard_map/ppermute | solution.py:34
  42.0 3.6 %collective-permute-start.4 = (bf16[2,2,2,80,128]{4,3,2,1,0:T(8,128)(2,1)S(1)}, bf16[2,2,2,80,128]{4,3,2,1,0:T(8,128)(2,1)}, u32[]{:S(2)}, u32[]{:S(2)}) collective-permute-start(bf16[2,2,2,80,128]{4,3,2,1,0:T(8,128)(2,1)S(1)} %bitcast.158), channel_id=1, source_target_pairs={{0,8},{4,12},{2,10},{6,14},{16,24},{20,28},{18,26},{22,30}} | collective-permute-start | bytes 491528 | tf_op jit(solution)/shard_map/ppermute | solution.py:34
  43.3 2.3 %collective-permute-start.3 = (bf16[2,2,2,80,128]{4,3,2,1,0:T(8,128)(2,1)S(1)}, bf16[2,2,2,80,128]{4,3,2,1,0:T(8,128)(2,1)}, u32[]{:S(2)}, u32[]{:S(2)}) collective-permute-start(bf16[2,2,2,80,128]{4,3,2,1,0:T(8,128)(2,1)S(1)} %bitcast.159), channel_id=1, source_target_pairs={{0,12},{2,14},{16,28},{18,30}} | collective-permute-start | bytes 491528 | tf_op jit(solution)/shard_map/ppermute | solution.py:34
  50.6 16.3 %collective-permute-start.7 = (bf16[2,128,1280]{2,1,0:T(8,128)(2,1)S(1)}, bf16[2,128,1280]{2,1,0:T(8,128)(2,1)}, u32[]{:S(2)}, u32[]{:S(2)}) collective-permute-start(bf16[2,128,1280]{2,1,0:T(8,128)(2,1)S(1)} %convolution_convert_fusion), channel_id=1, source_target_pairs={{0,3},{2,1},{4,7},{6,5},{8,11},{10,9},{12,15},{14,13},{16,19},{18,... | collective-permute-start | bytes 1966088 | tf_op jit(solution)/shard_map/ppermute | solution.py:222
  51.9 15.0 %collective-permute-start.6 = (bf16[2,128,1280]{2,1,0:T(8,128)(2,1)S(1)}, bf16[2,128,1280]{2,1,0:T(8,128)(2,1)}, u32[]{:S(2)}, u32[]{:S(2)}) collective-permute-start(bf16[2,128,1280]{2,1,0:T(8,128)(2,1)S(1)} %convolution_convert_fusion), channel_id=1, source_target_pairs={{0,1},{2,3},{4,5},{6,7},{8,9},{10,11},{12,13},{14,15},{16,17},{18,... | collective-permute-start | bytes 1966088 | tf_op jit(solution)/shard_map/ppermute | solution.py:222
  53.2 15.4 %copy-start.5 = (bf16[1,1280,160]{1,2,0:T(8,128)(2,1)S(1)}, bf16[1,1280,160]{1,2,0:T(8,128)(2,1)}, u32[]{:S(2)}) copy-start(bf16[1,1280,160]{1,2,0:T(8,128)(2,1)} %param.14) | copy-start | bytes 1228804
  53.2 15.4 %copy-start.6 = (bf16[1,1280,160]{1,2,0:T(8,128)(2,1)S(1)}, bf16[1,1280,160]{1,2,0:T(8,128)(2,1)}, u32[]{:S(2)}) copy-start(bf16[1,1280,160]{1,2,0:T(8,128)(2,1)} %param.13) | copy-start | bytes 1228804
  68.6 11.3 %copy-start.4 = (bf16[1,1280,640]{2,1,0:T(8,128)(2,1)S(1)}, bf16[1,1280,640]{2,1,0:T(8,128)(2,1)}, u32[]{:S(2)}) copy-start(bf16[1,1280,640]{2,1,0:T(8,128)(2,1)} %param.12) | copy-start | bytes 4915204
  69.2 13.4 %collective-permute-start.10 = (bf16[2,2,2,80,128]{4,3,2,1,0:T(8,128)(2,1)S(1)}, bf16[2,2,2,80,128]{4,3,2,1,0:T(8,128)(2,1)S(1)}, u32[]{:S(2)}, u32[]{:S(2)}) collective-permute-start(bf16[2,2,2,80,128]{4,3,2,1,0:T(8,128)(2,1)S(1)} %bitcast.162), channel_id=1, source_target_pairs={{1,5},{5,9},{9,13},{3,7},{7,11},{11,15},{17,21},{21,25},{25,29},{1... | collective-permute-start | bytes 491528 | tf_op jit(solution)/shard_map/ppermute | solution.py:34
  72.8 9.8 %collective-permute-start.9 = (bf16[2,2,2,80,128]{4,3,2,1,0:T(8,128)(2,1)S(1)}, bf16[2,2,2,80,128]{4,3,2,1,0:T(8,128)(2,1)S(1)}, u32[]{:S(2)}, u32[]{:S(2)}) collective-permute-start(bf16[2,2,2,80,128]{4,3,2,1,0:T(8,128)(2,1)S(1)} %bitcast.163), channel_id=1, source_target_pairs={{1,9},{5,13},{3,11},{7,15},{17,25},{21,29},{19,27},{23,31}} | collective-permute-start | bytes 491528 | tf_op jit(solution)/shard_map/ppermute | solution.py:34
  77.9 4.7 %collective-permute-start.8 = (bf16[2,2,2,80,128]{4,3,2,1,0:T(8,128)(2,1)S(1)}, bf16[2,2,2,80,128]{4,3,2,1,0:T(8,128)(2,1)}, u32[]{:S(2)}, u32[]{:S(2)}) collective-permute-start(bf16[2,2,2,80,128]{4,3,2,1,0:T(8,128)(2,1)S(1)} %bitcast.164), channel_id=1, source_target_pairs={{1,13},{3,15},{17,29},{19,31}} | collective-permute-start | bytes 491528 | tf_op jit(solution)/shard_map/ppermute | solution.py:34
  87.6 6.6 %collective-permute-start.13 = (bf16[1,128,640]{2,1,0:T(8,128)(2,1)S(1)}, bf16[1,128,640]{2,1,0:T(8,128)(2,1)S(1)}, u32[]{:S(2)}, u32[]{:S(2)}) collective-permute-start(bf16[1,128,640]{2,1,0:T(8,128)(2,1)S(1)} %dynamic-slice_convert_fusion), channel_id=1, source_target_pairs={{1,3},{3,1},{5,7},{7,5},{9,11},{11,9},{13,15},{15,13},{17,19},{19,... | collective-permute-start | bytes 491528 | tf_op jit(solution)/shard_map/ppermute | solution.py:251
  90.8 4.0 %collective-permute-start.12 = (bf16[1,128,640]{2,1,0:T(8,128)(2,1)S(1)}, bf16[1,128,640]{2,1,0:T(8,128)(2,1)S(1)}, u32[]{:S(2)}, u32[]{:S(2)}) collective-permute-start(bf16[1,128,640]{2,1,0:T(8,128)(2,1)S(1)} %dynamic-slice_convert_fusion.1), channel_id=1, source_target_pairs={{1,2},{3,0},{5,6},{7,4},{9,10},{11,8},{13,14},{15,12},{17,18},{19,... | collective-permute-start | bytes 491528 | tf_op jit(solution)/shard_map/ppermute | solution.py:247
  92.2 2.6 %collective-permute-start.11 = (bf16[1,128,640]{2,1,0:T(8,128)(2,1)S(1)}, bf16[1,128,640]{2,1,0:T(8,128)(2,1)S(1)}, u32[]{:S(2)}, u32[]{:S(2)}) collective-permute-start(bf16[1,128,640]{2,1,0:T(8,128)(2,1)S(1)} %add_convert_fusion), channel_id=1, source_target_pairs={{1,0},{3,2},{5,4},{7,6},{9,8},{11,10},{13,12},{15,14},{17,16},{19,... | collective-permute-start | bytes 491528 | tf_op jit(solution)/shard_map/ppermute | solution.py:247

commit v21 on v17

--- a/solution.py
+++ b/solution.py
@@ -179,7 +179,7 @@
     variance = spread_total / history
     inv_std = lax.rsqrt(variance + 1e-05)[..., None]
 
-    padded = jnp.concatenate([prior_raw, series.astype(jnp.float32)], -1)
+    padded = jnp.concatenate([prior_raw.astype(jnp.bfloat16), series], -1).astype(jnp.float32)
     padded_pos = tm_at * steps_dev - STRIDE + jnp.arange(steps_dev + STRIDE, dtype=jnp.int32)
     padded_valid = (
         (padded_pos[None, :] >= first_step[:, None]) & (padded_pos[None, :] >= 0)

time: 96.3 us -> 92.9 us (0.965)
  other arithmetic: 15.5 us -> 12.6 us
  local copies, waits for them, and re-layouts: 12.2 us -> 11.2 us
    convert_element_type x1 -> x0, other arithmetic: 1.58 us -> none  [per_device(): values = series.astype(jnp.float32)]
    convert_element_type x1, other arithmetic: 2.28 us -> 0.83 us  [per_device(): normed = ((padded * padded_valid - channel_mean[..., None]) * padded_vali...]
  transfers between devices with their start and end apart: 14 -> 14, of which waited for: 2 -> 3; matrix products, arithmetic and copies ran while one was open for 12% -> 9% of each run, Pallas kernels for 0% -> 0%
where the time goes in v21:
time: 92.9 us; the launch traced here: 91.1 us
  starting transfers between devices  27.6 us (30%)
  waiting for transfers between devices  14.9 us (16%)
  matrix products  14.3 us (15%)
  other arithmetic  12.6 us (14%)
  local copies, waits for them, and re-layouts  11.2 us (12%)
  blocking collectives  9.24 us (10%)
  between operations  1.22 us (1%)
    ppermute x6, starting transfers between devices, gather_causal(): pieces.append(lax.ppermute(value, ('tm', 'section'), pairs))  14.6 us
    ppermute x2, waiting for transfers between devices, per_device(): lax.ppermute(partial0.astype(jnp.bfloat16), feat_axes, pairs)  13.7 us
    all_gather x1, blocking collectives, per_device(): hidden0 = lax.all_gather(tokens, feat_axes, axis=2, tiled=True)  9.24 us
    conv_general_dilated x1, matrix products, per_device(): lax.conv_general_dilated(chunks, kernel, window_strides=(STRIDE,), paddin...  5.67 us
    unnamed x16, local copies, waits for them, and re-layouts  4.68 us
    ppermute x3, starting transfers between devices, shift_from(): return lax.ppermute(value, axis, pairs)  4.66 us
    another operation x2, local copies, waits for them, and re-layouts, per_device(): jnp.stack([normed[:, :, q * chunk_tok * STRIDE:(q + 1) * chunk_tok * STRI...  3.27 us
    ppermute x1, starting transfers between devices, per_device(): lax.ppermute(cols_high.astype(jnp.bfloat16), feat_axes, pairs)  3.18 us
  transfers between devices with their start and end apart: 14, of which 3 were waited for; matrix products, arithmetic and copies ran while one was open for 9% of the time, Pallas kernels for 0%

profile of v21, /device:TPU:1, one launch (start us, length us, event | category | flops | bytes accessed | tf_op | source)
XLA Modules:
  0.0 91.1 jit_solution(2307179407562354158)
XLA Ops:
  2.8 1.5 %fusion.8 = f32[2,64]{1,0:T(2,128)S(1)} fusion(bf16[2,64,4096]{2,1,0:T(8,128)(2,1)} %param.8, f32[2,4096]{1,0:T(2,128)S(1)} %compare_convert_fusion), kind=kLoop, calls=%fused_computation.17 | loop fusion | flops 1572736 | bytes 1081856 | tf_op jit(solution)/shard_map/reduce_sum | solution.py:148
  4.9 2.2 %collective-permute-start = (f32[2,64,34]{1,0,2:T(2,128)S(1)}, f32[2,64,34]{1,0,2:T(2,128)S(1)}, u32[]{:S(2)}, u32[]{:S(2)}) collective-permute-start(f32[2,64,34]{1,0,2:T(2,128)S(1)} %pad_maximum_fusion.1), channel_id=1, source_target_pairs={{0,4},{4,8},{8,12},{12,0},{1,5},{5,9},{9,13},{13,1},{2,6},{6,10},{... | collective-permute-start | bytes 52232 | tf_op jit(solution)/shard_map/ppermute | solution.py:13
  7.1 2.1 %collective-permute-start.2 = (f32[2,64,34]{1,0,2:T(2,128)S(1)}, f32[2,64,34]{1,0,2:T(2,128)S(1)}, u32[]{:S(2)}, u32[]{:S(2)}) collective-permute-start(f32[2,64,34]{1,0,2:T(2,128)S(1)} %pad_maximum_fusion.1), channel_id=1, source_target_pairs={{0,12},{4,0},{8,4},{12,8},{1,13},{5,1},{9,5},{13,9},{2,14},{6,2},{... | collective-permute-start | bytes 52232 | tf_op jit(solution)/shard_map/ppermute | solution.py:13
  10.4 4.5 %copy.42 = bf16[4096,320]{1,0:T(8,128)(2,1)} copy(bf16[4096,320]{0,1:T(8,128)(2,1)} %param.10) | data formatting | bytes 5242880 | tf_op args[2]
  17.2 3.2 %copy.41 = bf16[2,4,64,1056]{2,1,0,3:T(4,128)(2,1)} copy(bf16[2,4,64,1056]{3,2,0,1:T(8,128)(2,1)S(1)} %pad_maximum_fusion) | data formatting | bytes 2162688 | tf_op jit(solution)/shard_map/stack | solution.py:193
  20.4 5.7 %fusion.60 = bf16[8,32,320]{2,0,1:T(8,128)(2,1)S(1)} fusion(bf16[8,64,1056]{1,0,2:T(8,128)(2,1)} %bitcast.186, bf16[64,64,320]{2,1,0:T(8,128)(2,1)} %bitcast.185), kind=kOutput, calls=%fused_computation.57 | convolution fusion | flops 671170560 | bytes 3866624 | tf_op jit(solution)/shard_map/conv_general_dilated | solution.py:200
  26.3 9.2 %all_gather.3 = bf16[2,128,1280]{1,0,2:T(2,128)(2,1)S(1)} all-gather(bf16[2,128,320]{1,0,2:T(2,128)(2,1)S(1)} %copy.45), channel_id=1, replica_groups=mesh['groups'=2,'tm'=4,'mp'=2,'section'=2] {'mp','section'}, dimensions={2}, use_global_device_ids=true | all-gather | bytes 819200 | tf_op jit(solution)/shard_map/all_gather | solution.py:210
  36.7 1.7 %convolution_convert_fusion.2 = bf16[320,2,128]{2,0,1:T(8,128)(2,1)S(1)} fusion(bf16[1280,160]{0,1:T(8,128)(2,1)} %bitcast.208, bf16[1280,160]{0,1:T(8,128)(2,1)} %bitcast.210, bf16[2,128,1280]{2,1,0:T(8,128)(2,1)S(1)} %copy.46, f32[1280]{0:T(1024)S(1)} %convert_reduce_fusion, f32[2,128]{1,0:T(2,128)S(1)} %add_rsqrt_fusion.1), kind=kOutput, calls=%fused_computation.59 | convolution fusion | flops 212746240 | bytes 1644544 | tf_op jit(solution)/shard_map/btd,de->ebt/dot_general | solution.py:77
  39.1 1.3 %collective-permute-start.4 = (bf16[2,2,2,80,128]{4,3,2,1,0:T(8,128)(2,1)S(1)}, bf16[2,2,2,80,128]{4,3,2,1,0:T(8,128)(2,1)}, u32[]{:S(2)}, u32[]{:S(2)}) collective-permute-start(bf16[2,2,2,80,128]{4,3,2,1,0:T(8,128)(2,1)S(1)} %bitcast.188), channel_id=1, source_target_pairs={{0,8},{4,12},{2,10},{6,14},{16,24},{20,28},{18,26},{22,30}} | collective-permute-start | bytes 491528 | tf_op jit(solution)/shard_map/ppermute | solution.py:34
  40.4 1.3 %collective-permute-start.3 = (bf16[2,2,2,80,128]{4,3,2,1,0:T(8,128)(2,1)S(1)}, bf16[2,2,2,80,128]{4,3,2,1,0:T(8,128)(2,1)}, u32[]{:S(2)}, u32[]{:S(2)}) collective-permute-start(bf16[2,2,2,80,128]{4,3,2,1,0:T(8,128)(2,1)S(1)} %bitcast.189), channel_id=1, source_target_pairs={{0,12},{2,14},{16,28},{18,30}} | collective-permute-start | bytes 491528 | tf_op jit(solution)/shard_map/ppermute | solution.py:34
  42.7 1.1 %maximum_bitcast_fusion.1 = bf16[1,2,2,2,80,512]{5,4,3,2,1,0:T(8,128)(2,1)S(1)} fusion(bf16[2,2,2,80,128]{4,3,2,1,0:T(8,128)(2,1)S(1)} %bitcast.190, bf16[2,2,2,80,128]{4,3,2,1,0:T(8,128)(2,1)S(1)} %collective-permute-done.5, bf16[2,2,2,80,128]{4,3,2,1,0:T(8,128)(2,1)} %collective-permute-done.4, bf16[2,2,2,80,128]{4,3,2,1,0:T(8,128)(2,1)} %collective-permute-done.3), kind=kLoop, calls=%fused_computation.65 | loop fusion | flops 2621440 | bytes 1310720 | tf_op jit(solution)/shard_map/transpose;reshape | solution.py:91
  45.4 1.0 %fusion.72 = bf16[2,128,2,4,80]{1,4,3,2,0:T(8,128)(2,1)S(1)} fusion(f32[2,2,512,128,4]{3,2,4,1,0:T(8,128)S(1)} %get-tuple-element.25, f32[2,2,4,128]{3,2,1,0:T(4,128)S(1)} %get-tuple-element.18, pred[2,128,512]{1,2,0:T(8,128)(4,1)S(1)} %or_and_fusion, bf16[1,2,2,2,80,512]{5,4,3,2,1,0:T(8,128)(2,1)S(1)} %maximum_bitcast_fusion.1, ...), kind=kOutput, calls=%fused_computation.63 | convolution fusion | flops 171409408 | bytes 5005312 | tf_op jit(solution)/shard_map/bkgtn,bkhn->bkgth/dot_general | solution.py:55
  47.1 1.3 %collective-permute-start.7 = (bf16[2,128,1280]{2,1,0:T(8,128)(2,1)S(1)}, bf16[2,128,1280]{2,1,0:T(8,128)(2,1)}, u32[]{:S(2)}, u32[]{:S(2)}) collective-permute-start(bf16[2,128,1280]{2,1,0:T(8,128)(2,1)S(1)} %convolution_convert_fusion), channel_id=1, source_target_pairs={{0,3},{2,1},{4,7},{6,5},{8,11},{10,9},{12,15},{14,13},{16,19},{18,... | collective-permute-start | bytes 1966088 | tf_op jit(solution)/shard_map/ppermute | solution.py:222
  48.4 1.3 %collective-permute-start.6 = (bf16[2,128,1280]{2,1,0:T(8,128)(2,1)S(1)}, bf16[2,128,1280]{2,1,0:T(8,128)(2,1)}, u32[]{:S(2)}, u32[]{:S(2)}) collective-permute-start(bf16[2,128,1280]{2,1,0:T(8,128)(2,1)S(1)} %convolution_convert_fusion), channel_id=1, source_target_pairs={{0,1},{2,3},{4,5},{6,7},{8,9},{10,11},{12,13},{14,15},{16,17},{18,... | collective-permute-start | bytes 1966088 | tf_op jit(solution)/shard_map/ppermute | solution.py:222
  49.7 13.7 %collective-permute-done.7 = bf16[2,128,1280]{2,1,0:T(8,128)(2,1)} collective-permute-done((bf16[2,128,1280]{2,1,0:T(8,128)(2,1)S(1)}, bf16[2,128,1280]{2,1,0:T(8,128)(2,1)}, u32[]{:S(2)}, u32[]{:S(2)}) %collective-permute-start.7) | collective-permute-done | bytes 655392 | tf_op jit(solution)/shard_map/ppermute | solution.py:222
  63.4 1.7 %fusion.29 = (f32[2,128]{1,0:T(2,128)S(1)}, bf16[2,128,1280]{2,1,0:T(8,128)(2,1)S(1)}) fusion(bf16[2,128,1280]{2,1,0:T(8,128)(2,1)} %collective-permute-done.7, bf16[2,128,1280]{2,1,0:T(8,128)(2,1)} %collective-permute-done.6, bf16[2,128,1280]{2,1,0:T(8,128)(2,1)S(1)} %copy.46), kind=kLoop, calls=%fused_computation.41 | loop fusion | flops 2948864 | bytes 2622464 | tf_op jit(solution)/shard_map/reduce_sum | solution.py:69
  65.7 4.3 %collective-permute-start.10 = (bf16[2,2,2,80,128]{4,3,2,1,0:T(8,128)(2,1)S(1)}, bf16[2,2,2,80,128]{4,3,2,1,0:T(8,128)(2,1)}, u32[]{:S(2)}, u32[]{:S(2)}) collective-permute-start(bf16[2,2,2,80,128]{4,3,2,1,0:T(8,128)(2,1)S(1)} %bitcast.192), channel_id=1, source_target_pairs={{1,5},{5,9},{9,13},{3,7},{7,11},{11,15},{17,21},{21,25},{25,29},{1... | collective-permute-start | bytes 491528 | tf_op jit(solution)/shard_map/ppermute | solution.py:34
  69.9 5.1 %collective-permute-start.9 = (bf16[2,2,2,80,128]{4,3,2,1,0:T(8,128)(2,1)S(1)}, bf16[2,2,2,80,128]{4,3,2,1,0:T(8,128)(2,1)}, u32[]{:S(2)}, u32[]{:S(2)}) collective-permute-start(bf16[2,2,2,80,128]{4,3,2,1,0:T(8,128)(2,1)S(1)} %bitcast.193), channel_id=1, source_target_pairs={{1,9},{5,13},{3,11},{7,15},{17,25},{21,29},{19,27},{23,31}} | collective-permute-start | bytes 491528 | tf_op jit(solution)/shard_map/ppermute | solution.py:34
  75.0 1.9 %collective-permute-start.8 = (bf16[2,2,2,80,128]{4,3,2,1,0:T(8,128)(2,1)S(1)}, bf16[2,2,2,80,128]{4,3,2,1,0:T(8,128)(2,1)}, u32[]{:S(2)}, u32[]{:S(2)}) collective-permute-start(bf16[2,2,2,80,128]{4,3,2,1,0:T(8,128)(2,1)S(1)} %bitcast.194), channel_id=1, source_target_pairs={{1,13},{3,15},{17,29},{19,31}} | collective-permute-start | bytes 491528 | tf_op jit(solution)/shard_map/ppermute | solution.py:34
  78.6 1.1 %maximum_bitcast_fusion.2 = bf16[1,2,2,2,80,512]{5,4,3,2,1,0:T(8,128)(2,1)S(1)} fusion(bf16[2,2,2,80,128]{4,3,2,1,0:T(8,128)(2,1)S(1)} %bitcast.195, bf16[2,2,2,80,128]{4,3,2,1,0:T(8,128)(2,1)} %collective-permute-done.10, bf16[2,2,2,80,128]{4,3,2,1,0:T(8,128)(2,1)} %collective-permute-done.9, bf16[2,2,2,80,128]{4,3,2,1,0:T(8,128)(2,1)} %collective-permute-done.8), kind=kLoop, calls=%fused_computation.66 | loop fusion | flops 2621440 | bytes 1310720 | tf_op jit(solution)/shard_map/transpose;reshape | solution.py:91
  81.3 1.0 %fusion.66 = bf16[2,128,2,4,80]{1,4,3,2,0:T(8,128)(2,1)S(1)} fusion(f32[2,2,512,128,4]{3,2,4,1,0:T(8,128)S(1)} %get-tuple-element.27, f32[2,2,4,128]{3,2,1,0:T(4,128)S(1)} %get-tuple-element.16, pred[2,128,512]{1,2,0:T(8,128)(4,1)S(1)} %or_and_fusion, bf16[1,2,2,2,80,512]{5,4,3,2,1,0:T(8,128)(2,1)S(1)} %maximum_bitcast_fusion.2, ...), kind=kOutput, calls=%fused_computation.61 | convolution fusion | flops 171409408 | bytes 5005312 | tf_op jit(solution)/shard_map/bkgtn,bkhn->bkgth/dot_general | solution.py:55
  83.1 3.2 %collective-permute-start.13 = (bf16[1,128,640]{2,1,0:T(8,128)(2,1)S(1)}, bf16[1,128,640]{2,1,0:T(8,128)(2,1)S(1)}, u32[]{:S(2)}, u32[]{:S(2)}) collective-permute-start(bf16[1,128,640]{2,1,0:T(8,128)(2,1)S(1)} %dynamic-slice_convert_fusion), channel_id=1, source_target_pairs={{1,3},{3,1},{5,7},{7,5},{9,11},{11,9},{13,15},{15,13},{17,19},{19,... | collective-permute-start | bytes 491528 | tf_op jit(solution)/shard_map/ppermute | solution.py:251
  86.3 1.3 %collective-permute-start.12 = (bf16[1,128,640]{2,1,0:T(8,128)(2,1)S(1)}, bf16[1,128,640]{2,1,0:T(8,128)(2,1)S(1)}, u32[]{:S(2)}, u32[]{:S(2)}) collective-permute-start(bf16[1,128,640]{2,1,0:T(8,128)(2,1)S(1)} %dynamic-slice_convert_fusion.1), channel_id=1, source_target_pairs={{1,2},{3,0},{5,6},{7,4},{9,10},{11,8},{13,14},{15,12},{17,18},{19,... | collective-permute-start | bytes 491528 | tf_op jit(solution)/shard_map/ppermute | solution.py:247
  87.7 1.3 %collective-permute-start.11 = (bf16[1,128,640]{2,1,0:T(8,128)(2,1)S(1)}, bf16[1,128,640]{2,1,0:T(8,128)(2,1)S(1)}, u32[]{:S(2)}, u32[]{:S(2)}) collective-permute-start(bf16[1,128,640]{2,1,0:T(8,128)(2,1)S(1)} %add_convert_fusion), channel_id=1, source_target_pairs={{1,0},{3,2},{5,4},{7,6},{9,8},{11,10},{13,12},{15,14},{17,16},{19,... | collective-permute-start | bytes 491528 | tf_op jit(solution)/shard_map/ppermute | solution.py:247
  (102 shorter events, 17.9 us)
Async XLA Ops:
  0.6 45.7 %copy-start = (bf16[1,640,1280]{2,1,0:T(8,128)(2,1)S(1)}, bf16[1,640,1280]{2,1,0:T(8,128)(2,1)}, u32[]{:S(2)}) copy-start(bf16[1,640,1280]{2,1,0:T(8,128)(2,1)} %param.15) | copy-start | bytes 4915204
  0.6 3.7 %copy-start.1 = (bf16[2,64,4096]{2,1,0:T(8,128)(2,1)S(1)}, bf16[2,64,4096]{2,1,0:T(8,128)(2,1)}, u32[]{:S(2)}) copy-start(bf16[2,64,4096]{2,1,0:T(8,128)(2,1)} %param.8) | copy-start | bytes 3145732
  0.7 9.4 %copy-start.2 = (bf16[1,1280]{1,0:T(2,128)(2,1)S(1)}, bf16[1,1280]{1,0:T(2,128)(2,1)}, u32[]{:S(2)}) copy-start(bf16[1,1280]{1,0:T(2,128)(2,1)} %param.11) | copy-start | bytes 7684
  4.9 10.1 %collective-permute-start = (f32[2,64,34]{1,0,2:T(2,128)S(1)}, f32[2,64,34]{1,0,2:T(2,128)S(1)}, u32[]{:S(2)}, u32[]{:S(2)}) collective-permute-start(f32[2,64,34]{1,0,2:T(2,128)S(1)} %pad_maximum_fusion.1), channel_id=1, source_target_pairs={{0,4},{4,8},{8,12},{12,0},{1,5},{5,9},{9,13},{13,1},{2,6},{6,10},{... | collective-permute-start | bytes 52232 | tf_op jit(solution)/shard_map/ppermute | solution.py:13
  7.1 7.9 %collective-permute-start.2 = (f32[2,64,34]{1,0,2:T(2,128)S(1)}, f32[2,64,34]{1,0,2:T(2,128)S(1)}, u32[]{:S(2)}, u32[]{:S(2)}) collective-permute-start(f32[2,64,34]{1,0,2:T(2,128)S(1)} %pad_maximum_fusion.1), channel_id=1, source_target_pairs={{0,12},{4,0},{8,4},{12,8},{1,13},{5,1},{9,5},{13,9},{2,14},{6,2},{... | collective-permute-start | bytes 52232 | tf_op jit(solution)/shard_map/ppermute | solution.py:13
  9.2 5.9 %collective-permute-start.1 = (f32[2,64,34]{1,0,2:T(2,128)S(1)}, f32[2,64,34]{1,0,2:T(2,128)S(1)}, u32[]{:S(2)}, u32[]{:S(2)}) collective-permute-start(f32[2,64,34]{1,0,2:T(2,128)S(1)} %pad_maximum_fusion.1), channel_id=1, source_target_pairs={{0,8},{4,12},{8,0},{12,4},{1,9},{5,13},{9,1},{13,5},{2,10},{6,14},... | collective-permute-start | bytes 52232 | tf_op jit(solution)/shard_map/ppermute | solution.py:13
  36.7 5.1 %copy-start.3 = (bf16[1,1280,640]{2,1,0:T(8,128)(2,1)S(1)}, bf16[1,1280,640]{2,1,0:T(8,128)(2,1)}, u32[]{:S(2)}) copy-start(bf16[1,1280,640]{2,1,0:T(8,128)(2,1)} %param.12) | copy-start | bytes 4915204
  38.4 4.3 %collective-permute-start.5 = (bf16[2,2,2,80,128]{4,3,2,1,0:T(8,128)(2,1)S(1)}, bf16[2,2,2,80,128]{4,3,2,1,0:T(8,128)(2,1)S(1)}, u32[]{:S(2)}, u32[]{:S(2)}) collective-permute-start(bf16[2,2,2,80,128]{4,3,2,1,0:T(8,128)(2,1)S(1)} %bitcast.187), channel_id=1, source_target_pairs={{0,4},{4,8},{8,12},{2,6},{6,10},{10,14},{16,20},{20,24},{24,28},{1... | collective-permute-start | bytes 491528 | tf_op jit(solution)/shard_map/ppermute | solution.py:34
  39.1 3.6 %collective-permute-start.4 = (bf16[2,2,2,80,128]{4,3,2,1,0:T(8,128)(2,1)S(1)}, bf16[2,2,2,80,128]{4,3,2,1,0:T(8,128)(2,1)}, u32[]{:S(2)}, u32[]{:S(2)}) collective-permute-start(bf16[2,2,2,80,128]{4,3,2,1,0:T(8,128)(2,1)S(1)} %bitcast.188), channel_id=1, source_target_pairs={{0,8},{4,12},{2,10},{6,14},{16,24},{20,28},{18,26},{22,30}} | collective-permute-start | bytes 491528 | tf_op jit(solution)/shard_map/ppermute | solution.py:34
  40.4 2.3 %collective-permute-start.3 = (bf16[2,2,2,80,128]{4,3,2,1,0:T(8,128)(2,1)S(1)}, bf16[2,2,2,80,128]{4,3,2,1,0:T(8,128)(2,1)}, u32[]{:S(2)}, u32[]{:S(2)}) collective-permute-start(bf16[2,2,2,80,128]{4,3,2,1,0:T(8,128)(2,1)S(1)} %bitcast.189), channel_id=1, source_target_pairs={{0,12},{2,14},{16,28},{18,30}} | collective-permute-start | bytes 491528 | tf_op jit(solution)/shard_map/ppermute | solution.py:34
  47.1 16.3 %collective-permute-start.7 = (bf16[2,128,1280]{2,1,0:T(8,128)(2,1)S(1)}, bf16[2,128,1280]{2,1,0:T(8,128)(2,1)}, u32[]{:S(2)}, u32[]{:S(2)}) collective-permute-start(bf16[2,128,1280]{2,1,0:T(8,128)(2,1)S(1)} %convolution_convert_fusion), channel_id=1, source_target_pairs={{0,3},{2,1},{4,7},{6,5},{8,11},{10,9},{12,15},{14,13},{16,19},{18,... | collective-permute-start | bytes 1966088 | tf_op jit(solution)/shard_map/ppermute | solution.py:222
  48.4 15.0 %collective-permute-start.6 = (bf16[2,128,1280]{2,1,0:T(8,128)(2,1)S(1)}, bf16[2,128,1280]{2,1,0:T(8,128)(2,1)}, u32[]{:S(2)}, u32[]{:S(2)}) collective-permute-start(bf16[2,128,1280]{2,1,0:T(8,128)(2,1)S(1)} %convolution_convert_fusion), channel_id=1, source_target_pairs={{0,1},{2,3},{4,5},{6,7},{8,9},{10,11},{12,13},{14,15},{16,17},{18,... | collective-permute-start | bytes 1966088 | tf_op jit(solution)/shard_map/ppermute | solution.py:222
  49.7 15.4 %copy-start.5 = (bf16[1,1280,160]{1,2,0:T(8,128)(2,1)S(1)}, bf16[1,1280,160]{1,2,0:T(8,128)(2,1)}, u32[]{:S(2)}) copy-start(bf16[1,1280,160]{1,2,0:T(8,128)(2,1)} %param.14) | copy-start | bytes 1228804
  49.7 15.4 %copy-start.6 = (bf16[1,1280,160]{1,2,0:T(8,128)(2,1)S(1)}, bf16[1,1280,160]{1,2,0:T(8,128)(2,1)}, u32[]{:S(2)}) copy-start(bf16[1,1280,160]{1,2,0:T(8,128)(2,1)} %param.13) | copy-start | bytes 1228804
  65.1 11.9 %copy-start.4 = (bf16[1,1280,640]{2,1,0:T(8,128)(2,1)S(1)}, bf16[1,1280,640]{2,1,0:T(8,128)(2,1)}, u32[]{:S(2)}) copy-start(bf16[1,1280,640]{2,1,0:T(8,128)(2,1)} %param.12) | copy-start | bytes 4915204
  65.7 12.3 %collective-permute-start.10 = (bf16[2,2,2,80,128]{4,3,2,1,0:T(8,128)(2,1)S(1)}, bf16[2,2,2,80,128]{4,3,2,1,0:T(8,128)(2,1)}, u32[]{:S(2)}, u32[]{:S(2)}) collective-permute-start(bf16[2,2,2,80,128]{4,3,2,1,0:T(8,128)(2,1)S(1)} %bitcast.192), channel_id=1, source_target_pairs={{1,5},{5,9},{9,13},{3,7},{7,11},{11,15},{17,21},{21,25},{25,29},{1... | collective-permute-start | bytes 491528 | tf_op jit(solution)/shard_map/ppermute | solution.py:34
  69.9 8.1 %collective-permute-start.9 = (bf16[2,2,2,80,128]{4,3,2,1,0:T(8,128)(2,1)S(1)}, bf16[2,2,2,80,128]{4,3,2,1,0:T(8,128)(2,1)}, u32[]{:S(2)}, u32[]{:S(2)}) collective-permute-start(bf16[2,2,2,80,128]{4,3,2,1,0:T(8,128)(2,1)S(1)} %bitcast.193), channel_id=1, source_target_pairs={{1,9},{5,13},{3,11},{7,15},{17,25},{21,29},{19,27},{23,31}} | collective-permute-start | bytes 491528 | tf_op jit(solution)/shard_map/ppermute | solution.py:34
  75.0 3.5 %collective-permute-start.8 = (bf16[2,2,2,80,128]{4,3,2,1,0:T(8,128)(2,1)S(1)}, bf16[2,2,2,80,128]{4,3,2,1,0:T(8,128)(2,1)}, u32[]{:S(2)}, u32[]{:S(2)}) collective-permute-start(bf16[2,2,2,80,128]{4,3,2,1,0:T(8,128)(2,1)S(1)} %bitcast.194), channel_id=1, source_target_pairs={{1,13},{3,15},{17,29},{19,31}} | collective-permute-start | bytes 491528 | tf_op jit(solution)/shard_map/ppermute | solution.py:34
  83.1 6.6 %collective-permute-start.13 = (bf16[1,128,640]{2,1,0:T(8,128)(2,1)S(1)}, bf16[1,128,640]{2,1,0:T(8,128)(2,1)S(1)}, u32[]{:S(2)}, u32[]{:S(2)}) collective-permute-start(bf16[1,128,640]{2,1,0:T(8,128)(2,1)S(1)} %dynamic-slice_convert_fusion), channel_id=1, source_target_pairs={{1,3},{3,1},{5,7},{7,5},{9,11},{11,9},{13,15},{15,13},{17,19},{19,... | collective-permute-start | bytes 491528 | tf_op jit(solution)/shard_map/ppermute | solution.py:251
  86.3 4.0 %collective-permute-start.12 = (bf16[1,128,640]{2,1,0:T(8,128)(2,1)S(1)}, bf16[1,128,640]{2,1,0:T(8,128)(2,1)S(1)}, u32[]{:S(2)}, u32[]{:S(2)}) collective-permute-start(bf16[1,128,640]{2,1,0:T(8,128)(2,1)S(1)} %dynamic-slice_convert_fusion.1), channel_id=1, source_target_pairs={{1,2},{3,0},{5,6},{7,4},{9,10},{11,8},{13,14},{15,12},{17,18},{19,... | collective-permute-start | bytes 491528 | tf_op jit(solution)/shard_map/ppermute | solution.py:247
  87.7 2.6 %collective-permute-start.11 = (bf16[1,128,640]{2,1,0:T(8,128)(2,1)S(1)}, bf16[1,128,640]{2,1,0:T(8,128)(2,1)S(1)}, u32[]{:S(2)}, u32[]{:S(2)}) collective-permute-start(bf16[1,128,640]{2,1,0:T(8,128)(2,1)S(1)} %add_convert_fusion), channel_id=1, source_target_pairs={{1,0},{3,2},{5,4},{7,6},{9,8},{11,10},{13,12},{15,14},{17,16},{19,... | collective-permute-start | bytes 491528 | tf_op jit(solution)/shard_map/ppermute | solution.py:247
